TPU v7x, 512 devices: a whole 4x8x8 slice. The times are simulated.
512 devices in a mesh: region: 8 (over z), dom: 64 (over y, x, core).
Axes of the slice: x: 4, y: 8, z: 8, core: 2. Of those that a mesh axis runs over, the one named last changes fastest.
Arguments:
- gauges: bfloat16 [524288, 384], P(('region', 'dom')), may hold values from -24 to 24
- couplings: bfloat16 [4096, 3, 128, 128], P(('region', 'dom')), may hold values from -0.3125 to 0.3125
- adjacency: int32 [4096, 3], P(('region', 'dom')), may hold values from 0 to 15
- send_list: int32 [1024], P(('region', 'dom')), may hold values from 0 to 7
- coverage: int32 [4096, 2], P(('region', 'dom')), may hold values from 0 to 4
- positive: int32 [524288], P(('region', 'dom')), may hold values from 0 to 255
- patches: bfloat16 [65536, 512], P(('region', 'dom')), may hold values from -24 to 24
- message_weight: bfloat16 [384, 384], replicated, may hold values from -0.3125 to 0.3125
- self_weight: bfloat16 [384, 384], replicated, may hold values from -0.3125 to 0.3125
- output_weight: bfloat16 [384, 512], replicated, may hold values from -0.3125 to 0.3125
- patch_weight: bfloat16 [512, 512], replicated, may hold values from -0.25 to 0.25
Outputs:
- grad_message: bfloat16 [384, 384], P('dom')
- grad_self: bfloat16 [384, 384], P('dom')
- grad_output: bfloat16 [384, 512], P('dom')
- grad_patch: bfloat16 [512, 512], P('dom')
Inputs may be any that keep to these rules, and one draw needn't show every extreme that they name: `adjacency`: indexes the partition's block table of 16 entries. `send_list`: indexes the partition's own blocks. `coverage`: indexes the partition's patch table of 5 entries.
All inputs are finite; a program needn't handle non-finite values.
Results may differ from a plain program's by a relative error of at most 0.015.
Values may be sent and summed in bfloat16 or wider, within the bound.
No kernel may reach another device: no remote copies, remote signals or barrier semaphores. Data moves between devices by JAX's collectives and lax.ppermute only.
A program may use at most 64 MiB of HBM per device.

v0:
```python
import math

import jax
import jax.numpy as jnp
from jax import lax
from jax.sharding import PartitionSpec as P

BLOCK = 128


loss_gain = 16.0
offsets_by = (1, 2, -1, -2)


def passed_along(shard, axis, by):
    count = lax.axis_size(axis)
    return lax.ppermute(shard, axis, [(i, (i + by) % count) for i in range(count)])


def silu_slope(argument):
    sigmoid_v = jax.nn.sigmoid(argument)
    return sigmoid_v * (1.0 + argument * (1.0 - sigmoid_v))


def boundary_table(blocks, send_list):
    outgoing = blocks[send_list]
    pieces = [blocks]
    for step_by in offsets_by:
        pieces.append(passed_along(outgoing, "dom", step_by))
    return jnp.concatenate(pieces, axis=0)


def patch_table_near(patch_blocks):
    pieces = [patch_blocks]
    for step_by in offsets_by:
        pieces.append(passed_along(patch_blocks, "dom", step_by))
    return jnp.concatenate(pieces, axis=0)


def shards(
    gauges,
    couplings,
    adjacency,
    send_list,
    coverage,
    positive,
    patches,
    message_weight,
    self_weight,
    output_weight,
    patch_weight,
):
    f32 = jnp.float32
    bf16 = jnp.bfloat16
    width = gauges.shape[1]
    wide = patches.shape[1]
    count = couplings.shape[0]
    blocks = gauges.reshape(count, BLOCK, width)
    block_table = boundary_table(blocks, send_list)
    picked = block_table[adjacency]
    message = (
        jnp.einsum("bkij,bkjd->bid", couplings, picked, preferred_element_type=f32)
        .astype(bf16)
        .reshape(-1, width)
    )
    pre_act = jnp.dot(message, message_weight, preferred_element_type=f32) + jnp.dot(
        gauges, self_weight, preferred_element_type=f32
    )
    hidden = (gauges.astype(f32) + jax.nn.silu(pre_act)).astype(bf16)
    queries = jnp.dot(hidden, output_weight, preferred_element_type=f32).astype(bf16)
    patch_blocks = patches.reshape(-1, BLOCK, wide)
    covered = patch_table_near(patch_blocks)[coverage]
    flat_cover = covered.reshape(-1, wide)
    key_rows = (
        jnp.dot(flat_cover, patch_weight, preferred_element_type=f32)
        .astype(bf16)
        .reshape(count, -1, wide)
    )
    query_blocks = queries.reshape(count, BLOCK, wide)
    inv_root = 1.0 / math.sqrt(wide)
    logits = (
        jnp.einsum("bie,bje->bij", query_blocks, key_rows, preferred_element_type=f32) * inv_root
    )
    soft = jax.nn.softmax(logits, axis=-1)
    columns = jnp.arange(logits.shape[2], dtype=jnp.int32)
    target = (positive.reshape(count, BLOCK)[:, :, None] == columns).astype(f32)
    total_gauges = gauges.shape[0] * lax.axis_size("region") * lax.axis_size("dom")
    loss_scale = loss_gain / math.sqrt(total_gauges)
    logit_grad = ((soft - target) * loss_scale).astype(bf16)
    query_grad = (
        (jnp.einsum("bij,bje->bie", logit_grad, key_rows, preferred_element_type=f32) * inv_root)
        .astype(bf16)
        .reshape(-1, wide)
    )
    key_grad = (
        (
            jnp.einsum("bij,bie->bje", logit_grad, query_blocks, preferred_element_type=f32)
            * inv_root
        )
        .astype(bf16)
        .reshape(-1, wide)
    )
    grad_patch = jnp.dot(flat_cover.T, key_grad, preferred_element_type=f32)
    grad_output = jnp.dot(hidden.T, query_grad, preferred_element_type=f32)
    hidden_grad = jnp.dot(query_grad, output_weight.T, preferred_element_type=f32)
    act_grad = (hidden_grad * silu_slope(pre_act)).astype(bf16)
    grad_message = jnp.dot(message.T, act_grad, preferred_element_type=f32)
    grad_self = jnp.dot(gauges.T, act_grad, preferred_element_type=f32)
    summed = (
        lax.psum(grad_message.astype(jnp.bfloat16), "region").astype(jnp.float32),
        lax.psum(grad_self.astype(jnp.bfloat16), "region").astype(jnp.float32),
        lax.psum(grad_output.astype(jnp.bfloat16), "region").astype(jnp.float32),
        lax.psum(grad_patch.astype(jnp.bfloat16), "region").astype(jnp.float32),
    )
    shares = (
        lax.psum_scatter(summed[0], "dom", scatter_dimension=0, tiled=True),
        lax.psum_scatter(summed[1], "dom", scatter_dimension=0, tiled=True),
        lax.psum_scatter(summed[2], "dom", scatter_dimension=0, tiled=True),
        lax.psum_scatter(summed[3], "dom", scatter_dimension=0, tiled=True),
    )
    return (
        shares[0].astype(bf16),
        shares[1].astype(bf16),
        shares[2].astype(bf16),
        shares[3].astype(bf16),
    )


def solution(mesh):
    placed = (
        P(("region", "dom"), None),
        P(("region", "dom"), None, None, None),
        P(("region", "dom"), None),
        P(("region", "dom")),
        P(("region", "dom"), None),
        P(("region", "dom")),
        P(("region", "dom"), None),
        P(),
        P(),
        P(),
        P(),
    )
    return jax.shard_map(
        shards,
        mesh=mesh,
        in_specs=placed,
        out_specs=(P("dom", None), P("dom", None), P("dom", None), P("dom", None)),
        check_vma=False,
    )
```

profile of v0, /device:TPU:6, one launch (start us, length us, event | category | flops | bytes accessed | tf_op | source)
XLA Modules:
  0.0 388.1 jit_solution(838861163296844405)
XLA Ops:
  8.0 2.4 gather_fusion
  10.4 1.9 collective-permute-start
  12.3 3.4 collective-permute-start.1
  15.7 3.4 collective-permute-start.2
  19.1 1.9 collective-permute-start.4
  21.0 5.5 %collective-permute-start.5 = (bf16[1,128,512]{2,1,0:T(8,128)(2,1)}, bf16[1,128,512]{2,1,0:T(8,128)(2,1)S(1)}, u32[]{:S(2)}, u32[]{:S(2)}) collective-permute-start(bf16[1,128,512]{2,1,0:T(8,128)(2,1)} %bitcast.58), channel_id=1, source_target_pairs={{0,2},{1,3},{2,4},{3,5},{4,6},{5,7},{6,8},{7,9},{8,10},{9,11},{10,... | collective-permute-start | bytes 393224 | tf_op jit(solution)/shard_map/ppermute | solution.py:17
  26.5 2.1 constant_dynamic-update-slice_fusion.4
  30.0 3.4 collective-permute-start.6
  33.4 1.9 collective-permute-start.7
  35.8 3.5 collective-permute-start.3
  39.3 3.0 collective-permute-done.7
  43.0 4.0 %convolution_convert_fusion = bf16[2048,512]{1,0:T(8,128)(2,1)} fusion(bf16[2048,512]{1,0:T(8,128)(2,1)S(1)} %bitcast.48, bf16[512,512]{1,0:T(8,128)(2,1)} %param.21), kind=kOutput, calls=%fused_computation.6 | convolution fusion | flops 1074790400 | bytes 4718592 | tf_op jit(solution)/shard_map/dot_general | solution.py:75
  47.0 1.6 constant_dynamic-update-slice_fusion.3
  48.7 1.6 constant_dynamic-update-slice_fusion.2
  50.3 1.6 constant_dynamic-update-slice_fusion.1
  51.9 1.6 constant_dynamic-update-slice_fusion
  53.6 2.5 gather_fusion.1
  58.3 2.0 add_convert_fusion
  61.1 5.9 %multiply_convert_fusion.1 = bf16[8,128,512]{2,1,0:T(8,128)(2,1)} fusion(bf16[8,256,512]{2,1,0:T(8,128)(2,1)} %bitcast.63, s32[8,128]{1,0:T(8,128)S(1)} %bitcast.61, bf16[8,128,512]{2,1,0:T(8,128)(2,1)S(1)} %bitcast.55), kind=kOutput, calls=%fused_computation.7 | convolution fusion | flops 540019200 | bytes 4198400 | tf_op jit(solution)/shard_map/bij,bje->bie/dot_general | solution.py:91
  67.0 2.7 convolution_convert_fusion.3
  69.6 2.4 multiply_convert_fusion.2
  72.1 1.3 convolution_convert_fusion.5
  73.4 1.3 fusion.8
  74.7 6.1 %multiply_convert_fusion = bf16[8,256,512]{2,1,0:T(8,128)(2,1)} fusion(bf16[8,128,512]{2,1,0:T(8,128)(2,1)} %bitcast.56, s32[8,128]{1,0:T(8,128)S(1)} %bitcast.62, bf16[8,256,512]{2,1,0:T(8,128)(2,1)} %bitcast.64), kind=kOutput, calls=%fused_computation.5 | convolution fusion | flops 541067776 | bytes 5246976 | tf_op jit(solution)/shard_map/bij,bie->bje/dot_general | solution.py:97
  80.8 3.7 convolution_convert_fusion.2
  84.5 90.5 %all-reduce.11.cloned.1.call-done = (bf16[384,384]{1,0:T(8,128)(2,1)}, bf16[384,384]{0,1:T(8,128)(2,1)}, bf16[384,512]{1,0:T(8,128)(2,1)}, bf16[512,512]{1,0:T(8,128)(2,1)}) async-done(((bf16[384,384]{1,0:T(8,128)(2,1)}, bf16[384,384]{0,1:T(8,128)(2,1)}, bf16[384,512]{1,0:T(8,128)(2,1)}, bf16[512,512]{1,0:T(8,128)(2,1)}), (bf16[384,384]{1,0:T(8,128)(2,1)}, bf16[384,384]{0,1:T(8,128)(2,1)}, ...) | async-done | bytes 1507344 | tf_op jit(solution)/shard_map/psum | solution.py:110
  175.1 1.3 dynamic-slice
  177.6 198.0 %all-reduce.9.cloned.1.call-done = (bf16[384,384]{1,0:T(8,128)(2,1)}, bf16[384,384]{0,1:T(8,128)(2,1)}, bf16[384,512]{1,0:T(8,128)(2,1)}, bf16[512,512]{1,0:T(8,128)(2,1)}) async-done(((bf16[384,384]{1,0:T(8,128)(2,1)}, bf16[384,384]{0,1:T(8,128)(2,1)}, bf16[384,512]{1,0:T(8,128)(2,1)}, bf16[512,512]{1,0:T(8,128)(2,1)}), (bf16[384,384]{1,0:T(8,128)(2,1)}, bf16[384,384]{0,1:T(8,128)(2,1)}, ...) | async-done | bytes 1507344
  375.6 1.0 dynamic-slice_convert_fusion
  377.3 1.3 dynamic-slice_convert_fusion.2
  378.7 1.3 dynamic-slice_convert_fusion.3
  380.0 1.3 dynamic-slice_convert_fusion.1
  (63 shorter events, 7.0 us)
Async XLA Ops:
  7.2 49.0 %copy-start = (bf16[8,3,128,128]{3,2,1,0:T(8,128)(2,1)S(1)}, bf16[8,3,128,128]{3,2,1,0:T(8,128)(2,1)}, u32[]{:S(2)}) copy-start(bf16[8,3,128,128]{3,2,1,0:T(8,128)(2,1)} %param.12) | copy-start | bytes 2359300
  7.2 22.8 %copy-start.10 = (bf16[128,512]{1,0:T(8,128)(2,1)S(1)}, bf16[128,512]{1,0:T(8,128)(2,1)}, u32[]{:S(2)}) copy-start(bf16[128,512]{1,0:T(8,128)(2,1)} %param.17) | copy-start | bytes 393220
  7.2 22.4 %copy-start.11 = (s32[8,3]{0,1:T(4,128)S(1)}, s32[8,3]{0,1:T(4,128)}, u32[]{:S(2)}) copy-start(s32[8,3]{0,1:T(4,128)} %param.13) | copy-start | bytes 292
  7.2 22.5 %copy-start.12 = (s32[8,2]{0,1:T(2,128)S(1)}, s32[8,2]{0,1:T(2,128)}, u32[]{:S(2)}) copy-start(s32[8,2]{0,1:T(2,128)} %param.15) | copy-start | bytes 196
  7.2 167.8 %all-reduce.11.cloned.1.call-start = ((), (), s32[]{:S(2)}) async-start(), calls=%async_computation.1 | async-start | bytes 3014656 | tf_op jit(solution)/shard_map/psum | solution.py:110
  10.4 36.6 %collective-permute-start = (bf16[2,128,384]{2,1,0:T(8,128)(2,1)}, bf16[2,128,384]{2,1,0:T(8,128)(2,1)}, u32[]{:S(2)}, u32[]{:S(2)}) collective-permute-start(bf16[2,128,384]{2,1,0:T(8,128)(2,1)} %gather_fusion), channel_id=1, source_target_pairs={{0,1},{1,2},{2,3},{3,4},{4,5},{5,6},{6,7},{7,8},{8,9},{9,10},{10,1... | collective-permute-start | bytes 589832 | tf_op jit(solution)/shard_map/ppermute | solution.py:17
  12.3 36.4 %collective-permute-start.1 = (bf16[2,128,384]{2,1,0:T(8,128)(2,1)}, bf16[2,128,384]{2,1,0:T(8,128)(2,1)}, u32[]{:S(2)}, u32[]{:S(2)}) collective-permute-start(bf16[2,128,384]{2,1,0:T(8,128)(2,1)} %gather_fusion), channel_id=1, source_target_pairs={{0,2},{1,3},{2,4},{3,5},{4,6},{5,7},{6,8},{7,9},{8,10},{9,11},{10,... | collective-permute-start | bytes 589832 | tf_op jit(solution)/shard_map/ppermute | solution.py:17
  15.7 34.6 %collective-permute-start.2 = (bf16[2,128,384]{2,1,0:T(8,128)(2,1)}, bf16[2,128,384]{2,1,0:T(8,128)(2,1)}, u32[]{:S(2)}, u32[]{:S(2)}) collective-permute-start(bf16[2,128,384]{2,1,0:T(8,128)(2,1)} %gather_fusion), channel_id=1, source_target_pairs={{0,63},{1,0},{2,1},{3,2},{4,3},{5,4},{6,5},{7,6},{8,7},{9,8},{10,9... | collective-permute-start | bytes 589832 | tf_op jit(solution)/shard_map/ppermute | solution.py:17
  19.1 10.8 %collective-permute-start.4 = (bf16[1,128,512]{2,1,0:T(8,128)(2,1)}, bf16[1,128,512]{2,1,0:T(8,128)(2,1)S(1)}, u32[]{:S(2)}, u32[]{:S(2)}) collective-permute-start(bf16[1,128,512]{2,1,0:T(8,128)(2,1)} %bitcast.57), channel_id=1, source_target_pairs={{0,1},{1,2},{2,3},{3,4},{4,5},{5,6},{6,7},{7,8},{8,9},{9,10},{10,1... | collective-permute-start | bytes 393224 | tf_op jit(solution)/shard_map/ppermute | solution.py:17
  21.0 12.3 %collective-permute-start.5 = (bf16[1,128,512]{2,1,0:T(8,128)(2,1)}, bf16[1,128,512]{2,1,0:T(8,128)(2,1)S(1)}, u32[]{:S(2)}, u32[]{:S(2)}) collective-permute-start(bf16[1,128,512]{2,1,0:T(8,128)(2,1)} %bitcast.58), channel_id=1, source_target_pairs={{0,2},{1,3},{2,4},{3,5},{4,6},{5,7},{6,8},{7,9},{8,10},{9,11},{10,... | collective-permute-start | bytes 393224 | tf_op jit(solution)/shard_map/ppermute | solution.py:17
  30.0 5.9 %collective-permute-start.6 = (bf16[1,128,512]{2,1,0:T(8,128)(2,1)S(1)}, bf16[1,128,512]{2,1,0:T(8,128)(2,1)S(1)}, u32[]{:S(2)}, u32[]{:S(2)}) collective-permute-start(bf16[1,128,512]{2,1,0:T(8,128)(2,1)S(1)} %bitcast.59), channel_id=1, source_target_pairs={{0,63},{1,0},{2,1},{3,2},{4,3},{5,4},{6,5},{7,6},{8,7},{9,8},{10,9... | collective-permute-start | bytes 393224 | tf_op jit(solution)/shard_map/ppermute | solution.py:17
  33.4 9.0 %collective-permute-start.7 = (bf16[1,128,512]{2,1,0:T(8,128)(2,1)S(1)}, bf16[1,128,512]{2,1,0:T(8,128)(2,1)S(1)}, u32[]{:S(2)}, u32[]{:S(2)}) collective-permute-start(bf16[1,128,512]{2,1,0:T(8,128)(2,1)S(1)} %bitcast.60), channel_id=1, source_target_pairs={{0,62},{1,63},{2,0},{3,1},{4,2},{5,3},{6,4},{7,5},{8,6},{9,7},{10,... | collective-permute-start | bytes 393224 | tf_op jit(solution)/shard_map/ppermute | solution.py:17
  35.8 16.1 %collective-permute-start.3 = (bf16[2,128,384]{2,1,0:T(8,128)(2,1)}, bf16[2,128,384]{2,1,0:T(8,128)(2,1)}, u32[]{:S(2)}, u32[]{:S(2)}) collective-permute-start(bf16[2,128,384]{2,1,0:T(8,128)(2,1)} %gather_fusion), channel_id=1, source_target_pairs={{0,62},{1,63},{2,0},{3,1},{4,2},{5,3},{6,4},{7,5},{8,6},{9,7},{10,... | collective-permute-start | bytes 589832 | tf_op jit(solution)/shard_map/ppermute | solution.py:17
  43.0 4.0 %copy-start.1 = (bf16[16,128,512]{2,1,0:T(8,128)(2,1)}, bf16[16,128,512]{2,1,0:T(8,128)(2,1)S(1)}, u32[]{:S(2)}) copy-start(bf16[16,128,512]{2,1,0:T(8,128)(2,1)S(1)} %gather_fusion.2) | copy-start | bytes 6291460
  56.1 1.0 copy-start.9
  56.8 3.5 copy-start.3
  56.8 1.4 copy-start.5
  56.8 1.5 copy-start.13
  58.3 2.0 copy-start.7
  60.4 0.7 copy-start.14
  61.1 5.9 %copy-start.6 = (bf16[1024,512]{1,0:T(8,128)(2,1)}, bf16[1024,512]{1,0:T(8,128)(2,1)S(1)}, u32[]{:S(2)}) copy-start(bf16[1024,512]{1,0:T(8,128)(2,1)S(1)} %convolution_convert_fusion.1) | copy-start | bytes 3145732
  67.0 2.7 copy-start.8
  67.0 2.7 copy-start.15
  69.6 2.4 copy-start.4
  74.7 6.1 %copy-start.2 = (bf16[16,128,512]{2,1,0:T(8,128)(2,1)S(1)}, bf16[16,128,512]{2,1,0:T(8,128)(2,1)}, u32[]{:S(2)}) copy-start(bf16[16,128,512]{2,1,0:T(8,128)(2,1)} %copy-done.1) | copy-start | bytes 6291460
  84.5 291.1 %all-reduce.9.cloned.1.call-start = ((), (), s32[]{:S(2)}) async-start(), calls=%async_computation | async-start | bytes 3014656
Sparse Core Ops, SparseCore 0:
  84.6 90.4 all-reduce.10
  178.8 196.7 all-reduce.8
where the time goes:
time: 391 us; the launch traced here: 388 us
  waiting for transfers between devices  292 us (75%)
  matrix products  31.3 us (8%)
  starting transfers between devices  25 us (6%)
  local copies, waits for them, and re-layouts  23.3 us (6%)
  between operations  15.7 us (4%)
    unnamed x3, waiting for transfers between devices  198 us
    psum x1, waiting for transfers between devices, shards(): lax.psum(grad_message.astype(jnp.bfloat16), 'region').astype(jnp.float32)  90.5 us
    ppermute x8, starting transfers between devices, passed_along(): lax.ppermute(shard, axis, [(i, (i + by) % count) for i in range(count)])  24.9 us
    unnamed x42, local copies, waits for them, and re-layouts  10.8 us
  transfers between devices with their start and end apart: 10, of which 4 were waited for; matrix products, arithmetic and copies ran while one was open for 4% of the time, Pallas kernels for 0%

commit v1 on v0

--- a/solution.py
+++ b/solution.py
@@ -10,6 +10,7 @@
 
 loss_gain = 16.0
 offsets_by = (1, 2, -1, -2)
+halving_bits = (0, 1, 3, 2, 4, 5)
 
 
 def passed_along(shard, axis, by):
@@ -17,24 +18,56 @@
     return lax.ppermute(shard, axis, [(i, (i + by) % count) for i in range(count)])
 
 
+def swapped(shard, axis, mask):
+    count = lax.axis_size(axis)
+    return lax.ppermute(shard, axis, [(i, i ^ mask) for i in range(count)])
+
+
 def silu_slope(argument):
     sigmoid_v = jax.nn.sigmoid(argument)
     return sigmoid_v * (1.0 + argument * (1.0 - sigmoid_v))
 
 
-def boundary_table(blocks, send_list):
+def neighbour_tables(blocks, send_list, patch_blocks):
     outgoing = blocks[send_list]
-    pieces = [blocks]
+    n_send = outgoing.shape[0]
+    gauge_size = outgoing.size
+    packed = jnp.concatenate([outgoing.reshape(-1), patch_blocks.reshape(-1)])
+    block_parts = [blocks]
+    patch_parts = [patch_blocks]
     for step_by in offsets_by:
-        pieces.append(passed_along(outgoing, "dom", step_by))
-    return jnp.concatenate(pieces, axis=0)
+        got = passed_along(packed, "dom", step_by)
+        block_parts.append(got[:gauge_size].reshape(n_send, BLOCK, blocks.shape[2]))
+        patch_parts.append(got[gauge_size:].reshape(patch_blocks.shape))
+    return jnp.concatenate(block_parts, axis=0), jnp.concatenate(patch_parts, axis=0)
 
 
-def patch_table_near(patch_blocks):
-    pieces = [patch_blocks]
-    for step_by in offsets_by:
-        pieces.append(passed_along(patch_blocks, "dom", step_by))
-    return jnp.concatenate(pieces, axis=0)
+def reduce_to_share(terms, n_dom):
+    flat = jnp.concatenate([t.reshape(n_dom, -1) for t in terms], axis=1)
+    n_bits = n_dom.bit_length() - 1
+    me = lax.axis_index("dom")
+    held = flat.reshape((2,) * n_bits + (flat.shape[1],))
+    axes = list(range(n_bits))
+    for bit in halving_bits[:n_bits]:
+        pos = axes.index(n_bits - 1 - bit)
+        mine_bit = (me >> bit) & 1
+        mine = lax.dynamic_index_in_dim(held, mine_bit, pos, keepdims=False)
+        other = lax.dynamic_index_in_dim(held, 1 - mine_bit, pos, keepdims=False)
+        held = mine + swapped(other, "dom", 1 << bit)
+        axes.pop(pos)
+    share = held.reshape(-1)
+    n_region = lax.axis_size("region")
+    step = 1
+    while step < n_region:
+        share = share + swapped(share, "region", step)
+        step *= 2
+    pieces = []
+    start = 0
+    for t in terms:
+        size = t.size // n_dom
+        pieces.append(share[start : start + size].reshape(t.shape[0] // n_dom, t.shape[1]))
+        start += size
+    return pieces
 
 
 def shards(
@@ -56,7 +89,8 @@
     wide = patches.shape[1]
     count = couplings.shape[0]
     blocks = gauges.reshape(count, BLOCK, width)
-    block_table = boundary_table(blocks, send_list)
+    patch_blocks = patches.reshape(-1, BLOCK, wide)
+    block_table, patch_table = neighbour_tables(blocks, send_list, patch_blocks)
     picked = block_table[adjacency]
     message = (
         jnp.einsum("bkij,bkjd->bid", couplings, picked, preferred_element_type=f32)
@@ -68,14 +102,13 @@
     )
     hidden = (gauges.astype(f32) + jax.nn.silu(pre_act)).astype(bf16)
     queries = jnp.dot(hidden, output_weight, preferred_element_type=f32).astype(bf16)
-    patch_blocks = patches.reshape(-1, BLOCK, wide)
-    covered = patch_table_near(patch_blocks)[coverage]
-    flat_cover = covered.reshape(-1, wide)
-    key_rows = (
-        jnp.dot(flat_cover, patch_weight, preferred_element_type=f32)
+    table_keys = (
+        jnp.dot(patch_table.reshape(-1, wide), patch_weight, preferred_element_type=f32)
         .astype(bf16)
-        .reshape(count, -1, wide)
+        .reshape(patch_table.shape)
     )
+    key_rows = table_keys[coverage].reshape(count, -1, wide)
+    flat_cover = patch_table[coverage].reshape(-1, wide)
     query_blocks = queries.reshape(count, BLOCK, wide)
     inv_root = 1.0 / math.sqrt(wide)
     logits = (
@@ -106,24 +139,10 @@
     act_grad = (hidden_grad * silu_slope(pre_act)).astype(bf16)
     grad_message = jnp.dot(message.T, act_grad, preferred_element_type=f32)
     grad_self = jnp.dot(gauges.T, act_grad, preferred_element_type=f32)
-    summed = (
-        lax.psum(grad_message.astype(jnp.bfloat16), "region").astype(jnp.float32),
-        lax.psum(grad_self.astype(jnp.bfloat16), "region").astype(jnp.float32),
-        lax.psum(grad_output.astype(jnp.bfloat16), "region").astype(jnp.float32),
-        lax.psum(grad_patch.astype(jnp.bfloat16), "region").astype(jnp.float32),
+    shares = reduce_to_share(
+        [grad_message, grad_self, grad_output, grad_patch], lax.axis_size("dom")
     )
-    shares = (
-        lax.psum_scatter(summed[0], "dom", scatter_dimension=0, tiled=True),
-        lax.psum_scatter(summed[1], "dom", scatter_dimension=0, tiled=True),
-        lax.psum_scatter(summed[2], "dom", scatter_dimension=0, tiled=True),
-        lax.psum_scatter(summed[3], "dom", scatter_dimension=0, tiled=True),
-    )
-    return (
-        shares[0].astype(bf16),
-        shares[1].astype(bf16),
-        shares[2].astype(bf16),
-        shares[3].astype(bf16),
-    )
+    return tuple(s.astype(bf16) for s in shares)
 
 
 def solution(mesh):

time: 391 us -> 183 us (0.47)
  waiting for transfers between devices: 292 us -> 56.8 us
  starting transfers between devices: 25 us -> 57.7 us
  between operations: 15.7 us -> 1.3 us
  local copies, waits for them, and re-layouts: 23.3 us -> 35.7 us
  matrix products: 31.3 us -> 25.3 us
    unnamed x3 -> x0, waiting for transfers between devices: 198 us -> none
    psum x1 -> x0, waiting for transfers between devices: 90.5 us -> none  [shards(): lax.psum(grad_message.astype(jnp.bfloat16), 'region').astype(jnp.float32)]
    ppermute x0 -> x9, waiting for transfers between devices: none -> 52.2 us  [swapped(): return lax.ppermute(shard, axis, [(i, i ^ mask) for i in range(count)])]
    ppermute x0 -> x9, starting transfers between devices: none -> 45.7 us  [swapped(): return lax.ppermute(shard, axis, [(i, i ^ mask) for i in range(count)])]
    ppermute x8 -> x4, starting transfers between devices: 24.9 us -> 12 us  [passed_along(): lax.ppermute(shard, axis, [(i, (i + by) % count) for i in range(count)])]
    dynamic_slice x0 -> x5, local copies, waits for them, and re-layouts: none -> 5.04 us  [the longest x4 4.77 us: reduce_to_share(): mine = lax.dynamic_index_in_dim(held, mine_bit, pos, keepdims=False)]
    concatenate x2 -> x8, local copies, waits for them, and re-layouts: 1.64 us -> 5.69 us  [the longest x5 4.33 us: reduce_to_share(): flat = jnp.concatenate([t.reshape(n_dom, -1) for t in terms], axis=1)]
    unnamed x42 -> x53, local copies, waits for them, and re-layouts: 10.8 us -> 11.9 us
  transfers between devices with their start and end apart: 10 -> 13, of which waited for: 4 -> 12; matrix products, arithmetic and copies ran while one was open for 4% -> 2% of each run, Pallas kernels for 0% -> 0%
where the time goes in v1:
time: 183 us; the launch traced here: 181 us
  starting transfers between devices  57.7 us (32%)
  waiting for transfers between devices  56.8 us (31%)
  local copies, waits for them, and re-layouts  35.7 us (20%)
  matrix products  25.3 us (14%)
  other arithmetic  4.16 us (2%)
    ppermute x9, waiting for transfers between devices, swapped(): return lax.ppermute(shard, axis, [(i, i ^ mask) for i in range(count)])  52.2 us
    ppermute x9, starting transfers between devices, swapped(): return lax.ppermute(shard, axis, [(i, i ^ mask) for i in range(count)])  45.7 us
    ppermute x4, starting transfers between devices, passed_along(): lax.ppermute(shard, axis, [(i, (i + by) % count) for i in range(count)])  12 us
    unnamed x53, local copies, waits for them, and re-layouts  11.9 us
    dot_general x1, matrix products, shards(): jnp.einsum('bij,bie->bje', logit_grad, query_blocks, preferred_element_ty...  5.25 us
    dynamic_slice x4, local copies, waits for them, and re-layouts, reduce_to_share(): mine = lax.dynamic_index_in_dim(held, mine_bit, pos, keepdims=False)  4.77 us
    dot_general x1, matrix products, shards(): grad_patch = jnp.dot(flat_cover.T, key_grad, preferred_element_type=f32)  4.67 us
    ppermute x4, waiting for transfers between devices, passed_along(): lax.ppermute(shard, axis, [(i, (i + by) % count) for i in range(count)])  4.64 us
  transfers between devices with their start and end apart: 13, of which 12 were waited for; matrix products, arithmetic and copies ran while one was open for 2% of the time, Pallas kernels for 0%

profile of v1, /device:TPU:6, one launch (start us, length us, event | category | flops | bytes accessed | tf_op | source)
XLA Modules:
  0.0 180.9 jit_solution(18375064343651515110)
XLA Ops:
  5.6 2.7 %collective-permute-start.3 = (bf16[163840]{0:T(1024)(128)(2,1)}, bf16[163840]{0:T(1024)(128)(2,1)S(1)}, u32[]{:S(2)}, u32[]{:S(2)}) collective-permute-start(bf16[163840]{0:T(1024)(128)(2,1)} %constant_dynamic-update-slice_fusion.14), channel_id=1, source_target_pairs={{0,62},{1,63},{2,0},{3,1},{4,2},{5,3},{6,4},{7,5},{8,6},{9,7},{10,... | collective-permute-start | bytes 983048 | tf_op jit(solution)/shard_map/ppermute | solution.py:18
  10.3 5.2 %collective-permute-start.1 = (bf16[163840]{0:T(1024)(128)(2,1)}, bf16[163840]{0:T(1024)(128)(2,1)S(1)}, u32[]{:S(2)}, u32[]{:S(2)}) collective-permute-start(bf16[163840]{0:T(1024)(128)(2,1)} %constant_dynamic-update-slice_fusion.14), channel_id=1, source_target_pairs={{0,2},{1,3},{2,4},{3,5},{4,6},{5,7},{6,8},{7,9},{8,10},{9,11},{10,... | collective-permute-start | bytes 983048 | tf_op jit(solution)/shard_map/ppermute | solution.py:18
  15.5 2.1 %collective-permute-start = (bf16[163840]{0:T(1024)(128)(2,1)}, bf16[163840]{0:T(1024)(128)(2,1)S(1)}, u32[]{:S(2)}, u32[]{:S(2)}) collective-permute-start(bf16[163840]{0:T(1024)(128)(2,1)} %constant_dynamic-update-slice_fusion.14), channel_id=1, source_target_pairs={{0,1},{1,2},{2,3},{3,4},{4,5},{5,6},{6,7},{7,8},{8,9},{9,10},{10,1... | collective-permute-start | bytes 983048 | tf_op jit(solution)/shard_map/ppermute | solution.py:18
  21.4 2.4 %collective-permute-done.1 = bf16[163840]{0:T(1024)(128)(2,1)S(1)} collective-permute-done((bf16[163840]{0:T(1024)(128)(2,1)}, bf16[163840]{0:T(1024)(128)(2,1)S(1)}, u32[]{:S(2)}, u32[]{:S(2)}) %collective-permute-start.1) | collective-permute-done | bytes 327712 | tf_op jit(solution)/shard_map/ppermute | solution.py:18
  24.0 1.9 %collective-permute-done = bf16[163840]{0:T(1024)(128)(2,1)S(1)} collective-permute-done((bf16[163840]{0:T(1024)(128)(2,1)}, bf16[163840]{0:T(1024)(128)(2,1)S(1)}, u32[]{:S(2)}, u32[]{:S(2)}) %collective-permute-start) | collective-permute-done | bytes 327712 | tf_op jit(solution)/shard_map/ppermute | solution.py:18
  26.3 2.0 %gather_fusion.3 = bf16[16,128,512]{2,1,0:T(8,128)(2,1)} fusion(bf16[5,128,512]{2,1,0:T(8,128)(2,1)S(1)} %constant_dynamic-update-slice_fusion.6, s32[1024]{0:T(1024)S(1)} %get-tuple-element.18), kind=kCustom, calls=%fused_computation.3 | custom fusion | bytes 4194368 | tf_op jit(solution)/shard_map/gather | solution.py:111
  29.9 2.0 %gather_fusion.2 = bf16[16,128,512]{2,1,0:T(8,128)(2,1)} fusion(bf16[5,128,512]{2,1,0:T(8,128)(2,1)S(1)} %bitcast.74, s32[1024]{0:T(1024)S(1)} %get-tuple-element.18), kind=kCustom, calls=%fused_computation.2 | custom fusion | bytes 4194368 | tf_op jit(solution)/shard_map/gather | solution.py:110
  34.7 2.5 %gather_fusion.1 = bf16[24,128,384]{2,1,0:T(8,128)(2,1)S(1)} fusion(bf16[16,128,384]{2,1,0:T(8,128)(2,1)} %constant_dynamic-update-slice_fusion.1, s32[1024]{0:T(1024)S(1)} %get-tuple-element.19), kind=kCustom, calls=%fused_computation.1 | custom fusion | bytes 4718688 | tf_op jit(solution)/shard_map/gather | solution.py:94
  39.4 2.1 %add_convert_fusion = (bf16[1024,384]{1,0:T(8,128)(2,1)S(1)}, f32[1024,384]{1,0:T(8,128)}) fusion(bf16[1024,384]{1,0:T(8,128)(2,1)S(1)} %copy-done.5, f32[1024,384]{1,0:T(8,128)S(1)} %fusion.19, bf16[384,384]{1,0:T(8,128)(2,1)S(1)} %copy-done.14), kind=kOutput, calls=%fused_computation.10 | convolution fusion | flops 305135616 | bytes 5013504 | tf_op jit(solution)/shard_map/dot_general | solution.py:100
  44.1 4.4 %multiply_convert_fusion.1 = bf16[8,128,512]{2,1,0:T(8,128)(2,1)} fusion(bf16[8,256,512]{2,1,0:T(8,128)(2,1)S(1)} %bitcast.78, s32[8,128]{1,0:T(8,128)S(1)} %bitcast.89, bf16[8,128,512]{2,1,0:T(8,128)(2,1)} %bitcast.82), kind=kOutput, calls=%fused_computation.7 | convolution fusion | flops 540019200 | bytes 4198400 | tf_op jit(solution)/shard_map/bij,bje->bie/dot_general | solution.py:124
  48.5 5.2 %multiply_convert_fusion = bf16[8,256,512]{2,1,0:T(8,128)(2,1)} fusion(bf16[8,128,512]{2,1,0:T(8,128)(2,1)} %bitcast.83, s32[8,128]{1,0:T(8,128)S(1)} %bitcast.90, bf16[8,256,512]{2,1,0:T(8,128)(2,1)S(1)} %bitcast.79), kind=kOutput, calls=%fused_computation.6 | convolution fusion | flops 541067776 | bytes 5246976 | tf_op jit(solution)/shard_map/bij,bie->bje/dot_general | solution.py:130
  53.8 2.2 %fusion.21 = f32[384,512]{1,0:T(8,128)S(1)} fusion(bf16[1024,384]{1,0:T(8,128)(2,1)} %copy-done.7, bf16[1024,512]{1,0:T(8,128)(2,1)} %bitcast.92), kind=kOutput, calls=%fused_computation.80 | convolution fusion | flops 402653184 | bytes 2621440 | tf_op jit(solution)/shard_map/dot_general | solution.py:137
  61.2 4.7 %fusion.22 = f32[512,512]{1,0:T(8,128)} fusion(bf16[2048,512]{1,0:T(8,128)(2,1)} %bitcast.77, bf16[2048,512]{1,0:T(8,128)(2,1)} %bitcast.91), kind=kOutput, calls=%fused_computation.81 | convolution fusion | flops 1073741824 | bytes 5242880 | tf_op jit(solution)/shard_map/dot_general | solution.py:136
  65.9 2.1 %concatenate.27 = f32[2,2,2,2,2,2,4096]{6,5,4,3,2,1,0:T(2,128)S(1)} reshape(f32[512,512]{1,0:T(8,128)} %fusion.22) | data formatting | bytes 2097152 | tf_op jit(solution)/shard_map/concatenate | solution.py:46
  69.5 2.9 %constant_dynamic-slice_fusion.7 = (f32[2,2,2,2,2,1,11776]{6,5,4,3,2,1,0:T(1,128)S(1)}, f32[2,2,2,2,2,1,11776]{6,5,4,3,2,1,0:T(1,128)S(1)}) fusion(f32[2,2,2,2,2,2,11776]{6,5,4,3,2,1,0:T(2,128)S(1)} %constant_dynamic-update-slice_fusion.10, s32[]{:T(128)S(6)} %select_n.55, s32[]{:T(128)S(6)} %select_n.56), kind=kLoop, calls=%fused_computation.71 | loop fusion | bytes 6029320 | tf_op jit(solution)/shard_map/jit(dynamic_index_in_dim)/dynamic_slice | solution.py:54
  74.4 2.9 %collective-permute-start.4 = (f32[2,2,2,2,2,11776]{5,4,3,2,1,0:T(2,128)}, f32[2,2,2,2,2,11776]{5,4,3,2,1,0:T(2,128)}, u32[]{:S(2)}, u32[]{:S(2)}) collective-permute-start(f32[2,2,2,2,2,11776]{5,4,3,2,1,0:T(2,128)} %bitcast.68), channel_id=1, source_target_pairs={{0,1},{1,0},{2,3},{3,2},{4,5},{5,4},{6,7},{7,6},{8,9},{9,8},{10,11... | collective-permute-start | bytes 4521992 | tf_op jit(solution)/shard_map/ppermute | solution.py:23
  77.3 3.3 %collective-permute-done.4 = f32[2,2,2,2,2,11776]{5,4,3,2,1,0:T(2,128)} collective-permute-done((f32[2,2,2,2,2,11776]{5,4,3,2,1,0:T(2,128)}, f32[2,2,2,2,2,11776]{5,4,3,2,1,0:T(2,128)}, u32[]{:S(2)}, u32[]{:S(2)}) %collective-permute-start.4) | collective-permute-done | bytes 1507360 | tf_op jit(solution)/shard_map/ppermute | solution.py:23
  80.6 2.4 %bitcast_add_fusion = f32[2,2,2,2,2,11776]{5,4,3,2,1,0:T(2,128)S(1)} fusion(f32[2,2,2,2,2,11776]{5,4,3,2,1,0:T(2,128)} %collective-permute-done.4, f32[2,2,2,2,2,1,11776]{6,5,4,3,2,1,0:T(1,128)S(1)} %get-tuple-element.6), kind=kLoop, calls=%fused_computation.13 | loop fusion | flops 376832 | bytes 4521984 | tf_op jit(solution)/shard_map/add | solution.py:56
  84.8 6.0 %collective-permute-start.5 = (f32[2,2,2,2,11776]{4,3,2,1,0:T(2,128)S(1)}, f32[2,2,2,2,11776]{4,3,2,1,0:T(2,128)S(1)}, u32[]{:S(2)}, u32[]{:S(2)}) collective-permute-start(f32[2,2,2,2,11776]{4,3,2,1,0:T(2,128)S(1)} %bitcast.84), channel_id=1, source_target_pairs={{0,2},{1,3},{2,0},{3,1},{4,6},{5,7},{6,4},{7,5},{8,10},{9,11},{10,... | collective-permute-start | bytes 2261000 | tf_op jit(solution)/shard_map/ppermute | solution.py:23
  90.7 17.1 %collective-permute-done.5 = f32[2,2,2,2,11776]{4,3,2,1,0:T(2,128)S(1)} collective-permute-done((f32[2,2,2,2,11776]{4,3,2,1,0:T(2,128)S(1)}, f32[2,2,2,2,11776]{4,3,2,1,0:T(2,128)S(1)}, u32[]{:S(2)}, u32[]{:S(2)}) %collective-permute-start.5) | collective-permute-done | bytes 753696 | tf_op jit(solution)/shard_map/ppermute | solution.py:23
  110.4 10.3 %collective-permute-done.6 = f32[2,2,2,11776]{3,2,1,0:T(2,128)S(1)} collective-permute-done((f32[2,2,2,11776]{3,2,1,0:T(2,128)S(1)}, f32[2,2,2,11776]{3,2,1,0:T(2,128)S(1)}, u32[]{:S(2)}, u32[]{:S(2)}) %collective-permute-start.6) | collective-permute-done | bytes 376864 | tf_op jit(solution)/shard_map/ppermute | solution.py:23
  121.3 7.3 %collective-permute-start.7 = (f32[2,2,11776]{2,1,0:T(2,128)S(1)}, f32[2,2,11776]{2,1,0:T(2,128)S(1)}, u32[]{:S(2)}, u32[]{:S(2)}) collective-permute-start(f32[2,2,11776]{2,1,0:T(2,128)S(1)} %bitcast.87), channel_id=1, source_target_pairs={{0,4},{1,5},{2,6},{3,7},{4,0},{5,1},{6,2},{7,3},{8,12},{9,13},{10,... | collective-permute-start | bytes 565256 | tf_op jit(solution)/shard_map/ppermute | solution.py:23
  128.6 3.6 %collective-permute-done.7 = f32[2,2,11776]{2,1,0:T(2,128)S(1)} collective-permute-done((f32[2,2,11776]{2,1,0:T(2,128)S(1)}, f32[2,2,11776]{2,1,0:T(2,128)S(1)}, u32[]{:S(2)}, u32[]{:S(2)}) %collective-permute-start.7) | collective-permute-done | bytes 188448 | tf_op jit(solution)/shard_map/ppermute | solution.py:23
  134.5 6.4 %collective-permute-done.8 = f32[2,11776]{1,0:T(2,128)S(1)} collective-permute-done((f32[2,11776]{1,0:T(2,128)S(1)}, f32[2,11776]{1,0:T(2,128)S(1)}, u32[]{:S(2)}, u32[]{:S(2)}) %collective-permute-start.8) | collective-permute-done | bytes 94240 | tf_op jit(solution)/shard_map/ppermute | solution.py:23
  141.2 4.6 %collective-permute-start.9 = (f32[11776]{0:T(1024)S(1)}, f32[11776]{0:T(1024)S(1)}, u32[]{:S(2)}, u32[]{:S(2)}) collective-permute-start(f32[11776]{0:T(1024)S(1)} %get-tuple-element.4), channel_id=1, source_target_pairs={{0,32},{1,33},{2,34},{3,35},{4,36},{5,37},{6,38},{7,39},{8,40},{9,... | collective-permute-start | bytes 141320 | tf_op jit(solution)/shard_map/ppermute | solution.py:23
  145.8 5.3 %collective-permute-done.9 = f32[11776]{0:T(1024)S(1)} collective-permute-done((f32[11776]{0:T(1024)S(1)}, f32[11776]{0:T(1024)S(1)}, u32[]{:S(2)}, u32[]{:S(2)}) %collective-permute-start.9) | collective-permute-done | bytes 47136 | tf_op jit(solution)/shard_map/ppermute | solution.py:23
  151.1 4.3 %collective-permute-start.10 = (f32[11776]{0:T(1024)S(1)}, f32[11776]{0:T(1024)S(1)}, u32[]{:S(2)}, u32[]{:S(2)}) collective-permute-start(f32[11776]{0:T(1024)S(1)} %add.123), channel_id=1, source_target_pairs={{0,64},{64,0},{128,192},{192,128},{256,320},{320,256},{384,448},{4... | collective-permute-start | bytes 141320 | tf_op jit(solution)/shard_map/ppermute | solution.py:23
  155.4 2.1 %collective-permute-done.10 = f32[11776]{0:T(1024)S(1)} collective-permute-done((f32[11776]{0:T(1024)S(1)}, f32[11776]{0:T(1024)S(1)}, u32[]{:S(2)}, u32[]{:S(2)}) %collective-permute-start.10) | collective-permute-done | bytes 47136 | tf_op jit(solution)/shard_map/ppermute | solution.py:23
  157.5 6.4 %collective-permute-start.11 = (f32[11776]{0:T(1024)S(1)}, f32[11776]{0:T(1024)S(1)}, u32[]{:S(2)}, u32[]{:S(2)}) collective-permute-start(f32[11776]{0:T(1024)S(1)} %add.124), channel_id=1, source_target_pairs={{0,128},{64,192},{128,0},{192,64},{256,384},{320,448},{384,256},{4... | collective-permute-start | bytes 141320 | tf_op jit(solution)/shard_map/ppermute | solution.py:23
  163.8 2.1 %collective-permute-done.11 = f32[11776]{0:T(1024)S(1)} collective-permute-done((f32[11776]{0:T(1024)S(1)}, f32[11776]{0:T(1024)S(1)}, u32[]{:S(2)}, u32[]{:S(2)}) %collective-permute-start.11) | collective-permute-done | bytes 47136 | tf_op jit(solution)/shard_map/ppermute | solution.py:23
  165.9 10.4 %collective-permute-start.12 = (f32[11776]{0:T(1024)S(1)}, f32[11776]{0:T(1024)S(1)}, u32[]{:S(2)}, u32[]{:S(2)}) collective-permute-start(f32[11776]{0:T(1024)S(1)} %add.125), channel_id=1, source_target_pairs={{0,256},{64,320},{128,384},{192,448},{256,0},{320,64},{384,128},{4... | collective-permute-start | bytes 141320 | tf_op jit(solution)/shard_map/ppermute | solution.py:23
  176.4 2.1 %collective-permute-done.12 = f32[11776]{0:T(1024)S(1)} collective-permute-done((f32[11776]{0:T(1024)S(1)}, f32[11776]{0:T(1024)S(1)}, u32[]{:S(2)}, u32[]{:S(2)}) %collective-permute-start.12) | collective-permute-done | bytes 47136 | tf_op jit(solution)/shard_map/ppermute | solution.py:23
  (120 shorter events, 38.6 us)
Async XLA Ops:
  0.6 36.6 %copy-start = (bf16[8,3,128,128]{3,2,1,0:T(8,128)(2,1)S(1)}, bf16[8,3,128,128]{3,2,1,0:T(8,128)(2,1)}, u32[]{:S(2)}) copy-start(bf16[8,3,128,128]{3,2,1,0:T(8,128)(2,1)} %param.12) | copy-start | bytes 2359300
  0.6 18.3 %copy-start.8 = (bf16[128,512]{1,0:T(8,128)(2,1)S(1)}, bf16[128,512]{1,0:T(8,128)(2,1)}, u32[]{:S(2)}) copy-start(bf16[128,512]{1,0:T(8,128)(2,1)} %param.17) | copy-start | bytes 393220
  0.7 17.0 %copy-start.4 = (bf16[1024,384]{1,0:T(8,128)(2,1)S(1)}, bf16[1024,384]{1,0:T(8,128)(2,1)}, u32[]{:S(2)}) copy-start(bf16[1024,384]{1,0:T(8,128)(2,1)} %param.11) | copy-start | bytes 2359300
  0.7 17.9 %copy-start.13 = (s32[8,2]{0,1:T(2,128)S(1)}, s32[8,2]{0,1:T(2,128)}, u32[]{:S(2)}) copy-start(s32[8,2]{0,1:T(2,128)} %param.15) | copy-start | bytes 196
  0.7 17.9 %copy-start.12 = (s32[8,3]{0,1:T(4,128)S(1)}, s32[8,3]{0,1:T(4,128)}, u32[]{:S(2)}) copy-start(s32[8,3]{0,1:T(4,128)} %param.13) | copy-start | bytes 292
  5.6 13.7 %collective-permute-start.3 = (bf16[163840]{0:T(1024)(128)(2,1)}, bf16[163840]{0:T(1024)(128)(2,1)S(1)}, u32[]{:S(2)}, u32[]{:S(2)}) collective-permute-start(bf16[163840]{0:T(1024)(128)(2,1)} %constant_dynamic-update-slice_fusion.14), channel_id=1, source_target_pairs={{0,62},{1,63},{2,0},{3,1},{4,2},{5,3},{6,4},{7,5},{8,6},{9,7},{10,... | collective-permute-start | bytes 983048 | tf_op jit(solution)/shard_map/ppermute | solution.py:18
  8.3 11.2 %collective-permute-start.2 = (bf16[163840]{0:T(1024)(128)(2,1)}, bf16[163840]{0:T(1024)(128)(2,1)S(1)}, u32[]{:S(2)}, u32[]{:S(2)}) collective-permute-start(bf16[163840]{0:T(1024)(128)(2,1)} %constant_dynamic-update-slice_fusion.14), channel_id=1, source_target_pairs={{0,63},{1,0},{2,1},{3,2},{4,3},{5,4},{6,5},{7,6},{8,7},{9,8},{10,9... | collective-permute-start | bytes 983048 | tf_op jit(solution)/shard_map/ppermute | solution.py:18
  10.3 13.5 %collective-permute-start.1 = (bf16[163840]{0:T(1024)(128)(2,1)}, bf16[163840]{0:T(1024)(128)(2,1)S(1)}, u32[]{:S(2)}, u32[]{:S(2)}) collective-permute-start(bf16[163840]{0:T(1024)(128)(2,1)} %constant_dynamic-update-slice_fusion.14), channel_id=1, source_target_pairs={{0,2},{1,3},{2,4},{3,5},{4,6},{5,7},{6,8},{7,9},{8,10},{9,11},{10,... | collective-permute-start | bytes 983048 | tf_op jit(solution)/shard_map/ppermute | solution.py:18
  15.5 10.5 %collective-permute-start = (bf16[163840]{0:T(1024)(128)(2,1)}, bf16[163840]{0:T(1024)(128)(2,1)S(1)}, u32[]{:S(2)}, u32[]{:S(2)}) collective-permute-start(bf16[163840]{0:T(1024)(128)(2,1)} %constant_dynamic-update-slice_fusion.14), channel_id=1, source_target_pairs={{0,1},{1,2},{2,3},{3,4},{4,5},{5,6},{6,7},{7,8},{8,9},{9,10},{10,1... | collective-permute-start | bytes 983048 | tf_op jit(solution)/shard_map/ppermute | solution.py:18
  19.5 0.7 copy-start.10
  37.2 1.0 copy-start.11
  37.9 3.6 %copy-start.1 = (bf16[8,384,128]{1,2,0:T(8,128)(2,1)}, bf16[8,384,128]{1,2,0:T(8,128)(2,1)S(1)}, u32[]{:S(2)}) copy-start(bf16[8,384,128]{1,2,0:T(8,128)(2,1)S(1)} %bitcast_convert_fusion) | copy-start | bytes 2359300
  37.9 1.4 copy-start.5
  37.9 1.5 copy-start.14
  39.4 3.0 %copy-start.9 = (bf16[384,512]{1,0:T(8,128)(2,1)S(1)}, bf16[384,512]{1,0:T(8,128)(2,1)}, u32[]{:S(2)}) copy-start(bf16[384,512]{1,0:T(8,128)(2,1)} %param.20) | copy-start | bytes 1179652
  41.5 0.9 copy-start.7
  41.5 2.6 %copy-start.3 = (bf16[16,128,512]{2,1,0:T(8,128)(2,1)S(1)}, bf16[16,128,512]{2,1,0:T(8,128)(2,1)}, u32[]{:S(2)}) copy-start(bf16[16,128,512]{2,1,0:T(8,128)(2,1)} %gather_fusion.2) | copy-start | bytes 6291460
  41.5 2.6 %copy-start.15 = (s32[1024]{0:T(1024)S(1)}, s32[1024]{0:T(1024)}, u32[]{:S(2)}) copy-start(s32[1024]{0:T(1024)} %param.16) | copy-start | bytes 12292
  53.8 2.2 %copy-start.16 = (bf16[8,128,512]{2,1,0:T(8,128)(2,1)S(1)}, bf16[8,128,512]{2,1,0:T(8,128)(2,1)}, u32[]{:S(2)}) copy-start(bf16[8,128,512]{2,1,0:T(8,128)(2,1)} %multiply_convert_fusion.1) | copy-start | bytes 3145732
  53.8 2.3 %copy-start.17 = (f32[1024,384]{1,0:T(8,128)S(1)}, f32[1024,384]{1,0:T(8,128)}, u32[]{:S(2)}) copy-start(f32[1024,384]{1,0:T(8,128)} %get-tuple-element.17) | copy-start | bytes 4718596
  56.0 1.1 copy-start.2
  57.2 1.1 copy-start.6
  74.4 6.2 %collective-permute-start.4 = (f32[2,2,2,2,2,11776]{5,4,3,2,1,0:T(2,128)}, f32[2,2,2,2,2,11776]{5,4,3,2,1,0:T(2,128)}, u32[]{:S(2)}, u32[]{:S(2)}) collective-permute-start(f32[2,2,2,2,2,11776]{5,4,3,2,1,0:T(2,128)} %bitcast.68), channel_id=1, source_target_pairs={{0,1},{1,0},{2,3},{3,2},{4,5},{5,4},{6,7},{7,6},{8,9},{9,8},{10,11... | collective-permute-start | bytes 4521992 | tf_op jit(solution)/shard_map/ppermute | solution.py:23
  84.8 23.1 %collective-permute-start.5 = (f32[2,2,2,2,11776]{4,3,2,1,0:T(2,128)S(1)}, f32[2,2,2,2,11776]{4,3,2,1,0:T(2,128)S(1)}, u32[]{:S(2)}, u32[]{:S(2)}) collective-permute-start(f32[2,2,2,2,11776]{4,3,2,1,0:T(2,128)S(1)} %bitcast.84), channel_id=1, source_target_pairs={{0,2},{1,3},{2,0},{3,1},{4,6},{5,7},{6,4},{7,5},{8,10},{9,11},{10,... | collective-permute-start | bytes 2261000 | tf_op jit(solution)/shard_map/ppermute | solution.py:23
  108.4 12.2 %collective-permute-start.6 = (f32[2,2,2,11776]{3,2,1,0:T(2,128)S(1)}, f32[2,2,2,11776]{3,2,1,0:T(2,128)S(1)}, u32[]{:S(2)}, u32[]{:S(2)}) collective-permute-start(f32[2,2,2,11776]{3,2,1,0:T(2,128)S(1)} %dynamic-slice_bitcast_fusion), channel_id=1, source_target_pairs={{0,8},{1,9},{2,10},{3,11},{4,12},{5,13},{6,14},{7,15},{8,0},{9,1},... | collective-permute-start | bytes 1130504 | tf_op jit(solution)/shard_map/ppermute | solution.py:23
  121.3 10.9 %collective-permute-start.7 = (f32[2,2,11776]{2,1,0:T(2,128)S(1)}, f32[2,2,11776]{2,1,0:T(2,128)S(1)}, u32[]{:S(2)}, u32[]{:S(2)}) collective-permute-start(f32[2,2,11776]{2,1,0:T(2,128)S(1)} %bitcast.87), channel_id=1, source_target_pairs={{0,4},{1,5},{2,6},{3,7},{4,0},{5,1},{6,2},{7,3},{8,12},{9,13},{10,... | collective-permute-start | bytes 565256 | tf_op jit(solution)/shard_map/ppermute | solution.py:23
  132.5 8.4 %collective-permute-start.8 = (f32[2,11776]{1,0:T(2,128)S(1)}, f32[2,11776]{1,0:T(2,128)S(1)}, u32[]{:S(2)}, u32[]{:S(2)}) collective-permute-start(f32[2,11776]{1,0:T(2,128)S(1)} %bitcast.88), channel_id=1, source_target_pairs={{0,16},{1,17},{2,18},{3,19},{4,20},{5,21},{6,22},{7,23},{8,24},{9,... | collective-permute-start | bytes 282632 | tf_op jit(solution)/shard_map/ppermute | solution.py:23
  141.2 9.9 %collective-permute-start.9 = (f32[11776]{0:T(1024)S(1)}, f32[11776]{0:T(1024)S(1)}, u32[]{:S(2)}, u32[]{:S(2)}) collective-permute-start(f32[11776]{0:T(1024)S(1)} %get-tuple-element.4), channel_id=1, source_target_pairs={{0,32},{1,33},{2,34},{3,35},{4,36},{5,37},{6,38},{7,39},{8,40},{9,... | collective-permute-start | bytes 141320 | tf_op jit(solution)/shard_map/ppermute | solution.py:23
  151.1 6.3 %collective-permute-start.10 = (f32[11776]{0:T(1024)S(1)}, f32[11776]{0:T(1024)S(1)}, u32[]{:S(2)}, u32[]{:S(2)}) collective-permute-start(f32[11776]{0:T(1024)S(1)} %add.123), channel_id=1, source_target_pairs={{0,64},{64,0},{128,192},{192,128},{256,320},{320,256},{384,448},{4... | collective-permute-start | bytes 141320 | tf_op jit(solution)/shard_map/ppermute | solution.py:23
  157.5 8.4 %collective-permute-start.11 = (f32[11776]{0:T(1024)S(1)}, f32[11776]{0:T(1024)S(1)}, u32[]{:S(2)}, u32[]{:S(2)}) collective-permute-start(f32[11776]{0:T(1024)S(1)} %add.124), channel_id=1, source_target_pairs={{0,128},{64,192},{128,0},{192,64},{256,384},{320,448},{384,256},{4... | collective-permute-start | bytes 141320 | tf_op jit(solution)/shard_map/ppermute | solution.py:23
  165.9 12.5 %collective-permute-start.12 = (f32[11776]{0:T(1024)S(1)}, f32[11776]{0:T(1024)S(1)}, u32[]{:S(2)}, u32[]{:S(2)}) collective-permute-start(f32[11776]{0:T(1024)S(1)} %add.125), channel_id=1, source_target_pairs={{0,256},{64,320},{128,384},{192,448},{256,0},{320,64},{384,128},{4... | collective-permute-start | bytes 141320 | tf_op jit(solution)/shard_map/ppermute | solution.py:23

commit v2 on v1

--- a/solution.py
+++ b/solution.py
@@ -10,7 +10,6 @@
 
 loss_gain = 16.0
 offsets_by = (1, 2, -1, -2)
-halving_bits = (0, 1, 3, 2, 4, 5)
 
 
 def passed_along(shard, axis, by):
@@ -42,25 +41,68 @@
     return jnp.concatenate(block_parts, axis=0), jnp.concatenate(patch_parts, axis=0)
 
 
-def reduce_to_share(terms, n_dom):
+def logical_pairs(n_y, n_x, axis_is_x, mask):
+    pairs = []
+    for y in range(n_y):
+        for x in range(n_x):
+            for c in range(2):
+                lx, ly = (x - c) % n_x, (y - c) % n_y
+                if axis_is_x:
+                    lx ^= mask
+                else:
+                    ly ^= mask
+                px, py = (lx + c) % n_x, (ly + c) % n_y
+                pairs.append(((y * n_x + x) * 2 + c, (py * n_x + px) * 2 + c))
+    return pairs
+
+
+def reduce_to_share(terms, n_dom, n_x):
+    bf16 = jnp.bfloat16
+    f32 = jnp.float32
+    n_y = n_dom // (2 * n_x)
     flat = jnp.concatenate([t.reshape(n_dom, -1) for t in terms], axis=1)
-    n_bits = n_dom.bit_length() - 1
+    width = flat.shape[1]
     me = lax.axis_index("dom")
-    held = flat.reshape((2,) * n_bits + (flat.shape[1],))
-    axes = list(range(n_bits))
-    for bit in halving_bits[:n_bits]:
-        pos = axes.index(n_bits - 1 - bit)
-        mine_bit = (me >> bit) & 1
+    core = me % 2
+    grid = flat.reshape(n_y, n_x, 2, width)
+    mine = lax.dynamic_index_in_dim(grid, core, 2, keepdims=False)
+    other = lax.dynamic_index_in_dim(grid, 1 - core, 2, keepdims=False)
+    held = mine + swapped(other, "dom", 1)
+    wrapped = jnp.concatenate([held, held[:1]], axis=0)
+    wrapped = jnp.concatenate([wrapped, wrapped[:, :1]], axis=1)
+    held = lax.dynamic_slice(wrapped, (core, core, 0), (n_y, n_x, width))
+    lx = (me // 2 % n_x - core) % n_x
+    ly = (me // (2 * n_x) - core) % n_y
+    x_bits = n_x.bit_length() - 1
+    y_bits = n_y.bit_length() - 1
+    held = held.reshape((2,) * y_bits + (2,) * x_bits + (width,))
+    names = ["y%d" % b for b in reversed(range(y_bits))] + ["x%d" % b for b in reversed(range(x_bits))]
+    order = []
+    for b in range(max(x_bits, y_bits)):
+        if b < x_bits:
+            order.append(("x", b))
+        if b < y_bits:
+            order.append(("y", b))
+    for step, (kind, b) in enumerate(order):
+        pos = names.index("%s%d" % (kind, b))
+        coord = lx if kind == "x" else ly
+        mine_bit = (coord >> b) & 1
         mine = lax.dynamic_index_in_dim(held, mine_bit, pos, keepdims=False)
         other = lax.dynamic_index_in_dim(held, 1 - mine_bit, pos, keepdims=False)
-        held = mine + swapped(other, "dom", 1 << bit)
-        axes.pop(pos)
+        pairs = logical_pairs(n_y, n_x, kind == "x", 1 << b)
+        if step < 2:
+            got = lax.ppermute(other.astype(bf16), "dom", pairs).astype(f32)
+        else:
+            got = lax.ppermute(other, "dom", pairs)
+        held = mine + got
+        names.pop(pos)
     share = held.reshape(-1)
     n_region = lax.axis_size("region")
-    step = 1
-    while step < n_region:
-        share = share + swapped(share, "region", step)
-        step *= 2
+    region = lax.axis_index("region")
+    gathered = [share] + [passed_along(share, "region", k) for k in range(1, n_region)]
+    stacked = jnp.stack(gathered)
+    ordered = jnp.take(stacked, (region - jnp.arange(n_region)) % n_region, axis=0)
+    share = jnp.sum(ordered, axis=0)
     pieces = []
     start = 0
     for t in terms:
@@ -140,7 +182,7 @@
     grad_message = jnp.dot(message.T, act_grad, preferred_element_type=f32)
     grad_self = jnp.dot(gauges.T, act_grad, preferred_element_type=f32)
     shares = reduce_to_share(
-        [grad_message, grad_self, grad_output, grad_patch], lax.axis_size("dom")
+        [grad_message, grad_self, grad_output, grad_patch], lax.axis_size("dom"), 4
     )
     return tuple(s.astype(bf16) for s in shares)
 

time: 183 us -> 182 us (level)
  waiting for transfers between devices: 56.8 us -> 38.9 us
  starting transfers between devices: 57.7 us -> 69.5 us
  local copies, waits for them, and re-layouts: 35.7 us -> 39.4 us
    ppermute x9 -> x1, waiting for transfers between devices: 52.2 us -> 3.18 us  [swapped(): return lax.ppermute(shard, axis, [(i, i ^ mask) for i in range(count)])]
    ppermute x9 -> x1, starting transfers between devices: 45.7 us -> 2.95 us  [swapped(): return lax.ppermute(shard, axis, [(i, i ^ mask) for i in range(count)])]
    ppermute x4 -> x11, starting transfers between devices: 12 us -> 44.3 us  [passed_along(): lax.ppermute(shard, axis, [(i, (i + by) % count) for i in range(count)])]
    ppermute x0 -> x5, waiting for transfers between devices: none -> 28 us  [the longest x3 16.9 us: reduce_to_share(): got = lax.ppermute(other, 'dom', pairs)]
    ppermute x0 -> x5, starting transfers between devices: none -> 22.2 us  [the longest x3 14.3 us: reduce_to_share(): got = lax.ppermute(other, 'dom', pairs)]
    dynamic_slice x0 -> x2, local copies, waits for them, and re-layouts: none -> 4.52 us  [the longest x1 2.91 us: reduce_to_share(): mine = lax.dynamic_index_in_dim(grid, core, 2, keepdims=False)]
    dynamic_slice x4 -> x3, local copies, waits for them, and re-layouts: 4.77 us -> 0.56 us  [reduce_to_share(): mine = lax.dynamic_index_in_dim(held, mine_bit, pos, keepdims=False)]
    ppermute x4 -> x11, waiting for transfers between devices: 4.64 us -> 7.73 us  [passed_along(): lax.ppermute(shard, axis, [(i, (i + by) % count) for i in range(count)])]
  transfers between devices with their start and end apart: 13 -> 17, of which waited for: 12 -> 12; matrix products, arithmetic and copies ran while one was open for 2% -> 2% of each run, Pallas kernels for 0% -> 0%
where the time goes in v2:
time: 182 us; the launch traced here: 180 us
  starting transfers between devices  69.5 us (38%)
  local copies, waits for them, and re-layouts  39.4 us (22%)
  waiting for transfers between devices  38.9 us (21%)
  matrix products  25.4 us (14%)
  other arithmetic  5.4 us (3%)
    ppermute x11, starting transfers between devices, passed_along(): lax.ppermute(shard, axis, [(i, (i + by) % count) for i in range(count)])  44.3 us
    ppermute x3, waiting for transfers between devices, reduce_to_share(): got = lax.ppermute(other, 'dom', pairs)  16.9 us
    ppermute x3, starting transfers between devices, reduce_to_share(): got = lax.ppermute(other, 'dom', pairs)  14.3 us
    ppermute x2, waiting for transfers between devices, reduce_to_share(): got = lax.ppermute(other.astype(bf16), 'dom', pairs).astype(f32)  11 us
    unnamed x53, local copies, waits for them, and re-layouts  9.59 us
    ppermute x2, starting transfers between devices, reduce_to_share(): got = lax.ppermute(other.astype(bf16), 'dom', pairs).astype(f32)  7.86 us
    ppermute x11, waiting for transfers between devices, passed_along(): lax.ppermute(shard, axis, [(i, (i + by) % count) for i in range(count)])  7.73 us
    dot_general x1, matrix products, shards(): jnp.einsum('bij,bie->bje', logit_grad, query_blocks, preferred_element_ty...  5.32 us
  transfers between devices with their start and end apart: 17, of which 12 were waited for; matrix products, arithmetic and copies ran while one was open for 2% of the time, Pallas kernels for 0%

profile of v2, /device:TPU:6, one launch (start us, length us, event | category | flops | bytes accessed | tf_op | source)
XLA Modules:
  0.0 180.1 jit_solution(14801503865164189461)
XLA Ops:
  5.6 2.7 %collective-permute-start.3 = (bf16[163840]{0:T(1024)(128)(2,1)}, bf16[163840]{0:T(1024)(128)(2,1)S(1)}, u32[]{:S(2)}, u32[]{:S(2)}) collective-permute-start(bf16[163840]{0:T(1024)(128)(2,1)} %constant_dynamic-update-slice_fusion.14), channel_id=1, source_target_pairs={{0,62},{1,63},{2,0},{3,1},{4,2},{5,3},{6,4},{7,5},{8,6},{9,7},{10,... | collective-permute-start | bytes 983048 | tf_op jit(solution)/shard_map/ppermute | solution.py:17
  10.3 5.2 %collective-permute-start.1 = (bf16[163840]{0:T(1024)(128)(2,1)}, bf16[163840]{0:T(1024)(128)(2,1)S(1)}, u32[]{:S(2)}, u32[]{:S(2)}) collective-permute-start(bf16[163840]{0:T(1024)(128)(2,1)} %constant_dynamic-update-slice_fusion.14), channel_id=1, source_target_pairs={{0,2},{1,3},{2,4},{3,5},{4,6},{5,7},{6,8},{7,9},{8,10},{9,11},{10,... | collective-permute-start | bytes 983048 | tf_op jit(solution)/shard_map/ppermute | solution.py:17
  15.5 2.1 %collective-permute-start = (bf16[163840]{0:T(1024)(128)(2,1)}, bf16[163840]{0:T(1024)(128)(2,1)S(1)}, u32[]{:S(2)}, u32[]{:S(2)}) collective-permute-start(bf16[163840]{0:T(1024)(128)(2,1)} %constant_dynamic-update-slice_fusion.14), channel_id=1, source_target_pairs={{0,1},{1,2},{2,3},{3,4},{4,5},{5,6},{6,7},{7,8},{8,9},{9,10},{10,1... | collective-permute-start | bytes 983048 | tf_op jit(solution)/shard_map/ppermute | solution.py:17
  21.4 2.4 %collective-permute-done.1 = bf16[163840]{0:T(1024)(128)(2,1)S(1)} collective-permute-done((bf16[163840]{0:T(1024)(128)(2,1)}, bf16[163840]{0:T(1024)(128)(2,1)S(1)}, u32[]{:S(2)}, u32[]{:S(2)}) %collective-permute-start.1) | collective-permute-done | bytes 327712 | tf_op jit(solution)/shard_map/ppermute | solution.py:17
  24.1 1.9 %collective-permute-done = bf16[163840]{0:T(1024)(128)(2,1)S(1)} collective-permute-done((bf16[163840]{0:T(1024)(128)(2,1)}, bf16[163840]{0:T(1024)(128)(2,1)S(1)}, u32[]{:S(2)}, u32[]{:S(2)}) %collective-permute-start) | collective-permute-done | bytes 327712 | tf_op jit(solution)/shard_map/ppermute | solution.py:17
  26.4 2.0 %gather_fusion.3 = bf16[16,128,512]{2,1,0:T(8,128)(2,1)} fusion(bf16[5,128,512]{2,1,0:T(8,128)(2,1)S(1)} %constant_dynamic-update-slice_fusion.6, s32[1024]{0:T(1024)S(1)} %get-tuple-element.16), kind=kCustom, calls=%fused_computation.3 | custom fusion | bytes 4194368 | tf_op jit(solution)/shard_map/gather | solution.py:153
  29.9 2.0 %gather_fusion.2 = bf16[16,128,512]{2,1,0:T(8,128)(2,1)} fusion(bf16[5,128,512]{2,1,0:T(8,128)(2,1)S(1)} %bitcast.78, s32[1024]{0:T(1024)S(1)} %get-tuple-element.16), kind=kCustom, calls=%fused_computation.2 | custom fusion | bytes 4194368 | tf_op jit(solution)/shard_map/gather | solution.py:152
  34.7 2.5 %gather_fusion.1 = bf16[24,128,384]{2,1,0:T(8,128)(2,1)S(1)} fusion(bf16[16,128,384]{2,1,0:T(8,128)(2,1)} %constant_dynamic-update-slice_fusion.1, s32[1024]{0:T(1024)S(1)} %get-tuple-element.17), kind=kCustom, calls=%fused_computation.1 | custom fusion | bytes 4718688 | tf_op jit(solution)/shard_map/gather | solution.py:136
  39.5 2.0 %add_convert_fusion = (bf16[1024,384]{1,0:T(8,128)(2,1)S(1)}, f32[1024,384]{1,0:T(8,128)}) fusion(bf16[1024,384]{1,0:T(8,128)(2,1)S(1)} %copy-done.6, f32[1024,384]{1,0:T(8,128)S(1)} %fusion.26, bf16[384,384]{1,0:T(8,128)(2,1)S(1)} %copy-done.15), kind=kOutput, calls=%fused_computation.15 | convolution fusion | flops 305135616 | bytes 5013504 | tf_op jit(solution)/shard_map/dot_general | solution.py:142
  44.2 4.4 %multiply_convert_fusion.1 = bf16[8,128,512]{2,1,0:T(8,128)(2,1)} fusion(bf16[8,256,512]{2,1,0:T(8,128)(2,1)S(1)} %bitcast.82, s32[8,128]{1,0:T(8,128)S(1)} %bitcast.93, bf16[8,128,512]{2,1,0:T(8,128)(2,1)} %bitcast.86), kind=kOutput, calls=%fused_computation.12 | convolution fusion | flops 540019200 | bytes 4198400 | tf_op jit(solution)/shard_map/bij,bje->bie/dot_general | solution.py:166
  48.6 5.3 %multiply_convert_fusion = bf16[8,256,512]{2,1,0:T(8,128)(2,1)} fusion(bf16[8,128,512]{2,1,0:T(8,128)(2,1)} %bitcast.87, s32[8,128]{1,0:T(8,128)S(1)} %bitcast.94, bf16[8,256,512]{2,1,0:T(8,128)(2,1)S(1)} %bitcast.83), kind=kOutput, calls=%fused_computation.7 | convolution fusion | flops 541067776 | bytes 5246976 | tf_op jit(solution)/shard_map/bij,bie->bje/dot_general | solution.py:172
  53.9 2.2 %fusion.28 = f32[384,512]{1,0:T(8,128)S(1)} fusion(bf16[1024,384]{1,0:T(8,128)(2,1)} %copy-done.8, bf16[1024,512]{1,0:T(8,128)(2,1)} %bitcast.96), kind=kOutput, calls=%fused_computation.102 | convolution fusion | flops 402653184 | bytes 2621440 | tf_op jit(solution)/shard_map/dot_general | solution.py:179
  61.4 4.7 %fusion.29 = f32[512,512]{1,0:T(8,128)} fusion(bf16[2048,512]{1,0:T(8,128)(2,1)} %bitcast.81, bf16[2048,512]{1,0:T(8,128)(2,1)} %bitcast.95), kind=kOutput, calls=%fused_computation.103 | convolution fusion | flops 1073741824 | bytes 5242880 | tf_op jit(solution)/shard_map/dot_general | solution.py:178
  66.1 2.1 %concatenate.33 = f32[8,4,2,4096]{3,2,1,0:T(2,128)S(1)} reshape(f32[512,512]{1,0:T(8,128)} %fusion.29) | data formatting | bytes 2097152 | tf_op jit(solution)/shard_map/concatenate | solution.py:63
  69.7 2.9 %constant_dynamic-slice_fusion.6 = (f32[8,4,1,11776]{3,2,1,0:T(1,128)S(1)}, f32[8,4,1,11776]{3,2,1,0:T(1,128)S(1)}) fusion(f32[8,4,2,11776]{3,2,1,0:T(2,128)S(1)} %constant_dynamic-update-slice_fusion.10, s32[]{:T(128)S(6)} %select_n.127, s32[]{:T(128)S(6)} %select_n.128), kind=kLoop, calls=%fused_computation.80 | loop fusion | bytes 6029320 | tf_op jit(solution)/shard_map/jit(dynamic_index_in_dim)/dynamic_slice | solution.py:68
  74.2 3.0 %collective-permute-start.4 = (f32[8,4,11776]{2,0,1:T(8,128)}, f32[8,4,11776]{2,0,1:T(8,128)}, u32[]{:S(2)}, u32[]{:S(2)}) collective-permute-start(f32[8,4,11776]{2,0,1:T(8,128)} %bitcast.72), channel_id=1, source_target_pairs={{0,1},{1,0},{2,3},{3,2},{4,5},{5,4},{6,7},{7,6},{8,9},{9,8},{10,11... | collective-permute-start | bytes 4521992 | tf_op jit(solution)/shard_map/ppermute | solution.py:22
  77.3 3.2 %collective-permute-done.4 = f32[8,4,11776]{2,0,1:T(8,128)} collective-permute-done((f32[8,4,11776]{2,0,1:T(8,128)}, f32[8,4,11776]{2,0,1:T(8,128)}, u32[]{:S(2)}, u32[]{:S(2)}) %collective-permute-start.4) | collective-permute-done | bytes 1507360 | tf_op jit(solution)/shard_map/ppermute | solution.py:22
  83.7 2.0 %reshape.183 = f32[2,2,2,2,2,11776]{5,2,1,0,4,3:T(2,128)} reshape(f32[8,4,11776]{2,0,1:T(8,128)S(1)} %fusion.3) | data formatting | bytes 3014656 | tf_op jit(solution)/shard_map/reshape | solution.py:78
  87.6 5.9 %collective-permute-start.5 = (bf16[2,2,2,2,11776]{4,3,2,1,0:T(2,128)(2,1)S(1)}, bf16[2,2,2,2,11776]{4,3,2,1,0:T(2,128)(2,1)S(1)}, u32[]{:S(2)}, u32[]{:S(2)}) collective-permute-start(bf16[2,2,2,2,11776]{4,3,2,1,0:T(2,128)(2,1)S(1)} %bitcast.90), channel_id=1, source_target_pairs={{0,2},{1,7},{2,0},{3,5},{4,6},{5,3},{6,4},{7,1},{8,10},{9,15},{10,... | collective-permute-start | bytes 1130504 | tf_op jit(solution)/shard_map/ppermute | solution.py:94
  93.6 5.5 %collective-permute-done.5 = bf16[2,2,2,2,11776]{4,3,2,1,0:T(2,128)(2,1)S(1)} collective-permute-done((bf16[2,2,2,2,11776]{4,3,2,1,0:T(2,128)(2,1)S(1)}, bf16[2,2,2,2,11776]{4,3,2,1,0:T(2,128)(2,1)S(1)}, u32[]{:S(2)}, u32[]{:S(2)}) %collective-permute-start.5) | collective-permute-done | bytes 376864 | tf_op jit(solution)/shard_map/ppermute | solution.py:94
  102.0 5.5 %collective-permute-done.6 = bf16[2,2,2,11776]{3,2,1,0:T(2,128)(2,1)S(1)} collective-permute-done((bf16[2,2,2,11776]{3,2,1,0:T(2,128)(2,1)S(1)}, bf16[2,2,2,11776]{3,2,1,0:T(2,128)(2,1)S(1)}, u32[]{:S(2)}, u32[]{:S(2)}) %collective-permute-start.6) | collective-permute-done | bytes 188448 | tf_op jit(solution)/shard_map/ppermute | solution.py:94
  108.1 7.3 %collective-permute-start.7 = (f32[2,2,11776]{2,1,0:T(2,128)S(1)}, f32[2,2,11776]{2,1,0:T(2,128)S(1)}, u32[]{:S(2)}, u32[]{:S(2)}) collective-permute-start(f32[2,2,11776]{2,1,0:T(2,128)S(1)} %bitcast.91), channel_id=1, source_target_pairs={{0,4},{1,5},{2,6},{3,7},{4,0},{5,1},{6,2},{7,3},{8,12},{9,13},{10,... | collective-permute-start | bytes 565256 | tf_op jit(solution)/shard_map/ppermute | solution.py:96
  115.5 5.2 %collective-permute-done.7 = f32[2,2,11776]{2,1,0:T(2,128)S(1)} collective-permute-done((f32[2,2,11776]{2,1,0:T(2,128)S(1)}, f32[2,2,11776]{2,1,0:T(2,128)S(1)}, u32[]{:S(2)}, u32[]{:S(2)}) %collective-permute-start.7) | collective-permute-done | bytes 188448 | tf_op jit(solution)/shard_map/ppermute | solution.py:96
  123.0 5.6 %collective-permute-done.8 = f32[2,11776]{1,0:T(2,128)S(1)} collective-permute-done((f32[2,11776]{1,0:T(2,128)S(1)}, f32[2,11776]{1,0:T(2,128)S(1)}, u32[]{:S(2)}, u32[]{:S(2)}) %collective-permute-start.8) | collective-permute-done | bytes 94240 | tf_op jit(solution)/shard_map/ppermute | solution.py:96
  128.9 5.1 %collective-permute-start.9 = (f32[11776]{0:T(1024)S(1)}, f32[11776]{0:T(1024)S(1)}, u32[]{:S(2)}, u32[]{:S(2)}) collective-permute-start(f32[11776]{0:T(1024)S(1)} %get-tuple-element.4), channel_id=1, source_target_pairs={{0,32},{1,33},{2,34},{3,35},{4,36},{5,37},{6,38},{7,39},{8,40},{9,... | collective-permute-start | bytes 141320 | tf_op jit(solution)/shard_map/ppermute | solution.py:96
  134.0 6.1 %collective-permute-done.9 = f32[11776]{0:T(1024)S(1)} collective-permute-done((f32[11776]{0:T(1024)S(1)}, f32[11776]{0:T(1024)S(1)}, u32[]{:S(2)}, u32[]{:S(2)}) %collective-permute-start.9) | collective-permute-done | bytes 47136 | tf_op jit(solution)/shard_map/ppermute | solution.py:96
  140.2 10.9 %collective-permute-start.16 = (f32[11776]{0:T(1024)S(1)}, f32[11776]{0:T(1024)S(1)}, u32[]{:S(2)}, u32[]{:S(2)}) collective-permute-start(f32[11776]{0:T(1024)S(1)} %add.175), channel_id=1, source_target_pairs={{0,448},{64,0},{128,64},{192,128},{256,192},{320,256},{384,320},{4... | collective-permute-start | bytes 141320 | tf_op jit(solution)/shard_map/ppermute | solution.py:17
  151.1 2.4 %collective-permute-start.15 = (f32[11776]{0:T(1024)S(1)}, f32[11776]{0:T(1024)S(1)}, u32[]{:S(2)}, u32[]{:S(2)}) collective-permute-start(f32[11776]{0:T(1024)S(1)} %add.175), channel_id=1, source_target_pairs={{0,384},{64,448},{128,0},{192,64},{256,128},{320,192},{384,256},{4... | collective-permute-start | bytes 141320 | tf_op jit(solution)/shard_map/ppermute | solution.py:17
  155.5 7.8 %collective-permute-start.13 = (f32[11776]{0:T(1024)S(1)}, f32[11776]{0:T(1024)S(1)}, u32[]{:S(2)}, u32[]{:S(2)}) collective-permute-start(f32[11776]{0:T(1024)S(1)} %add.175), channel_id=1, source_target_pairs={{0,256},{64,320},{128,384},{192,448},{256,0},{320,64},{384,128},{4... | collective-permute-start | bytes 141320 | tf_op jit(solution)/shard_map/ppermute | solution.py:17
  165.3 3.4 %collective-permute-start.11 = (f32[11776]{0:T(1024)S(1)}, f32[11776]{0:T(1024)S(1)}, u32[]{:S(2)}, u32[]{:S(2)}) collective-permute-start(f32[11776]{0:T(1024)S(1)} %add.175), channel_id=1, source_target_pairs={{0,128},{64,192},{128,256},{192,320},{256,384},{320,448},{384,0},{... | collective-permute-start | bytes 141320 | tf_op jit(solution)/shard_map/ppermute | solution.py:17
  168.7 3.9 %collective-permute-start.10 = (f32[11776]{0:T(1024)S(1)}, f32[11776]{0:T(1024)S(1)}, u32[]{:S(2)}, u32[]{:S(2)}) collective-permute-start(f32[11776]{0:T(1024)S(1)} %add.175), channel_id=1, source_target_pairs={{0,64},{64,128},{128,192},{192,256},{256,320},{320,384},{384,448},... | collective-permute-start | bytes 141320 | tf_op jit(solution)/shard_map/ppermute | solution.py:17
  173.6 2.1 %collective-permute-done.11 = f32[11776]{0:T(1024)S(1)} collective-permute-done((f32[11776]{0:T(1024)S(1)}, f32[11776]{0:T(1024)S(1)}, u32[]{:S(2)}, u32[]{:S(2)}) %collective-permute-start.11) | collective-permute-done | bytes 47136 | tf_op jit(solution)/shard_map/ppermute | solution.py:17
  (145 shorter events, 48.8 us)
Async XLA Ops:
  0.6 36.6 %copy-start = (bf16[8,3,128,128]{3,2,1,0:T(8,128)(2,1)S(1)}, bf16[8,3,128,128]{3,2,1,0:T(8,128)(2,1)}, u32[]{:S(2)}) copy-start(bf16[8,3,128,128]{3,2,1,0:T(8,128)(2,1)} %param.12) | copy-start | bytes 2359300
  0.6 17.0 %copy-start.5 = (bf16[1024,384]{1,0:T(8,128)(2,1)S(1)}, bf16[1024,384]{1,0:T(8,128)(2,1)}, u32[]{:S(2)}) copy-start(bf16[1024,384]{1,0:T(8,128)(2,1)} %param.11) | copy-start | bytes 2359300
  2.4 16.3 %copy-start.14 = (s32[8,2]{0,1:T(2,128)S(1)}, s32[8,2]{0,1:T(2,128)}, u32[]{:S(2)}) copy-start(s32[8,2]{0,1:T(2,128)} %param.15) | copy-start | bytes 196
  2.4 16.3 %copy-start.13 = (s32[8,3]{0,1:T(4,128)S(1)}, s32[8,3]{0,1:T(4,128)}, u32[]{:S(2)}) copy-start(s32[8,3]{0,1:T(4,128)} %param.13) | copy-start | bytes 292
  2.4 16.6 %copy-start.9 = (bf16[128,512]{1,0:T(8,128)(2,1)S(1)}, bf16[128,512]{1,0:T(8,128)(2,1)}, u32[]{:S(2)}) copy-start(bf16[128,512]{1,0:T(8,128)(2,1)} %param.17) | copy-start | bytes 393220
  5.6 13.7 %collective-permute-start.3 = (bf16[163840]{0:T(1024)(128)(2,1)}, bf16[163840]{0:T(1024)(128)(2,1)S(1)}, u32[]{:S(2)}, u32[]{:S(2)}) collective-permute-start(bf16[163840]{0:T(1024)(128)(2,1)} %constant_dynamic-update-slice_fusion.14), channel_id=1, source_target_pairs={{0,62},{1,63},{2,0},{3,1},{4,2},{5,3},{6,4},{7,5},{8,6},{9,7},{10,... | collective-permute-start | bytes 983048 | tf_op jit(solution)/shard_map/ppermute | solution.py:17
  8.4 11.2 %collective-permute-start.2 = (bf16[163840]{0:T(1024)(128)(2,1)}, bf16[163840]{0:T(1024)(128)(2,1)S(1)}, u32[]{:S(2)}, u32[]{:S(2)}) collective-permute-start(bf16[163840]{0:T(1024)(128)(2,1)} %constant_dynamic-update-slice_fusion.14), channel_id=1, source_target_pairs={{0,63},{1,0},{2,1},{3,2},{4,3},{5,4},{6,5},{7,6},{8,7},{9,8},{10,9... | collective-permute-start | bytes 983048 | tf_op jit(solution)/shard_map/ppermute | solution.py:17
  10.3 13.5 %collective-permute-start.1 = (bf16[163840]{0:T(1024)(128)(2,1)}, bf16[163840]{0:T(1024)(128)(2,1)S(1)}, u32[]{:S(2)}, u32[]{:S(2)}) collective-permute-start(bf16[163840]{0:T(1024)(128)(2,1)} %constant_dynamic-update-slice_fusion.14), channel_id=1, source_target_pairs={{0,2},{1,3},{2,4},{3,5},{4,6},{5,7},{6,8},{7,9},{8,10},{9,11},{10,... | collective-permute-start | bytes 983048 | tf_op jit(solution)/shard_map/ppermute | solution.py:17
  15.5 10.5 %collective-permute-start = (bf16[163840]{0:T(1024)(128)(2,1)}, bf16[163840]{0:T(1024)(128)(2,1)S(1)}, u32[]{:S(2)}, u32[]{:S(2)}) collective-permute-start(bf16[163840]{0:T(1024)(128)(2,1)} %constant_dynamic-update-slice_fusion.14), channel_id=1, source_target_pairs={{0,1},{1,2},{2,3},{3,4},{4,5},{5,6},{6,7},{7,8},{8,9},{9,10},{10,1... | collective-permute-start | bytes 983048 | tf_op jit(solution)/shard_map/ppermute | solution.py:17
  38.0 3.6 %copy-start.2 = (bf16[8,384,128]{1,2,0:T(8,128)(2,1)}, bf16[8,384,128]{1,2,0:T(8,128)(2,1)S(1)}, u32[]{:S(2)}) copy-start(bf16[8,384,128]{1,2,0:T(8,128)(2,1)S(1)} %bitcast_convert_fusion) | copy-start | bytes 2359300
  38.0 1.4 copy-start.6
  38.0 1.5 copy-start.15
  39.5 3.0 %copy-start.10 = (bf16[384,512]{1,0:T(8,128)(2,1)S(1)}, bf16[384,512]{1,0:T(8,128)(2,1)}, u32[]{:S(2)}) copy-start(bf16[384,512]{1,0:T(8,128)(2,1)} %param.20) | copy-start | bytes 1179652
  41.5 2.6 %copy-start.4 = (bf16[16,128,512]{2,1,0:T(8,128)(2,1)S(1)}, bf16[16,128,512]{2,1,0:T(8,128)(2,1)}, u32[]{:S(2)}) copy-start(bf16[16,128,512]{2,1,0:T(8,128)(2,1)} %gather_fusion.2) | copy-start | bytes 6291460
  41.5 2.6 %copy-start.16 = (s32[1024]{0:T(1024)S(1)}, s32[1024]{0:T(1024)}, u32[]{:S(2)}) copy-start(s32[1024]{0:T(1024)} %param.16) | copy-start | bytes 12292
  53.9 2.2 %copy-start.17 = (bf16[8,128,512]{2,1,0:T(8,128)(2,1)S(1)}, bf16[8,128,512]{2,1,0:T(8,128)(2,1)}, u32[]{:S(2)}) copy-start(bf16[8,128,512]{2,1,0:T(8,128)(2,1)} %multiply_convert_fusion.1) | copy-start | bytes 3145732
  53.9 2.3 %copy-start.18 = (f32[1024,384]{1,0:T(8,128)S(1)}, f32[1024,384]{1,0:T(8,128)}, u32[]{:S(2)}) copy-start(f32[1024,384]{1,0:T(8,128)} %get-tuple-element.15) | copy-start | bytes 4718596
  56.2 1.1 copy-start.3
  74.2 6.2 %collective-permute-start.4 = (f32[8,4,11776]{2,0,1:T(8,128)}, f32[8,4,11776]{2,0,1:T(8,128)}, u32[]{:S(2)}, u32[]{:S(2)}) collective-permute-start(f32[8,4,11776]{2,0,1:T(8,128)} %bitcast.72), channel_id=1, source_target_pairs={{0,1},{1,0},{2,3},{3,2},{4,5},{5,4},{6,7},{7,6},{8,9},{9,8},{10,11... | collective-permute-start | bytes 4521992 | tf_op jit(solution)/shard_map/ppermute | solution.py:22
  85.8 7.8 %copy-start.1 = (f32[2,2,2,2,2,11776]{5,2,1,0,4,3:T(2,128)S(1)}, f32[2,2,2,2,2,11776]{5,2,1,0,4,3:T(2,128)}, u32[]{:S(2)}) copy-start(f32[2,2,2,2,2,11776]{5,2,1,0,4,3:T(2,128)} %reshape.183) | copy-start | bytes 4521988
  87.6 11.5 %collective-permute-start.5 = (bf16[2,2,2,2,11776]{4,3,2,1,0:T(2,128)(2,1)S(1)}, bf16[2,2,2,2,11776]{4,3,2,1,0:T(2,128)(2,1)S(1)}, u32[]{:S(2)}, u32[]{:S(2)}) collective-permute-start(bf16[2,2,2,2,11776]{4,3,2,1,0:T(2,128)(2,1)S(1)} %bitcast.90), channel_id=1, source_target_pairs={{0,2},{1,7},{2,0},{3,5},{4,6},{5,3},{6,4},{7,1},{8,10},{9,15},{10,... | collective-permute-start | bytes 1130504 | tf_op jit(solution)/shard_map/ppermute | solution.py:94
  100.0 7.5 %collective-permute-start.6 = (bf16[2,2,2,11776]{3,2,1,0:T(2,128)(2,1)S(1)}, bf16[2,2,2,11776]{3,2,1,0:T(2,128)(2,1)S(1)}, u32[]{:S(2)}, u32[]{:S(2)}) collective-permute-start(bf16[2,2,2,11776]{3,2,1,0:T(2,128)(2,1)S(1)} %fusion.17), channel_id=1, source_target_pairs={{0,8},{1,57},{2,10},{3,59},{4,12},{5,61},{6,14},{7,63},{8,0},{9,17... | collective-permute-start | bytes 565256 | tf_op jit(solution)/shard_map/ppermute | solution.py:94
  108.1 12.5 %collective-permute-start.7 = (f32[2,2,11776]{2,1,0:T(2,128)S(1)}, f32[2,2,11776]{2,1,0:T(2,128)S(1)}, u32[]{:S(2)}, u32[]{:S(2)}) collective-permute-start(f32[2,2,11776]{2,1,0:T(2,128)S(1)} %bitcast.91), channel_id=1, source_target_pairs={{0,4},{1,5},{2,6},{3,7},{4,0},{5,1},{6,2},{7,3},{8,12},{9,13},{10,... | collective-permute-start | bytes 565256 | tf_op jit(solution)/shard_map/ppermute | solution.py:96
  121.0 7.5 %collective-permute-start.8 = (f32[2,11776]{1,0:T(2,128)S(1)}, f32[2,11776]{1,0:T(2,128)S(1)}, u32[]{:S(2)}, u32[]{:S(2)}) collective-permute-start(f32[2,11776]{1,0:T(2,128)S(1)} %bitcast.92), channel_id=1, source_target_pairs={{0,16},{1,49},{2,18},{3,51},{4,20},{5,53},{6,22},{7,55},{8,24},{9,... | collective-permute-start | bytes 282632 | tf_op jit(solution)/shard_map/ppermute | solution.py:96
  128.9 11.3 %collective-permute-start.9 = (f32[11776]{0:T(1024)S(1)}, f32[11776]{0:T(1024)S(1)}, u32[]{:S(2)}, u32[]{:S(2)}) collective-permute-start(f32[11776]{0:T(1024)S(1)} %get-tuple-element.4), channel_id=1, source_target_pairs={{0,32},{1,33},{2,34},{3,35},{4,36},{5,37},{6,38},{7,39},{8,40},{9,... | collective-permute-start | bytes 141320 | tf_op jit(solution)/shard_map/ppermute | solution.py:96
  140.2 25.1 %collective-permute-start.16 = (f32[11776]{0:T(1024)S(1)}, f32[11776]{0:T(1024)S(1)}, u32[]{:S(2)}, u32[]{:S(2)}) collective-permute-start(f32[11776]{0:T(1024)S(1)} %add.175), channel_id=1, source_target_pairs={{0,448},{64,0},{128,64},{192,128},{256,192},{320,256},{384,320},{4... | collective-permute-start | bytes 141320 | tf_op jit(solution)/shard_map/ppermute | solution.py:17
  151.1 17.6 %collective-permute-start.15 = (f32[11776]{0:T(1024)S(1)}, f32[11776]{0:T(1024)S(1)}, u32[]{:S(2)}, u32[]{:S(2)}) collective-permute-start(f32[11776]{0:T(1024)S(1)} %add.175), channel_id=1, source_target_pairs={{0,384},{64,448},{128,0},{192,64},{256,128},{320,192},{384,256},{4... | collective-permute-start | bytes 141320 | tf_op jit(solution)/shard_map/ppermute | solution.py:17
  153.6 19.2 %collective-permute-start.14 = (f32[11776]{0:T(1024)S(1)}, f32[11776]{0:T(1024)S(1)}, u32[]{:S(2)}, u32[]{:S(2)}) collective-permute-start(f32[11776]{0:T(1024)S(1)} %add.175), channel_id=1, source_target_pairs={{0,320},{64,384},{128,448},{192,0},{256,64},{320,128},{384,192},{4... | collective-permute-start | bytes 141320 | tf_op jit(solution)/shard_map/ppermute | solution.py:17
  155.5 17.3 %collective-permute-start.13 = (f32[11776]{0:T(1024)S(1)}, f32[11776]{0:T(1024)S(1)}, u32[]{:S(2)}, u32[]{:S(2)}) collective-permute-start(f32[11776]{0:T(1024)S(1)} %add.175), channel_id=1, source_target_pairs={{0,256},{64,320},{128,384},{192,448},{256,0},{320,64},{384,128},{4... | collective-permute-start | bytes 141320 | tf_op jit(solution)/shard_map/ppermute | solution.py:17
  163.4 10.2 %collective-permute-start.12 = (f32[11776]{0:T(1024)S(1)}, f32[11776]{0:T(1024)S(1)}, u32[]{:S(2)}, u32[]{:S(2)}) collective-permute-start(f32[11776]{0:T(1024)S(1)} %add.175), channel_id=1, source_target_pairs={{0,192},{64,256},{128,320},{192,384},{256,448},{320,0},{384,64},{4... | collective-permute-start | bytes 141320 | tf_op jit(solution)/shard_map/ppermute | solution.py:17
  165.3 10.3 %collective-permute-start.11 = (f32[11776]{0:T(1024)S(1)}, f32[11776]{0:T(1024)S(1)}, u32[]{:S(2)}, u32[]{:S(2)}) collective-permute-start(f32[11776]{0:T(1024)S(1)} %add.175), channel_id=1, source_target_pairs={{0,128},{64,192},{128,256},{192,320},{256,384},{320,448},{384,0},{... | collective-permute-start | bytes 141320 | tf_op jit(solution)/shard_map/ppermute | solution.py:17
  168.7 7.3 %collective-permute-start.10 = (f32[11776]{0:T(1024)S(1)}, f32[11776]{0:T(1024)S(1)}, u32[]{:S(2)}, u32[]{:S(2)}) collective-permute-start(f32[11776]{0:T(1024)S(1)} %add.175), channel_id=1, source_target_pairs={{0,64},{64,128},{128,192},{192,256},{256,320},{320,384},{384,448},... | collective-permute-start | bytes 141320 | tf_op jit(solution)/shard_map/ppermute | solution.py:17
  (4 other events, 3.8 us)

commit v3 on v2

--- a/solution.py
+++ b/solution.py
@@ -1,3 +1,4 @@
+import functools
 import math
 
 import jax
@@ -56,21 +57,31 @@
     return pairs
 
 
+def share_order(rows, n_dom, n_x):
+    n_y = n_dom // (2 * n_x)
+    per = rows // n_dom
+    order = []
+    for c in range(2):
+        for ly in range(n_y):
+            for lx in range(n_x):
+                d = ((ly + c) % n_y * n_x + (lx + c) % n_x) * 2 + c
+                order.extend(range(d * per, (d + 1) * per))
+    return jnp.array(order, dtype=jnp.int32)
+
+
 def reduce_to_share(terms, n_dom, n_x):
     bf16 = jnp.bfloat16
     f32 = jnp.float32
     n_y = n_dom // (2 * n_x)
-    flat = jnp.concatenate([t.reshape(n_dom, -1) for t in terms], axis=1)
-    width = flat.shape[1]
+    flat = jnp.concatenate(
+        [t[share_order(t.shape[0], n_dom, n_x)].reshape(2, n_y * n_x, -1) for t in terms], axis=2
+    )
+    width = flat.shape[2]
     me = lax.axis_index("dom")
     core = me % 2
-    grid = flat.reshape(n_y, n_x, 2, width)
-    mine = lax.dynamic_index_in_dim(grid, core, 2, keepdims=False)
-    other = lax.dynamic_index_in_dim(grid, 1 - core, 2, keepdims=False)
+    mine = lax.dynamic_index_in_dim(flat, core, 0, keepdims=False)
+    other = lax.dynamic_index_in_dim(flat, 1 - core, 0, keepdims=False)
     held = mine + swapped(other, "dom", 1)
-    wrapped = jnp.concatenate([held, held[:1]], axis=0)
-    wrapped = jnp.concatenate([wrapped, wrapped[:, :1]], axis=1)
-    held = lax.dynamic_slice(wrapped, (core, core, 0), (n_y, n_x, width))
     lx = (me // 2 % n_x - core) % n_x
     ly = (me // (2 * n_x) - core) % n_y
     x_bits = n_x.bit_length() - 1
@@ -98,11 +109,10 @@
         names.pop(pos)
     share = held.reshape(-1)
     n_region = lax.axis_size("region")
-    region = lax.axis_index("region")
-    gathered = [share] + [passed_along(share, "region", k) for k in range(1, n_region)]
-    stacked = jnp.stack(gathered)
-    ordered = jnp.take(stacked, (region - jnp.arange(n_region)) % n_region, axis=0)
-    share = jnp.sum(ordered, axis=0)
+    step = 1
+    while step < n_region:
+        share = share + swapped(share, "region", step)
+        step *= 2
     pieces = []
     start = 0
     for t in terms:
@@ -113,6 +123,7 @@
 
 
 def shards(
+    n_x,
     gauges,
     couplings,
     adjacency,
@@ -182,7 +193,7 @@
     grad_message = jnp.dot(message.T, act_grad, preferred_element_type=f32)
     grad_self = jnp.dot(gauges.T, act_grad, preferred_element_type=f32)
     shares = reduce_to_share(
-        [grad_message, grad_self, grad_output, grad_patch], lax.axis_size("dom"), 4
+        [grad_message, grad_self, grad_output, grad_patch], lax.axis_size("dom"), n_x
     )
     return tuple(s.astype(bf16) for s in shares)
 
@@ -201,8 +212,9 @@
         P(),
         P(),
     )
+    n_x = len({device.coords[0] for device in mesh.devices.flat})
     return jax.shard_map(
-        shards,
+        functools.partial(shards, n_x),
         mesh=mesh,
         in_specs=placed,
         out_specs=(P("dom", None), P("dom", None), P("dom", None), P("dom", None)),

time: 182 us -> 172 us (0.945)
  starting transfers between devices: 69.5 us -> 56.6 us
  local copies, waits for them, and re-layouts: 39.4 us -> 42.4 us
  waiting for transfers between devices: 38.9 us -> 41.3 us
    ppermute x11 -> x4, starting transfers between devices: 44.3 us -> 12 us  [passed_along(): lax.ppermute(shard, axis, [(i, (i + by) % count) for i in range(count)])]
    ppermute x1 -> x4, starting transfers between devices: 2.95 us -> 22.3 us  [swapped(): return lax.ppermute(shard, axis, [(i, i ^ mask) for i in range(count)])]
    ppermute x1 -> x4, waiting for transfers between devices: 3.18 us -> 9.44 us  [swapped(): return lax.ppermute(shard, axis, [(i, i ^ mask) for i in range(count)])]
    gather x1 -> x4, local copies, waits for them, and re-layouts: 0.67 us -> 6.89 us  [reduce_to_share(): t[share_order(t.shape[0], n_dom, n_x)].reshape(2, n_y * n_x, -1)]
    dynamic_slice x2 -> x0, local copies, waits for them, and re-layouts: 4.52 us -> none  [the longest x1 2.91 us: reduce_to_share(): mine = lax.dynamic_index_in_dim(grid, core, 2, keepdims=False)]
    concatenate x5 -> x1, local copies, waits for them, and re-layouts: 4.33 us -> 0.07 us  [reduce_to_share(): jnp.concatenate([t[share_order(t.shape[0], n_dom, n_x)].reshape(2, n_y *...]
    reshape x0 -> x4, local copies, waits for them, and re-layouts: none -> 3.35 us  [reduce_to_share(): t[share_order(t.shape[0], n_dom, n_x)].reshape(2, n_y * n_x, -1)]
    ppermute x11 -> x4, waiting for transfers between devices: 7.73 us -> 4.62 us  [passed_along(): lax.ppermute(shard, axis, [(i, (i + by) % count) for i in range(count)])]
  transfers between devices with their start and end apart: 17 -> 13, of which waited for: 12 -> 12; matrix products, arithmetic and copies ran while one was open for 2% -> 2% of each run, Pallas kernels for 0% -> 0%
where the time goes in v3:
time: 172 us; the launch traced here: 170 us
  starting transfers between devices  56.6 us (33%)
  local copies, waits for them, and re-layouts  42.4 us (25%)
  waiting for transfers between devices  41.3 us (24%)
  matrix products  24.1 us (14%)
  other arithmetic  3.73 us (2%)
    ppermute x4, starting transfers between devices, swapped(): return lax.ppermute(shard, axis, [(i, i ^ mask) for i in range(count)])  22.3 us
    ppermute x3, waiting for transfers between devices, reduce_to_share(): got = lax.ppermute(other, 'dom', pairs)  16.9 us
    ppermute x3, starting transfers between devices, reduce_to_share(): got = lax.ppermute(other, 'dom', pairs)  14.4 us
    ppermute x4, starting transfers between devices, passed_along(): lax.ppermute(shard, axis, [(i, (i + by) % count) for i in range(count)])  12 us
    unnamed x64, local copies, waits for them, and re-layouts  11.6 us
    ppermute x2, waiting for transfers between devices, reduce_to_share(): got = lax.ppermute(other.astype(bf16), 'dom', pairs).astype(f32)  10.3 us
    ppermute x4, waiting for transfers between devices, swapped(): return lax.ppermute(shard, axis, [(i, i ^ mask) for i in range(count)])  9.44 us
    ppermute x2, starting transfers between devices, reduce_to_share(): got = lax.ppermute(other.astype(bf16), 'dom', pairs).astype(f32)  7.87 us
  transfers between devices with their start and end apart: 13, of which 12 were waited for; matrix products, arithmetic and copies ran while one was open for 2% of the time, Pallas kernels for 0%

profile of v3, /device:TPU:6, one launch (start us, length us, event | category | flops | bytes accessed | tf_op | source)
XLA Modules:
  0.0 169.6 jit_solution(902862537730830052)
XLA Ops:
  5.6 2.7 %collective-permute-start.3 = (bf16[163840]{0:T(1024)(128)(2,1)}, bf16[163840]{0:T(1024)(128)(2,1)S(1)}, u32[]{:S(2)}, u32[]{:S(2)}) collective-permute-start(bf16[163840]{0:T(1024)(128)(2,1)} %constant_dynamic-update-slice_fusion.14), channel_id=1, source_target_pairs={{0,62},{1,63},{2,0},{3,1},{4,2},{5,3},{6,4},{7,5},{8,6},{9,7},{10,... | collective-permute-start | bytes 983048 | tf_op jit(solution)/shard_map/ppermute | solution.py:18
  10.3 5.2 %collective-permute-start.1 = (bf16[163840]{0:T(1024)(128)(2,1)}, bf16[163840]{0:T(1024)(128)(2,1)S(1)}, u32[]{:S(2)}, u32[]{:S(2)}) collective-permute-start(bf16[163840]{0:T(1024)(128)(2,1)} %constant_dynamic-update-slice_fusion.14), channel_id=1, source_target_pairs={{0,2},{1,3},{2,4},{3,5},{4,6},{5,7},{6,8},{7,9},{8,10},{9,11},{10,... | collective-permute-start | bytes 983048 | tf_op jit(solution)/shard_map/ppermute | solution.py:18
  15.5 2.1 %collective-permute-start = (bf16[163840]{0:T(1024)(128)(2,1)}, bf16[163840]{0:T(1024)(128)(2,1)S(1)}, u32[]{:S(2)}, u32[]{:S(2)}) collective-permute-start(bf16[163840]{0:T(1024)(128)(2,1)} %constant_dynamic-update-slice_fusion.14), channel_id=1, source_target_pairs={{0,1},{1,2},{2,3},{3,4},{4,5},{5,6},{6,7},{7,8},{8,9},{9,10},{10,1... | collective-permute-start | bytes 983048 | tf_op jit(solution)/shard_map/ppermute | solution.py:18
  21.4 2.4 %collective-permute-done.1 = bf16[163840]{0:T(1024)(128)(2,1)S(1)} collective-permute-done((bf16[163840]{0:T(1024)(128)(2,1)}, bf16[163840]{0:T(1024)(128)(2,1)S(1)}, u32[]{:S(2)}, u32[]{:S(2)}) %collective-permute-start.1) | collective-permute-done | bytes 327712 | tf_op jit(solution)/shard_map/ppermute | solution.py:18
  24.1 1.9 %collective-permute-done = bf16[163840]{0:T(1024)(128)(2,1)S(1)} collective-permute-done((bf16[163840]{0:T(1024)(128)(2,1)}, bf16[163840]{0:T(1024)(128)(2,1)S(1)}, u32[]{:S(2)}, u32[]{:S(2)}) %collective-permute-start) | collective-permute-done | bytes 327712 | tf_op jit(solution)/shard_map/ppermute | solution.py:18
  26.3 2.0 %gather_fusion.6 = bf16[16,128,512]{2,1,0:T(8,128)(2,1)} fusion(bf16[5,128,512]{2,1,0:T(8,128)(2,1)S(1)} %constant_dynamic-update-slice_fusion.6, s32[1024]{0:T(1024)S(1)} %get-tuple-element.16), kind=kCustom, calls=%fused_computation.6 | custom fusion | bytes 4194368 | tf_op jit(solution)/shard_map/gather | solution.py:164
  29.9 2.0 %gather_fusion.2 = bf16[16,128,512]{2,1,0:T(8,128)(2,1)} fusion(bf16[5,128,512]{2,1,0:T(8,128)(2,1)S(1)} %bitcast.73, s32[1024]{0:T(1024)S(1)} %get-tuple-element.16), kind=kCustom, calls=%fused_computation.2 | custom fusion | bytes 4194368 | tf_op jit(solution)/shard_map/gather | solution.py:163
  34.7 2.5 %gather_fusion.1 = bf16[24,128,384]{2,1,0:T(8,128)(2,1)S(1)} fusion(bf16[16,128,384]{2,1,0:T(8,128)(2,1)} %constant_dynamic-update-slice_fusion.1, s32[1024]{0:T(1024)S(1)} %get-tuple-element.17), kind=kCustom, calls=%fused_computation.1 | custom fusion | bytes 4718688 | tf_op jit(solution)/shard_map/gather | solution.py:147
  39.5 2.0 %add_convert_fusion = (bf16[1024,384]{1,0:T(8,128)(2,1)S(1)}, f32[1024,384]{1,0:T(8,128)}) fusion(bf16[1024,384]{1,0:T(8,128)(2,1)S(1)} %copy-done.9, f32[1024,384]{1,0:T(8,128)S(1)} %fusion.20, bf16[384,384]{1,0:T(8,128)(2,1)S(1)} %copy-done.20), kind=kOutput, calls=%fused_computation.14 | convolution fusion | flops 305135616 | bytes 5013504 | tf_op jit(solution)/shard_map/dot_general | solution.py:153
  44.2 4.4 %multiply_convert_fusion.1 = bf16[8,128,512]{2,1,0:T(8,128)(2,1)} fusion(bf16[8,256,512]{2,1,0:T(8,128)(2,1)S(1)} %bitcast.77, s32[8,128]{1,0:T(8,128)S(1)} %bitcast.88, bf16[8,128,512]{2,1,0:T(8,128)(2,1)} %bitcast.81), kind=kOutput, calls=%fused_computation.11 | convolution fusion | flops 540019200 | bytes 4198400 | tf_op jit(solution)/shard_map/bij,bje->bie/dot_general | solution.py:177
  48.6 5.3 %multiply_convert_fusion = bf16[8,256,512]{2,1,0:T(8,128)(2,1)} fusion(bf16[8,128,512]{2,1,0:T(8,128)(2,1)} %bitcast.82, s32[8,128]{1,0:T(8,128)S(1)} %bitcast.89, bf16[8,256,512]{2,1,0:T(8,128)(2,1)S(1)} %bitcast.78), kind=kOutput, calls=%fused_computation.10 | convolution fusion | flops 541067776 | bytes 5246976 | tf_op jit(solution)/shard_map/bij,bie->bje/dot_general | solution.py:183
  53.9 2.2 %fusion.22 = f32[384,512]{1,0:T(8,128)S(1)} fusion(bf16[1024,384]{1,0:T(8,128)(2,1)} %copy-done.11, bf16[1024,512]{1,0:T(8,128)(2,1)} %bitcast.91), kind=kOutput, calls=%fused_computation.85 | convolution fusion | flops 402653184 | bytes 2621440 | tf_op jit(solution)/shard_map/dot_general | solution.py:190
  67.7 3.5 %fusion.23 = f32[512,512]{1,0:T(8,128)S(1)} fusion(bf16[2048,512]{1,0:T(8,128)(2,1)} %bitcast.76, bf16[2048,512]{1,0:T(8,128)(2,1)} %bitcast.90), kind=kOutput, calls=%fused_computation.86 | convolution fusion | flops 1073741824 | bytes 5242880 | tf_op jit(solution)/shard_map/dot_general | solution.py:189
  76.3 2.9 %collective-permute-start.4 = (f32[32,11776]{1,0:T(8,128)S(1)}, f32[32,11776]{1,0:T(8,128)}, u32[]{:S(2)}, u32[]{:S(2)}) collective-permute-start(f32[32,11776]{1,0:T(8,128)S(1)} %dynamic-slice_bitcast_fusion), channel_id=1, source_target_pairs={{0,1},{1,0},{2,3},{3,2},{4,5},{5,4},{6,7},{7,6},{8,9},{9,8},{10,11... | collective-permute-start | bytes 4521992 | tf_op jit(solution)/shard_map/ppermute | solution.py:23
  79.3 3.0 %collective-permute-done.4 = f32[32,11776]{1,0:T(8,128)} collective-permute-done((f32[32,11776]{1,0:T(8,128)S(1)}, f32[32,11776]{1,0:T(8,128)}, u32[]{:S(2)}, u32[]{:S(2)}) %collective-permute-start.4) | collective-permute-done | bytes 1507360 | tf_op jit(solution)/shard_map/ppermute | solution.py:23
  82.3 2.0 %bitcast_add_fusion = f32[32,11776]{1,0:T(8,128)S(1)} fusion(f32[32,11776]{1,0:T(8,128)} %collective-permute-done.4, f32[2,32,11776]{2,1,0:T(8,128)} %copy-done.2, s32[]{:T(128)S(6)} %select_n.98), kind=kLoop, calls=%fused_computation.16 | loop fusion | flops 376832 | bytes 4521988 | tf_op jit(solution)/shard_map/add | solution.py:84
  84.3 2.0 %reshape.132 = f32[2,2,2,2,2,11776]{5,4,3,2,1,0:T(2,128)} reshape(f32[32,11776]{1,0:T(8,128)S(1)} %bitcast_add_fusion) | data formatting | bytes 3014656 | tf_op jit(solution)/shard_map/reshape | solution.py:89
  86.3 2.2 %dynamic-slice_convert_fusion = bf16[2,2,2,2,1,11776]{5,4,3,2,1,0:T(2,128)(2,1)S(1)} fusion(f32[2,2,2,2,2,11776]{5,4,3,2,1,0:T(2,128)} %reshape.132, s32[]{:T(128)S(6)} %select_n.104), kind=kLoop, calls=%fused_computation.33 | loop fusion | bytes 753668 | tf_op jit(solution)/shard_map/convert_element_type | solution.py:105
  88.9 5.9 %collective-permute-start.5 = (bf16[2,2,2,2,11776]{4,3,2,1,0:T(2,128)(2,1)S(1)}, bf16[2,2,2,2,11776]{4,3,2,1,0:T(2,128)(2,1)S(1)}, u32[]{:S(2)}, u32[]{:S(2)}) collective-permute-start(bf16[2,2,2,2,11776]{4,3,2,1,0:T(2,128)(2,1)S(1)} %bitcast.85), channel_id=1, source_target_pairs={{0,2},{1,7},{2,0},{3,5},{4,6},{5,3},{6,4},{7,1},{8,10},{9,15},{10,... | collective-permute-start | bytes 1130504 | tf_op jit(solution)/shard_map/ppermute | solution.py:105
  95.6 4.8 %collective-permute-done.5 = bf16[2,2,2,2,11776]{4,3,2,1,0:T(2,128)(2,1)S(1)} collective-permute-done((bf16[2,2,2,2,11776]{4,3,2,1,0:T(2,128)(2,1)S(1)}, bf16[2,2,2,2,11776]{4,3,2,1,0:T(2,128)(2,1)S(1)}, u32[]{:S(2)}, u32[]{:S(2)}) %collective-permute-start.5) | collective-permute-done | bytes 376864 | tf_op jit(solution)/shard_map/ppermute | solution.py:105
  103.0 5.5 %collective-permute-done.6 = bf16[2,2,2,11776]{3,2,1,0:T(2,128)(2,1)S(1)} collective-permute-done((bf16[2,2,2,11776]{3,2,1,0:T(2,128)(2,1)S(1)}, bf16[2,2,2,11776]{3,2,1,0:T(2,128)(2,1)S(1)}, u32[]{:S(2)}, u32[]{:S(2)}) %collective-permute-start.6) | collective-permute-done | bytes 188448 | tf_op jit(solution)/shard_map/ppermute | solution.py:105
  109.2 7.3 %collective-permute-start.7 = (f32[2,2,11776]{2,1,0:T(2,128)S(1)}, f32[2,2,11776]{2,1,0:T(2,128)S(1)}, u32[]{:S(2)}, u32[]{:S(2)}) collective-permute-start(f32[2,2,11776]{2,1,0:T(2,128)S(1)} %bitcast.86), channel_id=1, source_target_pairs={{0,4},{1,5},{2,6},{3,7},{4,0},{5,1},{6,2},{7,3},{8,12},{9,13},{10,... | collective-permute-start | bytes 565256 | tf_op jit(solution)/shard_map/ppermute | solution.py:107
  116.5 5.2 %collective-permute-done.7 = f32[2,2,11776]{2,1,0:T(2,128)S(1)} collective-permute-done((f32[2,2,11776]{2,1,0:T(2,128)S(1)}, f32[2,2,11776]{2,1,0:T(2,128)S(1)}, u32[]{:S(2)}, u32[]{:S(2)}) %collective-permute-start.7) | collective-permute-done | bytes 188448 | tf_op jit(solution)/shard_map/ppermute | solution.py:107
  124.0 5.6 %collective-permute-done.8 = f32[2,11776]{1,0:T(2,128)S(1)} collective-permute-done((f32[2,11776]{1,0:T(2,128)S(1)}, f32[2,11776]{1,0:T(2,128)S(1)}, u32[]{:S(2)}, u32[]{:S(2)}) %collective-permute-start.8) | collective-permute-done | bytes 94240 | tf_op jit(solution)/shard_map/ppermute | solution.py:107
  129.9 5.1 %collective-permute-start.9 = (f32[11776]{0:T(1024)S(1)}, f32[11776]{0:T(1024)S(1)}, u32[]{:S(2)}, u32[]{:S(2)}) collective-permute-start(f32[11776]{0:T(1024)S(1)} %get-tuple-element.4), channel_id=1, source_target_pairs={{0,32},{1,33},{2,34},{3,35},{4,36},{5,37},{6,38},{7,39},{8,40},{9,... | collective-permute-start | bytes 141320 | tf_op jit(solution)/shard_map/ppermute | solution.py:107
  135.1 6.1 %collective-permute-done.9 = f32[11776]{0:T(1024)S(1)} collective-permute-done((f32[11776]{0:T(1024)S(1)}, f32[11776]{0:T(1024)S(1)}, u32[]{:S(2)}, u32[]{:S(2)}) %collective-permute-start.9) | collective-permute-done | bytes 47136 | tf_op jit(solution)/shard_map/ppermute | solution.py:107
  141.2 4.3 %collective-permute-start.10 = (f32[11776]{0:T(1024)S(1)}, f32[11776]{0:T(1024)S(1)}, u32[]{:S(2)}, u32[]{:S(2)}) collective-permute-start(f32[11776]{0:T(1024)S(1)} %add.162), channel_id=1, source_target_pairs={{0,64},{64,0},{128,192},{192,128},{256,320},{320,256},{384,448},{4... | collective-permute-start | bytes 141320 | tf_op jit(solution)/shard_map/ppermute | solution.py:23
  145.5 2.1 %collective-permute-done.10 = f32[11776]{0:T(1024)S(1)} collective-permute-done((f32[11776]{0:T(1024)S(1)}, f32[11776]{0:T(1024)S(1)}, u32[]{:S(2)}, u32[]{:S(2)}) %collective-permute-start.10) | collective-permute-done | bytes 47136 | tf_op jit(solution)/shard_map/ppermute | solution.py:23
  147.6 6.1 %collective-permute-start.11 = (f32[11776]{0:T(1024)S(1)}, f32[11776]{0:T(1024)S(1)}, u32[]{:S(2)}, u32[]{:S(2)}) collective-permute-start(f32[11776]{0:T(1024)S(1)} %add.163), channel_id=1, source_target_pairs={{0,128},{64,192},{128,0},{192,64},{256,384},{320,448},{384,256},{4... | collective-permute-start | bytes 141320 | tf_op jit(solution)/shard_map/ppermute | solution.py:23
  153.7 2.3 %collective-permute-done.11 = f32[11776]{0:T(1024)S(1)} collective-permute-done((f32[11776]{0:T(1024)S(1)}, f32[11776]{0:T(1024)S(1)}, u32[]{:S(2)}, u32[]{:S(2)}) %collective-permute-start.11) | collective-permute-done | bytes 47136 | tf_op jit(solution)/shard_map/ppermute | solution.py:23
  156.0 9.0 %collective-permute-start.12 = (f32[11776]{0:T(1024)S(1)}, f32[11776]{0:T(1024)S(1)}, u32[]{:S(2)}, u32[]{:S(2)}) collective-permute-start(f32[11776]{0:T(1024)S(1)} %add.164), channel_id=1, source_target_pairs={{0,256},{64,320},{128,384},{192,448},{256,0},{320,64},{384,128},{4... | collective-permute-start | bytes 141320 | tf_op jit(solution)/shard_map/ppermute | solution.py:23
  165.0 2.1 %collective-permute-done.12 = f32[11776]{0:T(1024)S(1)} collective-permute-done((f32[11776]{0:T(1024)S(1)}, f32[11776]{0:T(1024)S(1)}, u32[]{:S(2)}, u32[]{:S(2)}) %collective-permute-start.12) | collective-permute-done | bytes 47136 | tf_op jit(solution)/shard_map/ppermute | solution.py:23
  (138 shorter events, 46.1 us)
Async XLA Ops:
  0.6 36.6 %copy-start = (bf16[8,3,128,128]{3,2,1,0:T(8,128)(2,1)S(1)}, bf16[8,3,128,128]{3,2,1,0:T(8,128)(2,1)}, u32[]{:S(2)}) copy-start(bf16[8,3,128,128]{3,2,1,0:T(8,128)(2,1)} %param.16) | copy-start | bytes 2359300
  0.6 18.4 %copy-start.17 = (s32[512]{0:T(512)S(1)}, s32[512]{0:T(512)}, u32[]{:S(2)}) copy-start(s32[512]{0:T(512)} %constant.155) | copy-start | bytes 6148
  0.7 18.4 %copy-start.18 = (s32[384]{0:T(512)S(1)}, s32[384]{0:T(512)}, u32[]{:S(2)}) copy-start(s32[384]{0:T(512)} %constant.152) | copy-start | bytes 4612
  0.7 18.4 %copy-start.12 = (bf16[128,512]{1,0:T(8,128)(2,1)S(1)}, bf16[128,512]{1,0:T(8,128)(2,1)}, u32[]{:S(2)}) copy-start(bf16[128,512]{1,0:T(8,128)(2,1)} %param.21) | copy-start | bytes 393220
  0.7 17.0 %copy-start.8 = (bf16[1024,384]{1,0:T(8,128)(2,1)S(1)}, bf16[1024,384]{1,0:T(8,128)(2,1)}, u32[]{:S(2)}) copy-start(bf16[1024,384]{1,0:T(8,128)(2,1)} %param.15) | copy-start | bytes 2359300
  0.7 17.9 %copy-start.19 = (s32[8,2]{0,1:T(2,128)S(1)}, s32[8,2]{0,1:T(2,128)}, u32[]{:S(2)}) copy-start(s32[8,2]{0,1:T(2,128)} %param.19) | copy-start | bytes 196
  0.7 17.9 %copy-start.16 = (s32[8,3]{0,1:T(4,128)S(1)}, s32[8,3]{0,1:T(4,128)}, u32[]{:S(2)}) copy-start(s32[8,3]{0,1:T(4,128)} %param.17) | copy-start | bytes 292
  5.6 13.7 %collective-permute-start.3 = (bf16[163840]{0:T(1024)(128)(2,1)}, bf16[163840]{0:T(1024)(128)(2,1)S(1)}, u32[]{:S(2)}, u32[]{:S(2)}) collective-permute-start(bf16[163840]{0:T(1024)(128)(2,1)} %constant_dynamic-update-slice_fusion.14), channel_id=1, source_target_pairs={{0,62},{1,63},{2,0},{3,1},{4,2},{5,3},{6,4},{7,5},{8,6},{9,7},{10,... | collective-permute-start | bytes 983048 | tf_op jit(solution)/shard_map/ppermute | solution.py:18
  8.4 11.2 %collective-permute-start.2 = (bf16[163840]{0:T(1024)(128)(2,1)}, bf16[163840]{0:T(1024)(128)(2,1)S(1)}, u32[]{:S(2)}, u32[]{:S(2)}) collective-permute-start(bf16[163840]{0:T(1024)(128)(2,1)} %constant_dynamic-update-slice_fusion.14), channel_id=1, source_target_pairs={{0,63},{1,0},{2,1},{3,2},{4,3},{5,4},{6,5},{7,6},{8,7},{9,8},{10,9... | collective-permute-start | bytes 983048 | tf_op jit(solution)/shard_map/ppermute | solution.py:18
  10.3 13.5 %collective-permute-start.1 = (bf16[163840]{0:T(1024)(128)(2,1)}, bf16[163840]{0:T(1024)(128)(2,1)S(1)}, u32[]{:S(2)}, u32[]{:S(2)}) collective-permute-start(bf16[163840]{0:T(1024)(128)(2,1)} %constant_dynamic-update-slice_fusion.14), channel_id=1, source_target_pairs={{0,2},{1,3},{2,4},{3,5},{4,6},{5,7},{6,8},{7,9},{8,10},{9,11},{10,... | collective-permute-start | bytes 983048 | tf_op jit(solution)/shard_map/ppermute | solution.py:18
  15.5 10.5 %collective-permute-start = (bf16[163840]{0:T(1024)(128)(2,1)}, bf16[163840]{0:T(1024)(128)(2,1)S(1)}, u32[]{:S(2)}, u32[]{:S(2)}) collective-permute-start(bf16[163840]{0:T(1024)(128)(2,1)} %constant_dynamic-update-slice_fusion.14), channel_id=1, source_target_pairs={{0,1},{1,2},{2,3},{3,4},{4,5},{5,6},{6,7},{7,8},{8,9},{9,10},{10,1... | collective-permute-start | bytes 983048 | tf_op jit(solution)/shard_map/ppermute | solution.py:18
  38.0 3.6 %copy-start.4 = (bf16[8,384,128]{1,2,0:T(8,128)(2,1)}, bf16[8,384,128]{1,2,0:T(8,128)(2,1)S(1)}, u32[]{:S(2)}) copy-start(bf16[8,384,128]{1,2,0:T(8,128)(2,1)S(1)} %bitcast_convert_fusion) | copy-start | bytes 2359300
  38.0 1.4 copy-start.9
  38.0 1.5 copy-start.20
  39.5 3.0 %copy-start.13 = (bf16[384,512]{1,0:T(8,128)(2,1)S(1)}, bf16[384,512]{1,0:T(8,128)(2,1)}, u32[]{:S(2)}) copy-start(bf16[384,512]{1,0:T(8,128)(2,1)} %param.24) | copy-start | bytes 1179652
  41.5 2.6 %copy-start.7 = (bf16[16,128,512]{2,1,0:T(8,128)(2,1)S(1)}, bf16[16,128,512]{2,1,0:T(8,128)(2,1)}, u32[]{:S(2)}) copy-start(bf16[16,128,512]{2,1,0:T(8,128)(2,1)} %gather_fusion.2) | copy-start | bytes 6291460
  41.5 2.6 %copy-start.21 = (s32[1024]{0:T(1024)S(1)}, s32[1024]{0:T(1024)}, u32[]{:S(2)}) copy-start(s32[1024]{0:T(1024)} %param.20) | copy-start | bytes 12292
  53.9 2.2 %copy-start.22 = (bf16[8,128,512]{2,1,0:T(8,128)(2,1)S(1)}, bf16[8,128,512]{2,1,0:T(8,128)(2,1)}, u32[]{:S(2)}) copy-start(bf16[8,128,512]{2,1,0:T(8,128)(2,1)} %multiply_convert_fusion.1) | copy-start | bytes 3145732
  53.9 2.3 %copy-start.23 = (f32[1024,384]{1,0:T(8,128)S(1)}, f32[1024,384]{1,0:T(8,128)}, u32[]{:S(2)}) copy-start(f32[1024,384]{1,0:T(8,128)} %get-tuple-element.13) | copy-start | bytes 4718596
  72.8 1.4 copy-start.6
  73.1 1.4 copy-start.3
  74.6 1.6 copy-start.2
  76.3 6.0 %collective-permute-start.4 = (f32[32,11776]{1,0:T(8,128)S(1)}, f32[32,11776]{1,0:T(8,128)}, u32[]{:S(2)}, u32[]{:S(2)}) collective-permute-start(f32[32,11776]{1,0:T(8,128)S(1)} %dynamic-slice_bitcast_fusion), channel_id=1, source_target_pairs={{0,1},{1,0},{2,3},{3,2},{4,5},{5,4},{6,7},{7,6},{8,9},{9,8},{10,11... | collective-permute-start | bytes 4521992 | tf_op jit(solution)/shard_map/ppermute | solution.py:23
  86.3 8.5 %copy-start.1 = (f32[2,2,2,2,2,11776]{5,4,3,2,1,0:T(2,128)S(1)}, f32[2,2,2,2,2,11776]{5,4,3,2,1,0:T(2,128)}, u32[]{:S(2)}) copy-start(f32[2,2,2,2,2,11776]{5,4,3,2,1,0:T(2,128)} %reshape.132) | copy-start | bytes 4521988
  88.9 11.5 %collective-permute-start.5 = (bf16[2,2,2,2,11776]{4,3,2,1,0:T(2,128)(2,1)S(1)}, bf16[2,2,2,2,11776]{4,3,2,1,0:T(2,128)(2,1)S(1)}, u32[]{:S(2)}, u32[]{:S(2)}) collective-permute-start(bf16[2,2,2,2,11776]{4,3,2,1,0:T(2,128)(2,1)S(1)} %bitcast.85), channel_id=1, source_target_pairs={{0,2},{1,7},{2,0},{3,5},{4,6},{5,3},{6,4},{7,1},{8,10},{9,15},{10,... | collective-permute-start | bytes 1130504 | tf_op jit(solution)/shard_map/ppermute | solution.py:105
  101.1 7.5 %collective-permute-start.6 = (bf16[2,2,2,11776]{3,2,1,0:T(2,128)(2,1)S(1)}, bf16[2,2,2,11776]{3,2,1,0:T(2,128)(2,1)S(1)}, u32[]{:S(2)}, u32[]{:S(2)}) collective-permute-start(bf16[2,2,2,11776]{3,2,1,0:T(2,128)(2,1)S(1)} %fusion.14), channel_id=1, source_target_pairs={{0,8},{1,57},{2,10},{3,59},{4,12},{5,61},{6,14},{7,63},{8,0},{9,17... | collective-permute-start | bytes 565256 | tf_op jit(solution)/shard_map/ppermute | solution.py:105
  109.2 12.5 %collective-permute-start.7 = (f32[2,2,11776]{2,1,0:T(2,128)S(1)}, f32[2,2,11776]{2,1,0:T(2,128)S(1)}, u32[]{:S(2)}, u32[]{:S(2)}) collective-permute-start(f32[2,2,11776]{2,1,0:T(2,128)S(1)} %bitcast.86), channel_id=1, source_target_pairs={{0,4},{1,5},{2,6},{3,7},{4,0},{5,1},{6,2},{7,3},{8,12},{9,13},{10,... | collective-permute-start | bytes 565256 | tf_op jit(solution)/shard_map/ppermute | solution.py:107
  122.1 7.5 %collective-permute-start.8 = (f32[2,11776]{1,0:T(2,128)S(1)}, f32[2,11776]{1,0:T(2,128)S(1)}, u32[]{:S(2)}, u32[]{:S(2)}) collective-permute-start(f32[2,11776]{1,0:T(2,128)S(1)} %bitcast.87), channel_id=1, source_target_pairs={{0,16},{1,49},{2,18},{3,51},{4,20},{5,53},{6,22},{7,55},{8,24},{9,... | collective-permute-start | bytes 282632 | tf_op jit(solution)/shard_map/ppermute | solution.py:107
  129.9 11.3 %collective-permute-start.9 = (f32[11776]{0:T(1024)S(1)}, f32[11776]{0:T(1024)S(1)}, u32[]{:S(2)}, u32[]{:S(2)}) collective-permute-start(f32[11776]{0:T(1024)S(1)} %get-tuple-element.4), channel_id=1, source_target_pairs={{0,32},{1,33},{2,34},{3,35},{4,36},{5,37},{6,38},{7,39},{8,40},{9,... | collective-permute-start | bytes 141320 | tf_op jit(solution)/shard_map/ppermute | solution.py:107
  141.2 6.3 %collective-permute-start.10 = (f32[11776]{0:T(1024)S(1)}, f32[11776]{0:T(1024)S(1)}, u32[]{:S(2)}, u32[]{:S(2)}) collective-permute-start(f32[11776]{0:T(1024)S(1)} %add.162), channel_id=1, source_target_pairs={{0,64},{64,0},{128,192},{192,128},{256,320},{320,256},{384,448},{4... | collective-permute-start | bytes 141320 | tf_op jit(solution)/shard_map/ppermute | solution.py:23
  147.6 8.4 %collective-permute-start.11 = (f32[11776]{0:T(1024)S(1)}, f32[11776]{0:T(1024)S(1)}, u32[]{:S(2)}, u32[]{:S(2)}) collective-permute-start(f32[11776]{0:T(1024)S(1)} %add.163), channel_id=1, source_target_pairs={{0,128},{64,192},{128,0},{192,64},{256,384},{320,448},{384,256},{4... | collective-permute-start | bytes 141320 | tf_op jit(solution)/shard_map/ppermute | solution.py:23
  156.0 11.2 %collective-permute-start.12 = (f32[11776]{0:T(1024)S(1)}, f32[11776]{0:T(1024)S(1)}, u32[]{:S(2)}, u32[]{:S(2)}) collective-permute-start(f32[11776]{0:T(1024)S(1)} %add.164), channel_id=1, source_target_pairs={{0,256},{64,320},{128,384},{192,448},{256,0},{320,64},{384,128},{4... | collective-permute-start | bytes 141320 | tf_op jit(solution)/shard_map/ppermute | solution.py:23
  (5 other events, 4.9 us)

commit v4 on v3

--- a/solution.py
+++ b/solution.py
@@ -57,25 +57,17 @@
     return pairs
 
 
-def share_order(rows, n_dom, n_x):
-    n_y = n_dom // (2 * n_x)
-    per = rows // n_dom
-    order = []
-    for c in range(2):
-        for ly in range(n_y):
-            for lx in range(n_x):
-                d = ((ly + c) % n_y * n_x + (lx + c) % n_x) * 2 + c
-                order.extend(range(d * per, (d + 1) * per))
-    return jnp.array(order, dtype=jnp.int32)
-
-
 def reduce_to_share(terms, n_dom, n_x):
     bf16 = jnp.bfloat16
     f32 = jnp.float32
     n_y = n_dom // (2 * n_x)
-    flat = jnp.concatenate(
-        [t[share_order(t.shape[0], n_dom, n_x)].reshape(2, n_y * n_x, -1) for t in terms], axis=2
-    )
+    halves = []
+    for t in terms:
+        grid = t.reshape(n_y, n_x, 2, -1)
+        first = grid[:, :, 0]
+        second = jnp.roll(grid[:, :, 1], (-1, -1), axis=(0, 1))
+        halves.append(jnp.stack([first, second]).reshape(2, n_y * n_x, -1))
+    flat = jnp.concatenate(halves, axis=2)
     width = flat.shape[2]
     me = lax.axis_index("dom")
     core = me % 2
@@ -172,7 +164,7 @@
     target = (positive.reshape(count, BLOCK)[:, :, None] == columns).astype(f32)
     total_gauges = gauges.shape[0] * lax.axis_size("region") * lax.axis_size("dom")
     loss_scale = loss_gain / math.sqrt(total_gauges)
-    logit_grad = ((soft - target) * loss_scale).astype(bf16)
+    logit_grad = lax.optimization_barrier(((soft - target) * loss_scale).astype(bf16))
     query_grad = (
         (jnp.einsum("bij,bje->bie", logit_grad, key_rows, preferred_element_type=f32) * inv_root)
         .astype(bf16)

time: 172 us -> 188 us (1.093)
  the two profiles are of different devices: /device:TPU:6 before, /device:TPU:14 now
where the time goes in v4:
time: 188 us; the launch traced here: 186 us
  local copies, waits for them, and re-layouts  53.9 us (29%)
  starting transfers between devices  53.9 us (29%)
  waiting for transfers between devices  44.6 us (24%)
  matrix products  27 us (14%)
  other arithmetic  5.17 us (3%)
    ppermute x4, starting transfers between devices, swapped(): return lax.ppermute(shard, axis, [(i, i ^ mask) for i in range(count)])  21.5 us
    ppermute x3, starting transfers between devices, reduce_to_share(): got = lax.ppermute(other, 'dom', pairs)  17 us
    ppermute x3, waiting for transfers between devices, reduce_to_share(): got = lax.ppermute(other, 'dom', pairs)  13.9 us
    ppermute x2, waiting for transfers between devices, reduce_to_share(): got = lax.ppermute(other.astype(bf16), 'dom', pairs).astype(f32)  11.9 us
    ppermute x4, starting transfers between devices, passed_along(): lax.ppermute(shard, axis, [(i, (i + by) % count) for i in range(count)])  11.1 us
    ppermute x4, waiting for transfers between devices, swapped(): return lax.ppermute(shard, axis, [(i, i ^ mask) for i in range(count)])  9.65 us
    unnamed x91, local copies, waits for them, and re-layouts  9.64 us
    ppermute x4, waiting for transfers between devices, passed_along(): lax.ppermute(shard, axis, [(i, (i + by) % count) for i in range(count)])  9.21 us
  transfers between devices with their start and end apart: 13, of which 11 were waited for; matrix products, arithmetic and copies ran while one was open for 3% of the time, Pallas kernels for 0%

profile of v4, /device:TPU:14, one launch (start us, length us, event | category | flops | bytes accessed | tf_op | source)
XLA Modules:
  0.0 186.3 jit_solution(4698715301384897458)
XLA Ops:
  7.5 3.4 %collective-permute-start.1 = (bf16[163840]{0:T(1024)(128)(2,1)}, bf16[163840]{0:T(1024)(128)(2,1)}, u32[]{:S(2)}, u32[]{:S(2)}) collective-permute-start(bf16[163840]{0:T(1024)(128)(2,1)} %constant_dynamic-update-slice_fusion.10), channel_id=1, source_target_pairs={{0,2},{1,3},{2,4},{3,5},{4,6},{5,7},{6,8},{7,9},{8,10},{9,11},{10,... | collective-permute-start | bytes 983048 | tf_op jit(solution)/shard_map/ppermute | solution.py:18
  11.0 3.4 %collective-permute-start.2 = (bf16[163840]{0:T(1024)(128)(2,1)}, bf16[163840]{0:T(1024)(128)(2,1)}, u32[]{:S(2)}, u32[]{:S(2)}) collective-permute-start(bf16[163840]{0:T(1024)(128)(2,1)} %constant_dynamic-update-slice_fusion.10), channel_id=1, source_target_pairs={{0,63},{1,0},{2,1},{3,2},{4,3},{5,4},{6,5},{7,6},{8,7},{9,8},{10,9... | collective-permute-start | bytes 983048 | tf_op jit(solution)/shard_map/ppermute | solution.py:18
  14.3 2.4 %collective-permute-start.3 = (bf16[163840]{0:T(1024)(128)(2,1)}, bf16[163840]{0:T(1024)(128)(2,1)}, u32[]{:S(2)}, u32[]{:S(2)}) collective-permute-start(bf16[163840]{0:T(1024)(128)(2,1)} %constant_dynamic-update-slice_fusion.10), channel_id=1, source_target_pairs={{0,62},{1,63},{2,0},{3,1},{4,2},{5,3},{6,4},{7,5},{8,6},{9,7},{10,... | collective-permute-start | bytes 983048 | tf_op jit(solution)/shard_map/ppermute | solution.py:18
  22.5 7.8 %collective-permute-done.3 = bf16[163840]{0:T(1024)(128)(2,1)} collective-permute-done((bf16[163840]{0:T(1024)(128)(2,1)}, bf16[163840]{0:T(1024)(128)(2,1)}, u32[]{:S(2)}, u32[]{:S(2)}) %collective-permute-start.3) | collective-permute-done | bytes 327712 | tf_op jit(solution)/shard_map/ppermute | solution.py:18
  40.5 2.5 %gather_fusion.1 = bf16[24,128,384]{2,1,0:T(8,128)(2,1)S(1)} fusion(bf16[16,128,384]{2,1,0:T(8,128)(2,1)} %copy-done.3, s32[1024]{0:T(1024)S(1)} %get-tuple-element.15), kind=kCustom, calls=%fused_computation.1 | custom fusion | bytes 4718688 | tf_op jit(solution)/shard_map/gather | solution.py:139
  45.2 2.0 %add_convert_fusion = (bf16[1024,384]{1,0:T(8,128)(2,1)S(1)}, f32[1024,384]{1,0:T(8,128)}) fusion(bf16[1024,384]{1,0:T(8,128)(2,1)S(1)} %copy-done.15, f32[1024,384]{1,0:T(8,128)S(1)} %fusion.15, bf16[384,384]{1,0:T(8,128)(2,1)S(1)} %copy-done.33), kind=kOutput, calls=%fused_computation.11 | convolution fusion | flops 305135616 | bytes 5013504 | tf_op jit(solution)/shard_map/dot_general | solution.py:145
  52.2 4.2 %fusion.7 = bf16[8,128,256]{2,1,0:T(8,128)(2,1)} fusion(s32[8,128]{1,0:T(8,128)S(1)} %bitcast.127, bf16[8,128,512]{2,1,0:T(8,128)(2,1)} %bitcast.100, bf16[8,256,512]{2,1,0:T(8,128)(2,1)S(1)} %bitcast.96), kind=kOutput, calls=%fused_computation.24 | convolution fusion | flops 270535168 | bytes 3674112 | tf_op jit(solution)/shard_map/div | solution.py:162
  62.5 2.5 %convolution_bitcast_fusion = f32[384,384]{0,1:T(8,128)} fusion(bf16[1024,384]{1,0:T(8,128)(2,1)} %copy-done.35, bf16[1024,384]{1,0:T(8,128)(2,1)S(1)} %copy-done.16), kind=kOutput, calls=%fused_computation.25 | convolution fusion | flops 301989888 | bytes 2162688 | tf_op jit(solution)/shard_map/dot_general | solution.py:186
  68.2 3.0 %fusion.17 = f32[384,512]{1,0:T(8,128)} fusion(bf16[1024,384]{1,0:T(8,128)(2,1)} %copy-done.21, bf16[1024,512]{1,0:T(8,128)(2,1)} %bitcast.121), kind=kOutput, calls=%fused_computation.87 | convolution fusion | flops 402653184 | bytes 2621440 | tf_op jit(solution)/shard_map/dot_general | solution.py:182
  74.8 3.1 %multiply_convert_fusion = bf16[8,256,512]{2,1,0:T(8,128)(2,1)} fusion(bf16[8,128,256]{2,1,0:T(8,128)(2,1)} %fusion.7, bf16[8,128,512]{2,1,0:T(8,128)(2,1)S(1)} %bitcast.101), kind=kOutput, calls=%fused_computation.6 | convolution fusion | flops 270532608 | bytes 3670016 | tf_op jit(solution)/shard_map/bij,bie->bje/dot_general | solution.py:175
  77.9 2.2 %gather_fusion.3 = bf16[16,128,512]{2,1,0:T(8,128)(2,1)} fusion(bf16[5,128,512]{2,1,0:T(8,128)(2,1)S(1)} %constant_dynamic-update-slice_fusion.6, s32[1024]{0:T(1024)S(1)} %get-tuple-element.14), kind=kCustom, calls=%fused_computation.3 | custom fusion | bytes 4194368 | tf_op jit(solution)/shard_map/gather | solution.py:156
  80.1 4.5 %fusion.18 = f32[512,512]{1,0:T(8,128)} fusion(bf16[2048,512]{1,0:T(8,128)(2,1)} %bitcast.117, bf16[2048,512]{1,0:T(8,128)(2,1)} %bitcast.116), kind=kOutput, calls=%fused_computation.88 | convolution fusion | flops 1073741824 | bytes 5242880 | tf_op jit(solution)/shard_map/dot_general | solution.py:181
  84.6 2.1 %reshape.159 = f32[8,4,2,4096]{3,2,1,0:T(2,128)S(1)} reshape(f32[512,512]{1,0:T(8,128)} %fusion.18) | data formatting | bytes 2097152 | tf_op jit(solution)/shard_map/reshape | solution.py:66
  97.9 3.3 %collective-permute-done.4 = f32[32,11776]{1,0:T(8,128)} collective-permute-done((f32[32,11776]{1,0:T(8,128)S(1)}, f32[32,11776]{1,0:T(8,128)}, u32[]{:S(2)}, u32[]{:S(2)}) %collective-permute-start.4) | collective-permute-done | bytes 1507360 | tf_op jit(solution)/shard_map/ppermute | solution.py:23
  101.3 2.0 %bitcast_add_fusion = f32[32,11776]{1,0:T(8,128)S(1)} fusion(f32[32,11776]{1,0:T(8,128)} %collective-permute-done.4, f32[2,32,11776]{2,1,0:T(8,128)} %copy-done.1, s32[]{:T(128)S(6)} %select_n.82), kind=kLoop, calls=%fused_computation.13 | loop fusion | flops 376832 | bytes 4521988 | tf_op jit(solution)/shard_map/add | solution.py:76
  103.3 2.0 %reshape.160 = f32[2,2,2,2,2,11776]{5,4,3,2,1,0:T(2,128)} reshape(f32[32,11776]{1,0:T(8,128)S(1)} %bitcast_add_fusion) | data formatting | bytes 3014656 | tf_op jit(solution)/shard_map/reshape | solution.py:81
  105.3 2.2 %dynamic-slice_convert_fusion = bf16[2,2,2,2,1,11776]{5,4,3,2,1,0:T(2,128)(2,1)S(1)} fusion(f32[2,2,2,2,2,11776]{5,4,3,2,1,0:T(2,128)} %reshape.160, s32[]{:T(128)S(6)} %select_n.88), kind=kLoop, calls=%fused_computation.28 | loop fusion | bytes 753668 | tf_op jit(solution)/shard_map/convert_element_type | solution.py:97
  110.6 6.8 %collective-permute-done.5 = bf16[2,2,2,2,11776]{4,3,2,1,0:T(2,128)(2,1)S(1)} collective-permute-done((bf16[2,2,2,2,11776]{4,3,2,1,0:T(2,128)(2,1)S(1)}, bf16[2,2,2,2,11776]{4,3,2,1,0:T(2,128)(2,1)S(1)}, u32[]{:S(2)}, u32[]{:S(2)}) %collective-permute-start.5) | collective-permute-done | bytes 376864 | tf_op jit(solution)/shard_map/ppermute | solution.py:97
  118.1 2.4 %collective-permute-start.6 = (bf16[2,2,2,11776]{3,2,1,0:T(2,128)(2,1)S(1)}, bf16[2,2,2,11776]{3,2,1,0:T(2,128)(2,1)S(1)}, u32[]{:S(2)}, u32[]{:S(2)}) collective-permute-start(bf16[2,2,2,11776]{3,2,1,0:T(2,128)(2,1)S(1)} %fusion.12), channel_id=1, source_target_pairs={{0,8},{1,57},{2,10},{3,59},{4,12},{5,61},{6,14},{7,63},{8,0},{9,17... | collective-permute-start | bytes 565256 | tf_op jit(solution)/shard_map/ppermute | solution.py:97
  120.4 5.1 %collective-permute-done.6 = bf16[2,2,2,11776]{3,2,1,0:T(2,128)(2,1)S(1)} collective-permute-done((bf16[2,2,2,11776]{3,2,1,0:T(2,128)(2,1)S(1)}, bf16[2,2,2,11776]{3,2,1,0:T(2,128)(2,1)S(1)}, u32[]{:S(2)}, u32[]{:S(2)}) %collective-permute-start.6) | collective-permute-done | bytes 188448 | tf_op jit(solution)/shard_map/ppermute | solution.py:97
  126.2 3.7 %collective-permute-start.7 = (f32[2,2,11776]{2,1,0:T(2,128)S(1)}, f32[2,2,11776]{2,1,0:T(2,128)S(1)}, u32[]{:S(2)}, u32[]{:S(2)}) collective-permute-start(f32[2,2,11776]{2,1,0:T(2,128)S(1)} %bitcast.125), channel_id=1, source_target_pairs={{0,4},{1,5},{2,6},{3,7},{4,0},{5,1},{6,2},{7,3},{8,12},{9,13},{10,... | collective-permute-start | bytes 565256 | tf_op jit(solution)/shard_map/ppermute | solution.py:99
  129.9 5.6 %collective-permute-done.7 = f32[2,2,11776]{2,1,0:T(2,128)S(1)} collective-permute-done((f32[2,2,11776]{2,1,0:T(2,128)S(1)}, f32[2,2,11776]{2,1,0:T(2,128)S(1)}, u32[]{:S(2)}, u32[]{:S(2)}) %collective-permute-start.7) | collective-permute-done | bytes 188448 | tf_op jit(solution)/shard_map/ppermute | solution.py:99
  135.9 7.8 %collective-permute-start.8 = (f32[2,11776]{1,0:T(2,128)S(1)}, f32[2,11776]{1,0:T(2,128)S(1)}, u32[]{:S(2)}, u32[]{:S(2)}) collective-permute-start(f32[2,11776]{1,0:T(2,128)S(1)} %bitcast.126), channel_id=1, source_target_pairs={{0,16},{1,49},{2,18},{3,51},{4,20},{5,53},{6,22},{7,55},{8,24},{9,... | collective-permute-start | bytes 282632 | tf_op jit(solution)/shard_map/ppermute | solution.py:99
  143.8 3.3 %collective-permute-done.8 = f32[2,11776]{1,0:T(2,128)S(1)} collective-permute-done((f32[2,11776]{1,0:T(2,128)S(1)}, f32[2,11776]{1,0:T(2,128)S(1)}, u32[]{:S(2)}, u32[]{:S(2)}) %collective-permute-start.8) | collective-permute-done | bytes 94240 | tf_op jit(solution)/shard_map/ppermute | solution.py:99
  147.4 5.4 %collective-permute-start.9 = (f32[11776]{0:T(1024)S(1)}, f32[11776]{0:T(1024)S(1)}, u32[]{:S(2)}, u32[]{:S(2)}) collective-permute-start(f32[11776]{0:T(1024)S(1)} %get-tuple-element.4), channel_id=1, source_target_pairs={{0,32},{1,33},{2,34},{3,35},{4,36},{5,37},{6,38},{7,39},{8,40},{9,... | collective-permute-start | bytes 141320 | tf_op jit(solution)/shard_map/ppermute | solution.py:99
  152.8 5.0 %collective-permute-done.9 = f32[11776]{0:T(1024)S(1)} collective-permute-done((f32[11776]{0:T(1024)S(1)}, f32[11776]{0:T(1024)S(1)}, u32[]{:S(2)}, u32[]{:S(2)}) %collective-permute-start.9) | collective-permute-done | bytes 47136 | tf_op jit(solution)/shard_map/ppermute | solution.py:99
  157.8 4.2 %collective-permute-start.10 = (f32[11776]{0:T(1024)S(1)}, f32[11776]{0:T(1024)S(1)}, u32[]{:S(2)}, u32[]{:S(2)}) collective-permute-start(f32[11776]{0:T(1024)S(1)} %add.142), channel_id=1, source_target_pairs={{0,64},{64,0},{128,192},{192,128},{256,320},{320,256},{384,448},{4... | collective-permute-start | bytes 141320 | tf_op jit(solution)/shard_map/ppermute | solution.py:23
  162.1 2.1 %collective-permute-done.10 = f32[11776]{0:T(1024)S(1)} collective-permute-done((f32[11776]{0:T(1024)S(1)}, f32[11776]{0:T(1024)S(1)}, u32[]{:S(2)}, u32[]{:S(2)}) %collective-permute-start.10) | collective-permute-done | bytes 47136 | tf_op jit(solution)/shard_map/ppermute | solution.py:23
  164.2 6.1 %collective-permute-start.11 = (f32[11776]{0:T(1024)S(1)}, f32[11776]{0:T(1024)S(1)}, u32[]{:S(2)}, u32[]{:S(2)}) collective-permute-start(f32[11776]{0:T(1024)S(1)} %add.143), channel_id=1, source_target_pairs={{0,128},{64,192},{128,0},{192,64},{256,384},{320,448},{384,256},{4... | collective-permute-start | bytes 141320 | tf_op jit(solution)/shard_map/ppermute | solution.py:23
  170.2 2.1 %collective-permute-done.11 = f32[11776]{0:T(1024)S(1)} collective-permute-done((f32[11776]{0:T(1024)S(1)}, f32[11776]{0:T(1024)S(1)}, u32[]{:S(2)}, u32[]{:S(2)}) %collective-permute-start.11) | collective-permute-done | bytes 47136 | tf_op jit(solution)/shard_map/ppermute | solution.py:23
  172.3 9.3 %collective-permute-start.12 = (f32[11776]{0:T(1024)S(1)}, f32[11776]{0:T(1024)S(1)}, u32[]{:S(2)}, u32[]{:S(2)}) collective-permute-start(f32[11776]{0:T(1024)S(1)} %add.144), channel_id=1, source_target_pairs={{0,256},{64,320},{128,384},{192,448},{256,0},{320,64},{384,128},{4... | collective-permute-start | bytes 141320 | tf_op jit(solution)/shard_map/ppermute | solution.py:23
  181.6 2.2 %collective-permute-done.12 = f32[11776]{0:T(1024)S(1)} collective-permute-done((f32[11776]{0:T(1024)S(1)}, f32[11776]{0:T(1024)S(1)}, u32[]{:S(2)}, u32[]{:S(2)}) %collective-permute-start.12) | collective-permute-done | bytes 47136 | tf_op jit(solution)/shard_map/ppermute | solution.py:23
  (197 shorter events, 60.7 us)
Async XLA Ops:
  0.6 42.4 %copy-start = (bf16[8,3,128,128]{3,2,1,0:T(8,128)(2,1)S(1)}, bf16[8,3,128,128]{3,2,1,0:T(8,128)(2,1)}, u32[]{:S(2)}) copy-start(bf16[8,3,128,128]{3,2,1,0:T(8,128)(2,1)} %param.12) | copy-start | bytes 2359300
  0.6 16.1 %copy-start.14 = (bf16[1024,384]{1,0:T(8,128)(2,1)S(1)}, bf16[1024,384]{1,0:T(8,128)(2,1)}, u32[]{:S(2)}) copy-start(bf16[1024,384]{1,0:T(8,128)(2,1)} %param.11) | copy-start | bytes 2359300
  0.7 16.6 %copy-start.22 = (bf16[128,512]{1,0:T(8,128)(2,1)S(1)}, bf16[128,512]{1,0:T(8,128)(2,1)}, u32[]{:S(2)}) copy-start(bf16[128,512]{1,0:T(8,128)(2,1)} %param.17) | copy-start | bytes 393220
  0.7 16.2 %copy-start.30 = (s32[8,3]{0,1:T(4,128)S(1)}, s32[8,3]{0,1:T(4,128)}, u32[]{:S(2)}) copy-start(s32[8,3]{0,1:T(4,128)} %param.13) | copy-start | bytes 292
  0.7 16.4 %copy-start.31 = (s32[8,2]{0,1:T(2,128)S(1)}, s32[8,2]{0,1:T(2,128)}, u32[]{:S(2)}) copy-start(s32[8,2]{0,1:T(2,128)} %param.15) | copy-start | bytes 196
  5.6 12.3 %collective-permute-start = (bf16[163840]{0:T(1024)(128)(2,1)}, bf16[163840]{0:T(1024)(128)(2,1)}, u32[]{:S(2)}, u32[]{:S(2)}) collective-permute-start(bf16[163840]{0:T(1024)(128)(2,1)} %constant_dynamic-update-slice_fusion.10), channel_id=1, source_target_pairs={{0,1},{1,2},{2,3},{3,4},{4,5},{5,6},{6,7},{7,8},{8,9},{9,10},{10,1... | collective-permute-start | bytes 983048 | tf_op jit(solution)/shard_map/ppermute | solution.py:18
  7.5 12.9 %collective-permute-start.1 = (bf16[163840]{0:T(1024)(128)(2,1)}, bf16[163840]{0:T(1024)(128)(2,1)}, u32[]{:S(2)}, u32[]{:S(2)}) collective-permute-start(bf16[163840]{0:T(1024)(128)(2,1)} %constant_dynamic-update-slice_fusion.10), channel_id=1, source_target_pairs={{0,2},{1,3},{2,4},{3,5},{4,6},{5,7},{6,8},{7,9},{8,10},{9,11},{10,... | collective-permute-start | bytes 983048 | tf_op jit(solution)/shard_map/ppermute | solution.py:18
  11.0 10.5 %collective-permute-start.2 = (bf16[163840]{0:T(1024)(128)(2,1)}, bf16[163840]{0:T(1024)(128)(2,1)}, u32[]{:S(2)}, u32[]{:S(2)}) collective-permute-start(bf16[163840]{0:T(1024)(128)(2,1)} %constant_dynamic-update-slice_fusion.10), channel_id=1, source_target_pairs={{0,63},{1,0},{2,1},{3,2},{4,3},{5,4},{6,5},{7,6},{8,7},{9,8},{10,9... | collective-permute-start | bytes 983048 | tf_op jit(solution)/shard_map/ppermute | solution.py:18
  14.3 16.0 %collective-permute-start.3 = (bf16[163840]{0:T(1024)(128)(2,1)}, bf16[163840]{0:T(1024)(128)(2,1)}, u32[]{:S(2)}, u32[]{:S(2)}) collective-permute-start(bf16[163840]{0:T(1024)(128)(2,1)} %constant_dynamic-update-slice_fusion.10), channel_id=1, source_target_pairs={{0,62},{1,63},{2,0},{3,1},{4,2},{5,3},{6,4},{7,5},{8,6},{9,7},{10,... | collective-permute-start | bytes 983048 | tf_op jit(solution)/shard_map/ppermute | solution.py:18
  43.7 3.5 %copy-start.8 = (bf16[8,384,128]{1,2,0:T(8,128)(2,1)}, bf16[8,384,128]{1,2,0:T(8,128)(2,1)S(1)}, u32[]{:S(2)}) copy-start(bf16[8,384,128]{1,2,0:T(8,128)(2,1)S(1)} %bitcast_convert_fusion) | copy-start | bytes 2359300
  45.2 2.1 %copy-start.24 = (bf16[384,512]{1,0:T(8,128)(2,1)S(1)}, bf16[384,512]{1,0:T(8,128)(2,1)}, u32[]{:S(2)}) copy-start(bf16[384,512]{1,0:T(8,128)(2,1)} %param.20) | copy-start | bytes 1179652
  47.3 3.2 %copy-start.21 = (bf16[1024,384]{1,0:T(8,128)(2,1)}, bf16[1024,384]{1,0:T(8,128)(2,1)S(1)}, u32[]{:S(2)}) copy-start(bf16[1024,384]{1,0:T(8,128)(2,1)S(1)} %get-tuple-element.12) | copy-start | bytes 2359300
  47.3 1.8 copy-start.32
  50.4 1.8 copy-start.34
  58.1 1.9 %copy-start.9 = (bf16[8,384,128]{1,2,0:T(8,128)(2,1)S(1)}, bf16[8,384,128]{1,2,0:T(8,128)(2,1)}, u32[]{:S(2)}) copy-start(bf16[8,384,128]{1,2,0:T(8,128)(2,1)} %copy-done.8) | copy-start | bytes 2359300
  60.0 2.6 %copy-start.16 = (bf16[1024,384]{1,0:T(8,128)(2,1)S(1)}, bf16[1024,384]{1,0:T(8,128)(2,1)}, u32[]{:S(2)}) copy-start(bf16[1024,384]{1,0:T(8,128)(2,1)} %param.11) | copy-start | bytes 2359300
  60.9 5.8 %copy-start.10 = (f32[8,4,2,2304]{3,2,1,0:T(2,128)}, f32[8,4,2,2304]{3,2,1,0:T(2,128)S(1)}, u32[]{:S(2)}) copy-start(f32[8,4,2,2304]{3,2,1,0:T(2,128)S(1)} %reshape.154) | copy-start | bytes 1769476
  68.2 6.6 %copy-start.5 = (bf16[1024,512]{1,0:T(8,128)(2,1)S(1)}, bf16[1024,512]{1,0:T(8,128)(2,1)}, u32[]{:S(2)}) copy-start(bf16[1024,512]{1,0:T(8,128)(2,1)} %convolution_convert_fusion) | copy-start | bytes 3145732
  73.0 14.3 %copy-start.7 = (f32[8,4,2,3072]{3,2,1,0:T(2,128)}, f32[8,4,2,3072]{3,2,1,0:T(2,128)S(1)}, u32[]{:S(2)}) copy-start(f32[8,4,2,3072]{3,2,1,0:T(2,128)S(1)} %reshape.156) | copy-start | bytes 2359300
  87.3 1.9 %copy-start.28 = (f32[1,4,2304]{2,0,1:T(1,128)S(1)}, f32[1,4,2304]{2,0,1:T(1,128)}, u32[]{:S(2)}) copy-start(f32[1,4,2304]{2,0,1:T(1,128)} %slice_bitcast_fusion.2) | copy-start | bytes 110596
  88.2 2.2 %copy-start.13 = (f32[7,4,1,3072]{3,2,1,0:T(1,128)S(1)}, f32[7,4,1,3072]{3,2,1,0:T(1,128)}, u32[]{:S(2)}) copy-start(f32[7,4,1,3072]{3,2,1,0:T(1,128)} %slice.231) | copy-start | bytes 1032196
  88.3 2.1 %copy-start.27 = (f32[1,4,3072]{2,0,1:T(1,128)S(1)}, f32[1,4,3072]{2,0,1:T(1,128)}, u32[]{:S(2)}) copy-start(f32[1,4,3072]{2,0,1:T(1,128)} %slice_bitcast_fusion.1) | copy-start | bytes 147460
  95.9 5.3 %collective-permute-start.4 = (f32[32,11776]{1,0:T(8,128)S(1)}, f32[32,11776]{1,0:T(8,128)}, u32[]{:S(2)}, u32[]{:S(2)}) collective-permute-start(f32[32,11776]{1,0:T(8,128)S(1)} %dynamic-slice_bitcast_fusion), channel_id=1, source_target_pairs={{0,1},{1,0},{2,3},{3,2},{4,5},{5,4},{6,7},{7,6},{8,9},{9,8},{10,11... | collective-permute-start | bytes 4521992 | tf_op jit(solution)/shard_map/ppermute | solution.py:23
  105.3 4.5 %copy-start.4 = (f32[2,2,2,2,2,11776]{5,4,3,2,1,0:T(2,128)S(1)}, f32[2,2,2,2,2,11776]{5,4,3,2,1,0:T(2,128)}, u32[]{:S(2)}) copy-start(f32[2,2,2,2,2,11776]{5,4,3,2,1,0:T(2,128)} %reshape.160) | copy-start | bytes 4521988
  107.9 9.5 %collective-permute-start.5 = (bf16[2,2,2,2,11776]{4,3,2,1,0:T(2,128)(2,1)S(1)}, bf16[2,2,2,2,11776]{4,3,2,1,0:T(2,128)(2,1)S(1)}, u32[]{:S(2)}, u32[]{:S(2)}) collective-permute-start(bf16[2,2,2,2,11776]{4,3,2,1,0:T(2,128)(2,1)S(1)} %bitcast.124), channel_id=1, source_target_pairs={{0,2},{1,7},{2,0},{3,5},{4,6},{5,3},{6,4},{7,1},{8,10},{9,15},{10,... | collective-permute-start | bytes 1130504 | tf_op jit(solution)/shard_map/ppermute | solution.py:97
  118.1 7.5 %collective-permute-start.6 = (bf16[2,2,2,11776]{3,2,1,0:T(2,128)(2,1)S(1)}, bf16[2,2,2,11776]{3,2,1,0:T(2,128)(2,1)S(1)}, u32[]{:S(2)}, u32[]{:S(2)}) collective-permute-start(bf16[2,2,2,11776]{3,2,1,0:T(2,128)(2,1)S(1)} %fusion.12), channel_id=1, source_target_pairs={{0,8},{1,57},{2,10},{3,59},{4,12},{5,61},{6,14},{7,63},{8,0},{9,17... | collective-permute-start | bytes 565256 | tf_op jit(solution)/shard_map/ppermute | solution.py:97
  126.2 9.4 %collective-permute-start.7 = (f32[2,2,11776]{2,1,0:T(2,128)S(1)}, f32[2,2,11776]{2,1,0:T(2,128)S(1)}, u32[]{:S(2)}, u32[]{:S(2)}) collective-permute-start(f32[2,2,11776]{2,1,0:T(2,128)S(1)} %bitcast.125), channel_id=1, source_target_pairs={{0,4},{1,5},{2,6},{3,7},{4,0},{5,1},{6,2},{7,3},{8,12},{9,13},{10,... | collective-permute-start | bytes 565256 | tf_op jit(solution)/shard_map/ppermute | solution.py:99
  135.9 11.1 %collective-permute-start.8 = (f32[2,11776]{1,0:T(2,128)S(1)}, f32[2,11776]{1,0:T(2,128)S(1)}, u32[]{:S(2)}, u32[]{:S(2)}) collective-permute-start(f32[2,11776]{1,0:T(2,128)S(1)} %bitcast.126), channel_id=1, source_target_pairs={{0,16},{1,49},{2,18},{3,51},{4,20},{5,53},{6,22},{7,55},{8,24},{9,... | collective-permute-start | bytes 282632 | tf_op jit(solution)/shard_map/ppermute | solution.py:99
  147.4 10.4 %collective-permute-start.9 = (f32[11776]{0:T(1024)S(1)}, f32[11776]{0:T(1024)S(1)}, u32[]{:S(2)}, u32[]{:S(2)}) collective-permute-start(f32[11776]{0:T(1024)S(1)} %get-tuple-element.4), channel_id=1, source_target_pairs={{0,32},{1,33},{2,34},{3,35},{4,36},{5,37},{6,38},{7,39},{8,40},{9,... | collective-permute-start | bytes 141320 | tf_op jit(solution)/shard_map/ppermute | solution.py:99
  157.8 6.3 %collective-permute-start.10 = (f32[11776]{0:T(1024)S(1)}, f32[11776]{0:T(1024)S(1)}, u32[]{:S(2)}, u32[]{:S(2)}) collective-permute-start(f32[11776]{0:T(1024)S(1)} %add.142), channel_id=1, source_target_pairs={{0,64},{64,0},{128,192},{192,128},{256,320},{320,256},{384,448},{4... | collective-permute-start | bytes 141320 | tf_op jit(solution)/shard_map/ppermute | solution.py:23
  164.2 8.1 %collective-permute-start.11 = (f32[11776]{0:T(1024)S(1)}, f32[11776]{0:T(1024)S(1)}, u32[]{:S(2)}, u32[]{:S(2)}) collective-permute-start(f32[11776]{0:T(1024)S(1)} %add.143), channel_id=1, source_target_pairs={{0,128},{64,192},{128,0},{192,64},{256,384},{320,448},{384,256},{4... | collective-permute-start | bytes 141320 | tf_op jit(solution)/shard_map/ppermute | solution.py:23
  172.3 11.5 %collective-permute-start.12 = (f32[11776]{0:T(1024)S(1)}, f32[11776]{0:T(1024)S(1)}, u32[]{:S(2)}, u32[]{:S(2)}) collective-permute-start(f32[11776]{0:T(1024)S(1)} %add.144), channel_id=1, source_target_pairs={{0,256},{64,320},{128,384},{192,448},{256,0},{320,64},{384,128},{4... | collective-permute-start | bytes 141320 | tf_op jit(solution)/shard_map/ppermute | solution.py:23
  (22 other events, 27.9 us)

commit v5 on v3

--- a/solution.py
+++ b/solution.py
@@ -172,7 +172,7 @@
     target = (positive.reshape(count, BLOCK)[:, :, None] == columns).astype(f32)
     total_gauges = gauges.shape[0] * lax.axis_size("region") * lax.axis_size("dom")
     loss_scale = loss_gain / math.sqrt(total_gauges)
-    logit_grad = ((soft - target) * loss_scale).astype(bf16)
+    logit_grad = lax.optimization_barrier(((soft - target) * loss_scale).astype(bf16))
     query_grad = (
         (jnp.einsum("bij,bje->bie", logit_grad, key_rows, preferred_element_type=f32) * inv_root)
         .astype(bf16)

time: 172 us -> 170 us (0.988)
  matrix products: 24.1 us -> 19.5 us
  local copies, waits for them, and re-layouts: 42.4 us -> 44.7 us
    dot_general x1, matrix products: 4.44 us -> 0.44 us  [shards(): jnp.einsum('bij,bje->bie', logit_grad, key_rows, preferred_element_type=f32)]
    div x0 -> x1, matrix products: none -> 3.32 us  [shards(): soft = jax.nn.softmax(logits, axis=-1)]
    dot_general x1, matrix products: 5.28 us -> 2.08 us  [shards(): jnp.einsum('bij,bie->bje', logit_grad, query_blocks, preferred_element_ty...]
    unnamed x64 -> x68, local copies, waits for them, and re-layouts: 11.6 us -> 12.8 us
where the time goes in v5:
time: 170 us; the launch traced here: 167 us
  starting transfers between devices  56.5 us (33%)
  local copies, waits for them, and re-layouts  44.7 us (26%)
  waiting for transfers between devices  41.3 us (24%)
  matrix products  19.5 us (11%)
  other arithmetic  3.73 us (2%)
    ppermute x4, starting transfers between devices, swapped(): return lax.ppermute(shard, axis, [(i, i ^ mask) for i in range(count)])  22.3 us
    ppermute x3, waiting for transfers between devices, reduce_to_share(): got = lax.ppermute(other, 'dom', pairs)  16.9 us
    ppermute x3, starting transfers between devices, reduce_to_share(): got = lax.ppermute(other, 'dom', pairs)  14.3 us
    unnamed x68, local copies, waits for them, and re-layouts  12.8 us
    ppermute x4, starting transfers between devices, passed_along(): lax.ppermute(shard, axis, [(i, (i + by) % count) for i in range(count)])  12 us
    ppermute x2, waiting for transfers between devices, reduce_to_share(): got = lax.ppermute(other.astype(bf16), 'dom', pairs).astype(f32)  10.3 us
    ppermute x4, waiting for transfers between devices, swapped(): return lax.ppermute(shard, axis, [(i, i ^ mask) for i in range(count)])  9.43 us
    ppermute x2, starting transfers between devices, reduce_to_share(): got = lax.ppermute(other.astype(bf16), 'dom', pairs).astype(f32)  7.87 us
  transfers between devices with their start and end apart: 13, of which 12 were waited for; matrix products, arithmetic and copies ran while one was open for 2% of the time, Pallas kernels for 0%

profile of v5, /device:TPU:6, one launch (start us, length us, event | category | flops | bytes accessed | tf_op | source)
XLA Modules:
  0.0 167.3 jit_solution(8722271244063375519)
XLA Ops:
  5.7 2.7 %collective-permute-start.3 = (bf16[163840]{0:T(1024)(128)(2,1)}, bf16[163840]{0:T(1024)(128)(2,1)S(1)}, u32[]{:S(2)}, u32[]{:S(2)}) collective-permute-start(bf16[163840]{0:T(1024)(128)(2,1)} %constant_dynamic-update-slice_fusion.14), channel_id=1, source_target_pairs={{0,62},{1,63},{2,0},{3,1},{4,2},{5,3},{6,4},{7,5},{8,6},{9,7},{10,... | collective-permute-start | bytes 983048 | tf_op jit(solution)/shard_map/ppermute | solution.py:18
  10.3 5.2 %collective-permute-start.1 = (bf16[163840]{0:T(1024)(128)(2,1)}, bf16[163840]{0:T(1024)(128)(2,1)S(1)}, u32[]{:S(2)}, u32[]{:S(2)}) collective-permute-start(bf16[163840]{0:T(1024)(128)(2,1)} %constant_dynamic-update-slice_fusion.14), channel_id=1, source_target_pairs={{0,2},{1,3},{2,4},{3,5},{4,6},{5,7},{6,8},{7,9},{8,10},{9,11},{10,... | collective-permute-start | bytes 983048 | tf_op jit(solution)/shard_map/ppermute | solution.py:18
  15.6 2.1 %collective-permute-start = (bf16[163840]{0:T(1024)(128)(2,1)}, bf16[163840]{0:T(1024)(128)(2,1)S(1)}, u32[]{:S(2)}, u32[]{:S(2)}) collective-permute-start(bf16[163840]{0:T(1024)(128)(2,1)} %constant_dynamic-update-slice_fusion.14), channel_id=1, source_target_pairs={{0,1},{1,2},{2,3},{3,4},{4,5},{5,6},{6,7},{7,8},{8,9},{9,10},{10,1... | collective-permute-start | bytes 983048 | tf_op jit(solution)/shard_map/ppermute | solution.py:18
  21.4 2.5 %collective-permute-done.1 = bf16[163840]{0:T(1024)(128)(2,1)S(1)} collective-permute-done((bf16[163840]{0:T(1024)(128)(2,1)}, bf16[163840]{0:T(1024)(128)(2,1)S(1)}, u32[]{:S(2)}, u32[]{:S(2)}) %collective-permute-start.1) | collective-permute-done | bytes 327712 | tf_op jit(solution)/shard_map/ppermute | solution.py:18
  24.1 1.9 %collective-permute-done = bf16[163840]{0:T(1024)(128)(2,1)S(1)} collective-permute-done((bf16[163840]{0:T(1024)(128)(2,1)}, bf16[163840]{0:T(1024)(128)(2,1)S(1)}, u32[]{:S(2)}, u32[]{:S(2)}) %collective-permute-start) | collective-permute-done | bytes 327712 | tf_op jit(solution)/shard_map/ppermute | solution.py:18
  26.4 2.0 %gather_fusion.6 = bf16[16,128,512]{2,1,0:T(8,128)(2,1)} fusion(bf16[5,128,512]{2,1,0:T(8,128)(2,1)S(1)} %constant_dynamic-update-slice_fusion.6, s32[1024]{0:T(1024)S(1)} %get-tuple-element.16), kind=kCustom, calls=%fused_computation.6 | custom fusion | bytes 4194368 | tf_op jit(solution)/shard_map/gather | solution.py:164
  30.0 2.0 %gather_fusion.2 = bf16[16,128,512]{2,1,0:T(8,128)(2,1)} fusion(bf16[5,128,512]{2,1,0:T(8,128)(2,1)S(1)} %bitcast.75, s32[1024]{0:T(1024)S(1)} %get-tuple-element.16), kind=kCustom, calls=%fused_computation.2 | custom fusion | bytes 4194368 | tf_op jit(solution)/shard_map/gather | solution.py:163
  34.8 2.5 %gather_fusion.1 = bf16[24,128,384]{2,1,0:T(8,128)(2,1)S(1)} fusion(bf16[16,128,384]{2,1,0:T(8,128)(2,1)} %constant_dynamic-update-slice_fusion.1, s32[1024]{0:T(1024)S(1)} %get-tuple-element.17), kind=kCustom, calls=%fused_computation.1 | custom fusion | bytes 4718688 | tf_op jit(solution)/shard_map/gather | solution.py:147
  39.6 2.0 %add_convert_fusion = (bf16[1024,384]{1,0:T(8,128)(2,1)S(1)}, f32[1024,384]{1,0:T(8,128)}) fusion(bf16[1024,384]{1,0:T(8,128)(2,1)S(1)} %copy-done.10, f32[1024,384]{1,0:T(8,128)S(1)} %fusion.11, bf16[384,384]{1,0:T(8,128)(2,1)S(1)} %copy-done.23), kind=kOutput, calls=%fused_computation.14 | convolution fusion | flops 305135616 | bytes 5013504 | tf_op jit(solution)/shard_map/dot_general | solution.py:153
  43.8 3.3 %fusion.7 = bf16[8,128,256]{2,1,0:T(8,128)(2,1)S(1)} fusion(s32[8,128]{1,0:T(8,128)S(1)} %bitcast.91, bf16[8,128,512]{2,1,0:T(8,128)(2,1)} %bitcast.76, bf16[8,256,512]{2,1,0:T(8,128)(2,1)S(1)} %bitcast.72), kind=kOutput, calls=%fused_computation.27 | convolution fusion | flops 270535168 | bytes 3674112 | tf_op jit(solution)/shard_map/div | solution.py:170
  53.5 2.1 %multiply_convert_fusion = bf16[8,256,512]{2,1,0:T(8,128)(2,1)} fusion(bf16[8,128,256]{2,1,0:T(8,128)(2,1)S(1)} %fusion.7, bf16[8,128,512]{2,1,0:T(8,128)(2,1)S(1)} %bitcast.77), kind=kOutput, calls=%fused_computation.10 | convolution fusion | flops 270532608 | bytes 3670016 | tf_op jit(solution)/shard_map/bij,bie->bje/dot_general | solution.py:183
  65.3 3.5 %fusion.14 = f32[512,512]{1,0:T(8,128)S(1)} fusion(bf16[2048,512]{1,0:T(8,128)(2,1)} %bitcast.80, bf16[2048,512]{1,0:T(8,128)(2,1)} %bitcast.81), kind=kOutput, calls=%fused_computation.77 | convolution fusion | flops 1073741824 | bytes 5242880 | tf_op jit(solution)/shard_map/dot_general | solution.py:189
  73.9 3.0 %collective-permute-start.4 = (f32[32,11776]{1,0:T(8,128)S(1)}, f32[32,11776]{1,0:T(8,128)}, u32[]{:S(2)}, u32[]{:S(2)}) collective-permute-start(f32[32,11776]{1,0:T(8,128)S(1)} %dynamic-slice_bitcast_fusion), channel_id=1, source_target_pairs={{0,1},{1,0},{2,3},{3,2},{4,5},{5,4},{6,7},{7,6},{8,9},{9,8},{10,11... | collective-permute-start | bytes 4521992 | tf_op jit(solution)/shard_map/ppermute | solution.py:23
  76.9 3.0 %collective-permute-done.4 = f32[32,11776]{1,0:T(8,128)} collective-permute-done((f32[32,11776]{1,0:T(8,128)S(1)}, f32[32,11776]{1,0:T(8,128)}, u32[]{:S(2)}, u32[]{:S(2)}) %collective-permute-start.4) | collective-permute-done | bytes 1507360 | tf_op jit(solution)/shard_map/ppermute | solution.py:23
  79.9 2.0 %bitcast_add_fusion = f32[32,11776]{1,0:T(8,128)S(1)} fusion(f32[32,11776]{1,0:T(8,128)} %collective-permute-done.4, f32[2,32,11776]{2,1,0:T(8,128)} %copy-done.3, s32[]{:T(128)S(6)} %select_n.98), kind=kLoop, calls=%fused_computation.16 | loop fusion | flops 376832 | bytes 4521988 | tf_op jit(solution)/shard_map/add | solution.py:84
  81.9 2.1 %reshape.132 = f32[2,2,2,2,2,11776]{5,4,3,2,1,0:T(2,128)} reshape(f32[32,11776]{1,0:T(8,128)S(1)} %bitcast_add_fusion) | data formatting | bytes 3014656 | tf_op jit(solution)/shard_map/reshape | solution.py:89
  84.0 2.2 %dynamic-slice_convert_fusion = bf16[2,2,2,2,1,11776]{5,4,3,2,1,0:T(2,128)(2,1)S(1)} fusion(f32[2,2,2,2,2,11776]{5,4,3,2,1,0:T(2,128)} %reshape.132, s32[]{:T(128)S(6)} %select_n.104), kind=kLoop, calls=%fused_computation.31 | loop fusion | bytes 753668 | tf_op jit(solution)/shard_map/convert_element_type | solution.py:105
  86.5 5.9 %collective-permute-start.5 = (bf16[2,2,2,2,11776]{4,3,2,1,0:T(2,128)(2,1)S(1)}, bf16[2,2,2,2,11776]{4,3,2,1,0:T(2,128)(2,1)S(1)}, u32[]{:S(2)}, u32[]{:S(2)}) collective-permute-start(bf16[2,2,2,2,11776]{4,3,2,1,0:T(2,128)(2,1)S(1)} %bitcast.88), channel_id=1, source_target_pairs={{0,2},{1,7},{2,0},{3,5},{4,6},{5,3},{6,4},{7,1},{8,10},{9,15},{10,... | collective-permute-start | bytes 1130504 | tf_op jit(solution)/shard_map/ppermute | solution.py:105
  93.3 4.8 %collective-permute-done.5 = bf16[2,2,2,2,11776]{4,3,2,1,0:T(2,128)(2,1)S(1)} collective-permute-done((bf16[2,2,2,2,11776]{4,3,2,1,0:T(2,128)(2,1)S(1)}, bf16[2,2,2,2,11776]{4,3,2,1,0:T(2,128)(2,1)S(1)}, u32[]{:S(2)}, u32[]{:S(2)}) %collective-permute-start.5) | collective-permute-done | bytes 376864 | tf_op jit(solution)/shard_map/ppermute | solution.py:105
  98.7 1.9 %collective-permute-start.6 = (bf16[2,2,2,11776]{3,2,1,0:T(2,128)(2,1)S(1)}, bf16[2,2,2,11776]{3,2,1,0:T(2,128)(2,1)S(1)}, u32[]{:S(2)}, u32[]{:S(2)}) collective-permute-start(bf16[2,2,2,11776]{3,2,1,0:T(2,128)(2,1)S(1)} %fusion.8), channel_id=1, source_target_pairs={{0,8},{1,57},{2,10},{3,59},{4,12},{5,61},{6,14},{7,63},{8,0},{9,17... | collective-permute-start | bytes 565256 | tf_op jit(solution)/shard_map/ppermute | solution.py:105
  100.7 5.5 %collective-permute-done.6 = bf16[2,2,2,11776]{3,2,1,0:T(2,128)(2,1)S(1)} collective-permute-done((bf16[2,2,2,11776]{3,2,1,0:T(2,128)(2,1)S(1)}, bf16[2,2,2,11776]{3,2,1,0:T(2,128)(2,1)S(1)}, u32[]{:S(2)}, u32[]{:S(2)}) %collective-permute-start.6) | collective-permute-done | bytes 188448 | tf_op jit(solution)/shard_map/ppermute | solution.py:105
  106.8 7.3 %collective-permute-start.7 = (f32[2,2,11776]{2,1,0:T(2,128)S(1)}, f32[2,2,11776]{2,1,0:T(2,128)S(1)}, u32[]{:S(2)}, u32[]{:S(2)}) collective-permute-start(f32[2,2,11776]{2,1,0:T(2,128)S(1)} %bitcast.89), channel_id=1, source_target_pairs={{0,4},{1,5},{2,6},{3,7},{4,0},{5,1},{6,2},{7,3},{8,12},{9,13},{10,... | collective-permute-start | bytes 565256 | tf_op jit(solution)/shard_map/ppermute | solution.py:107
  114.1 5.2 %collective-permute-done.7 = f32[2,2,11776]{2,1,0:T(2,128)S(1)} collective-permute-done((f32[2,2,11776]{2,1,0:T(2,128)S(1)}, f32[2,2,11776]{2,1,0:T(2,128)S(1)}, u32[]{:S(2)}, u32[]{:S(2)}) %collective-permute-start.7) | collective-permute-done | bytes 188448 | tf_op jit(solution)/shard_map/ppermute | solution.py:107
  121.7 5.6 %collective-permute-done.8 = f32[2,11776]{1,0:T(2,128)S(1)} collective-permute-done((f32[2,11776]{1,0:T(2,128)S(1)}, f32[2,11776]{1,0:T(2,128)S(1)}, u32[]{:S(2)}, u32[]{:S(2)}) %collective-permute-start.8) | collective-permute-done | bytes 94240 | tf_op jit(solution)/shard_map/ppermute | solution.py:107
  127.6 5.1 %collective-permute-start.9 = (f32[11776]{0:T(1024)S(1)}, f32[11776]{0:T(1024)S(1)}, u32[]{:S(2)}, u32[]{:S(2)}) collective-permute-start(f32[11776]{0:T(1024)S(1)} %get-tuple-element.4), channel_id=1, source_target_pairs={{0,32},{1,33},{2,34},{3,35},{4,36},{5,37},{6,38},{7,39},{8,40},{9,... | collective-permute-start | bytes 141320 | tf_op jit(solution)/shard_map/ppermute | solution.py:107
  132.7 6.2 %collective-permute-done.9 = f32[11776]{0:T(1024)S(1)} collective-permute-done((f32[11776]{0:T(1024)S(1)}, f32[11776]{0:T(1024)S(1)}, u32[]{:S(2)}, u32[]{:S(2)}) %collective-permute-start.9) | collective-permute-done | bytes 47136 | tf_op jit(solution)/shard_map/ppermute | solution.py:107
  138.9 4.3 %collective-permute-start.10 = (f32[11776]{0:T(1024)S(1)}, f32[11776]{0:T(1024)S(1)}, u32[]{:S(2)}, u32[]{:S(2)}) collective-permute-start(f32[11776]{0:T(1024)S(1)} %add.162), channel_id=1, source_target_pairs={{0,64},{64,0},{128,192},{192,128},{256,320},{320,256},{384,448},{4... | collective-permute-start | bytes 141320 | tf_op jit(solution)/shard_map/ppermute | solution.py:23
  143.2 2.1 %collective-permute-done.10 = f32[11776]{0:T(1024)S(1)} collective-permute-done((f32[11776]{0:T(1024)S(1)}, f32[11776]{0:T(1024)S(1)}, u32[]{:S(2)}, u32[]{:S(2)}) %collective-permute-start.10) | collective-permute-done | bytes 47136 | tf_op jit(solution)/shard_map/ppermute | solution.py:23
  145.2 6.1 %collective-permute-start.11 = (f32[11776]{0:T(1024)S(1)}, f32[11776]{0:T(1024)S(1)}, u32[]{:S(2)}, u32[]{:S(2)}) collective-permute-start(f32[11776]{0:T(1024)S(1)} %add.163), channel_id=1, source_target_pairs={{0,128},{64,192},{128,0},{192,64},{256,384},{320,448},{384,256},{4... | collective-permute-start | bytes 141320 | tf_op jit(solution)/shard_map/ppermute | solution.py:23
  151.3 2.3 %collective-permute-done.11 = f32[11776]{0:T(1024)S(1)} collective-permute-done((f32[11776]{0:T(1024)S(1)}, f32[11776]{0:T(1024)S(1)}, u32[]{:S(2)}, u32[]{:S(2)}) %collective-permute-start.11) | collective-permute-done | bytes 47136 | tf_op jit(solution)/shard_map/ppermute | solution.py:23
  153.6 9.0 %collective-permute-start.12 = (f32[11776]{0:T(1024)S(1)}, f32[11776]{0:T(1024)S(1)}, u32[]{:S(2)}, u32[]{:S(2)}) collective-permute-start(f32[11776]{0:T(1024)S(1)} %add.164), channel_id=1, source_target_pairs={{0,256},{64,320},{128,384},{192,448},{256,0},{320,64},{384,128},{4... | collective-permute-start | bytes 141320 | tf_op jit(solution)/shard_map/ppermute | solution.py:23
  162.7 2.1 %collective-permute-done.12 = f32[11776]{0:T(1024)S(1)} collective-permute-done((f32[11776]{0:T(1024)S(1)}, f32[11776]{0:T(1024)S(1)}, u32[]{:S(2)}, u32[]{:S(2)}) %collective-permute-start.12) | collective-permute-done | bytes 47136 | tf_op jit(solution)/shard_map/ppermute | solution.py:23
  (143 shorter events, 48.3 us)
Async XLA Ops:
  0.6 36.7 %copy-start = (bf16[8,3,128,128]{3,2,1,0:T(8,128)(2,1)S(1)}, bf16[8,3,128,128]{3,2,1,0:T(8,128)(2,1)}, u32[]{:S(2)}) copy-start(bf16[8,3,128,128]{3,2,1,0:T(8,128)(2,1)} %param.16) | copy-start | bytes 2359300
  0.6 17.1 %copy-start.9 = (bf16[1024,384]{1,0:T(8,128)(2,1)S(1)}, bf16[1024,384]{1,0:T(8,128)(2,1)}, u32[]{:S(2)}) copy-start(bf16[1024,384]{1,0:T(8,128)(2,1)} %param.15) | copy-start | bytes 2359300
  2.4 16.3 %copy-start.22 = (s32[8,2]{0,1:T(2,128)S(1)}, s32[8,2]{0,1:T(2,128)}, u32[]{:S(2)}) copy-start(s32[8,2]{0,1:T(2,128)} %param.19) | copy-start | bytes 196
  2.4 16.3 %copy-start.19 = (s32[8,3]{0,1:T(4,128)S(1)}, s32[8,3]{0,1:T(4,128)}, u32[]{:S(2)}) copy-start(s32[8,3]{0,1:T(4,128)} %param.17) | copy-start | bytes 292
  2.4 16.6 %copy-start.20 = (s32[512]{0:T(512)S(1)}, s32[512]{0:T(512)}, u32[]{:S(2)}) copy-start(s32[512]{0:T(512)} %constant.155) | copy-start | bytes 6148
  2.4 16.6 %copy-start.21 = (s32[384]{0:T(512)S(1)}, s32[384]{0:T(512)}, u32[]{:S(2)}) copy-start(s32[384]{0:T(512)} %constant.152) | copy-start | bytes 4612
  2.4 16.6 %copy-start.14 = (bf16[128,512]{1,0:T(8,128)(2,1)S(1)}, bf16[128,512]{1,0:T(8,128)(2,1)}, u32[]{:S(2)}) copy-start(bf16[128,512]{1,0:T(8,128)(2,1)} %param.21) | copy-start | bytes 393220
  5.7 13.7 %collective-permute-start.3 = (bf16[163840]{0:T(1024)(128)(2,1)}, bf16[163840]{0:T(1024)(128)(2,1)S(1)}, u32[]{:S(2)}, u32[]{:S(2)}) collective-permute-start(bf16[163840]{0:T(1024)(128)(2,1)} %constant_dynamic-update-slice_fusion.14), channel_id=1, source_target_pairs={{0,62},{1,63},{2,0},{3,1},{4,2},{5,3},{6,4},{7,5},{8,6},{9,7},{10,... | collective-permute-start | bytes 983048 | tf_op jit(solution)/shard_map/ppermute | solution.py:18
  8.4 11.2 %collective-permute-start.2 = (bf16[163840]{0:T(1024)(128)(2,1)}, bf16[163840]{0:T(1024)(128)(2,1)S(1)}, u32[]{:S(2)}, u32[]{:S(2)}) collective-permute-start(bf16[163840]{0:T(1024)(128)(2,1)} %constant_dynamic-update-slice_fusion.14), channel_id=1, source_target_pairs={{0,63},{1,0},{2,1},{3,2},{4,3},{5,4},{6,5},{7,6},{8,7},{9,8},{10,9... | collective-permute-start | bytes 983048 | tf_op jit(solution)/shard_map/ppermute | solution.py:18
  10.3 13.5 %collective-permute-start.1 = (bf16[163840]{0:T(1024)(128)(2,1)}, bf16[163840]{0:T(1024)(128)(2,1)S(1)}, u32[]{:S(2)}, u32[]{:S(2)}) collective-permute-start(bf16[163840]{0:T(1024)(128)(2,1)} %constant_dynamic-update-slice_fusion.14), channel_id=1, source_target_pairs={{0,2},{1,3},{2,4},{3,5},{4,6},{5,7},{6,8},{7,9},{8,10},{9,11},{10,... | collective-permute-start | bytes 983048 | tf_op jit(solution)/shard_map/ppermute | solution.py:18
  15.6 10.5 %collective-permute-start = (bf16[163840]{0:T(1024)(128)(2,1)}, bf16[163840]{0:T(1024)(128)(2,1)S(1)}, u32[]{:S(2)}, u32[]{:S(2)}) collective-permute-start(bf16[163840]{0:T(1024)(128)(2,1)} %constant_dynamic-update-slice_fusion.14), channel_id=1, source_target_pairs={{0,1},{1,2},{2,3},{3,4},{4,5},{5,6},{6,7},{7,8},{8,9},{9,10},{10,1... | collective-permute-start | bytes 983048 | tf_op jit(solution)/shard_map/ppermute | solution.py:18
  38.1 3.5 %copy-start.6 = (bf16[8,384,128]{1,2,0:T(8,128)(2,1)}, bf16[8,384,128]{1,2,0:T(8,128)(2,1)S(1)}, u32[]{:S(2)}) copy-start(bf16[8,384,128]{1,2,0:T(8,128)(2,1)S(1)} %bitcast_convert_fusion) | copy-start | bytes 2359300
  38.1 1.4 copy-start.10
  38.1 1.5 copy-start.23
  39.6 2.0 %copy-start.15 = (bf16[384,512]{1,0:T(8,128)(2,1)S(1)}, bf16[384,512]{1,0:T(8,128)(2,1)}, u32[]{:S(2)}) copy-start(bf16[384,512]{1,0:T(8,128)(2,1)} %param.24) | copy-start | bytes 1179652
  41.6 1.7 %copy-start.12 = (bf16[1024,384]{1,0:T(8,128)(2,1)}, bf16[1024,384]{1,0:T(8,128)(2,1)S(1)}, u32[]{:S(2)}) copy-start(bf16[1024,384]{1,0:T(8,128)(2,1)S(1)} %get-tuple-element.12) | copy-start | bytes 2359300
  41.6 2.3 %copy-start.1 = (bf16[16,128,512]{2,1,0:T(8,128)(2,1)S(1)}, bf16[16,128,512]{2,1,0:T(8,128)(2,1)}, u32[]{:S(2)}) copy-start(bf16[16,128,512]{2,1,0:T(8,128)(2,1)} %gather_fusion.2) | copy-start | bytes 6291460
  41.6 2.3 %copy-start.24 = (s32[1024]{0:T(1024)S(1)}, s32[1024]{0:T(1024)}, u32[]{:S(2)}) copy-start(s32[1024]{0:T(1024)} %param.20) | copy-start | bytes 12292
  48.3 1.5 copy-start.25
  52.1 1.4 copy-start.4
  70.5 1.4 copy-start.8
  72.2 1.6 copy-start.3
  73.9 6.0 %collective-permute-start.4 = (f32[32,11776]{1,0:T(8,128)S(1)}, f32[32,11776]{1,0:T(8,128)}, u32[]{:S(2)}, u32[]{:S(2)}) collective-permute-start(f32[32,11776]{1,0:T(8,128)S(1)} %dynamic-slice_bitcast_fusion), channel_id=1, source_target_pairs={{0,1},{1,0},{2,3},{3,2},{4,5},{5,4},{6,7},{7,6},{8,9},{9,8},{10,11... | collective-permute-start | bytes 4521992 | tf_op jit(solution)/shard_map/ppermute | solution.py:23
  84.0 8.5 %copy-start.2 = (f32[2,2,2,2,2,11776]{5,4,3,2,1,0:T(2,128)S(1)}, f32[2,2,2,2,2,11776]{5,4,3,2,1,0:T(2,128)}, u32[]{:S(2)}) copy-start(f32[2,2,2,2,2,11776]{5,4,3,2,1,0:T(2,128)} %reshape.132) | copy-start | bytes 4521988
  86.5 11.5 %collective-permute-start.5 = (bf16[2,2,2,2,11776]{4,3,2,1,0:T(2,128)(2,1)S(1)}, bf16[2,2,2,2,11776]{4,3,2,1,0:T(2,128)(2,1)S(1)}, u32[]{:S(2)}, u32[]{:S(2)}) collective-permute-start(bf16[2,2,2,2,11776]{4,3,2,1,0:T(2,128)(2,1)S(1)} %bitcast.88), channel_id=1, source_target_pairs={{0,2},{1,7},{2,0},{3,5},{4,6},{5,3},{6,4},{7,1},{8,10},{9,15},{10,... | collective-permute-start | bytes 1130504 | tf_op jit(solution)/shard_map/ppermute | solution.py:105
  98.7 7.5 %collective-permute-start.6 = (bf16[2,2,2,11776]{3,2,1,0:T(2,128)(2,1)S(1)}, bf16[2,2,2,11776]{3,2,1,0:T(2,128)(2,1)S(1)}, u32[]{:S(2)}, u32[]{:S(2)}) collective-permute-start(bf16[2,2,2,11776]{3,2,1,0:T(2,128)(2,1)S(1)} %fusion.8), channel_id=1, source_target_pairs={{0,8},{1,57},{2,10},{3,59},{4,12},{5,61},{6,14},{7,63},{8,0},{9,17... | collective-permute-start | bytes 565256 | tf_op jit(solution)/shard_map/ppermute | solution.py:105
  106.8 12.5 %collective-permute-start.7 = (f32[2,2,11776]{2,1,0:T(2,128)S(1)}, f32[2,2,11776]{2,1,0:T(2,128)S(1)}, u32[]{:S(2)}, u32[]{:S(2)}) collective-permute-start(f32[2,2,11776]{2,1,0:T(2,128)S(1)} %bitcast.89), channel_id=1, source_target_pairs={{0,4},{1,5},{2,6},{3,7},{4,0},{5,1},{6,2},{7,3},{8,12},{9,13},{10,... | collective-permute-start | bytes 565256 | tf_op jit(solution)/shard_map/ppermute | solution.py:107
  119.7 7.5 %collective-permute-start.8 = (f32[2,11776]{1,0:T(2,128)S(1)}, f32[2,11776]{1,0:T(2,128)S(1)}, u32[]{:S(2)}, u32[]{:S(2)}) collective-permute-start(f32[2,11776]{1,0:T(2,128)S(1)} %bitcast.90), channel_id=1, source_target_pairs={{0,16},{1,49},{2,18},{3,51},{4,20},{5,53},{6,22},{7,55},{8,24},{9,... | collective-permute-start | bytes 282632 | tf_op jit(solution)/shard_map/ppermute | solution.py:107
  127.6 11.3 %collective-permute-start.9 = (f32[11776]{0:T(1024)S(1)}, f32[11776]{0:T(1024)S(1)}, u32[]{:S(2)}, u32[]{:S(2)}) collective-permute-start(f32[11776]{0:T(1024)S(1)} %get-tuple-element.4), channel_id=1, source_target_pairs={{0,32},{1,33},{2,34},{3,35},{4,36},{5,37},{6,38},{7,39},{8,40},{9,... | collective-permute-start | bytes 141320 | tf_op jit(solution)/shard_map/ppermute | solution.py:107
  138.9 6.3 %collective-permute-start.10 = (f32[11776]{0:T(1024)S(1)}, f32[11776]{0:T(1024)S(1)}, u32[]{:S(2)}, u32[]{:S(2)}) collective-permute-start(f32[11776]{0:T(1024)S(1)} %add.162), channel_id=1, source_target_pairs={{0,64},{64,0},{128,192},{192,128},{256,320},{320,256},{384,448},{4... | collective-permute-start | bytes 141320 | tf_op jit(solution)/shard_map/ppermute | solution.py:23
  145.2 8.4 %collective-permute-start.11 = (f32[11776]{0:T(1024)S(1)}, f32[11776]{0:T(1024)S(1)}, u32[]{:S(2)}, u32[]{:S(2)}) collective-permute-start(f32[11776]{0:T(1024)S(1)} %add.163), channel_id=1, source_target_pairs={{0,128},{64,192},{128,0},{192,64},{256,384},{320,448},{384,256},{4... | collective-permute-start | bytes 141320 | tf_op jit(solution)/shard_map/ppermute | solution.py:23
  153.6 11.1 %collective-permute-start.12 = (f32[11776]{0:T(1024)S(1)}, f32[11776]{0:T(1024)S(1)}, u32[]{:S(2)}, u32[]{:S(2)}) collective-permute-start(f32[11776]{0:T(1024)S(1)} %add.164), channel_id=1, source_target_pairs={{0,256},{64,320},{128,384},{192,448},{256,0},{320,64},{384,128},{4... | collective-permute-start | bytes 141320 | tf_op jit(solution)/shard_map/ppermute | solution.py:23
  (7 other events, 7.4 us)

commit v6 on v5

--- a/solution.py
+++ b/solution.py
@@ -57,15 +57,34 @@
     return pairs
 
 
+def halving_steps(n_y, n_x):
+    x_bits = n_x.bit_length() - 1
+    y_bits = n_y.bit_length() - 1
+    order = []
+    for b in range(max(x_bits, y_bits)):
+        if b < x_bits:
+            order.append(("x", b))
+        if b < y_bits:
+            order.append(("y", b))
+    return order
+
+
 def share_order(rows, n_dom, n_x):
     n_y = n_dom // (2 * n_x)
     per = rows // n_dom
-    order = []
+    steps = halving_steps(n_y, n_x)
+    slots = [None] * n_dom
     for c in range(2):
         for ly in range(n_y):
             for lx in range(n_x):
                 d = ((ly + c) % n_y * n_x + (lx + c) % n_x) * 2 + c
-                order.extend(range(d * per, (d + 1) * per))
+                slot = c
+                for kind, b in steps:
+                    slot = slot * 2 + (((lx if kind == "x" else ly) >> b) & 1)
+                slots[slot] = d
+    order = []
+    for d in slots:
+        order.extend(range(d * per, (d + 1) * per))
     return jnp.array(order, dtype=jnp.int32)
 
 
@@ -84,29 +103,18 @@
     held = mine + swapped(other, "dom", 1)
     lx = (me // 2 % n_x - core) % n_x
     ly = (me // (2 * n_x) - core) % n_y
-    x_bits = n_x.bit_length() - 1
-    y_bits = n_y.bit_length() - 1
-    held = held.reshape((2,) * y_bits + (2,) * x_bits + (width,))
-    names = ["y%d" % b for b in reversed(range(y_bits))] + ["x%d" % b for b in reversed(range(x_bits))]
-    order = []
-    for b in range(max(x_bits, y_bits)):
-        if b < x_bits:
-            order.append(("x", b))
-        if b < y_bits:
-            order.append(("y", b))
-    for step, (kind, b) in enumerate(order):
-        pos = names.index("%s%d" % (kind, b))
+    for step, (kind, b) in enumerate(halving_steps(n_y, n_x)):
+        held = held.reshape(2, -1, width)
         coord = lx if kind == "x" else ly
         mine_bit = (coord >> b) & 1
-        mine = lax.dynamic_index_in_dim(held, mine_bit, pos, keepdims=False)
-        other = lax.dynamic_index_in_dim(held, 1 - mine_bit, pos, keepdims=False)
+        mine = lax.dynamic_index_in_dim(held, mine_bit, 0, keepdims=False)
+        other = lax.dynamic_index_in_dim(held, 1 - mine_bit, 0, keepdims=False)
         pairs = logical_pairs(n_y, n_x, kind == "x", 1 << b)
         if step < 2:
             got = lax.ppermute(other.astype(bf16), "dom", pairs).astype(f32)
         else:
             got = lax.ppermute(other, "dom", pairs)
         held = mine + got
-        names.pop(pos)
     share = held.reshape(-1)
     n_region = lax.axis_size("region")
     step = 1

time: 170 us -> 164 us (0.965)
  local copies, waits for them, and re-layouts: 44.7 us -> 38.6 us
    convert_element_type x2, local copies, waits for them, and re-layouts: 2.32 us -> 0.08 us  [reduce_to_share(): got = lax.ppermute(other.astype(bf16), 'dom', pairs).astype(f32)]
    reshape x1 -> x2, local copies, waits for them, and re-layouts: 2.07 us -> 0.25 us  [reduce_to_share(): held = held.reshape(2, -1, width)]
    unnamed x68 -> x63, local copies, waits for them, and re-layouts: 12.8 us -> 12.2 us
where the time goes in v6:
time: 164 us; the launch traced here: 161 us
  starting transfers between devices  56.5 us (34%)
  waiting for transfers between devices  42 us (26%)
  local copies, waits for them, and re-layouts  38.6 us (24%)
  matrix products  19.5 us (12%)
  other arithmetic  3.17 us (2%)
    ppermute x4, starting transfers between devices, swapped(): return lax.ppermute(shard, axis, [(i, i ^ mask) for i in range(count)])  22.3 us
    ppermute x3, waiting for transfers between devices, reduce_to_share(): got = lax.ppermute(other, 'dom', pairs)  16.9 us
    ppermute x3, starting transfers between devices, reduce_to_share(): got = lax.ppermute(other, 'dom', pairs)  14.3 us
    unnamed x63, local copies, waits for them, and re-layouts  12.2 us
    ppermute x4, starting transfers between devices, passed_along(): lax.ppermute(shard, axis, [(i, (i + by) % count) for i in range(count)])  12 us
    ppermute x2, waiting for transfers between devices, reduce_to_share(): got = lax.ppermute(other.astype(bf16), 'dom', pairs).astype(f32)  11.1 us
    ppermute x4, waiting for transfers between devices, swapped(): return lax.ppermute(shard, axis, [(i, i ^ mask) for i in range(count)])  9.46 us
    ppermute x2, starting transfers between devices, reduce_to_share(): got = lax.ppermute(other.astype(bf16), 'dom', pairs).astype(f32)  7.89 us
  transfers between devices with their start and end apart: 13, of which 12 were waited for; matrix products, arithmetic and copies ran while one was open for 2% of the time, Pallas kernels for 0%

profile of v6, /device:TPU:6, one launch (start us, length us, event | category | flops | bytes accessed | tf_op | source)
XLA Modules:
  0.0 161.3 jit_solution(4602374925937728970)
XLA Ops:
  5.7 2.7 %collective-permute-start.3 = (bf16[163840]{0:T(1024)(128)(2,1)}, bf16[163840]{0:T(1024)(128)(2,1)S(1)}, u32[]{:S(2)}, u32[]{:S(2)}) collective-permute-start(bf16[163840]{0:T(1024)(128)(2,1)} %constant_dynamic-update-slice_fusion.14), channel_id=1, source_target_pairs={{0,62},{1,63},{2,0},{3,1},{4,2},{5,3},{6,4},{7,5},{8,6},{9,7},{10,... | collective-permute-start | bytes 983048 | tf_op jit(solution)/shard_map/ppermute | solution.py:18
  8.4 1.9 %collective-permute-start.2 = (bf16[163840]{0:T(1024)(128)(2,1)}, bf16[163840]{0:T(1024)(128)(2,1)S(1)}, u32[]{:S(2)}, u32[]{:S(2)}) collective-permute-start(bf16[163840]{0:T(1024)(128)(2,1)} %constant_dynamic-update-slice_fusion.14), channel_id=1, source_target_pairs={{0,63},{1,0},{2,1},{3,2},{4,3},{5,4},{6,5},{7,6},{8,7},{9,8},{10,9... | collective-permute-start | bytes 983048 | tf_op jit(solution)/shard_map/ppermute | solution.py:18
  10.3 5.2 %collective-permute-start.1 = (bf16[163840]{0:T(1024)(128)(2,1)}, bf16[163840]{0:T(1024)(128)(2,1)S(1)}, u32[]{:S(2)}, u32[]{:S(2)}) collective-permute-start(bf16[163840]{0:T(1024)(128)(2,1)} %constant_dynamic-update-slice_fusion.14), channel_id=1, source_target_pairs={{0,2},{1,3},{2,4},{3,5},{4,6},{5,7},{6,8},{7,9},{8,10},{9,11},{10,... | collective-permute-start | bytes 983048 | tf_op jit(solution)/shard_map/ppermute | solution.py:18
  15.6 2.1 %collective-permute-start = (bf16[163840]{0:T(1024)(128)(2,1)}, bf16[163840]{0:T(1024)(128)(2,1)S(1)}, u32[]{:S(2)}, u32[]{:S(2)}) collective-permute-start(bf16[163840]{0:T(1024)(128)(2,1)} %constant_dynamic-update-slice_fusion.14), channel_id=1, source_target_pairs={{0,1},{1,2},{2,3},{3,4},{4,5},{5,6},{6,7},{7,8},{8,9},{9,10},{10,1... | collective-permute-start | bytes 983048 | tf_op jit(solution)/shard_map/ppermute | solution.py:18
  21.4 2.5 %collective-permute-done.1 = bf16[163840]{0:T(1024)(128)(2,1)S(1)} collective-permute-done((bf16[163840]{0:T(1024)(128)(2,1)}, bf16[163840]{0:T(1024)(128)(2,1)S(1)}, u32[]{:S(2)}, u32[]{:S(2)}) %collective-permute-start.1) | collective-permute-done | bytes 327712 | tf_op jit(solution)/shard_map/ppermute | solution.py:18
  24.1 1.9 %collective-permute-done = bf16[163840]{0:T(1024)(128)(2,1)S(1)} collective-permute-done((bf16[163840]{0:T(1024)(128)(2,1)}, bf16[163840]{0:T(1024)(128)(2,1)S(1)}, u32[]{:S(2)}, u32[]{:S(2)}) %collective-permute-start) | collective-permute-done | bytes 327712 | tf_op jit(solution)/shard_map/ppermute | solution.py:18
  26.4 2.0 %gather_fusion.6 = bf16[16,128,512]{2,1,0:T(8,128)(2,1)} fusion(bf16[5,128,512]{2,1,0:T(8,128)(2,1)S(1)} %constant_dynamic-update-slice_fusion.6, s32[1024]{0:T(1024)S(1)} %get-tuple-element.10), kind=kCustom, calls=%fused_computation.6 | custom fusion | bytes 4194368 | tf_op jit(solution)/shard_map/gather | solution.py:172
  30.0 2.0 %gather_fusion.2 = bf16[16,128,512]{2,1,0:T(8,128)(2,1)} fusion(bf16[5,128,512]{2,1,0:T(8,128)(2,1)S(1)} %bitcast.77, s32[1024]{0:T(1024)S(1)} %get-tuple-element.10), kind=kCustom, calls=%fused_computation.2 | custom fusion | bytes 4194368 | tf_op jit(solution)/shard_map/gather | solution.py:171
  34.7 2.5 %gather_fusion.1 = bf16[24,128,384]{2,1,0:T(8,128)(2,1)S(1)} fusion(bf16[16,128,384]{2,1,0:T(8,128)(2,1)} %constant_dynamic-update-slice_fusion.1, s32[1024]{0:T(1024)S(1)} %get-tuple-element.11), kind=kCustom, calls=%fused_computation.1 | custom fusion | bytes 4718688 | tf_op jit(solution)/shard_map/gather | solution.py:155
  39.5 2.0 %add_convert_fusion = (bf16[1024,384]{1,0:T(8,128)(2,1)S(1)}, f32[1024,384]{1,0:T(8,128)}) fusion(bf16[1024,384]{1,0:T(8,128)(2,1)S(1)} %copy-done.9, f32[1024,384]{1,0:T(8,128)S(1)} %fusion.13, bf16[384,384]{1,0:T(8,128)(2,1)S(1)} %copy-done.22), kind=kOutput, calls=%fused_computation.14 | convolution fusion | flops 305135616 | bytes 5013504 | tf_op jit(solution)/shard_map/dot_general | solution.py:161
  43.8 3.3 %fusion.7 = bf16[8,128,256]{2,1,0:T(8,128)(2,1)S(1)} fusion(s32[8,128]{1,0:T(8,128)S(1)} %bitcast.92, bf16[8,128,512]{2,1,0:T(8,128)(2,1)} %bitcast.80, bf16[8,256,512]{2,1,0:T(8,128)(2,1)S(1)} %bitcast.74), kind=kOutput, calls=%fused_computation.27 | convolution fusion | flops 270535168 | bytes 3674112 | tf_op jit(solution)/shard_map/div | solution.py:178
  53.5 2.1 %multiply_convert_fusion = bf16[8,256,512]{2,1,0:T(8,128)(2,1)} fusion(bf16[8,128,256]{2,1,0:T(8,128)(2,1)S(1)} %fusion.7, bf16[8,128,512]{2,1,0:T(8,128)(2,1)S(1)} %bitcast.81), kind=kOutput, calls=%fused_computation.10 | convolution fusion | flops 270532608 | bytes 3670016 | tf_op jit(solution)/shard_map/bij,bie->bje/dot_general | solution.py:191
  65.3 3.5 %fusion.16 = f32[512,512]{1,0:T(8,128)S(1)} fusion(bf16[2048,512]{1,0:T(8,128)(2,1)} %bitcast.84, bf16[2048,512]{1,0:T(8,128)(2,1)} %bitcast.85), kind=kOutput, calls=%fused_computation.73 | convolution fusion | flops 1073741824 | bytes 5242880 | tf_op jit(solution)/shard_map/dot_general | solution.py:197
  73.8 3.0 %collective-permute-start.4 = (f32[32,11776]{1,0:T(8,128)S(1)}, f32[32,11776]{1,0:T(8,128)}, u32[]{:S(2)}, u32[]{:S(2)}) collective-permute-start(f32[32,11776]{1,0:T(8,128)S(1)} %dynamic-slice_bitcast_fusion), channel_id=1, source_target_pairs={{0,1},{1,0},{2,3},{3,2},{4,5},{5,4},{6,7},{7,6},{8,9},{9,8},{10,11... | collective-permute-start | bytes 4521992 | tf_op jit(solution)/shard_map/ppermute | solution.py:23
  76.8 3.0 %collective-permute-done.4 = f32[32,11776]{1,0:T(8,128)} collective-permute-done((f32[32,11776]{1,0:T(8,128)S(1)}, f32[32,11776]{1,0:T(8,128)}, u32[]{:S(2)}, u32[]{:S(2)}) %collective-permute-start.4) | collective-permute-done | bytes 1507360 | tf_op jit(solution)/shard_map/ppermute | solution.py:23
  79.8 2.0 %bitcast_add_fusion = f32[32,11776]{1,0:T(8,128)S(1)} fusion(f32[32,11776]{1,0:T(8,128)} %collective-permute-done.4, f32[2,32,11776]{2,1,0:T(8,128)} %copy-done.2, s32[]{:T(128)S(6)} %select_n.98), kind=kLoop, calls=%fused_computation.16 | loop fusion | flops 376832 | bytes 4521988 | tf_op jit(solution)/shard_map/add | solution.py:103
  81.9 6.0 %collective-permute-start.5 = (bf16[16,11776]{1,0:T(8,128)(2,1)S(1)}, bf16[16,11776]{1,0:T(8,128)(2,1)S(1)}, u32[]{:S(2)}, u32[]{:S(2)}) collective-permute-start(bf16[16,11776]{1,0:T(8,128)(2,1)S(1)} %fusion.9), channel_id=1, source_target_pairs={{0,2},{1,7},{2,0},{3,5},{4,6},{5,3},{6,4},{7,1},{8,10},{9,15},{10,... | collective-permute-start | bytes 1130504 | tf_op jit(solution)/shard_map/ppermute | solution.py:114
  87.9 5.5 %collective-permute-done.5 = bf16[16,11776]{1,0:T(8,128)(2,1)S(1)} collective-permute-done((bf16[16,11776]{1,0:T(8,128)(2,1)S(1)}, bf16[16,11776]{1,0:T(8,128)(2,1)S(1)}, u32[]{:S(2)}, u32[]{:S(2)}) %collective-permute-start.5) | collective-permute-done | bytes 376864 | tf_op jit(solution)/shard_map/ppermute | solution.py:114
  93.5 1.9 %collective-permute-start.6 = (bf16[8,11776]{1,0:T(8,128)(2,1)S(1)}, bf16[8,11776]{1,0:T(8,128)(2,1)S(1)}, u32[]{:S(2)}, u32[]{:S(2)}) collective-permute-start(bf16[8,11776]{1,0:T(8,128)(2,1)S(1)} %fusion.10), channel_id=1, source_target_pairs={{0,8},{1,57},{2,10},{3,59},{4,12},{5,61},{6,14},{7,63},{8,0},{9,17... | collective-permute-start | bytes 565256 | tf_op jit(solution)/shard_map/ppermute | solution.py:114
  95.4 5.5 %collective-permute-done.6 = bf16[8,11776]{1,0:T(8,128)(2,1)S(1)} collective-permute-done((bf16[8,11776]{1,0:T(8,128)(2,1)S(1)}, bf16[8,11776]{1,0:T(8,128)(2,1)S(1)}, u32[]{:S(2)}, u32[]{:S(2)}) %collective-permute-start.6) | collective-permute-done | bytes 188448 | tf_op jit(solution)/shard_map/ppermute | solution.py:114
  101.2 7.3 %collective-permute-start.7 = (f32[4,11776]{1,0:T(4,128)S(1)}, f32[4,11776]{1,0:T(4,128)S(1)}, u32[]{:S(2)}, u32[]{:S(2)}) collective-permute-start(f32[4,11776]{1,0:T(4,128)S(1)} %dynamic-slice_bitcast_fusion.1), channel_id=1, source_target_pairs={{0,4},{1,5},{2,6},{3,7},{4,0},{5,1},{6,2},{7,3},{8,12},{9,13},{10,... | collective-permute-start | bytes 565256 | tf_op jit(solution)/shard_map/ppermute | solution.py:116
  108.5 5.2 %collective-permute-done.7 = f32[4,11776]{1,0:T(4,128)S(1)} collective-permute-done((f32[4,11776]{1,0:T(4,128)S(1)}, f32[4,11776]{1,0:T(4,128)S(1)}, u32[]{:S(2)}, u32[]{:S(2)}) %collective-permute-start.7) | collective-permute-done | bytes 188448 | tf_op jit(solution)/shard_map/ppermute | solution.py:116
  113.9 1.9 %collective-permute-start.8 = (f32[2,11776]{1,0:T(2,128)S(1)}, f32[2,11776]{1,0:T(2,128)S(1)}, u32[]{:S(2)}, u32[]{:S(2)}) collective-permute-start(f32[2,11776]{1,0:T(2,128)S(1)} %dynamic-slice_bitcast_fusion.2), channel_id=1, source_target_pairs={{0,16},{1,49},{2,18},{3,51},{4,20},{5,53},{6,22},{7,55},{8,24},{9,... | collective-permute-start | bytes 282632 | tf_op jit(solution)/shard_map/ppermute | solution.py:116
  115.9 5.6 %collective-permute-done.8 = f32[2,11776]{1,0:T(2,128)S(1)} collective-permute-done((f32[2,11776]{1,0:T(2,128)S(1)}, f32[2,11776]{1,0:T(2,128)S(1)}, u32[]{:S(2)}, u32[]{:S(2)}) %collective-permute-start.8) | collective-permute-done | bytes 94240 | tf_op jit(solution)/shard_map/ppermute | solution.py:116
  121.6 5.1 %collective-permute-start.9 = (f32[1,11776]{1,0:T(1,128)S(1)}, f32[1,11776]{1,0:T(1,128)S(1)}, u32[]{:S(2)}, u32[]{:S(2)}) collective-permute-start(f32[1,11776]{1,0:T(1,128)S(1)} %constant_dynamic-slice_fusion), channel_id=1, source_target_pairs={{0,32},{1,33},{2,34},{3,35},{4,36},{5,37},{6,38},{7,39},{8,40},{9,... | collective-permute-start | bytes 141320 | tf_op jit(solution)/shard_map/ppermute | solution.py:116
  126.7 6.0 %collective-permute-done.9 = f32[1,11776]{1,0:T(1,128)S(1)} collective-permute-done((f32[1,11776]{1,0:T(1,128)S(1)}, f32[1,11776]{1,0:T(1,128)S(1)}, u32[]{:S(2)}, u32[]{:S(2)}) %collective-permute-start.9) | collective-permute-done | bytes 47136 | tf_op jit(solution)/shard_map/ppermute | solution.py:116
  132.9 4.3 %collective-permute-start.10 = (f32[11776]{0:T(1024)S(1)}, f32[11776]{0:T(1024)S(1)}, u32[]{:S(2)}, u32[]{:S(2)}) collective-permute-start(f32[11776]{0:T(1024)S(1)} %add_reduce_fusion), channel_id=1, source_target_pairs={{0,64},{64,0},{128,192},{192,128},{256,320},{320,256},{384,448},{4... | collective-permute-start | bytes 141320 | tf_op jit(solution)/shard_map/ppermute | solution.py:23
  137.2 2.1 %collective-permute-done.10 = f32[11776]{0:T(1024)S(1)} collective-permute-done((f32[11776]{0:T(1024)S(1)}, f32[11776]{0:T(1024)S(1)}, u32[]{:S(2)}, u32[]{:S(2)}) %collective-permute-start.10) | collective-permute-done | bytes 47136 | tf_op jit(solution)/shard_map/ppermute | solution.py:23
  139.2 6.1 %collective-permute-start.11 = (f32[11776]{0:T(1024)S(1)}, f32[11776]{0:T(1024)S(1)}, u32[]{:S(2)}, u32[]{:S(2)}) collective-permute-start(f32[11776]{0:T(1024)S(1)} %add.163), channel_id=1, source_target_pairs={{0,128},{64,192},{128,0},{192,64},{256,384},{320,448},{384,256},{4... | collective-permute-start | bytes 141320 | tf_op jit(solution)/shard_map/ppermute | solution.py:23
  145.3 2.3 %collective-permute-done.11 = f32[11776]{0:T(1024)S(1)} collective-permute-done((f32[11776]{0:T(1024)S(1)}, f32[11776]{0:T(1024)S(1)}, u32[]{:S(2)}, u32[]{:S(2)}) %collective-permute-start.11) | collective-permute-done | bytes 47136 | tf_op jit(solution)/shard_map/ppermute | solution.py:23
  147.6 9.0 %collective-permute-start.12 = (f32[11776]{0:T(1024)S(1)}, f32[11776]{0:T(1024)S(1)}, u32[]{:S(2)}, u32[]{:S(2)}) collective-permute-start(f32[11776]{0:T(1024)S(1)} %add.164), channel_id=1, source_target_pairs={{0,256},{64,320},{128,384},{192,448},{256,0},{320,64},{384,128},{4... | collective-permute-start | bytes 141320 | tf_op jit(solution)/shard_map/ppermute | solution.py:23
  156.7 2.1 %collective-permute-done.12 = f32[11776]{0:T(1024)S(1)} collective-permute-done((f32[11776]{0:T(1024)S(1)}, f32[11776]{0:T(1024)S(1)}, u32[]{:S(2)}, u32[]{:S(2)}) %collective-permute-start.12) | collective-permute-done | bytes 47136 | tf_op jit(solution)/shard_map/ppermute | solution.py:23
  (138 shorter events, 42.0 us)
Async XLA Ops:
  0.6 36.6 %copy-start = (bf16[8,3,128,128]{3,2,1,0:T(8,128)(2,1)S(1)}, bf16[8,3,128,128]{3,2,1,0:T(8,128)(2,1)}, u32[]{:S(2)}) copy-start(bf16[8,3,128,128]{3,2,1,0:T(8,128)(2,1)} %param.16) | copy-start | bytes 2359300
  0.6 17.1 %copy-start.8 = (bf16[1024,384]{1,0:T(8,128)(2,1)S(1)}, bf16[1024,384]{1,0:T(8,128)(2,1)}, u32[]{:S(2)}) copy-start(bf16[1024,384]{1,0:T(8,128)(2,1)} %param.15) | copy-start | bytes 2359300
  2.4 16.3 %copy-start.21 = (s32[8,2]{0,1:T(2,128)S(1)}, s32[8,2]{0,1:T(2,128)}, u32[]{:S(2)}) copy-start(s32[8,2]{0,1:T(2,128)} %param.19) | copy-start | bytes 196
  2.4 16.3 %copy-start.18 = (s32[8,3]{0,1:T(4,128)S(1)}, s32[8,3]{0,1:T(4,128)}, u32[]{:S(2)}) copy-start(s32[8,3]{0,1:T(4,128)} %param.17) | copy-start | bytes 292
  2.4 16.6 %copy-start.19 = (s32[512]{0:T(512)S(1)}, s32[512]{0:T(512)}, u32[]{:S(2)}) copy-start(s32[512]{0:T(512)} %constant.155) | copy-start | bytes 6148
  2.4 16.6 %copy-start.20 = (s32[384]{0:T(512)S(1)}, s32[384]{0:T(512)}, u32[]{:S(2)}) copy-start(s32[384]{0:T(512)} %constant.152) | copy-start | bytes 4612
  2.4 16.6 %copy-start.13 = (bf16[128,512]{1,0:T(8,128)(2,1)S(1)}, bf16[128,512]{1,0:T(8,128)(2,1)}, u32[]{:S(2)}) copy-start(bf16[128,512]{1,0:T(8,128)(2,1)} %param.21) | copy-start | bytes 393220
  5.7 13.7 %collective-permute-start.3 = (bf16[163840]{0:T(1024)(128)(2,1)}, bf16[163840]{0:T(1024)(128)(2,1)S(1)}, u32[]{:S(2)}, u32[]{:S(2)}) collective-permute-start(bf16[163840]{0:T(1024)(128)(2,1)} %constant_dynamic-update-slice_fusion.14), channel_id=1, source_target_pairs={{0,62},{1,63},{2,0},{3,1},{4,2},{5,3},{6,4},{7,5},{8,6},{9,7},{10,... | collective-permute-start | bytes 983048 | tf_op jit(solution)/shard_map/ppermute | solution.py:18
  8.4 11.2 %collective-permute-start.2 = (bf16[163840]{0:T(1024)(128)(2,1)}, bf16[163840]{0:T(1024)(128)(2,1)S(1)}, u32[]{:S(2)}, u32[]{:S(2)}) collective-permute-start(bf16[163840]{0:T(1024)(128)(2,1)} %constant_dynamic-update-slice_fusion.14), channel_id=1, source_target_pairs={{0,63},{1,0},{2,1},{3,2},{4,3},{5,4},{6,5},{7,6},{8,7},{9,8},{10,9... | collective-permute-start | bytes 983048 | tf_op jit(solution)/shard_map/ppermute | solution.py:18
  10.3 13.5 %collective-permute-start.1 = (bf16[163840]{0:T(1024)(128)(2,1)}, bf16[163840]{0:T(1024)(128)(2,1)S(1)}, u32[]{:S(2)}, u32[]{:S(2)}) collective-permute-start(bf16[163840]{0:T(1024)(128)(2,1)} %constant_dynamic-update-slice_fusion.14), channel_id=1, source_target_pairs={{0,2},{1,3},{2,4},{3,5},{4,6},{5,7},{6,8},{7,9},{8,10},{9,11},{10,... | collective-permute-start | bytes 983048 | tf_op jit(solution)/shard_map/ppermute | solution.py:18
  15.6 10.5 %collective-permute-start = (bf16[163840]{0:T(1024)(128)(2,1)}, bf16[163840]{0:T(1024)(128)(2,1)S(1)}, u32[]{:S(2)}, u32[]{:S(2)}) collective-permute-start(bf16[163840]{0:T(1024)(128)(2,1)} %constant_dynamic-update-slice_fusion.14), channel_id=1, source_target_pairs={{0,1},{1,2},{2,3},{3,4},{4,5},{5,6},{6,7},{7,8},{8,9},{9,10},{10,1... | collective-permute-start | bytes 983048 | tf_op jit(solution)/shard_map/ppermute | solution.py:18
  38.0 3.5 %copy-start.5 = (bf16[8,384,128]{1,2,0:T(8,128)(2,1)}, bf16[8,384,128]{1,2,0:T(8,128)(2,1)S(1)}, u32[]{:S(2)}) copy-start(bf16[8,384,128]{1,2,0:T(8,128)(2,1)S(1)} %bitcast_convert_fusion) | copy-start | bytes 2359300
  38.0 1.4 copy-start.9
  38.0 1.5 copy-start.22
  39.5 2.0 %copy-start.14 = (bf16[384,512]{1,0:T(8,128)(2,1)S(1)}, bf16[384,512]{1,0:T(8,128)(2,1)}, u32[]{:S(2)}) copy-start(bf16[384,512]{1,0:T(8,128)(2,1)} %param.24) | copy-start | bytes 1179652
  41.5 1.7 %copy-start.11 = (bf16[1024,384]{1,0:T(8,128)(2,1)}, bf16[1024,384]{1,0:T(8,128)(2,1)S(1)}, u32[]{:S(2)}) copy-start(bf16[1024,384]{1,0:T(8,128)(2,1)S(1)} %get-tuple-element.6) | copy-start | bytes 2359300
  41.5 2.3 %copy-start.1 = (bf16[16,128,512]{2,1,0:T(8,128)(2,1)S(1)}, bf16[16,128,512]{2,1,0:T(8,128)(2,1)}, u32[]{:S(2)}) copy-start(bf16[16,128,512]{2,1,0:T(8,128)(2,1)} %gather_fusion.2) | copy-start | bytes 6291460
  41.5 2.3 %copy-start.23 = (s32[1024]{0:T(1024)S(1)}, s32[1024]{0:T(1024)}, u32[]{:S(2)}) copy-start(s32[1024]{0:T(1024)} %param.20) | copy-start | bytes 12292
  48.2 1.5 copy-start.24
  52.0 1.4 copy-start.3
  70.4 1.4 copy-start.7
  70.6 1.4 copy-start.4
  72.1 1.6 copy-start.2
  73.8 6.0 %collective-permute-start.4 = (f32[32,11776]{1,0:T(8,128)S(1)}, f32[32,11776]{1,0:T(8,128)}, u32[]{:S(2)}, u32[]{:S(2)}) collective-permute-start(f32[32,11776]{1,0:T(8,128)S(1)} %dynamic-slice_bitcast_fusion), channel_id=1, source_target_pairs={{0,1},{1,0},{2,3},{3,2},{4,5},{5,4},{6,7},{7,6},{8,9},{9,8},{10,11... | collective-permute-start | bytes 4521992 | tf_op jit(solution)/shard_map/ppermute | solution.py:23
  81.9 11.5 %collective-permute-start.5 = (bf16[16,11776]{1,0:T(8,128)(2,1)S(1)}, bf16[16,11776]{1,0:T(8,128)(2,1)S(1)}, u32[]{:S(2)}, u32[]{:S(2)}) collective-permute-start(bf16[16,11776]{1,0:T(8,128)(2,1)S(1)} %fusion.9), channel_id=1, source_target_pairs={{0,2},{1,7},{2,0},{3,5},{4,6},{5,3},{6,4},{7,1},{8,10},{9,15},{10,... | collective-permute-start | bytes 1130504 | tf_op jit(solution)/shard_map/ppermute | solution.py:114
  93.5 7.5 %collective-permute-start.6 = (bf16[8,11776]{1,0:T(8,128)(2,1)S(1)}, bf16[8,11776]{1,0:T(8,128)(2,1)S(1)}, u32[]{:S(2)}, u32[]{:S(2)}) collective-permute-start(bf16[8,11776]{1,0:T(8,128)(2,1)S(1)} %fusion.10), channel_id=1, source_target_pairs={{0,8},{1,57},{2,10},{3,59},{4,12},{5,61},{6,14},{7,63},{8,0},{9,17... | collective-permute-start | bytes 565256 | tf_op jit(solution)/shard_map/ppermute | solution.py:114
  101.2 12.5 %collective-permute-start.7 = (f32[4,11776]{1,0:T(4,128)S(1)}, f32[4,11776]{1,0:T(4,128)S(1)}, u32[]{:S(2)}, u32[]{:S(2)}) collective-permute-start(f32[4,11776]{1,0:T(4,128)S(1)} %dynamic-slice_bitcast_fusion.1), channel_id=1, source_target_pairs={{0,4},{1,5},{2,6},{3,7},{4,0},{5,1},{6,2},{7,3},{8,12},{9,13},{10,... | collective-permute-start | bytes 565256 | tf_op jit(solution)/shard_map/ppermute | solution.py:116
  113.9 7.6 %collective-permute-start.8 = (f32[2,11776]{1,0:T(2,128)S(1)}, f32[2,11776]{1,0:T(2,128)S(1)}, u32[]{:S(2)}, u32[]{:S(2)}) collective-permute-start(f32[2,11776]{1,0:T(2,128)S(1)} %dynamic-slice_bitcast_fusion.2), channel_id=1, source_target_pairs={{0,16},{1,49},{2,18},{3,51},{4,20},{5,53},{6,22},{7,55},{8,24},{9,... | collective-permute-start | bytes 282632 | tf_op jit(solution)/shard_map/ppermute | solution.py:116
  121.6 11.1 %collective-permute-start.9 = (f32[1,11776]{1,0:T(1,128)S(1)}, f32[1,11776]{1,0:T(1,128)S(1)}, u32[]{:S(2)}, u32[]{:S(2)}) collective-permute-start(f32[1,11776]{1,0:T(1,128)S(1)} %constant_dynamic-slice_fusion), channel_id=1, source_target_pairs={{0,32},{1,33},{2,34},{3,35},{4,36},{5,37},{6,38},{7,39},{8,40},{9,... | collective-permute-start | bytes 141320 | tf_op jit(solution)/shard_map/ppermute | solution.py:116
  132.9 6.3 %collective-permute-start.10 = (f32[11776]{0:T(1024)S(1)}, f32[11776]{0:T(1024)S(1)}, u32[]{:S(2)}, u32[]{:S(2)}) collective-permute-start(f32[11776]{0:T(1024)S(1)} %add_reduce_fusion), channel_id=1, source_target_pairs={{0,64},{64,0},{128,192},{192,128},{256,320},{320,256},{384,448},{4... | collective-permute-start | bytes 141320 | tf_op jit(solution)/shard_map/ppermute | solution.py:23
  139.2 8.4 %collective-permute-start.11 = (f32[11776]{0:T(1024)S(1)}, f32[11776]{0:T(1024)S(1)}, u32[]{:S(2)}, u32[]{:S(2)}) collective-permute-start(f32[11776]{0:T(1024)S(1)} %add.163), channel_id=1, source_target_pairs={{0,128},{64,192},{128,0},{192,64},{256,384},{320,448},{384,256},{4... | collective-permute-start | bytes 141320 | tf_op jit(solution)/shard_map/ppermute | solution.py:23
  147.6 11.1 %collective-permute-start.12 = (f32[11776]{0:T(1024)S(1)}, f32[11776]{0:T(1024)S(1)}, u32[]{:S(2)}, u32[]{:S(2)}) collective-permute-start(f32[11776]{0:T(1024)S(1)} %add.164), channel_id=1, source_target_pairs={{0,256},{64,320},{128,384},{192,448},{256,0},{320,64},{384,128},{4... | collective-permute-start | bytes 141320 | tf_op jit(solution)/shard_map/ppermute | solution.py:23
  (6 other events, 6.1 us)

commit v7 on v6

--- a/solution.py
+++ b/solution.py
@@ -110,7 +110,7 @@
         mine = lax.dynamic_index_in_dim(held, mine_bit, 0, keepdims=False)
         other = lax.dynamic_index_in_dim(held, 1 - mine_bit, 0, keepdims=False)
         pairs = logical_pairs(n_y, n_x, kind == "x", 1 << b)
-        if step < 2:
+        if step < 4:
             got = lax.ppermute(other.astype(bf16), "dom", pairs).astype(f32)
         else:
             got = lax.ppermute(other, "dom", pairs)

time: 164 us -> 161 us (0.982)
  waiting for transfers between devices: 42 us -> 39 us
    ppermute x3 -> x1, waiting for transfers between devices: 16.9 us -> 5.88 us  [reduce_to_share(): got = lax.ppermute(other, 'dom', pairs)]
    ppermute x3 -> x1, starting transfers between devices: 14.3 us -> 4.78 us  [reduce_to_share(): got = lax.ppermute(other, 'dom', pairs)]
    ppermute x2 -> x4, starting transfers between devices: 7.89 us -> 17.1 us  [reduce_to_share(): got = lax.ppermute(other.astype(bf16), 'dom', pairs).astype(f32)]
    ppermute x2 -> x4, waiting for transfers between devices: 11.1 us -> 19.2 us  [reduce_to_share(): got = lax.ppermute(other.astype(bf16), 'dom', pairs).astype(f32)]
where the time goes in v7:
time: 161 us; the launch traced here: 158 us
  starting transfers between devices  56.4 us (35%)
  waiting for transfers between devices  39 us (24%)
  local copies, waits for them, and re-layouts  38.7 us (24%)
  matrix products  19.5 us (12%)
  other arithmetic  3.17 us (2%)
    ppermute x4, starting transfers between devices, swapped(): return lax.ppermute(shard, axis, [(i, i ^ mask) for i in range(count)])  22.5 us
    ppermute x4, waiting for transfers between devices, reduce_to_share(): got = lax.ppermute(other.astype(bf16), 'dom', pairs).astype(f32)  19.2 us
    ppermute x4, starting transfers between devices, reduce_to_share(): got = lax.ppermute(other.astype(bf16), 'dom', pairs).astype(f32)  17.1 us
    unnamed x63, local copies, waits for them, and re-layouts  12.2 us
    ppermute x4, starting transfers between devices, passed_along(): lax.ppermute(shard, axis, [(i, (i + by) % count) for i in range(count)])  12 us
    ppermute x4, waiting for transfers between devices, swapped(): return lax.ppermute(shard, axis, [(i, i ^ mask) for i in range(count)])  9.27 us
    gather x4, local copies, waits for them, and re-layouts, reduce_to_share(): t[share_order(t.shape[0], n_dom, n_x)].reshape(2, n_y * n_x, -1)  6.89 us
    ppermute x1, waiting for transfers between devices, reduce_to_share(): got = lax.ppermute(other, 'dom', pairs)  5.88 us
  transfers between devices with their start and end apart: 13, of which 12 were waited for; matrix products, arithmetic and copies ran while one was open for 2% of the time, Pallas kernels for 0%

profile of v7, /device:TPU:6, one launch (start us, length us, event | category | flops | bytes accessed | tf_op | source)
XLA Modules:
  0.0 158.1 jit_solution(12627638068572720897)
XLA Ops:
  5.7 2.7 %collective-permute-start.3 = (bf16[163840]{0:T(1024)(128)(2,1)}, bf16[163840]{0:T(1024)(128)(2,1)S(1)}, u32[]{:S(2)}, u32[]{:S(2)}) collective-permute-start(bf16[163840]{0:T(1024)(128)(2,1)} %constant_dynamic-update-slice_fusion.14), channel_id=1, source_target_pairs={{0,62},{1,63},{2,0},{3,1},{4,2},{5,3},{6,4},{7,5},{8,6},{9,7},{10,... | collective-permute-start | bytes 983048 | tf_op jit(solution)/shard_map/ppermute | solution.py:18
  8.4 1.9 %collective-permute-start.2 = (bf16[163840]{0:T(1024)(128)(2,1)}, bf16[163840]{0:T(1024)(128)(2,1)S(1)}, u32[]{:S(2)}, u32[]{:S(2)}) collective-permute-start(bf16[163840]{0:T(1024)(128)(2,1)} %constant_dynamic-update-slice_fusion.14), channel_id=1, source_target_pairs={{0,63},{1,0},{2,1},{3,2},{4,3},{5,4},{6,5},{7,6},{8,7},{9,8},{10,9... | collective-permute-start | bytes 983048 | tf_op jit(solution)/shard_map/ppermute | solution.py:18
  10.3 5.2 %collective-permute-start.1 = (bf16[163840]{0:T(1024)(128)(2,1)}, bf16[163840]{0:T(1024)(128)(2,1)S(1)}, u32[]{:S(2)}, u32[]{:S(2)}) collective-permute-start(bf16[163840]{0:T(1024)(128)(2,1)} %constant_dynamic-update-slice_fusion.14), channel_id=1, source_target_pairs={{0,2},{1,3},{2,4},{3,5},{4,6},{5,7},{6,8},{7,9},{8,10},{9,11},{10,... | collective-permute-start | bytes 983048 | tf_op jit(solution)/shard_map/ppermute | solution.py:18
  15.6 2.1 %collective-permute-start = (bf16[163840]{0:T(1024)(128)(2,1)}, bf16[163840]{0:T(1024)(128)(2,1)S(1)}, u32[]{:S(2)}, u32[]{:S(2)}) collective-permute-start(bf16[163840]{0:T(1024)(128)(2,1)} %constant_dynamic-update-slice_fusion.14), channel_id=1, source_target_pairs={{0,1},{1,2},{2,3},{3,4},{4,5},{5,6},{6,7},{7,8},{8,9},{9,10},{10,1... | collective-permute-start | bytes 983048 | tf_op jit(solution)/shard_map/ppermute | solution.py:18
  21.4 2.5 %collective-permute-done.1 = bf16[163840]{0:T(1024)(128)(2,1)S(1)} collective-permute-done((bf16[163840]{0:T(1024)(128)(2,1)}, bf16[163840]{0:T(1024)(128)(2,1)S(1)}, u32[]{:S(2)}, u32[]{:S(2)}) %collective-permute-start.1) | collective-permute-done | bytes 327712 | tf_op jit(solution)/shard_map/ppermute | solution.py:18
  24.1 1.9 %collective-permute-done = bf16[163840]{0:T(1024)(128)(2,1)S(1)} collective-permute-done((bf16[163840]{0:T(1024)(128)(2,1)}, bf16[163840]{0:T(1024)(128)(2,1)S(1)}, u32[]{:S(2)}, u32[]{:S(2)}) %collective-permute-start) | collective-permute-done | bytes 327712 | tf_op jit(solution)/shard_map/ppermute | solution.py:18
  26.4 2.0 %gather_fusion.6 = bf16[16,128,512]{2,1,0:T(8,128)(2,1)} fusion(bf16[5,128,512]{2,1,0:T(8,128)(2,1)S(1)} %constant_dynamic-update-slice_fusion.6, s32[1024]{0:T(1024)S(1)} %get-tuple-element.10), kind=kCustom, calls=%fused_computation.6 | custom fusion | bytes 4194368 | tf_op jit(solution)/shard_map/gather | solution.py:172
  30.0 2.0 %gather_fusion.2 = bf16[16,128,512]{2,1,0:T(8,128)(2,1)} fusion(bf16[5,128,512]{2,1,0:T(8,128)(2,1)S(1)} %bitcast.77, s32[1024]{0:T(1024)S(1)} %get-tuple-element.10), kind=kCustom, calls=%fused_computation.2 | custom fusion | bytes 4194368 | tf_op jit(solution)/shard_map/gather | solution.py:171
  34.7 2.5 %gather_fusion.1 = bf16[24,128,384]{2,1,0:T(8,128)(2,1)S(1)} fusion(bf16[16,128,384]{2,1,0:T(8,128)(2,1)} %constant_dynamic-update-slice_fusion.1, s32[1024]{0:T(1024)S(1)} %get-tuple-element.11), kind=kCustom, calls=%fused_computation.1 | custom fusion | bytes 4718688 | tf_op jit(solution)/shard_map/gather | solution.py:155
  39.5 2.0 %add_convert_fusion = (bf16[1024,384]{1,0:T(8,128)(2,1)S(1)}, f32[1024,384]{1,0:T(8,128)}) fusion(bf16[1024,384]{1,0:T(8,128)(2,1)S(1)} %copy-done.9, f32[1024,384]{1,0:T(8,128)S(1)} %fusion.15, bf16[384,384]{1,0:T(8,128)(2,1)S(1)} %copy-done.22), kind=kOutput, calls=%fused_computation.14 | convolution fusion | flops 305135616 | bytes 5013504 | tf_op jit(solution)/shard_map/dot_general | solution.py:161
  43.8 3.3 %fusion.7 = bf16[8,128,256]{2,1,0:T(8,128)(2,1)S(1)} fusion(s32[8,128]{1,0:T(8,128)S(1)} %bitcast.92, bf16[8,128,512]{2,1,0:T(8,128)(2,1)} %bitcast.80, bf16[8,256,512]{2,1,0:T(8,128)(2,1)S(1)} %bitcast.74), kind=kOutput, calls=%fused_computation.27 | convolution fusion | flops 270535168 | bytes 3674112 | tf_op jit(solution)/shard_map/div | solution.py:178
  53.5 2.1 %multiply_convert_fusion = bf16[8,256,512]{2,1,0:T(8,128)(2,1)} fusion(bf16[8,128,256]{2,1,0:T(8,128)(2,1)S(1)} %fusion.7, bf16[8,128,512]{2,1,0:T(8,128)(2,1)S(1)} %bitcast.81), kind=kOutput, calls=%fused_computation.10 | convolution fusion | flops 270532608 | bytes 3670016 | tf_op jit(solution)/shard_map/bij,bie->bje/dot_general | solution.py:191
  65.3 3.5 %fusion.18 = f32[512,512]{1,0:T(8,128)S(1)} fusion(bf16[2048,512]{1,0:T(8,128)(2,1)} %bitcast.84, bf16[2048,512]{1,0:T(8,128)(2,1)} %bitcast.85), kind=kOutput, calls=%fused_computation.75 | convolution fusion | flops 1073741824 | bytes 5242880 | tf_op jit(solution)/shard_map/dot_general | solution.py:197
  73.8 3.0 %collective-permute-start.4 = (f32[32,11776]{1,0:T(8,128)S(1)}, f32[32,11776]{1,0:T(8,128)}, u32[]{:S(2)}, u32[]{:S(2)}) collective-permute-start(f32[32,11776]{1,0:T(8,128)S(1)} %dynamic-slice_bitcast_fusion), channel_id=1, source_target_pairs={{0,1},{1,0},{2,3},{3,2},{4,5},{5,4},{6,7},{7,6},{8,9},{9,8},{10,11... | collective-permute-start | bytes 4521992 | tf_op jit(solution)/shard_map/ppermute | solution.py:23
  76.8 3.0 %collective-permute-done.4 = f32[32,11776]{1,0:T(8,128)} collective-permute-done((f32[32,11776]{1,0:T(8,128)S(1)}, f32[32,11776]{1,0:T(8,128)}, u32[]{:S(2)}, u32[]{:S(2)}) %collective-permute-start.4) | collective-permute-done | bytes 1507360 | tf_op jit(solution)/shard_map/ppermute | solution.py:23
  79.8 2.0 %bitcast_add_fusion = f32[32,11776]{1,0:T(8,128)S(1)} fusion(f32[32,11776]{1,0:T(8,128)} %collective-permute-done.4, f32[2,32,11776]{2,1,0:T(8,128)} %copy-done.2, s32[]{:T(128)S(6)} %select_n.98), kind=kLoop, calls=%fused_computation.16 | loop fusion | flops 376832 | bytes 4521988 | tf_op jit(solution)/shard_map/add | solution.py:103
  81.9 6.0 %collective-permute-start.5 = (bf16[16,11776]{1,0:T(8,128)(2,1)S(1)}, bf16[16,11776]{1,0:T(8,128)(2,1)S(1)}, u32[]{:S(2)}, u32[]{:S(2)}) collective-permute-start(bf16[16,11776]{1,0:T(8,128)(2,1)S(1)} %fusion.9), channel_id=1, source_target_pairs={{0,2},{1,7},{2,0},{3,5},{4,6},{5,3},{6,4},{7,1},{8,10},{9,15},{10,... | collective-permute-start | bytes 1130504 | tf_op jit(solution)/shard_map/ppermute | solution.py:114
  87.9 5.5 %collective-permute-done.5 = bf16[16,11776]{1,0:T(8,128)(2,1)S(1)} collective-permute-done((bf16[16,11776]{1,0:T(8,128)(2,1)S(1)}, bf16[16,11776]{1,0:T(8,128)(2,1)S(1)}, u32[]{:S(2)}, u32[]{:S(2)}) %collective-permute-start.5) | collective-permute-done | bytes 376864 | tf_op jit(solution)/shard_map/ppermute | solution.py:114
  93.5 1.9 %collective-permute-start.6 = (bf16[8,11776]{1,0:T(8,128)(2,1)S(1)}, bf16[8,11776]{1,0:T(8,128)(2,1)S(1)}, u32[]{:S(2)}, u32[]{:S(2)}) collective-permute-start(bf16[8,11776]{1,0:T(8,128)(2,1)S(1)} %fusion.10), channel_id=1, source_target_pairs={{0,8},{1,57},{2,10},{3,59},{4,12},{5,61},{6,14},{7,63},{8,0},{9,17... | collective-permute-start | bytes 565256 | tf_op jit(solution)/shard_map/ppermute | solution.py:114
  95.4 5.5 %collective-permute-done.6 = bf16[8,11776]{1,0:T(8,128)(2,1)S(1)} collective-permute-done((bf16[8,11776]{1,0:T(8,128)(2,1)S(1)}, bf16[8,11776]{1,0:T(8,128)(2,1)S(1)}, u32[]{:S(2)}, u32[]{:S(2)}) %collective-permute-start.6) | collective-permute-done | bytes 188448 | tf_op jit(solution)/shard_map/ppermute | solution.py:114
  101.2 7.3 %collective-permute-start.7 = (bf16[4,11776]{1,0:T(4,128)(2,1)S(1)}, bf16[4,11776]{1,0:T(4,128)(2,1)S(1)}, u32[]{:S(2)}, u32[]{:S(2)}) collective-permute-start(bf16[4,11776]{1,0:T(4,128)(2,1)S(1)} %fusion.11), channel_id=1, source_target_pairs={{0,4},{1,5},{2,6},{3,7},{4,0},{5,1},{6,2},{7,3},{8,12},{9,13},{10,... | collective-permute-start | bytes 282632 | tf_op jit(solution)/shard_map/ppermute | solution.py:114
  108.5 3.2 %collective-permute-done.7 = bf16[4,11776]{1,0:T(4,128)(2,1)S(1)} collective-permute-done((bf16[4,11776]{1,0:T(4,128)(2,1)S(1)}, bf16[4,11776]{1,0:T(4,128)(2,1)S(1)}, u32[]{:S(2)}, u32[]{:S(2)}) %collective-permute-start.7) | collective-permute-done | bytes 94240 | tf_op jit(solution)/shard_map/ppermute | solution.py:114
  112.0 1.9 %collective-permute-start.8 = (bf16[2,11776]{1,0:T(2,128)(2,1)S(1)}, bf16[2,11776]{1,0:T(2,128)(2,1)S(1)}, u32[]{:S(2)}, u32[]{:S(2)}) collective-permute-start(bf16[2,11776]{1,0:T(2,128)(2,1)S(1)} %fusion.12), channel_id=1, source_target_pairs={{0,16},{1,49},{2,18},{3,51},{4,20},{5,53},{6,22},{7,55},{8,24},{9,... | collective-permute-start | bytes 141320 | tf_op jit(solution)/shard_map/ppermute | solution.py:114
  113.9 4.9 %collective-permute-done.8 = bf16[2,11776]{1,0:T(2,128)(2,1)S(1)} collective-permute-done((bf16[2,11776]{1,0:T(2,128)(2,1)S(1)}, bf16[2,11776]{1,0:T(2,128)(2,1)S(1)}, u32[]{:S(2)}, u32[]{:S(2)}) %collective-permute-start.8) | collective-permute-done | bytes 47136 | tf_op jit(solution)/shard_map/ppermute | solution.py:114
  118.9 4.8 %collective-permute-start.9 = (f32[1,11776]{1,0:T(1,128)S(1)}, f32[1,11776]{1,0:T(1,128)S(1)}, u32[]{:S(2)}, u32[]{:S(2)}) collective-permute-start(f32[1,11776]{1,0:T(1,128)S(1)} %constant_dynamic-slice_fusion), channel_id=1, source_target_pairs={{0,32},{1,33},{2,34},{3,35},{4,36},{5,37},{6,38},{7,39},{8,40},{9,... | collective-permute-start | bytes 141320 | tf_op jit(solution)/shard_map/ppermute | solution.py:116
  123.7 5.9 %collective-permute-done.9 = f32[1,11776]{1,0:T(1,128)S(1)} collective-permute-done((f32[1,11776]{1,0:T(1,128)S(1)}, f32[1,11776]{1,0:T(1,128)S(1)}, u32[]{:S(2)}, u32[]{:S(2)}) %collective-permute-start.9) | collective-permute-done | bytes 47136 | tf_op jit(solution)/shard_map/ppermute | solution.py:116
  129.8 4.2 %collective-permute-start.10 = (f32[11776]{0:T(1024)S(1)}, f32[11776]{0:T(1024)S(1)}, u32[]{:S(2)}, u32[]{:S(2)}) collective-permute-start(f32[11776]{0:T(1024)S(1)} %add_reduce_fusion), channel_id=1, source_target_pairs={{0,64},{64,0},{128,192},{192,128},{256,320},{320,256},{384,448},{4... | collective-permute-start | bytes 141320 | tf_op jit(solution)/shard_map/ppermute | solution.py:23
  134.0 2.1 %collective-permute-done.10 = f32[11776]{0:T(1024)S(1)} collective-permute-done((f32[11776]{0:T(1024)S(1)}, f32[11776]{0:T(1024)S(1)}, u32[]{:S(2)}, u32[]{:S(2)}) %collective-permute-start.10) | collective-permute-done | bytes 47136 | tf_op jit(solution)/shard_map/ppermute | solution.py:23
  136.1 6.1 %collective-permute-start.11 = (f32[11776]{0:T(1024)S(1)}, f32[11776]{0:T(1024)S(1)}, u32[]{:S(2)}, u32[]{:S(2)}) collective-permute-start(f32[11776]{0:T(1024)S(1)} %add.163), channel_id=1, source_target_pairs={{0,128},{64,192},{128,0},{192,64},{256,384},{320,448},{384,256},{4... | collective-permute-start | bytes 141320 | tf_op jit(solution)/shard_map/ppermute | solution.py:23
  142.2 2.1 %collective-permute-done.11 = f32[11776]{0:T(1024)S(1)} collective-permute-done((f32[11776]{0:T(1024)S(1)}, f32[11776]{0:T(1024)S(1)}, u32[]{:S(2)}, u32[]{:S(2)}) %collective-permute-start.11) | collective-permute-done | bytes 47136 | tf_op jit(solution)/shard_map/ppermute | solution.py:23
  144.3 9.2 %collective-permute-start.12 = (f32[11776]{0:T(1024)S(1)}, f32[11776]{0:T(1024)S(1)}, u32[]{:S(2)}, u32[]{:S(2)}) collective-permute-start(f32[11776]{0:T(1024)S(1)} %add.164), channel_id=1, source_target_pairs={{0,256},{64,320},{128,384},{192,448},{256,0},{320,64},{384,128},{4... | collective-permute-start | bytes 141320 | tf_op jit(solution)/shard_map/ppermute | solution.py:23
  153.5 2.1 %collective-permute-done.12 = f32[11776]{0:T(1024)S(1)} collective-permute-done((f32[11776]{0:T(1024)S(1)}, f32[11776]{0:T(1024)S(1)}, u32[]{:S(2)}, u32[]{:S(2)}) %collective-permute-start.12) | collective-permute-done | bytes 47136 | tf_op jit(solution)/shard_map/ppermute | solution.py:23
  (138 shorter events, 42.1 us)
Async XLA Ops:
  0.6 36.6 %copy-start = (bf16[8,3,128,128]{3,2,1,0:T(8,128)(2,1)S(1)}, bf16[8,3,128,128]{3,2,1,0:T(8,128)(2,1)}, u32[]{:S(2)}) copy-start(bf16[8,3,128,128]{3,2,1,0:T(8,128)(2,1)} %param.16) | copy-start | bytes 2359300
  0.6 17.1 %copy-start.8 = (bf16[1024,384]{1,0:T(8,128)(2,1)S(1)}, bf16[1024,384]{1,0:T(8,128)(2,1)}, u32[]{:S(2)}) copy-start(bf16[1024,384]{1,0:T(8,128)(2,1)} %param.15) | copy-start | bytes 2359300
  2.4 16.3 %copy-start.21 = (s32[8,2]{0,1:T(2,128)S(1)}, s32[8,2]{0,1:T(2,128)}, u32[]{:S(2)}) copy-start(s32[8,2]{0,1:T(2,128)} %param.19) | copy-start | bytes 196
  2.4 16.3 %copy-start.18 = (s32[8,3]{0,1:T(4,128)S(1)}, s32[8,3]{0,1:T(4,128)}, u32[]{:S(2)}) copy-start(s32[8,3]{0,1:T(4,128)} %param.17) | copy-start | bytes 292
  2.4 16.6 %copy-start.19 = (s32[512]{0:T(512)S(1)}, s32[512]{0:T(512)}, u32[]{:S(2)}) copy-start(s32[512]{0:T(512)} %constant.155) | copy-start | bytes 6148
  2.4 16.6 %copy-start.20 = (s32[384]{0:T(512)S(1)}, s32[384]{0:T(512)}, u32[]{:S(2)}) copy-start(s32[384]{0:T(512)} %constant.152) | copy-start | bytes 4612
  2.4 16.6 %copy-start.13 = (bf16[128,512]{1,0:T(8,128)(2,1)S(1)}, bf16[128,512]{1,0:T(8,128)(2,1)}, u32[]{:S(2)}) copy-start(bf16[128,512]{1,0:T(8,128)(2,1)} %param.21) | copy-start | bytes 393220
  5.7 13.7 %collective-permute-start.3 = (bf16[163840]{0:T(1024)(128)(2,1)}, bf16[163840]{0:T(1024)(128)(2,1)S(1)}, u32[]{:S(2)}, u32[]{:S(2)}) collective-permute-start(bf16[163840]{0:T(1024)(128)(2,1)} %constant_dynamic-update-slice_fusion.14), channel_id=1, source_target_pairs={{0,62},{1,63},{2,0},{3,1},{4,2},{5,3},{6,4},{7,5},{8,6},{9,7},{10,... | collective-permute-start | bytes 983048 | tf_op jit(solution)/shard_map/ppermute | solution.py:18
  8.4 11.2 %collective-permute-start.2 = (bf16[163840]{0:T(1024)(128)(2,1)}, bf16[163840]{0:T(1024)(128)(2,1)S(1)}, u32[]{:S(2)}, u32[]{:S(2)}) collective-permute-start(bf16[163840]{0:T(1024)(128)(2,1)} %constant_dynamic-update-slice_fusion.14), channel_id=1, source_target_pairs={{0,63},{1,0},{2,1},{3,2},{4,3},{5,4},{6,5},{7,6},{8,7},{9,8},{10,9... | collective-permute-start | bytes 983048 | tf_op jit(solution)/shard_map/ppermute | solution.py:18
  10.3 13.5 %collective-permute-start.1 = (bf16[163840]{0:T(1024)(128)(2,1)}, bf16[163840]{0:T(1024)(128)(2,1)S(1)}, u32[]{:S(2)}, u32[]{:S(2)}) collective-permute-start(bf16[163840]{0:T(1024)(128)(2,1)} %constant_dynamic-update-slice_fusion.14), channel_id=1, source_target_pairs={{0,2},{1,3},{2,4},{3,5},{4,6},{5,7},{6,8},{7,9},{8,10},{9,11},{10,... | collective-permute-start | bytes 983048 | tf_op jit(solution)/shard_map/ppermute | solution.py:18
  15.6 10.5 %collective-permute-start = (bf16[163840]{0:T(1024)(128)(2,1)}, bf16[163840]{0:T(1024)(128)(2,1)S(1)}, u32[]{:S(2)}, u32[]{:S(2)}) collective-permute-start(bf16[163840]{0:T(1024)(128)(2,1)} %constant_dynamic-update-slice_fusion.14), channel_id=1, source_target_pairs={{0,1},{1,2},{2,3},{3,4},{4,5},{5,6},{6,7},{7,8},{8,9},{9,10},{10,1... | collective-permute-start | bytes 983048 | tf_op jit(solution)/shard_map/ppermute | solution.py:18
  38.0 3.5 %copy-start.5 = (bf16[8,384,128]{1,2,0:T(8,128)(2,1)}, bf16[8,384,128]{1,2,0:T(8,128)(2,1)S(1)}, u32[]{:S(2)}) copy-start(bf16[8,384,128]{1,2,0:T(8,128)(2,1)S(1)} %bitcast_convert_fusion) | copy-start | bytes 2359300
  38.0 1.4 copy-start.9
  38.0 1.5 copy-start.22
  39.5 2.0 %copy-start.14 = (bf16[384,512]{1,0:T(8,128)(2,1)S(1)}, bf16[384,512]{1,0:T(8,128)(2,1)}, u32[]{:S(2)}) copy-start(bf16[384,512]{1,0:T(8,128)(2,1)} %param.24) | copy-start | bytes 1179652
  41.5 1.7 %copy-start.11 = (bf16[1024,384]{1,0:T(8,128)(2,1)}, bf16[1024,384]{1,0:T(8,128)(2,1)S(1)}, u32[]{:S(2)}) copy-start(bf16[1024,384]{1,0:T(8,128)(2,1)S(1)} %get-tuple-element.6) | copy-start | bytes 2359300
  41.5 2.3 %copy-start.1 = (bf16[16,128,512]{2,1,0:T(8,128)(2,1)S(1)}, bf16[16,128,512]{2,1,0:T(8,128)(2,1)}, u32[]{:S(2)}) copy-start(bf16[16,128,512]{2,1,0:T(8,128)(2,1)} %gather_fusion.2) | copy-start | bytes 6291460
  41.5 2.3 %copy-start.23 = (s32[1024]{0:T(1024)S(1)}, s32[1024]{0:T(1024)}, u32[]{:S(2)}) copy-start(s32[1024]{0:T(1024)} %param.20) | copy-start | bytes 12292
  48.2 1.5 copy-start.24
  52.0 1.4 copy-start.3
  70.4 1.4 copy-start.7
  70.6 1.4 copy-start.4
  72.1 1.6 %copy-start.2 = (f32[2,32,11776]{2,1,0:T(8,128)}, f32[2,32,11776]{2,1,0:T(8,128)S(1)}, u32[]{:S(2)}) copy-start(f32[2,32,11776]{2,1,0:T(8,128)S(1)} %constant_dynamic-update-slice_fusion.10) | copy-start | bytes 9043972
  73.8 6.0 %collective-permute-start.4 = (f32[32,11776]{1,0:T(8,128)S(1)}, f32[32,11776]{1,0:T(8,128)}, u32[]{:S(2)}, u32[]{:S(2)}) collective-permute-start(f32[32,11776]{1,0:T(8,128)S(1)} %dynamic-slice_bitcast_fusion), channel_id=1, source_target_pairs={{0,1},{1,0},{2,3},{3,2},{4,5},{5,4},{6,7},{7,6},{8,9},{9,8},{10,11... | collective-permute-start | bytes 4521992 | tf_op jit(solution)/shard_map/ppermute | solution.py:23
  81.9 11.5 %collective-permute-start.5 = (bf16[16,11776]{1,0:T(8,128)(2,1)S(1)}, bf16[16,11776]{1,0:T(8,128)(2,1)S(1)}, u32[]{:S(2)}, u32[]{:S(2)}) collective-permute-start(bf16[16,11776]{1,0:T(8,128)(2,1)S(1)} %fusion.9), channel_id=1, source_target_pairs={{0,2},{1,7},{2,0},{3,5},{4,6},{5,3},{6,4},{7,1},{8,10},{9,15},{10,... | collective-permute-start | bytes 1130504 | tf_op jit(solution)/shard_map/ppermute | solution.py:114
  93.5 7.5 %collective-permute-start.6 = (bf16[8,11776]{1,0:T(8,128)(2,1)S(1)}, bf16[8,11776]{1,0:T(8,128)(2,1)S(1)}, u32[]{:S(2)}, u32[]{:S(2)}) collective-permute-start(bf16[8,11776]{1,0:T(8,128)(2,1)S(1)} %fusion.10), channel_id=1, source_target_pairs={{0,8},{1,57},{2,10},{3,59},{4,12},{5,61},{6,14},{7,63},{8,0},{9,17... | collective-permute-start | bytes 565256 | tf_op jit(solution)/shard_map/ppermute | solution.py:114
  101.2 10.5 %collective-permute-start.7 = (bf16[4,11776]{1,0:T(4,128)(2,1)S(1)}, bf16[4,11776]{1,0:T(4,128)(2,1)S(1)}, u32[]{:S(2)}, u32[]{:S(2)}) collective-permute-start(bf16[4,11776]{1,0:T(4,128)(2,1)S(1)} %fusion.11), channel_id=1, source_target_pairs={{0,4},{1,5},{2,6},{3,7},{4,0},{5,1},{6,2},{7,3},{8,12},{9,13},{10,... | collective-permute-start | bytes 282632 | tf_op jit(solution)/shard_map/ppermute | solution.py:114
  112.0 6.9 %collective-permute-start.8 = (bf16[2,11776]{1,0:T(2,128)(2,1)S(1)}, bf16[2,11776]{1,0:T(2,128)(2,1)S(1)}, u32[]{:S(2)}, u32[]{:S(2)}) collective-permute-start(bf16[2,11776]{1,0:T(2,128)(2,1)S(1)} %fusion.12), channel_id=1, source_target_pairs={{0,16},{1,49},{2,18},{3,51},{4,20},{5,53},{6,22},{7,55},{8,24},{9,... | collective-permute-start | bytes 141320 | tf_op jit(solution)/shard_map/ppermute | solution.py:114
  118.9 10.7 %collective-permute-start.9 = (f32[1,11776]{1,0:T(1,128)S(1)}, f32[1,11776]{1,0:T(1,128)S(1)}, u32[]{:S(2)}, u32[]{:S(2)}) collective-permute-start(f32[1,11776]{1,0:T(1,128)S(1)} %constant_dynamic-slice_fusion), channel_id=1, source_target_pairs={{0,32},{1,33},{2,34},{3,35},{4,36},{5,37},{6,38},{7,39},{8,40},{9,... | collective-permute-start | bytes 141320 | tf_op jit(solution)/shard_map/ppermute | solution.py:116
  129.8 6.3 %collective-permute-start.10 = (f32[11776]{0:T(1024)S(1)}, f32[11776]{0:T(1024)S(1)}, u32[]{:S(2)}, u32[]{:S(2)}) collective-permute-start(f32[11776]{0:T(1024)S(1)} %add_reduce_fusion), channel_id=1, source_target_pairs={{0,64},{64,0},{128,192},{192,128},{256,320},{320,256},{384,448},{4... | collective-permute-start | bytes 141320 | tf_op jit(solution)/shard_map/ppermute | solution.py:23
  136.1 8.2 %collective-permute-start.11 = (f32[11776]{0:T(1024)S(1)}, f32[11776]{0:T(1024)S(1)}, u32[]{:S(2)}, u32[]{:S(2)}) collective-permute-start(f32[11776]{0:T(1024)S(1)} %add.163), channel_id=1, source_target_pairs={{0,128},{64,192},{128,0},{192,64},{256,384},{320,448},{384,256},{4... | collective-permute-start | bytes 141320 | tf_op jit(solution)/shard_map/ppermute | solution.py:23
  144.3 11.3 %collective-permute-start.12 = (f32[11776]{0:T(1024)S(1)}, f32[11776]{0:T(1024)S(1)}, u32[]{:S(2)}, u32[]{:S(2)}) collective-permute-start(f32[11776]{0:T(1024)S(1)} %add.164), channel_id=1, source_target_pairs={{0,256},{64,320},{128,384},{192,448},{256,0},{320,64},{384,128},{4... | collective-permute-start | bytes 141320 | tf_op jit(solution)/shard_map/ppermute | solution.py:23
  (6 other events, 6.1 us)

commit v8 on v6

--- a/solution.py
+++ b/solution.py
@@ -57,35 +57,36 @@
     return pairs
 
 
-def halving_steps(n_y, n_x):
-    x_bits = n_x.bit_length() - 1
-    y_bits = n_y.bit_length() - 1
-    order = []
-    for b in range(max(x_bits, y_bits)):
-        if b < x_bits:
-            order.append(("x", b))
-        if b < y_bits:
-            order.append(("y", b))
-    return order
+def halving_steps(n_y):
+    return [("y", b) for b in range(n_y.bit_length() - 1)]
 
 
 def share_order(rows, n_dom, n_x):
     n_y = n_dom // (2 * n_x)
     per = rows // n_dom
-    steps = halving_steps(n_y, n_x)
+    steps = halving_steps(n_y)
     slots = [None] * n_dom
     for c in range(2):
         for ly in range(n_y):
             for lx in range(n_x):
                 d = ((ly + c) % n_y * n_x + (lx + c) % n_x) * 2 + c
-                slot = c
-                for kind, b in steps:
-                    slot = slot * 2 + (((lx if kind == "x" else ly) >> b) & 1)
+                slot = c * n_x + lx
+                for _, b in steps:
+                    slot = slot * 2 + ((ly >> b) & 1)
                 slots[slot] = d
     order = []
     for d in slots:
         order.extend(range(d * per, (d + 1) * per))
     return jnp.array(order, dtype=jnp.int32)
+
+
+def shifted_x(shard, n_y, n_x, by):
+    pairs = []
+    for y in range(n_y):
+        for x in range(n_x):
+            for c in range(2):
+                pairs.append(((y * n_x + x) * 2 + c, (y * n_x + (x + by) % n_x) * 2 + c))
+    return lax.ppermute(shard, "dom", pairs)
 
 
 def reduce_to_share(terms, n_dom, n_x):
@@ -103,13 +104,18 @@
     held = mine + swapped(other, "dom", 1)
     lx = (me // 2 % n_x - core) % n_x
     ly = (me // (2 * n_x) - core) % n_y
-    for step, (kind, b) in enumerate(halving_steps(n_y, n_x)):
+    held = held.reshape(n_x, -1, width)
+    total = lax.dynamic_index_in_dim(held, lx, 0, keepdims=False)
+    for by in range(1, n_x):
+        block = lax.dynamic_index_in_dim(held, (lx + by) % n_x, 0, keepdims=False)
+        total = total + shifted_x(block.astype(bf16), n_y, n_x, by).astype(f32)
+    held = total
+    for step, (kind, b) in enumerate(halving_steps(n_y)):
         held = held.reshape(2, -1, width)
-        coord = lx if kind == "x" else ly
-        mine_bit = (coord >> b) & 1
+        mine_bit = (ly >> b) & 1
         mine = lax.dynamic_index_in_dim(held, mine_bit, 0, keepdims=False)
         other = lax.dynamic_index_in_dim(held, 1 - mine_bit, 0, keepdims=False)
-        pairs = logical_pairs(n_y, n_x, kind == "x", 1 << b)
+        pairs = logical_pairs(n_y, n_x, False, 1 << b)
         if step < 2:
             got = lax.ppermute(other.astype(bf16), "dom", pairs).astype(f32)
         else:

time: 164 us -> 159 us (0.970); the launches traced: 161 us -> 158 us
  waiting for transfers between devices: 42 us -> 36.7 us
  starting transfers between devices: 56.5 us -> 58.6 us
    ppermute x0 -> x3, starting transfers between devices: none -> 15.2 us  [shifted_x(): return lax.ppermute(shard, 'dom', pairs)]
    ppermute x3 -> x1, waiting for transfers between devices: 16.9 us -> 5.2 us  [reduce_to_share(): got = lax.ppermute(other, 'dom', pairs)]
    ppermute x3 -> x1, starting transfers between devices: 14.3 us -> 5.03 us  [reduce_to_share(): got = lax.ppermute(other, 'dom', pairs)]
    ppermute x0 -> x3, waiting for transfers between devices: none -> 8.28 us  [shifted_x(): return lax.ppermute(shard, 'dom', pairs)]
    ppermute x2, starting transfers between devices: 7.89 us -> 3.84 us  [reduce_to_share(): got = lax.ppermute(other.astype(bf16), 'dom', pairs).astype(f32)]
    reshape x1, other arithmetic: 0.06 us -> 1.99 us  [reduce_to_share(): held = held.reshape(n_x, -1, width)]
    add x1, other arithmetic: 1.99 us -> 0.09 us  [reduce_to_share(): total = total + shifted_x(block.astype(bf16), n_y, n_x, by).astype(f32)]
  transfers between devices with their start and end apart: 13 -> 14, of which waited for: 12 -> 11; matrix products, arithmetic and copies ran while one was open for 2% -> 2% of each run, Pallas kernels for 0% -> 0%
where the time goes in v8:
time: 159 us; the launch traced here: 158 us
  starting transfers between devices  58.6 us (37%)
  local copies, waits for them, and re-layouts  38.6 us (24%)
  waiting for transfers between devices  36.7 us (23%)
  matrix products  19.5 us (12%)
  other arithmetic  3.16 us (2%)
    ppermute x4, starting transfers between devices, swapped(): return lax.ppermute(shard, axis, [(i, i ^ mask) for i in range(count)])  22.6 us
    ppermute x3, starting transfers between devices, shifted_x(): return lax.ppermute(shard, 'dom', pairs)  15.2 us
    unnamed x63, local copies, waits for them, and re-layouts  12.2 us
    ppermute x4, starting transfers between devices, passed_along(): lax.ppermute(shard, axis, [(i, (i + by) % count) for i in range(count)])  12 us
    ppermute x2, waiting for transfers between devices, reduce_to_share(): got = lax.ppermute(other.astype(bf16), 'dom', pairs).astype(f32)  9.46 us
    ppermute x4, waiting for transfers between devices, swapped(): return lax.ppermute(shard, axis, [(i, i ^ mask) for i in range(count)])  9.17 us
    ppermute x3, waiting for transfers between devices, shifted_x(): return lax.ppermute(shard, 'dom', pairs)  8.28 us
    gather x4, local copies, waits for them, and re-layouts, reduce_to_share(): t[share_order(t.shape[0], n_dom, n_x)].reshape(2, n_y * n_x, -1)  6.89 us
  transfers between devices with their start and end apart: 14, of which 11 were waited for; matrix products, arithmetic and copies ran while one was open for 2% of the time, Pallas kernels for 0%

profile of v8, /device:TPU:6, one launch (start us, length us, event | category | flops | bytes accessed | tf_op | source)
XLA Modules:
  0.0 158.1 jit_solution(3336715390581883903)
XLA Ops:
  5.7 2.7 %collective-permute-start.3 = (bf16[163840]{0:T(1024)(128)(2,1)}, bf16[163840]{0:T(1024)(128)(2,1)S(1)}, u32[]{:S(2)}, u32[]{:S(2)}) collective-permute-start(bf16[163840]{0:T(1024)(128)(2,1)} %constant_dynamic-update-slice_fusion.14), channel_id=1, source_target_pairs={{0,62},{1,63},{2,0},{3,1},{4,2},{5,3},{6,4},{7,5},{8,6},{9,7},{10,... | collective-permute-start | bytes 983048 | tf_op jit(solution)/shard_map/ppermute | solution.py:18
  8.4 1.9 %collective-permute-start.2 = (bf16[163840]{0:T(1024)(128)(2,1)}, bf16[163840]{0:T(1024)(128)(2,1)S(1)}, u32[]{:S(2)}, u32[]{:S(2)}) collective-permute-start(bf16[163840]{0:T(1024)(128)(2,1)} %constant_dynamic-update-slice_fusion.14), channel_id=1, source_target_pairs={{0,63},{1,0},{2,1},{3,2},{4,3},{5,4},{6,5},{7,6},{8,7},{9,8},{10,9... | collective-permute-start | bytes 983048 | tf_op jit(solution)/shard_map/ppermute | solution.py:18
  10.3 5.2 %collective-permute-start.1 = (bf16[163840]{0:T(1024)(128)(2,1)}, bf16[163840]{0:T(1024)(128)(2,1)S(1)}, u32[]{:S(2)}, u32[]{:S(2)}) collective-permute-start(bf16[163840]{0:T(1024)(128)(2,1)} %constant_dynamic-update-slice_fusion.14), channel_id=1, source_target_pairs={{0,2},{1,3},{2,4},{3,5},{4,6},{5,7},{6,8},{7,9},{8,10},{9,11},{10,... | collective-permute-start | bytes 983048 | tf_op jit(solution)/shard_map/ppermute | solution.py:18
  15.6 2.1 %collective-permute-start = (bf16[163840]{0:T(1024)(128)(2,1)}, bf16[163840]{0:T(1024)(128)(2,1)S(1)}, u32[]{:S(2)}, u32[]{:S(2)}) collective-permute-start(bf16[163840]{0:T(1024)(128)(2,1)} %constant_dynamic-update-slice_fusion.14), channel_id=1, source_target_pairs={{0,1},{1,2},{2,3},{3,4},{4,5},{5,6},{6,7},{7,8},{8,9},{9,10},{10,1... | collective-permute-start | bytes 983048 | tf_op jit(solution)/shard_map/ppermute | solution.py:18
  21.4 2.4 %collective-permute-done.1 = bf16[163840]{0:T(1024)(128)(2,1)S(1)} collective-permute-done((bf16[163840]{0:T(1024)(128)(2,1)}, bf16[163840]{0:T(1024)(128)(2,1)S(1)}, u32[]{:S(2)}, u32[]{:S(2)}) %collective-permute-start.1) | collective-permute-done | bytes 327712 | tf_op jit(solution)/shard_map/ppermute | solution.py:18
  24.1 1.9 %collective-permute-done = bf16[163840]{0:T(1024)(128)(2,1)S(1)} collective-permute-done((bf16[163840]{0:T(1024)(128)(2,1)}, bf16[163840]{0:T(1024)(128)(2,1)S(1)}, u32[]{:S(2)}, u32[]{:S(2)}) %collective-permute-start) | collective-permute-done | bytes 327712 | tf_op jit(solution)/shard_map/ppermute | solution.py:18
  26.4 2.0 %gather_fusion.6 = bf16[16,128,512]{2,1,0:T(8,128)(2,1)} fusion(bf16[5,128,512]{2,1,0:T(8,128)(2,1)S(1)} %constant_dynamic-update-slice_fusion.6, s32[1024]{0:T(1024)S(1)} %get-tuple-element.13), kind=kCustom, calls=%fused_computation.6 | custom fusion | bytes 4194368 | tf_op jit(solution)/shard_map/gather | solution.py:178
  30.0 2.0 %gather_fusion.2 = bf16[16,128,512]{2,1,0:T(8,128)(2,1)} fusion(bf16[5,128,512]{2,1,0:T(8,128)(2,1)S(1)} %bitcast.80, s32[1024]{0:T(1024)S(1)} %get-tuple-element.13), kind=kCustom, calls=%fused_computation.2 | custom fusion | bytes 4194368 | tf_op jit(solution)/shard_map/gather | solution.py:177
  34.8 2.5 %gather_fusion.1 = bf16[24,128,384]{2,1,0:T(8,128)(2,1)S(1)} fusion(bf16[16,128,384]{2,1,0:T(8,128)(2,1)} %constant_dynamic-update-slice_fusion.1, s32[1024]{0:T(1024)S(1)} %get-tuple-element.14), kind=kCustom, calls=%fused_computation.1 | custom fusion | bytes 4718688 | tf_op jit(solution)/shard_map/gather | solution.py:161
  39.5 2.0 %add_convert_fusion = (bf16[1024,384]{1,0:T(8,128)(2,1)S(1)}, f32[1024,384]{1,0:T(8,128)}) fusion(bf16[1024,384]{1,0:T(8,128)(2,1)S(1)} %copy-done.9, f32[1024,384]{1,0:T(8,128)S(1)} %fusion.18, bf16[384,384]{1,0:T(8,128)(2,1)S(1)} %copy-done.22), kind=kOutput, calls=%fused_computation.14 | convolution fusion | flops 305135616 | bytes 5013504 | tf_op jit(solution)/shard_map/dot_general | solution.py:167
  43.8 3.3 %fusion.8 = bf16[8,128,256]{2,1,0:T(8,128)(2,1)S(1)} fusion(s32[8,128]{1,0:T(8,128)S(1)} %bitcast.93, bf16[8,128,512]{2,1,0:T(8,128)(2,1)} %bitcast.81, bf16[8,256,512]{2,1,0:T(8,128)(2,1)S(1)} %bitcast.77), kind=kOutput, calls=%fused_computation.28 | convolution fusion | flops 270535168 | bytes 3674112 | tf_op jit(solution)/shard_map/div | solution.py:184
  53.5 2.1 %multiply_convert_fusion = bf16[8,256,512]{2,1,0:T(8,128)(2,1)} fusion(bf16[8,128,256]{2,1,0:T(8,128)(2,1)S(1)} %fusion.8, bf16[8,128,512]{2,1,0:T(8,128)(2,1)S(1)} %bitcast.82), kind=kOutput, calls=%fused_computation.10 | convolution fusion | flops 270532608 | bytes 3670016 | tf_op jit(solution)/shard_map/bij,bie->bje/dot_general | solution.py:197
  65.3 3.5 %fusion.21 = f32[512,512]{1,0:T(8,128)S(1)} fusion(bf16[2048,512]{1,0:T(8,128)(2,1)} %bitcast.85, bf16[2048,512]{1,0:T(8,128)(2,1)} %bitcast.86), kind=kOutput, calls=%fused_computation.78 | convolution fusion | flops 1073741824 | bytes 5242880 | tf_op jit(solution)/shard_map/dot_general | solution.py:203
  73.8 3.0 %collective-permute-start.4 = (f32[32,11776]{1,0:T(8,128)S(1)}, f32[32,11776]{1,0:T(8,128)}, u32[]{:S(2)}, u32[]{:S(2)}) collective-permute-start(f32[32,11776]{1,0:T(8,128)S(1)} %dynamic-slice_bitcast_fusion), channel_id=1, source_target_pairs={{0,1},{1,0},{2,3},{3,2},{4,5},{5,4},{6,7},{7,6},{8,9},{9,8},{10,11... | collective-permute-start | bytes 4521992 | tf_op jit(solution)/shard_map/ppermute | solution.py:23
  76.9 2.9 %collective-permute-done.4 = f32[32,11776]{1,0:T(8,128)} collective-permute-done((f32[32,11776]{1,0:T(8,128)S(1)}, f32[32,11776]{1,0:T(8,128)}, u32[]{:S(2)}, u32[]{:S(2)}) %collective-permute-start.4) | collective-permute-done | bytes 1507360 | tf_op jit(solution)/shard_map/ppermute | solution.py:23
  79.8 2.0 %fusion.2 = f32[4,8,11776]{2,1,0:T(8,128)S(1)} fusion(f32[32,11776]{1,0:T(8,128)} %collective-permute-done.4, f32[2,32,11776]{2,1,0:T(8,128)} %copy-done.2, s32[]{:T(128)S(6)} %select_n.109), kind=kLoop, calls=%fused_computation.17 | loop fusion | flops 376832 | bytes 4521988 | tf_op jit(solution)/shard_map/reshape | solution.py:107
  81.9 9.9 %collective-permute-start.5 = (bf16[8,11776]{1,0:T(8,128)(2,1)S(1)}, bf16[8,11776]{1,0:T(8,128)(2,1)S(1)}, u32[]{:S(2)}, u32[]{:S(2)}) collective-permute-start(bf16[8,11776]{1,0:T(8,128)(2,1)S(1)} %get-tuple-element.4), channel_id=1, source_target_pairs={{0,2},{1,3},{2,4},{3,5},{4,6},{5,7},{6,0},{7,1},{8,10},{9,11},{10,... | collective-permute-start | bytes 565256 | tf_op jit(solution)/shard_map/ppermute | solution.py:89
  91.8 1.9 %collective-permute-start.7 = (bf16[8,11776]{1,0:T(8,128)(2,1)S(1)}, bf16[8,11776]{1,0:T(8,128)(2,1)S(1)}, u32[]{:S(2)}, u32[]{:S(2)}) collective-permute-start(bf16[8,11776]{1,0:T(8,128)(2,1)S(1)} %get-tuple-element.5), channel_id=1, source_target_pairs={{0,6},{1,7},{2,0},{3,1},{4,2},{5,3},{6,4},{7,5},{8,14},{9,15},{10,... | collective-permute-start | bytes 565256 | tf_op jit(solution)/shard_map/ppermute | solution.py:89
  93.7 3.4 %collective-permute-start.6 = (bf16[8,11776]{1,0:T(8,128)(2,1)S(1)}, bf16[8,11776]{1,0:T(8,128)(2,1)S(1)}, u32[]{:S(2)}, u32[]{:S(2)}) collective-permute-start(bf16[8,11776]{1,0:T(8,128)(2,1)S(1)} %get-tuple-element.6), channel_id=1, source_target_pairs={{0,4},{1,5},{2,6},{3,7},{4,0},{5,1},{6,2},{7,3},{8,12},{9,13},{10,... | collective-permute-start | bytes 565256 | tf_op jit(solution)/shard_map/ppermute | solution.py:89
  97.1 8.3 %collective-permute-done.7 = bf16[8,11776]{1,0:T(8,128)(2,1)S(1)} collective-permute-done((bf16[8,11776]{1,0:T(8,128)(2,1)S(1)}, bf16[8,11776]{1,0:T(8,128)(2,1)S(1)}, u32[]{:S(2)}, u32[]{:S(2)}) %collective-permute-start.7) | collective-permute-done | bytes 188448 | tf_op jit(solution)/shard_map/ppermute | solution.py:89
  105.6 1.9 %collective-permute-start.8 = (bf16[4,11776]{1,0:T(4,128)(2,1)S(1)}, bf16[4,11776]{1,0:T(4,128)(2,1)S(1)}, u32[]{:S(2)}, u32[]{:S(2)}) collective-permute-start(bf16[4,11776]{1,0:T(4,128)(2,1)S(1)} %fusion.14), channel_id=1, source_target_pairs={{0,8},{1,57},{2,10},{3,59},{4,12},{5,61},{6,14},{7,63},{8,0},{9,17... | collective-permute-start | bytes 282632 | tf_op jit(solution)/shard_map/ppermute | solution.py:120
  107.6 4.5 %collective-permute-done.8 = bf16[4,11776]{1,0:T(4,128)(2,1)S(1)} collective-permute-done((bf16[4,11776]{1,0:T(4,128)(2,1)S(1)}, bf16[4,11776]{1,0:T(4,128)(2,1)S(1)}, u32[]{:S(2)}, u32[]{:S(2)}) %collective-permute-start.8) | collective-permute-done | bytes 94240 | tf_op jit(solution)/shard_map/ppermute | solution.py:120
  112.4 1.9 %collective-permute-start.9 = (bf16[2,11776]{1,0:T(2,128)(2,1)S(1)}, bf16[2,11776]{1,0:T(2,128)(2,1)S(1)}, u32[]{:S(2)}, u32[]{:S(2)}) collective-permute-start(bf16[2,11776]{1,0:T(2,128)(2,1)S(1)} %fusion.15), channel_id=1, source_target_pairs={{0,16},{1,49},{2,18},{3,51},{4,20},{5,53},{6,22},{7,55},{8,24},{9,... | collective-permute-start | bytes 141320 | tf_op jit(solution)/shard_map/ppermute | solution.py:120
  114.3 4.9 %collective-permute-done.9 = bf16[2,11776]{1,0:T(2,128)(2,1)S(1)} collective-permute-done((bf16[2,11776]{1,0:T(2,128)(2,1)S(1)}, bf16[2,11776]{1,0:T(2,128)(2,1)S(1)}, u32[]{:S(2)}, u32[]{:S(2)}) %collective-permute-start.9) | collective-permute-done | bytes 47136 | tf_op jit(solution)/shard_map/ppermute | solution.py:120
  119.4 5.0 %collective-permute-start.10 = (f32[1,11776]{1,0:T(1,128)S(1)}, f32[1,11776]{1,0:T(1,128)S(1)}, u32[]{:S(2)}, u32[]{:S(2)}) collective-permute-start(f32[1,11776]{1,0:T(1,128)S(1)} %constant_dynamic-slice_fusion), channel_id=1, source_target_pairs={{0,32},{1,33},{2,34},{3,35},{4,36},{5,37},{6,38},{7,39},{8,40},{9,... | collective-permute-start | bytes 141320 | tf_op jit(solution)/shard_map/ppermute | solution.py:122
  124.4 5.2 %collective-permute-done.10 = f32[1,11776]{1,0:T(1,128)S(1)} collective-permute-done((f32[1,11776]{1,0:T(1,128)S(1)}, f32[1,11776]{1,0:T(1,128)S(1)}, u32[]{:S(2)}, u32[]{:S(2)}) %collective-permute-start.10) | collective-permute-done | bytes 47136 | tf_op jit(solution)/shard_map/ppermute | solution.py:122
  129.7 4.3 %collective-permute-start.11 = (f32[11776]{0:T(1024)S(1)}, f32[11776]{0:T(1024)S(1)}, u32[]{:S(2)}, u32[]{:S(2)}) collective-permute-start(f32[11776]{0:T(1024)S(1)} %add_reduce_fusion), channel_id=1, source_target_pairs={{0,64},{64,0},{128,192},{192,128},{256,320},{320,256},{384,448},{4... | collective-permute-start | bytes 141320 | tf_op jit(solution)/shard_map/ppermute | solution.py:23
  134.0 2.1 %collective-permute-done.11 = f32[11776]{0:T(1024)S(1)} collective-permute-done((f32[11776]{0:T(1024)S(1)}, f32[11776]{0:T(1024)S(1)}, u32[]{:S(2)}, u32[]{:S(2)}) %collective-permute-start.11) | collective-permute-done | bytes 47136 | tf_op jit(solution)/shard_map/ppermute | solution.py:23
  136.1 6.1 %collective-permute-start.12 = (f32[11776]{0:T(1024)S(1)}, f32[11776]{0:T(1024)S(1)}, u32[]{:S(2)}, u32[]{:S(2)}) collective-permute-start(f32[11776]{0:T(1024)S(1)} %add.188), channel_id=1, source_target_pairs={{0,128},{64,192},{128,0},{192,64},{256,384},{320,448},{384,256},{4... | collective-permute-start | bytes 141320 | tf_op jit(solution)/shard_map/ppermute | solution.py:23
  142.2 2.1 %collective-permute-done.12 = f32[11776]{0:T(1024)S(1)} collective-permute-done((f32[11776]{0:T(1024)S(1)}, f32[11776]{0:T(1024)S(1)}, u32[]{:S(2)}, u32[]{:S(2)}) %collective-permute-start.12) | collective-permute-done | bytes 47136 | tf_op jit(solution)/shard_map/ppermute | solution.py:23
  144.2 9.3 %collective-permute-start.13 = (f32[11776]{0:T(1024)S(1)}, f32[11776]{0:T(1024)S(1)}, u32[]{:S(2)}, u32[]{:S(2)}) collective-permute-start(f32[11776]{0:T(1024)S(1)} %add.189), channel_id=1, source_target_pairs={{0,256},{64,320},{128,384},{192,448},{256,0},{320,64},{384,128},{4... | collective-permute-start | bytes 141320 | tf_op jit(solution)/shard_map/ppermute | solution.py:23
  153.5 2.1 %collective-permute-done.13 = f32[11776]{0:T(1024)S(1)} collective-permute-done((f32[11776]{0:T(1024)S(1)}, f32[11776]{0:T(1024)S(1)}, u32[]{:S(2)}, u32[]{:S(2)}) %collective-permute-start.13) | collective-permute-done | bytes 47136 | tf_op jit(solution)/shard_map/ppermute | solution.py:23
  (138 shorter events, 42.0 us)
Async XLA Ops:
  0.6 36.7 %copy-start = (bf16[8,3,128,128]{3,2,1,0:T(8,128)(2,1)S(1)}, bf16[8,3,128,128]{3,2,1,0:T(8,128)(2,1)}, u32[]{:S(2)}) copy-start(bf16[8,3,128,128]{3,2,1,0:T(8,128)(2,1)} %param.16) | copy-start | bytes 2359300
  0.6 17.1 %copy-start.8 = (bf16[1024,384]{1,0:T(8,128)(2,1)S(1)}, bf16[1024,384]{1,0:T(8,128)(2,1)}, u32[]{:S(2)}) copy-start(bf16[1024,384]{1,0:T(8,128)(2,1)} %param.15) | copy-start | bytes 2359300
  2.4 16.3 %copy-start.21 = (s32[8,2]{0,1:T(2,128)S(1)}, s32[8,2]{0,1:T(2,128)}, u32[]{:S(2)}) copy-start(s32[8,2]{0,1:T(2,128)} %param.19) | copy-start | bytes 196
  2.4 16.3 %copy-start.18 = (s32[8,3]{0,1:T(4,128)S(1)}, s32[8,3]{0,1:T(4,128)}, u32[]{:S(2)}) copy-start(s32[8,3]{0,1:T(4,128)} %param.17) | copy-start | bytes 292
  2.4 16.6 %copy-start.19 = (s32[512]{0:T(512)S(1)}, s32[512]{0:T(512)}, u32[]{:S(2)}) copy-start(s32[512]{0:T(512)} %constant.164) | copy-start | bytes 6148
  2.4 16.6 %copy-start.20 = (s32[384]{0:T(512)S(1)}, s32[384]{0:T(512)}, u32[]{:S(2)}) copy-start(s32[384]{0:T(512)} %constant.161) | copy-start | bytes 4612
  2.4 16.6 %copy-start.13 = (bf16[128,512]{1,0:T(8,128)(2,1)S(1)}, bf16[128,512]{1,0:T(8,128)(2,1)}, u32[]{:S(2)}) copy-start(bf16[128,512]{1,0:T(8,128)(2,1)} %param.21) | copy-start | bytes 393220
  5.7 13.7 %collective-permute-start.3 = (bf16[163840]{0:T(1024)(128)(2,1)}, bf16[163840]{0:T(1024)(128)(2,1)S(1)}, u32[]{:S(2)}, u32[]{:S(2)}) collective-permute-start(bf16[163840]{0:T(1024)(128)(2,1)} %constant_dynamic-update-slice_fusion.14), channel_id=1, source_target_pairs={{0,62},{1,63},{2,0},{3,1},{4,2},{5,3},{6,4},{7,5},{8,6},{9,7},{10,... | collective-permute-start | bytes 983048 | tf_op jit(solution)/shard_map/ppermute | solution.py:18
  8.4 11.2 %collective-permute-start.2 = (bf16[163840]{0:T(1024)(128)(2,1)}, bf16[163840]{0:T(1024)(128)(2,1)S(1)}, u32[]{:S(2)}, u32[]{:S(2)}) collective-permute-start(bf16[163840]{0:T(1024)(128)(2,1)} %constant_dynamic-update-slice_fusion.14), channel_id=1, source_target_pairs={{0,63},{1,0},{2,1},{3,2},{4,3},{5,4},{6,5},{7,6},{8,7},{9,8},{10,9... | collective-permute-start | bytes 983048 | tf_op jit(solution)/shard_map/ppermute | solution.py:18
  10.3 13.5 %collective-permute-start.1 = (bf16[163840]{0:T(1024)(128)(2,1)}, bf16[163840]{0:T(1024)(128)(2,1)S(1)}, u32[]{:S(2)}, u32[]{:S(2)}) collective-permute-start(bf16[163840]{0:T(1024)(128)(2,1)} %constant_dynamic-update-slice_fusion.14), channel_id=1, source_target_pairs={{0,2},{1,3},{2,4},{3,5},{4,6},{5,7},{6,8},{7,9},{8,10},{9,11},{10,... | collective-permute-start | bytes 983048 | tf_op jit(solution)/shard_map/ppermute | solution.py:18
  15.6 10.5 %collective-permute-start = (bf16[163840]{0:T(1024)(128)(2,1)}, bf16[163840]{0:T(1024)(128)(2,1)S(1)}, u32[]{:S(2)}, u32[]{:S(2)}) collective-permute-start(bf16[163840]{0:T(1024)(128)(2,1)} %constant_dynamic-update-slice_fusion.14), channel_id=1, source_target_pairs={{0,1},{1,2},{2,3},{3,4},{4,5},{5,6},{6,7},{7,8},{8,9},{9,10},{10,1... | collective-permute-start | bytes 983048 | tf_op jit(solution)/shard_map/ppermute | solution.py:18
  38.0 3.5 %copy-start.5 = (bf16[8,384,128]{1,2,0:T(8,128)(2,1)}, bf16[8,384,128]{1,2,0:T(8,128)(2,1)S(1)}, u32[]{:S(2)}) copy-start(bf16[8,384,128]{1,2,0:T(8,128)(2,1)S(1)} %bitcast_convert_fusion) | copy-start | bytes 2359300
  38.0 1.4 copy-start.9
  38.0 1.5 copy-start.22
  39.5 2.0 %copy-start.14 = (bf16[384,512]{1,0:T(8,128)(2,1)S(1)}, bf16[384,512]{1,0:T(8,128)(2,1)}, u32[]{:S(2)}) copy-start(bf16[384,512]{1,0:T(8,128)(2,1)} %param.24) | copy-start | bytes 1179652
  41.5 1.7 %copy-start.11 = (bf16[1024,384]{1,0:T(8,128)(2,1)}, bf16[1024,384]{1,0:T(8,128)(2,1)S(1)}, u32[]{:S(2)}) copy-start(bf16[1024,384]{1,0:T(8,128)(2,1)S(1)} %get-tuple-element.9) | copy-start | bytes 2359300
  41.5 2.3 %copy-start.1 = (bf16[16,128,512]{2,1,0:T(8,128)(2,1)S(1)}, bf16[16,128,512]{2,1,0:T(8,128)(2,1)}, u32[]{:S(2)}) copy-start(bf16[16,128,512]{2,1,0:T(8,128)(2,1)} %gather_fusion.2) | copy-start | bytes 6291460
  41.5 2.3 %copy-start.23 = (s32[1024]{0:T(1024)S(1)}, s32[1024]{0:T(1024)}, u32[]{:S(2)}) copy-start(s32[1024]{0:T(1024)} %param.20) | copy-start | bytes 12292
  48.3 1.5 copy-start.24
  52.1 1.4 copy-start.3
  70.4 1.4 copy-start.7
  72.1 1.6 %copy-start.2 = (f32[2,32,11776]{2,1,0:T(8,128)}, f32[2,32,11776]{2,1,0:T(8,128)S(1)}, u32[]{:S(2)}) copy-start(f32[2,32,11776]{2,1,0:T(8,128)S(1)} %constant_dynamic-update-slice_fusion.10) | copy-start | bytes 9043972
  73.8 6.0 %collective-permute-start.4 = (f32[32,11776]{1,0:T(8,128)S(1)}, f32[32,11776]{1,0:T(8,128)}, u32[]{:S(2)}, u32[]{:S(2)}) collective-permute-start(f32[32,11776]{1,0:T(8,128)S(1)} %dynamic-slice_bitcast_fusion), channel_id=1, source_target_pairs={{0,1},{1,0},{2,3},{3,2},{4,5},{5,4},{6,7},{7,6},{8,9},{9,8},{10,11... | collective-permute-start | bytes 4521992 | tf_op jit(solution)/shard_map/ppermute | solution.py:23
  81.9 15.2 %collective-permute-start.5 = (bf16[8,11776]{1,0:T(8,128)(2,1)S(1)}, bf16[8,11776]{1,0:T(8,128)(2,1)S(1)}, u32[]{:S(2)}, u32[]{:S(2)}) collective-permute-start(bf16[8,11776]{1,0:T(8,128)(2,1)S(1)} %get-tuple-element.4), channel_id=1, source_target_pairs={{0,2},{1,3},{2,4},{3,5},{4,6},{5,7},{6,0},{7,1},{8,10},{9,11},{10,... | collective-permute-start | bytes 565256 | tf_op jit(solution)/shard_map/ppermute | solution.py:89
  91.8 13.6 %collective-permute-start.7 = (bf16[8,11776]{1,0:T(8,128)(2,1)S(1)}, bf16[8,11776]{1,0:T(8,128)(2,1)S(1)}, u32[]{:S(2)}, u32[]{:S(2)}) collective-permute-start(bf16[8,11776]{1,0:T(8,128)(2,1)S(1)} %get-tuple-element.5), channel_id=1, source_target_pairs={{0,6},{1,7},{2,0},{3,1},{4,2},{5,3},{6,4},{7,5},{8,14},{9,15},{10,... | collective-permute-start | bytes 565256 | tf_op jit(solution)/shard_map/ppermute | solution.py:89
  93.7 11.7 %collective-permute-start.6 = (bf16[8,11776]{1,0:T(8,128)(2,1)S(1)}, bf16[8,11776]{1,0:T(8,128)(2,1)S(1)}, u32[]{:S(2)}, u32[]{:S(2)}) collective-permute-start(bf16[8,11776]{1,0:T(8,128)(2,1)S(1)} %get-tuple-element.6), channel_id=1, source_target_pairs={{0,4},{1,5},{2,6},{3,7},{4,0},{5,1},{6,2},{7,3},{8,12},{9,13},{10,... | collective-permute-start | bytes 565256 | tf_op jit(solution)/shard_map/ppermute | solution.py:89
  105.6 6.5 %collective-permute-start.8 = (bf16[4,11776]{1,0:T(4,128)(2,1)S(1)}, bf16[4,11776]{1,0:T(4,128)(2,1)S(1)}, u32[]{:S(2)}, u32[]{:S(2)}) collective-permute-start(bf16[4,11776]{1,0:T(4,128)(2,1)S(1)} %fusion.14), channel_id=1, source_target_pairs={{0,8},{1,57},{2,10},{3,59},{4,12},{5,61},{6,14},{7,63},{8,0},{9,17... | collective-permute-start | bytes 282632 | tf_op jit(solution)/shard_map/ppermute | solution.py:120
  112.4 6.9 %collective-permute-start.9 = (bf16[2,11776]{1,0:T(2,128)(2,1)S(1)}, bf16[2,11776]{1,0:T(2,128)(2,1)S(1)}, u32[]{:S(2)}, u32[]{:S(2)}) collective-permute-start(bf16[2,11776]{1,0:T(2,128)(2,1)S(1)} %fusion.15), channel_id=1, source_target_pairs={{0,16},{1,49},{2,18},{3,51},{4,20},{5,53},{6,22},{7,55},{8,24},{9,... | collective-permute-start | bytes 141320 | tf_op jit(solution)/shard_map/ppermute | solution.py:120
  119.4 10.2 %collective-permute-start.10 = (f32[1,11776]{1,0:T(1,128)S(1)}, f32[1,11776]{1,0:T(1,128)S(1)}, u32[]{:S(2)}, u32[]{:S(2)}) collective-permute-start(f32[1,11776]{1,0:T(1,128)S(1)} %constant_dynamic-slice_fusion), channel_id=1, source_target_pairs={{0,32},{1,33},{2,34},{3,35},{4,36},{5,37},{6,38},{7,39},{8,40},{9,... | collective-permute-start | bytes 141320 | tf_op jit(solution)/shard_map/ppermute | solution.py:122
  129.7 6.3 %collective-permute-start.11 = (f32[11776]{0:T(1024)S(1)}, f32[11776]{0:T(1024)S(1)}, u32[]{:S(2)}, u32[]{:S(2)}) collective-permute-start(f32[11776]{0:T(1024)S(1)} %add_reduce_fusion), channel_id=1, source_target_pairs={{0,64},{64,0},{128,192},{192,128},{256,320},{320,256},{384,448},{4... | collective-permute-start | bytes 141320 | tf_op jit(solution)/shard_map/ppermute | solution.py:23
  136.1 8.2 %collective-permute-start.12 = (f32[11776]{0:T(1024)S(1)}, f32[11776]{0:T(1024)S(1)}, u32[]{:S(2)}, u32[]{:S(2)}) collective-permute-start(f32[11776]{0:T(1024)S(1)} %add.188), channel_id=1, source_target_pairs={{0,128},{64,192},{128,0},{192,64},{256,384},{320,448},{384,256},{4... | collective-permute-start | bytes 141320 | tf_op jit(solution)/shard_map/ppermute | solution.py:23
  144.2 11.4 %collective-permute-start.13 = (f32[11776]{0:T(1024)S(1)}, f32[11776]{0:T(1024)S(1)}, u32[]{:S(2)}, u32[]{:S(2)}) collective-permute-start(f32[11776]{0:T(1024)S(1)} %add.189), channel_id=1, source_target_pairs={{0,256},{64,320},{128,384},{192,448},{256,0},{320,64},{384,128},{4... | collective-permute-start | bytes 141320 | tf_op jit(solution)/shard_map/ppermute | solution.py:23
  (7 other events, 7.4 us)

commit v9 on v8

--- a/solution.py
+++ b/solution.py
@@ -123,10 +123,12 @@
         held = mine + got
     share = held.reshape(-1)
     n_region = lax.axis_size("region")
-    step = 1
-    while step < n_region:
-        share = share + swapped(share, "region", step)
-        step *= 2
+    region = lax.axis_index("region")
+    share = share + swapped(share, "region", 1)
+    n_group = n_region // 2
+    got = [share] + [passed_along(share, "region", 2 * k) for k in range(1, n_group)]
+    ordered = jnp.take(jnp.stack(got), (region // 2 - jnp.arange(n_group)) % n_group, axis=0)
+    share = jnp.sum(ordered, axis=0)
     pieces = []
     start = 0
     for t in terms:

time: 159 us -> 162 us (1.019)
  starting transfers between devices: 58.6 us -> 60.5 us
    ppermute x4 -> x7, starting transfers between devices: 12 us -> 29.3 us  [passed_along(): lax.ppermute(shard, axis, [(i, (i + by) % count) for i in range(count)])]
    ppermute x4 -> x2, starting transfers between devices: 22.6 us -> 7.22 us  [swapped(): return lax.ppermute(shard, axis, [(i, i ^ mask) for i in range(count)])]
    ppermute x4 -> x2, waiting for transfers between devices: 9.17 us -> 4.98 us  [swapped(): return lax.ppermute(shard, axis, [(i, i ^ mask) for i in range(count)])]
    ppermute x4 -> x7, waiting for transfers between devices: 4.61 us -> 8.36 us  [passed_along(): lax.ppermute(shard, axis, [(i, (i + by) % count) for i in range(count)])]
  transfers between devices with their start and end apart: 14 -> 15, of which waited for: 11 -> 11; matrix products, arithmetic and copies ran while one was open for 2% -> 2% of each run, Pallas kernels for 0% -> 0%
where the time goes in v9:
time: 162 us; the launch traced here: 161 us
  starting transfers between devices  60.5 us (37%)
  local copies, waits for them, and re-layouts  39.4 us (24%)
  waiting for transfers between devices  36.2 us (22%)
  matrix products  19.5 us (12%)
  other arithmetic  3.57 us (2%)
  between operations  1.63 us (1%)
    ppermute x7, starting transfers between devices, passed_along(): lax.ppermute(shard, axis, [(i, (i + by) % count) for i in range(count)])  29.3 us
    ppermute x3, starting transfers between devices, shifted_x(): return lax.ppermute(shard, 'dom', pairs)  15.2 us
    unnamed x63, local copies, waits for them, and re-layouts  12.2 us
    ppermute x2, waiting for transfers between devices, reduce_to_share(): got = lax.ppermute(other.astype(bf16), 'dom', pairs).astype(f32)  9.45 us
    ppermute x7, waiting for transfers between devices, passed_along(): lax.ppermute(shard, axis, [(i, (i + by) % count) for i in range(count)])  8.36 us
    ppermute x3, waiting for transfers between devices, shifted_x(): return lax.ppermute(shard, 'dom', pairs)  8.28 us
    ppermute x2, starting transfers between devices, swapped(): return lax.ppermute(shard, axis, [(i, i ^ mask) for i in range(count)])  7.22 us
    gather x4, local copies, waits for them, and re-layouts, reduce_to_share(): t[share_order(t.shape[0], n_dom, n_x)].reshape(2, n_y * n_x, -1)  6.89 us
  transfers between devices with their start and end apart: 15, of which 11 were waited for; matrix products, arithmetic and copies ran while one was open for 2% of the time, Pallas kernels for 0%

profile of v9, /device:TPU:6, one launch (start us, length us, event | category | flops | bytes accessed | tf_op | source)
XLA Modules:
  0.0 160.8 jit_solution(17281742885097807523)
XLA Ops:
  5.7 2.7 %collective-permute-start.3 = (bf16[163840]{0:T(1024)(128)(2,1)}, bf16[163840]{0:T(1024)(128)(2,1)S(1)}, u32[]{:S(2)}, u32[]{:S(2)}) collective-permute-start(bf16[163840]{0:T(1024)(128)(2,1)} %constant_dynamic-update-slice_fusion.14), channel_id=1, source_target_pairs={{0,62},{1,63},{2,0},{3,1},{4,2},{5,3},{6,4},{7,5},{8,6},{9,7},{10,... | collective-permute-start | bytes 983048 | tf_op jit(solution)/shard_map/ppermute | solution.py:18
  8.4 1.9 %collective-permute-start.2 = (bf16[163840]{0:T(1024)(128)(2,1)}, bf16[163840]{0:T(1024)(128)(2,1)S(1)}, u32[]{:S(2)}, u32[]{:S(2)}) collective-permute-start(bf16[163840]{0:T(1024)(128)(2,1)} %constant_dynamic-update-slice_fusion.14), channel_id=1, source_target_pairs={{0,63},{1,0},{2,1},{3,2},{4,3},{5,4},{6,5},{7,6},{8,7},{9,8},{10,9... | collective-permute-start | bytes 983048 | tf_op jit(solution)/shard_map/ppermute | solution.py:18
  10.3 5.2 %collective-permute-start.1 = (bf16[163840]{0:T(1024)(128)(2,1)}, bf16[163840]{0:T(1024)(128)(2,1)S(1)}, u32[]{:S(2)}, u32[]{:S(2)}) collective-permute-start(bf16[163840]{0:T(1024)(128)(2,1)} %constant_dynamic-update-slice_fusion.14), channel_id=1, source_target_pairs={{0,2},{1,3},{2,4},{3,5},{4,6},{5,7},{6,8},{7,9},{8,10},{9,11},{10,... | collective-permute-start | bytes 983048 | tf_op jit(solution)/shard_map/ppermute | solution.py:18
  15.6 2.1 %collective-permute-start = (bf16[163840]{0:T(1024)(128)(2,1)}, bf16[163840]{0:T(1024)(128)(2,1)S(1)}, u32[]{:S(2)}, u32[]{:S(2)}) collective-permute-start(bf16[163840]{0:T(1024)(128)(2,1)} %constant_dynamic-update-slice_fusion.14), channel_id=1, source_target_pairs={{0,1},{1,2},{2,3},{3,4},{4,5},{5,6},{6,7},{7,8},{8,9},{9,10},{10,1... | collective-permute-start | bytes 983048 | tf_op jit(solution)/shard_map/ppermute | solution.py:18
  21.4 2.5 %collective-permute-done.1 = bf16[163840]{0:T(1024)(128)(2,1)S(1)} collective-permute-done((bf16[163840]{0:T(1024)(128)(2,1)}, bf16[163840]{0:T(1024)(128)(2,1)S(1)}, u32[]{:S(2)}, u32[]{:S(2)}) %collective-permute-start.1) | collective-permute-done | bytes 327712 | tf_op jit(solution)/shard_map/ppermute | solution.py:18
  24.1 1.9 %collective-permute-done = bf16[163840]{0:T(1024)(128)(2,1)S(1)} collective-permute-done((bf16[163840]{0:T(1024)(128)(2,1)}, bf16[163840]{0:T(1024)(128)(2,1)S(1)}, u32[]{:S(2)}, u32[]{:S(2)}) %collective-permute-start) | collective-permute-done | bytes 327712 | tf_op jit(solution)/shard_map/ppermute | solution.py:18
  26.4 2.0 %gather_fusion.6 = bf16[16,128,512]{2,1,0:T(8,128)(2,1)} fusion(bf16[5,128,512]{2,1,0:T(8,128)(2,1)S(1)} %constant_dynamic-update-slice_fusion.6, s32[1024]{0:T(1024)S(1)} %get-tuple-element.13), kind=kCustom, calls=%fused_computation.6 | custom fusion | bytes 4194368 | tf_op jit(solution)/shard_map/gather | solution.py:180
  30.0 2.0 %gather_fusion.2 = bf16[16,128,512]{2,1,0:T(8,128)(2,1)} fusion(bf16[5,128,512]{2,1,0:T(8,128)(2,1)S(1)} %bitcast.82, s32[1024]{0:T(1024)S(1)} %get-tuple-element.13), kind=kCustom, calls=%fused_computation.2 | custom fusion | bytes 4194368 | tf_op jit(solution)/shard_map/gather | solution.py:179
  34.7 2.5 %gather_fusion.1 = bf16[24,128,384]{2,1,0:T(8,128)(2,1)S(1)} fusion(bf16[16,128,384]{2,1,0:T(8,128)(2,1)} %constant_dynamic-update-slice_fusion.1, s32[1024]{0:T(1024)S(1)} %get-tuple-element.14), kind=kCustom, calls=%fused_computation.1 | custom fusion | bytes 4718688 | tf_op jit(solution)/shard_map/gather | solution.py:163
  39.5 2.0 %add_convert_fusion = (bf16[1024,384]{1,0:T(8,128)(2,1)S(1)}, f32[1024,384]{1,0:T(8,128)}) fusion(bf16[1024,384]{1,0:T(8,128)(2,1)S(1)} %copy-done.9, f32[1024,384]{1,0:T(8,128)S(1)} %fusion.21, bf16[384,384]{1,0:T(8,128)(2,1)S(1)} %copy-done.22), kind=kOutput, calls=%fused_computation.15 | convolution fusion | flops 305135616 | bytes 5013504 | tf_op jit(solution)/shard_map/dot_general | solution.py:169
  43.8 3.3 %fusion.8 = bf16[8,128,256]{2,1,0:T(8,128)(2,1)S(1)} fusion(s32[8,128]{1,0:T(8,128)S(1)} %bitcast.95, bf16[8,128,512]{2,1,0:T(8,128)(2,1)} %bitcast.83, bf16[8,256,512]{2,1,0:T(8,128)(2,1)S(1)} %bitcast.79), kind=kOutput, calls=%fused_computation.29 | convolution fusion | flops 270535168 | bytes 3674112 | tf_op jit(solution)/shard_map/div | solution.py:186
  53.5 2.1 %multiply_convert_fusion = bf16[8,256,512]{2,1,0:T(8,128)(2,1)} fusion(bf16[8,128,256]{2,1,0:T(8,128)(2,1)S(1)} %fusion.8, bf16[8,128,512]{2,1,0:T(8,128)(2,1)S(1)} %bitcast.84), kind=kOutput, calls=%fused_computation.11 | convolution fusion | flops 270532608 | bytes 3670016 | tf_op jit(solution)/shard_map/bij,bie->bje/dot_general | solution.py:199
  65.3 3.5 %fusion.24 = f32[512,512]{1,0:T(8,128)S(1)} fusion(bf16[2048,512]{1,0:T(8,128)(2,1)} %bitcast.87, bf16[2048,512]{1,0:T(8,128)(2,1)} %bitcast.88), kind=kOutput, calls=%fused_computation.93 | convolution fusion | flops 1073741824 | bytes 5242880 | tf_op jit(solution)/shard_map/dot_general | solution.py:205
  73.8 3.0 %collective-permute-start.4 = (f32[32,11776]{1,0:T(8,128)S(1)}, f32[32,11776]{1,0:T(8,128)}, u32[]{:S(2)}, u32[]{:S(2)}) collective-permute-start(f32[32,11776]{1,0:T(8,128)S(1)} %dynamic-slice_bitcast_fusion), channel_id=1, source_target_pairs={{0,1},{1,0},{2,3},{3,2},{4,5},{5,4},{6,7},{7,6},{8,9},{9,8},{10,11... | collective-permute-start | bytes 4521992 | tf_op jit(solution)/shard_map/ppermute | solution.py:23
  76.9 2.9 %collective-permute-done.4 = f32[32,11776]{1,0:T(8,128)} collective-permute-done((f32[32,11776]{1,0:T(8,128)S(1)}, f32[32,11776]{1,0:T(8,128)}, u32[]{:S(2)}, u32[]{:S(2)}) %collective-permute-start.4) | collective-permute-done | bytes 1507360 | tf_op jit(solution)/shard_map/ppermute | solution.py:23
  79.8 2.0 %fusion.2 = f32[4,8,11776]{2,1,0:T(8,128)S(1)} fusion(f32[32,11776]{1,0:T(8,128)} %collective-permute-done.4, f32[2,32,11776]{2,1,0:T(8,128)} %copy-done.2, s32[]{:T(128)S(6)} %select_n.152), kind=kLoop, calls=%fused_computation.18 | loop fusion | flops 376832 | bytes 4521988 | tf_op jit(solution)/shard_map/reshape | solution.py:107
  81.9 9.9 %collective-permute-start.5 = (bf16[8,11776]{1,0:T(8,128)(2,1)S(1)}, bf16[8,11776]{1,0:T(8,128)(2,1)S(1)}, u32[]{:S(2)}, u32[]{:S(2)}) collective-permute-start(bf16[8,11776]{1,0:T(8,128)(2,1)S(1)} %get-tuple-element.4), channel_id=1, source_target_pairs={{0,2},{1,3},{2,4},{3,5},{4,6},{5,7},{6,0},{7,1},{8,10},{9,11},{10,... | collective-permute-start | bytes 565256 | tf_op jit(solution)/shard_map/ppermute | solution.py:89
  91.8 1.9 %collective-permute-start.7 = (bf16[8,11776]{1,0:T(8,128)(2,1)S(1)}, bf16[8,11776]{1,0:T(8,128)(2,1)S(1)}, u32[]{:S(2)}, u32[]{:S(2)}) collective-permute-start(bf16[8,11776]{1,0:T(8,128)(2,1)S(1)} %get-tuple-element.5), channel_id=1, source_target_pairs={{0,6},{1,7},{2,0},{3,1},{4,2},{5,3},{6,4},{7,5},{8,14},{9,15},{10,... | collective-permute-start | bytes 565256 | tf_op jit(solution)/shard_map/ppermute | solution.py:89
  93.7 3.4 %collective-permute-start.6 = (bf16[8,11776]{1,0:T(8,128)(2,1)S(1)}, bf16[8,11776]{1,0:T(8,128)(2,1)S(1)}, u32[]{:S(2)}, u32[]{:S(2)}) collective-permute-start(bf16[8,11776]{1,0:T(8,128)(2,1)S(1)} %get-tuple-element.6), channel_id=1, source_target_pairs={{0,4},{1,5},{2,6},{3,7},{4,0},{5,1},{6,2},{7,3},{8,12},{9,13},{10,... | collective-permute-start | bytes 565256 | tf_op jit(solution)/shard_map/ppermute | solution.py:89
  97.1 8.3 %collective-permute-done.7 = bf16[8,11776]{1,0:T(8,128)(2,1)S(1)} collective-permute-done((bf16[8,11776]{1,0:T(8,128)(2,1)S(1)}, bf16[8,11776]{1,0:T(8,128)(2,1)S(1)}, u32[]{:S(2)}, u32[]{:S(2)}) %collective-permute-start.7) | collective-permute-done | bytes 188448 | tf_op jit(solution)/shard_map/ppermute | solution.py:89
  105.7 1.9 %collective-permute-start.8 = (bf16[4,11776]{1,0:T(4,128)(2,1)S(1)}, bf16[4,11776]{1,0:T(4,128)(2,1)S(1)}, u32[]{:S(2)}, u32[]{:S(2)}) collective-permute-start(bf16[4,11776]{1,0:T(4,128)(2,1)S(1)} %fusion.14), channel_id=1, source_target_pairs={{0,8},{1,57},{2,10},{3,59},{4,12},{5,61},{6,14},{7,63},{8,0},{9,17... | collective-permute-start | bytes 282632 | tf_op jit(solution)/shard_map/ppermute | solution.py:120
  107.6 4.5 %collective-permute-done.8 = bf16[4,11776]{1,0:T(4,128)(2,1)S(1)} collective-permute-done((bf16[4,11776]{1,0:T(4,128)(2,1)S(1)}, bf16[4,11776]{1,0:T(4,128)(2,1)S(1)}, u32[]{:S(2)}, u32[]{:S(2)}) %collective-permute-start.8) | collective-permute-done | bytes 94240 | tf_op jit(solution)/shard_map/ppermute | solution.py:120
  112.4 1.9 %collective-permute-start.9 = (bf16[2,11776]{1,0:T(2,128)(2,1)S(1)}, bf16[2,11776]{1,0:T(2,128)(2,1)S(1)}, u32[]{:S(2)}, u32[]{:S(2)}) collective-permute-start(bf16[2,11776]{1,0:T(2,128)(2,1)S(1)} %fusion.15), channel_id=1, source_target_pairs={{0,16},{1,49},{2,18},{3,51},{4,20},{5,53},{6,22},{7,55},{8,24},{9,... | collective-permute-start | bytes 141320 | tf_op jit(solution)/shard_map/ppermute | solution.py:120
  114.4 4.9 %collective-permute-done.9 = bf16[2,11776]{1,0:T(2,128)(2,1)S(1)} collective-permute-done((bf16[2,11776]{1,0:T(2,128)(2,1)S(1)}, bf16[2,11776]{1,0:T(2,128)(2,1)S(1)}, u32[]{:S(2)}, u32[]{:S(2)}) %collective-permute-start.9) | collective-permute-done | bytes 47136 | tf_op jit(solution)/shard_map/ppermute | solution.py:120
  119.4 5.0 %collective-permute-start.10 = (f32[1,11776]{1,0:T(1,128)S(1)}, f32[1,11776]{1,0:T(1,128)S(1)}, u32[]{:S(2)}, u32[]{:S(2)}) collective-permute-start(f32[1,11776]{1,0:T(1,128)S(1)} %constant_dynamic-slice_fusion), channel_id=1, source_target_pairs={{0,32},{1,33},{2,34},{3,35},{4,36},{5,37},{6,38},{7,39},{8,40},{9,... | collective-permute-start | bytes 141320 | tf_op jit(solution)/shard_map/ppermute | solution.py:122
  124.4 5.2 %collective-permute-done.10 = f32[1,11776]{1,0:T(1,128)S(1)} collective-permute-done((f32[1,11776]{1,0:T(1,128)S(1)}, f32[1,11776]{1,0:T(1,128)S(1)}, u32[]{:S(2)}, u32[]{:S(2)}) %collective-permute-start.10) | collective-permute-done | bytes 47136 | tf_op jit(solution)/shard_map/ppermute | solution.py:122
  129.8 4.3 %collective-permute-start.11 = (f32[11776]{0:T(1024)S(1)}, f32[11776]{0:T(1024)S(1)}, u32[]{:S(2)}, u32[]{:S(2)}) collective-permute-start(f32[11776]{0:T(1024)S(1)} %add_reduce_fusion), channel_id=1, source_target_pairs={{0,64},{64,0},{128,192},{192,128},{256,320},{320,256},{384,448},{4... | collective-permute-start | bytes 141320 | tf_op jit(solution)/shard_map/ppermute | solution.py:23
  134.0 2.0 %collective-permute-done.11 = f32[11776]{0:T(1024)S(1)} collective-permute-done((f32[11776]{0:T(1024)S(1)}, f32[11776]{0:T(1024)S(1)}, u32[]{:S(2)}, u32[]{:S(2)}) %collective-permute-start.11) | collective-permute-done | bytes 47136 | tf_op jit(solution)/shard_map/ppermute | solution.py:23
  136.1 10.6 %collective-permute-start.14 = (f32[11776]{0:T(1024)S(1)}, f32[11776]{0:T(1024)S(1)}, u32[]{:S(2)}, u32[]{:S(2)}) collective-permute-start(f32[11776]{0:T(1024)S(1)} %add.217), channel_id=1, source_target_pairs={{0,384},{64,448},{128,0},{192,64},{256,128},{320,192},{384,256},{4... | collective-permute-start | bytes 141320 | tf_op jit(solution)/shard_map/ppermute | solution.py:18
  146.7 1.9 %collective-permute-start.13 = (f32[11776]{0:T(1024)S(1)}, f32[11776]{0:T(1024)S(1)}, u32[]{:S(2)}, u32[]{:S(2)}) collective-permute-start(f32[11776]{0:T(1024)S(1)} %add.217), channel_id=1, source_target_pairs={{0,256},{64,320},{128,384},{192,448},{256,0},{320,64},{384,128},{4... | collective-permute-start | bytes 141320 | tf_op jit(solution)/shard_map/ppermute | solution.py:18
  148.6 4.8 %collective-permute-start.12 = (f32[11776]{0:T(1024)S(1)}, f32[11776]{0:T(1024)S(1)}, u32[]{:S(2)}, u32[]{:S(2)}) collective-permute-start(f32[11776]{0:T(1024)S(1)} %add.217), channel_id=1, source_target_pairs={{0,128},{64,192},{128,256},{192,320},{256,384},{320,448},{384,0},{... | collective-permute-start | bytes 141320 | tf_op jit(solution)/shard_map/ppermute | solution.py:18
  153.5 3.6 %collective-permute-done.13 = f32[11776]{0:T(1024)S(1)} collective-permute-done((f32[11776]{0:T(1024)S(1)}, f32[11776]{0:T(1024)S(1)}, u32[]{:S(2)}, u32[]{:S(2)}) %collective-permute-start.13) | collective-permute-done | bytes 47136 | tf_op jit(solution)/shard_map/ppermute | solution.py:18
  (148 shorter events, 43.4 us)
Async XLA Ops:
  0.6 36.6 %copy-start = (bf16[8,3,128,128]{3,2,1,0:T(8,128)(2,1)S(1)}, bf16[8,3,128,128]{3,2,1,0:T(8,128)(2,1)}, u32[]{:S(2)}) copy-start(bf16[8,3,128,128]{3,2,1,0:T(8,128)(2,1)} %param.16) | copy-start | bytes 2359300
  0.6 17.1 %copy-start.8 = (bf16[1024,384]{1,0:T(8,128)(2,1)S(1)}, bf16[1024,384]{1,0:T(8,128)(2,1)}, u32[]{:S(2)}) copy-start(bf16[1024,384]{1,0:T(8,128)(2,1)} %param.15) | copy-start | bytes 2359300
  2.4 16.3 %copy-start.21 = (s32[8,2]{0,1:T(2,128)S(1)}, s32[8,2]{0,1:T(2,128)}, u32[]{:S(2)}) copy-start(s32[8,2]{0,1:T(2,128)} %param.19) | copy-start | bytes 196
  2.4 16.3 %copy-start.18 = (s32[8,3]{0,1:T(4,128)S(1)}, s32[8,3]{0,1:T(4,128)}, u32[]{:S(2)}) copy-start(s32[8,3]{0,1:T(4,128)} %param.17) | copy-start | bytes 292
  2.4 16.6 %copy-start.19 = (s32[512]{0:T(512)S(1)}, s32[512]{0:T(512)}, u32[]{:S(2)}) copy-start(s32[512]{0:T(512)} %constant.199) | copy-start | bytes 6148
  2.4 16.6 %copy-start.20 = (s32[384]{0:T(512)S(1)}, s32[384]{0:T(512)}, u32[]{:S(2)}) copy-start(s32[384]{0:T(512)} %constant.196) | copy-start | bytes 4612
  2.4 16.6 %copy-start.13 = (bf16[128,512]{1,0:T(8,128)(2,1)S(1)}, bf16[128,512]{1,0:T(8,128)(2,1)}, u32[]{:S(2)}) copy-start(bf16[128,512]{1,0:T(8,128)(2,1)} %param.21) | copy-start | bytes 393220
  5.7 13.7 %collective-permute-start.3 = (bf16[163840]{0:T(1024)(128)(2,1)}, bf16[163840]{0:T(1024)(128)(2,1)S(1)}, u32[]{:S(2)}, u32[]{:S(2)}) collective-permute-start(bf16[163840]{0:T(1024)(128)(2,1)} %constant_dynamic-update-slice_fusion.14), channel_id=1, source_target_pairs={{0,62},{1,63},{2,0},{3,1},{4,2},{5,3},{6,4},{7,5},{8,6},{9,7},{10,... | collective-permute-start | bytes 983048 | tf_op jit(solution)/shard_map/ppermute | solution.py:18
  8.4 11.2 %collective-permute-start.2 = (bf16[163840]{0:T(1024)(128)(2,1)}, bf16[163840]{0:T(1024)(128)(2,1)S(1)}, u32[]{:S(2)}, u32[]{:S(2)}) collective-permute-start(bf16[163840]{0:T(1024)(128)(2,1)} %constant_dynamic-update-slice_fusion.14), channel_id=1, source_target_pairs={{0,63},{1,0},{2,1},{3,2},{4,3},{5,4},{6,5},{7,6},{8,7},{9,8},{10,9... | collective-permute-start | bytes 983048 | tf_op jit(solution)/shard_map/ppermute | solution.py:18
  10.3 13.5 %collective-permute-start.1 = (bf16[163840]{0:T(1024)(128)(2,1)}, bf16[163840]{0:T(1024)(128)(2,1)S(1)}, u32[]{:S(2)}, u32[]{:S(2)}) collective-permute-start(bf16[163840]{0:T(1024)(128)(2,1)} %constant_dynamic-update-slice_fusion.14), channel_id=1, source_target_pairs={{0,2},{1,3},{2,4},{3,5},{4,6},{5,7},{6,8},{7,9},{8,10},{9,11},{10,... | collective-permute-start | bytes 983048 | tf_op jit(solution)/shard_map/ppermute | solution.py:18
  15.6 10.5 %collective-permute-start = (bf16[163840]{0:T(1024)(128)(2,1)}, bf16[163840]{0:T(1024)(128)(2,1)S(1)}, u32[]{:S(2)}, u32[]{:S(2)}) collective-permute-start(bf16[163840]{0:T(1024)(128)(2,1)} %constant_dynamic-update-slice_fusion.14), channel_id=1, source_target_pairs={{0,1},{1,2},{2,3},{3,4},{4,5},{5,6},{6,7},{7,8},{8,9},{9,10},{10,1... | collective-permute-start | bytes 983048 | tf_op jit(solution)/shard_map/ppermute | solution.py:18
  38.0 3.5 %copy-start.5 = (bf16[8,384,128]{1,2,0:T(8,128)(2,1)}, bf16[8,384,128]{1,2,0:T(8,128)(2,1)S(1)}, u32[]{:S(2)}) copy-start(bf16[8,384,128]{1,2,0:T(8,128)(2,1)S(1)} %bitcast_convert_fusion) | copy-start | bytes 2359300
  38.0 1.4 copy-start.9
  38.0 1.5 copy-start.22
  39.5 2.0 %copy-start.14 = (bf16[384,512]{1,0:T(8,128)(2,1)S(1)}, bf16[384,512]{1,0:T(8,128)(2,1)}, u32[]{:S(2)}) copy-start(bf16[384,512]{1,0:T(8,128)(2,1)} %param.24) | copy-start | bytes 1179652
  41.5 1.7 %copy-start.11 = (bf16[1024,384]{1,0:T(8,128)(2,1)}, bf16[1024,384]{1,0:T(8,128)(2,1)S(1)}, u32[]{:S(2)}) copy-start(bf16[1024,384]{1,0:T(8,128)(2,1)S(1)} %get-tuple-element.9) | copy-start | bytes 2359300
  41.5 2.3 %copy-start.1 = (bf16[16,128,512]{2,1,0:T(8,128)(2,1)S(1)}, bf16[16,128,512]{2,1,0:T(8,128)(2,1)}, u32[]{:S(2)}) copy-start(bf16[16,128,512]{2,1,0:T(8,128)(2,1)} %gather_fusion.2) | copy-start | bytes 6291460
  41.5 2.3 %copy-start.23 = (s32[1024]{0:T(1024)S(1)}, s32[1024]{0:T(1024)}, u32[]{:S(2)}) copy-start(s32[1024]{0:T(1024)} %param.20) | copy-start | bytes 12292
  48.2 1.5 copy-start.24
  52.0 1.4 copy-start.3
  72.1 1.6 copy-start.2
  73.8 6.0 %collective-permute-start.4 = (f32[32,11776]{1,0:T(8,128)S(1)}, f32[32,11776]{1,0:T(8,128)}, u32[]{:S(2)}, u32[]{:S(2)}) collective-permute-start(f32[32,11776]{1,0:T(8,128)S(1)} %dynamic-slice_bitcast_fusion), channel_id=1, source_target_pairs={{0,1},{1,0},{2,3},{3,2},{4,5},{5,4},{6,7},{7,6},{8,9},{9,8},{10,11... | collective-permute-start | bytes 4521992 | tf_op jit(solution)/shard_map/ppermute | solution.py:23
  81.9 15.2 %collective-permute-start.5 = (bf16[8,11776]{1,0:T(8,128)(2,1)S(1)}, bf16[8,11776]{1,0:T(8,128)(2,1)S(1)}, u32[]{:S(2)}, u32[]{:S(2)}) collective-permute-start(bf16[8,11776]{1,0:T(8,128)(2,1)S(1)} %get-tuple-element.4), channel_id=1, source_target_pairs={{0,2},{1,3},{2,4},{3,5},{4,6},{5,7},{6,0},{7,1},{8,10},{9,11},{10,... | collective-permute-start | bytes 565256 | tf_op jit(solution)/shard_map/ppermute | solution.py:89
  91.8 13.6 %collective-permute-start.7 = (bf16[8,11776]{1,0:T(8,128)(2,1)S(1)}, bf16[8,11776]{1,0:T(8,128)(2,1)S(1)}, u32[]{:S(2)}, u32[]{:S(2)}) collective-permute-start(bf16[8,11776]{1,0:T(8,128)(2,1)S(1)} %get-tuple-element.5), channel_id=1, source_target_pairs={{0,6},{1,7},{2,0},{3,1},{4,2},{5,3},{6,4},{7,5},{8,14},{9,15},{10,... | collective-permute-start | bytes 565256 | tf_op jit(solution)/shard_map/ppermute | solution.py:89
  93.7 11.7 %collective-permute-start.6 = (bf16[8,11776]{1,0:T(8,128)(2,1)S(1)}, bf16[8,11776]{1,0:T(8,128)(2,1)S(1)}, u32[]{:S(2)}, u32[]{:S(2)}) collective-permute-start(bf16[8,11776]{1,0:T(8,128)(2,1)S(1)} %get-tuple-element.6), channel_id=1, source_target_pairs={{0,4},{1,5},{2,6},{3,7},{4,0},{5,1},{6,2},{7,3},{8,12},{9,13},{10,... | collective-permute-start | bytes 565256 | tf_op jit(solution)/shard_map/ppermute | solution.py:89
  105.7 6.5 %collective-permute-start.8 = (bf16[4,11776]{1,0:T(4,128)(2,1)S(1)}, bf16[4,11776]{1,0:T(4,128)(2,1)S(1)}, u32[]{:S(2)}, u32[]{:S(2)}) collective-permute-start(bf16[4,11776]{1,0:T(4,128)(2,1)S(1)} %fusion.14), channel_id=1, source_target_pairs={{0,8},{1,57},{2,10},{3,59},{4,12},{5,61},{6,14},{7,63},{8,0},{9,17... | collective-permute-start | bytes 282632 | tf_op jit(solution)/shard_map/ppermute | solution.py:120
  112.4 6.9 %collective-permute-start.9 = (bf16[2,11776]{1,0:T(2,128)(2,1)S(1)}, bf16[2,11776]{1,0:T(2,128)(2,1)S(1)}, u32[]{:S(2)}, u32[]{:S(2)}) collective-permute-start(bf16[2,11776]{1,0:T(2,128)(2,1)S(1)} %fusion.15), channel_id=1, source_target_pairs={{0,16},{1,49},{2,18},{3,51},{4,20},{5,53},{6,22},{7,55},{8,24},{9,... | collective-permute-start | bytes 141320 | tf_op jit(solution)/shard_map/ppermute | solution.py:120
  119.4 10.2 %collective-permute-start.10 = (f32[1,11776]{1,0:T(1,128)S(1)}, f32[1,11776]{1,0:T(1,128)S(1)}, u32[]{:S(2)}, u32[]{:S(2)}) collective-permute-start(f32[1,11776]{1,0:T(1,128)S(1)} %constant_dynamic-slice_fusion), channel_id=1, source_target_pairs={{0,32},{1,33},{2,34},{3,35},{4,36},{5,37},{6,38},{7,39},{8,40},{9,... | collective-permute-start | bytes 141320 | tf_op jit(solution)/shard_map/ppermute | solution.py:122
  129.8 6.3 %collective-permute-start.11 = (f32[11776]{0:T(1024)S(1)}, f32[11776]{0:T(1024)S(1)}, u32[]{:S(2)}, u32[]{:S(2)}) collective-permute-start(f32[11776]{0:T(1024)S(1)} %add_reduce_fusion), channel_id=1, source_target_pairs={{0,64},{64,0},{128,192},{192,128},{256,320},{320,256},{384,448},{4... | collective-permute-start | bytes 141320 | tf_op jit(solution)/shard_map/ppermute | solution.py:23
  136.1 17.4 %collective-permute-start.14 = (f32[11776]{0:T(1024)S(1)}, f32[11776]{0:T(1024)S(1)}, u32[]{:S(2)}, u32[]{:S(2)}) collective-permute-start(f32[11776]{0:T(1024)S(1)} %add.217), channel_id=1, source_target_pairs={{0,384},{64,448},{128,0},{192,64},{256,128},{320,192},{384,256},{4... | collective-permute-start | bytes 141320 | tf_op jit(solution)/shard_map/ppermute | solution.py:18
  146.7 10.4 %collective-permute-start.13 = (f32[11776]{0:T(1024)S(1)}, f32[11776]{0:T(1024)S(1)}, u32[]{:S(2)}, u32[]{:S(2)}) collective-permute-start(f32[11776]{0:T(1024)S(1)} %add.217), channel_id=1, source_target_pairs={{0,256},{64,320},{128,384},{192,448},{256,0},{320,64},{384,128},{4... | collective-permute-start | bytes 141320 | tf_op jit(solution)/shard_map/ppermute | solution.py:18
  148.6 8.7 %collective-permute-start.12 = (f32[11776]{0:T(1024)S(1)}, f32[11776]{0:T(1024)S(1)}, u32[]{:S(2)}, u32[]{:S(2)}) collective-permute-start(f32[11776]{0:T(1024)S(1)} %add.217), channel_id=1, source_target_pairs={{0,128},{64,192},{128,256},{192,320},{256,384},{320,448},{384,0},{... | collective-permute-start | bytes 141320 | tf_op jit(solution)/shard_map/ppermute | solution.py:18
  (8 other events, 8.8 us)

commit v10 on v8

--- a/solution.py
+++ b/solution.py
@@ -101,7 +101,7 @@
     core = me % 2
     mine = lax.dynamic_index_in_dim(flat, core, 0, keepdims=False)
     other = lax.dynamic_index_in_dim(flat, 1 - core, 0, keepdims=False)
-    held = mine + swapped(other, "dom", 1)
+    held = mine + swapped(other.astype(bf16), "dom", 1).astype(f32)
     lx = (me // 2 % n_x - core) % n_x
     ly = (me // (2 * n_x) - core) % n_y
     held = held.reshape(n_x, -1, width)

time: 159 us -> 157 us (0.987)
  no operation moved by 1% of the time
where the time goes in v10:
time: 157 us; the launch traced here: 156 us
  starting transfers between devices  58.6 us (37%)
  local copies, waits for them, and re-layouts  37.9 us (24%)
  waiting for transfers between devices  35.7 us (23%)
  matrix products  19.5 us (12%)
  other arithmetic  2.68 us (2%)
  between operations  1.57 us (1%)
    ppermute x4, starting transfers between devices, swapped(): return lax.ppermute(shard, axis, [(i, i ^ mask) for i in range(count)])  22.6 us
    ppermute x3, starting transfers between devices, shifted_x(): return lax.ppermute(shard, 'dom', pairs)  15.2 us
    ppermute x4, starting transfers between devices, passed_along(): lax.ppermute(shard, axis, [(i, (i + by) % count) for i in range(count)])  12 us
    unnamed x63, local copies, waits for them, and re-layouts  11.6 us
    ppermute x2, waiting for transfers between devices, reduce_to_share(): got = lax.ppermute(other.astype(bf16), 'dom', pairs).astype(f32)  9.46 us
    ppermute x3, waiting for transfers between devices, shifted_x(): return lax.ppermute(shard, 'dom', pairs)  8.28 us
    ppermute x4, waiting for transfers between devices, swapped(): return lax.ppermute(shard, axis, [(i, i ^ mask) for i in range(count)])  8.16 us
    gather x4, local copies, waits for them, and re-layouts, reduce_to_share(): t[share_order(t.shape[0], n_dom, n_x)].reshape(2, n_y * n_x, -1)  6.89 us
  transfers between devices with their start and end apart: 14, of which 11 were waited for; matrix products, arithmetic and copies ran while one was open for 2% of the time, Pallas kernels for 0%

profile of v10, /device:TPU:6, one launch (start us, length us, event | category | flops | bytes accessed | tf_op | source)
XLA Modules:
  0.0 156.0 jit_solution(4970737573742652980)
XLA Ops:
  5.6 2.7 %collective-permute-start.3 = (bf16[163840]{0:T(1024)(128)(2,1)}, bf16[163840]{0:T(1024)(128)(2,1)S(1)}, u32[]{:S(2)}, u32[]{:S(2)}) collective-permute-start(bf16[163840]{0:T(1024)(128)(2,1)} %constant_dynamic-update-slice_fusion.14), channel_id=1, source_target_pairs={{0,62},{1,63},{2,0},{3,1},{4,2},{5,3},{6,4},{7,5},{8,6},{9,7},{10,... | collective-permute-start | bytes 983048 | tf_op jit(solution)/shard_map/ppermute | solution.py:18
  8.4 1.9 %collective-permute-start.2 = (bf16[163840]{0:T(1024)(128)(2,1)}, bf16[163840]{0:T(1024)(128)(2,1)S(1)}, u32[]{:S(2)}, u32[]{:S(2)}) collective-permute-start(bf16[163840]{0:T(1024)(128)(2,1)} %constant_dynamic-update-slice_fusion.14), channel_id=1, source_target_pairs={{0,63},{1,0},{2,1},{3,2},{4,3},{5,4},{6,5},{7,6},{8,7},{9,8},{10,9... | collective-permute-start | bytes 983048 | tf_op jit(solution)/shard_map/ppermute | solution.py:18
  10.3 5.2 %collective-permute-start.1 = (bf16[163840]{0:T(1024)(128)(2,1)}, bf16[163840]{0:T(1024)(128)(2,1)S(1)}, u32[]{:S(2)}, u32[]{:S(2)}) collective-permute-start(bf16[163840]{0:T(1024)(128)(2,1)} %constant_dynamic-update-slice_fusion.14), channel_id=1, source_target_pairs={{0,2},{1,3},{2,4},{3,5},{4,6},{5,7},{6,8},{7,9},{8,10},{9,11},{10,... | collective-permute-start | bytes 983048 | tf_op jit(solution)/shard_map/ppermute | solution.py:18
  15.5 2.1 %collective-permute-start = (bf16[163840]{0:T(1024)(128)(2,1)}, bf16[163840]{0:T(1024)(128)(2,1)S(1)}, u32[]{:S(2)}, u32[]{:S(2)}) collective-permute-start(bf16[163840]{0:T(1024)(128)(2,1)} %constant_dynamic-update-slice_fusion.14), channel_id=1, source_target_pairs={{0,1},{1,2},{2,3},{3,4},{4,5},{5,6},{6,7},{7,8},{8,9},{9,10},{10,1... | collective-permute-start | bytes 983048 | tf_op jit(solution)/shard_map/ppermute | solution.py:18
  21.4 2.4 %collective-permute-done.1 = bf16[163840]{0:T(1024)(128)(2,1)S(1)} collective-permute-done((bf16[163840]{0:T(1024)(128)(2,1)}, bf16[163840]{0:T(1024)(128)(2,1)S(1)}, u32[]{:S(2)}, u32[]{:S(2)}) %collective-permute-start.1) | collective-permute-done | bytes 327712 | tf_op jit(solution)/shard_map/ppermute | solution.py:18
  24.1 1.9 %collective-permute-done = bf16[163840]{0:T(1024)(128)(2,1)S(1)} collective-permute-done((bf16[163840]{0:T(1024)(128)(2,1)}, bf16[163840]{0:T(1024)(128)(2,1)S(1)}, u32[]{:S(2)}, u32[]{:S(2)}) %collective-permute-start) | collective-permute-done | bytes 327712 | tf_op jit(solution)/shard_map/ppermute | solution.py:18
  26.3 2.0 %gather_fusion.6 = bf16[16,128,512]{2,1,0:T(8,128)(2,1)} fusion(bf16[5,128,512]{2,1,0:T(8,128)(2,1)S(1)} %constant_dynamic-update-slice_fusion.6, s32[1024]{0:T(1024)S(1)} %get-tuple-element.13), kind=kCustom, calls=%fused_computation.6 | custom fusion | bytes 4194368 | tf_op jit(solution)/shard_map/gather | solution.py:178
  29.9 2.0 %gather_fusion.2 = bf16[16,128,512]{2,1,0:T(8,128)(2,1)} fusion(bf16[5,128,512]{2,1,0:T(8,128)(2,1)S(1)} %bitcast.80, s32[1024]{0:T(1024)S(1)} %get-tuple-element.13), kind=kCustom, calls=%fused_computation.2 | custom fusion | bytes 4194368 | tf_op jit(solution)/shard_map/gather | solution.py:177
  34.7 2.5 %gather_fusion.1 = bf16[24,128,384]{2,1,0:T(8,128)(2,1)S(1)} fusion(bf16[16,128,384]{2,1,0:T(8,128)(2,1)} %constant_dynamic-update-slice_fusion.1, s32[1024]{0:T(1024)S(1)} %get-tuple-element.14), kind=kCustom, calls=%fused_computation.1 | custom fusion | bytes 4718688 | tf_op jit(solution)/shard_map/gather | solution.py:161
  39.5 2.0 %add_convert_fusion = (bf16[1024,384]{1,0:T(8,128)(2,1)S(1)}, f32[1024,384]{1,0:T(8,128)}) fusion(bf16[1024,384]{1,0:T(8,128)(2,1)S(1)} %copy-done.9, f32[1024,384]{1,0:T(8,128)S(1)} %fusion.19, bf16[384,384]{1,0:T(8,128)(2,1)S(1)} %copy-done.22), kind=kOutput, calls=%fused_computation.14 | convolution fusion | flops 305135616 | bytes 5013504 | tf_op jit(solution)/shard_map/dot_general | solution.py:167
  43.7 3.3 %fusion.8 = bf16[8,128,256]{2,1,0:T(8,128)(2,1)S(1)} fusion(s32[8,128]{1,0:T(8,128)S(1)} %bitcast.93, bf16[8,128,512]{2,1,0:T(8,128)(2,1)} %bitcast.81, bf16[8,256,512]{2,1,0:T(8,128)(2,1)S(1)} %bitcast.77), kind=kOutput, calls=%fused_computation.28 | convolution fusion | flops 270535168 | bytes 3674112 | tf_op jit(solution)/shard_map/div | solution.py:184
  52.8 2.1 %multiply_convert_fusion = bf16[8,256,512]{2,1,0:T(8,128)(2,1)} fusion(bf16[8,128,256]{2,1,0:T(8,128)(2,1)S(1)} %fusion.8, bf16[8,128,512]{2,1,0:T(8,128)(2,1)S(1)} %bitcast.82), kind=kOutput, calls=%fused_computation.10 | convolution fusion | flops 270532608 | bytes 3670016 | tf_op jit(solution)/shard_map/bij,bie->bje/dot_general | solution.py:197
  56.2 1.9 %gather_fusion.4 = f32[384,384]{1,0:T(8,128)S(1)} fusion(f32[384,384]{1,0:T(8,128)S(1)} %copy.25, s32[1024]{0:T(1024)S(1)} %get-tuple-element.12), kind=kCustom, calls=%fused_computation.4 | custom fusion | bytes 1181184 | tf_op jit(solution)/shard_map/gather | solution.py:97
  64.6 3.5 %fusion.22 = f32[512,512]{1,0:T(8,128)S(1)} fusion(bf16[2048,512]{1,0:T(8,128)(2,1)} %bitcast.85, bf16[2048,512]{1,0:T(8,128)(2,1)} %bitcast.86), kind=kOutput, calls=%fused_computation.79 | convolution fusion | flops 1073741824 | bytes 5242880 | tf_op jit(solution)/shard_map/dot_general | solution.py:203
  73.1 3.0 %collective-permute-start.4 = (bf16[32,11776]{1,0:T(8,128)(2,1)S(1)}, bf16[32,11776]{1,0:T(8,128)(2,1)S(1)}, u32[]{:S(2)}, u32[]{:S(2)}) collective-permute-start(bf16[32,11776]{1,0:T(8,128)(2,1)S(1)} %fusion.9), channel_id=1, source_target_pairs={{0,1},{1,0},{2,3},{3,2},{4,5},{5,4},{6,7},{7,6},{8,9},{9,8},{10,11... | collective-permute-start | bytes 2261000 | tf_op jit(solution)/shard_map/ppermute | solution.py:23
  76.2 1.7 %collective-permute-done.4 = bf16[32,11776]{1,0:T(8,128)(2,1)S(1)} collective-permute-done((bf16[32,11776]{1,0:T(8,128)(2,1)S(1)}, bf16[32,11776]{1,0:T(8,128)(2,1)S(1)}, u32[]{:S(2)}, u32[]{:S(2)}) %collective-permute-start.4) | collective-permute-done | bytes 753696 | tf_op jit(solution)/shard_map/ppermute | solution.py:23
  79.5 9.9 %collective-permute-start.5 = (bf16[8,11776]{1,0:T(8,128)(2,1)S(1)}, bf16[8,11776]{1,0:T(8,128)(2,1)S(1)}, u32[]{:S(2)}, u32[]{:S(2)}) collective-permute-start(bf16[8,11776]{1,0:T(8,128)(2,1)S(1)} %get-tuple-element.4), channel_id=1, source_target_pairs={{0,2},{1,3},{2,4},{3,5},{4,6},{5,7},{6,0},{7,1},{8,10},{9,11},{10,... | collective-permute-start | bytes 565256 | tf_op jit(solution)/shard_map/ppermute | solution.py:89
  89.4 1.9 %collective-permute-start.7 = (bf16[8,11776]{1,0:T(8,128)(2,1)S(1)}, bf16[8,11776]{1,0:T(8,128)(2,1)S(1)}, u32[]{:S(2)}, u32[]{:S(2)}) collective-permute-start(bf16[8,11776]{1,0:T(8,128)(2,1)S(1)} %get-tuple-element.5), channel_id=1, source_target_pairs={{0,6},{1,7},{2,0},{3,1},{4,2},{5,3},{6,4},{7,5},{8,14},{9,15},{10,... | collective-permute-start | bytes 565256 | tf_op jit(solution)/shard_map/ppermute | solution.py:89
  91.3 3.4 %collective-permute-start.6 = (bf16[8,11776]{1,0:T(8,128)(2,1)S(1)}, bf16[8,11776]{1,0:T(8,128)(2,1)S(1)}, u32[]{:S(2)}, u32[]{:S(2)}) collective-permute-start(bf16[8,11776]{1,0:T(8,128)(2,1)S(1)} %get-tuple-element.6), channel_id=1, source_target_pairs={{0,4},{1,5},{2,6},{3,7},{4,0},{5,1},{6,2},{7,3},{8,12},{9,13},{10,... | collective-permute-start | bytes 565256 | tf_op jit(solution)/shard_map/ppermute | solution.py:89
  94.7 8.3 %collective-permute-done.7 = bf16[8,11776]{1,0:T(8,128)(2,1)S(1)} collective-permute-done((bf16[8,11776]{1,0:T(8,128)(2,1)S(1)}, bf16[8,11776]{1,0:T(8,128)(2,1)S(1)}, u32[]{:S(2)}, u32[]{:S(2)}) %collective-permute-start.7) | collective-permute-done | bytes 188448 | tf_op jit(solution)/shard_map/ppermute | solution.py:89
  103.3 1.9 %collective-permute-start.8 = (bf16[4,11776]{1,0:T(4,128)(2,1)S(1)}, bf16[4,11776]{1,0:T(4,128)(2,1)S(1)}, u32[]{:S(2)}, u32[]{:S(2)}) collective-permute-start(bf16[4,11776]{1,0:T(4,128)(2,1)S(1)} %fusion.15), channel_id=1, source_target_pairs={{0,8},{1,57},{2,10},{3,59},{4,12},{5,61},{6,14},{7,63},{8,0},{9,17... | collective-permute-start | bytes 282632 | tf_op jit(solution)/shard_map/ppermute | solution.py:120
  105.2 4.5 %collective-permute-done.8 = bf16[4,11776]{1,0:T(4,128)(2,1)S(1)} collective-permute-done((bf16[4,11776]{1,0:T(4,128)(2,1)S(1)}, bf16[4,11776]{1,0:T(4,128)(2,1)S(1)}, u32[]{:S(2)}, u32[]{:S(2)}) %collective-permute-start.8) | collective-permute-done | bytes 94240 | tf_op jit(solution)/shard_map/ppermute | solution.py:120
  110.0 1.9 %collective-permute-start.9 = (bf16[2,11776]{1,0:T(2,128)(2,1)S(1)}, bf16[2,11776]{1,0:T(2,128)(2,1)S(1)}, u32[]{:S(2)}, u32[]{:S(2)}) collective-permute-start(bf16[2,11776]{1,0:T(2,128)(2,1)S(1)} %fusion.16), channel_id=1, source_target_pairs={{0,16},{1,49},{2,18},{3,51},{4,20},{5,53},{6,22},{7,55},{8,24},{9,... | collective-permute-start | bytes 141320 | tf_op jit(solution)/shard_map/ppermute | solution.py:120
  111.9 4.9 %collective-permute-done.9 = bf16[2,11776]{1,0:T(2,128)(2,1)S(1)} collective-permute-done((bf16[2,11776]{1,0:T(2,128)(2,1)S(1)}, bf16[2,11776]{1,0:T(2,128)(2,1)S(1)}, u32[]{:S(2)}, u32[]{:S(2)}) %collective-permute-start.9) | collective-permute-done | bytes 47136 | tf_op jit(solution)/shard_map/ppermute | solution.py:120
  117.0 5.0 %collective-permute-start.10 = (f32[1,11776]{1,0:T(1,128)S(1)}, f32[1,11776]{1,0:T(1,128)S(1)}, u32[]{:S(2)}, u32[]{:S(2)}) collective-permute-start(f32[1,11776]{1,0:T(1,128)S(1)} %constant_dynamic-slice_fusion), channel_id=1, source_target_pairs={{0,32},{1,33},{2,34},{3,35},{4,36},{5,37},{6,38},{7,39},{8,40},{9,... | collective-permute-start | bytes 141320 | tf_op jit(solution)/shard_map/ppermute | solution.py:122
  122.0 5.2 %collective-permute-done.10 = f32[1,11776]{1,0:T(1,128)S(1)} collective-permute-done((f32[1,11776]{1,0:T(1,128)S(1)}, f32[1,11776]{1,0:T(1,128)S(1)}, u32[]{:S(2)}, u32[]{:S(2)}) %collective-permute-start.10) | collective-permute-done | bytes 47136 | tf_op jit(solution)/shard_map/ppermute | solution.py:122
  127.3 4.3 %collective-permute-start.11 = (f32[11776]{0:T(1024)S(1)}, f32[11776]{0:T(1024)S(1)}, u32[]{:S(2)}, u32[]{:S(2)}) collective-permute-start(f32[11776]{0:T(1024)S(1)} %add_reduce_fusion), channel_id=1, source_target_pairs={{0,64},{64,0},{128,192},{192,128},{256,320},{320,256},{384,448},{4... | collective-permute-start | bytes 141320 | tf_op jit(solution)/shard_map/ppermute | solution.py:23
  131.6 2.1 %collective-permute-done.11 = f32[11776]{0:T(1024)S(1)} collective-permute-done((f32[11776]{0:T(1024)S(1)}, f32[11776]{0:T(1024)S(1)}, u32[]{:S(2)}, u32[]{:S(2)}) %collective-permute-start.11) | collective-permute-done | bytes 47136 | tf_op jit(solution)/shard_map/ppermute | solution.py:23
  133.7 6.1 %collective-permute-start.12 = (f32[11776]{0:T(1024)S(1)}, f32[11776]{0:T(1024)S(1)}, u32[]{:S(2)}, u32[]{:S(2)}) collective-permute-start(f32[11776]{0:T(1024)S(1)} %add.188), channel_id=1, source_target_pairs={{0,128},{64,192},{128,0},{192,64},{256,384},{320,448},{384,256},{4... | collective-permute-start | bytes 141320 | tf_op jit(solution)/shard_map/ppermute | solution.py:23
  139.8 2.1 %collective-permute-done.12 = f32[11776]{0:T(1024)S(1)} collective-permute-done((f32[11776]{0:T(1024)S(1)}, f32[11776]{0:T(1024)S(1)}, u32[]{:S(2)}, u32[]{:S(2)}) %collective-permute-start.12) | collective-permute-done | bytes 47136 | tf_op jit(solution)/shard_map/ppermute | solution.py:23
  141.9 9.3 %collective-permute-start.13 = (f32[11776]{0:T(1024)S(1)}, f32[11776]{0:T(1024)S(1)}, u32[]{:S(2)}, u32[]{:S(2)}) collective-permute-start(f32[11776]{0:T(1024)S(1)} %add.189), channel_id=1, source_target_pairs={{0,256},{64,320},{128,384},{192,448},{256,0},{320,64},{384,128},{4... | collective-permute-start | bytes 141320 | tf_op jit(solution)/shard_map/ppermute | solution.py:23
  151.1 2.3 %collective-permute-done.13 = f32[11776]{0:T(1024)S(1)} collective-permute-done((f32[11776]{0:T(1024)S(1)}, f32[11776]{0:T(1024)S(1)}, u32[]{:S(2)}, u32[]{:S(2)}) %collective-permute-start.13) | collective-permute-done | bytes 47136 | tf_op jit(solution)/shard_map/ppermute | solution.py:23
  (138 shorter events, 40.9 us)
Async XLA Ops:
  0.6 36.6 %copy-start = (bf16[8,3,128,128]{3,2,1,0:T(8,128)(2,1)S(1)}, bf16[8,3,128,128]{3,2,1,0:T(8,128)(2,1)}, u32[]{:S(2)}) copy-start(bf16[8,3,128,128]{3,2,1,0:T(8,128)(2,1)} %param.16) | copy-start | bytes 2359300
  0.6 18.4 %copy-start.19 = (s32[512]{0:T(512)S(1)}, s32[512]{0:T(512)}, u32[]{:S(2)}) copy-start(s32[512]{0:T(512)} %constant.164) | copy-start | bytes 6148
  0.7 18.4 %copy-start.20 = (s32[384]{0:T(512)S(1)}, s32[384]{0:T(512)}, u32[]{:S(2)}) copy-start(s32[384]{0:T(512)} %constant.161) | copy-start | bytes 4612
  0.7 18.4 %copy-start.13 = (bf16[128,512]{1,0:T(8,128)(2,1)S(1)}, bf16[128,512]{1,0:T(8,128)(2,1)}, u32[]{:S(2)}) copy-start(bf16[128,512]{1,0:T(8,128)(2,1)} %param.21) | copy-start | bytes 393220
  0.7 17.0 %copy-start.8 = (bf16[1024,384]{1,0:T(8,128)(2,1)S(1)}, bf16[1024,384]{1,0:T(8,128)(2,1)}, u32[]{:S(2)}) copy-start(bf16[1024,384]{1,0:T(8,128)(2,1)} %param.15) | copy-start | bytes 2359300
  0.7 18.0 %copy-start.21 = (s32[8,2]{0,1:T(2,128)S(1)}, s32[8,2]{0,1:T(2,128)}, u32[]{:S(2)}) copy-start(s32[8,2]{0,1:T(2,128)} %param.19) | copy-start | bytes 196
  0.7 18.0 %copy-start.18 = (s32[8,3]{0,1:T(4,128)S(1)}, s32[8,3]{0,1:T(4,128)}, u32[]{:S(2)}) copy-start(s32[8,3]{0,1:T(4,128)} %param.17) | copy-start | bytes 292
  5.6 13.7 %collective-permute-start.3 = (bf16[163840]{0:T(1024)(128)(2,1)}, bf16[163840]{0:T(1024)(128)(2,1)S(1)}, u32[]{:S(2)}, u32[]{:S(2)}) collective-permute-start(bf16[163840]{0:T(1024)(128)(2,1)} %constant_dynamic-update-slice_fusion.14), channel_id=1, source_target_pairs={{0,62},{1,63},{2,0},{3,1},{4,2},{5,3},{6,4},{7,5},{8,6},{9,7},{10,... | collective-permute-start | bytes 983048 | tf_op jit(solution)/shard_map/ppermute | solution.py:18
  8.4 11.2 %collective-permute-start.2 = (bf16[163840]{0:T(1024)(128)(2,1)}, bf16[163840]{0:T(1024)(128)(2,1)S(1)}, u32[]{:S(2)}, u32[]{:S(2)}) collective-permute-start(bf16[163840]{0:T(1024)(128)(2,1)} %constant_dynamic-update-slice_fusion.14), channel_id=1, source_target_pairs={{0,63},{1,0},{2,1},{3,2},{4,3},{5,4},{6,5},{7,6},{8,7},{9,8},{10,9... | collective-permute-start | bytes 983048 | tf_op jit(solution)/shard_map/ppermute | solution.py:18
  10.3 13.5 %collective-permute-start.1 = (bf16[163840]{0:T(1024)(128)(2,1)}, bf16[163840]{0:T(1024)(128)(2,1)S(1)}, u32[]{:S(2)}, u32[]{:S(2)}) collective-permute-start(bf16[163840]{0:T(1024)(128)(2,1)} %constant_dynamic-update-slice_fusion.14), channel_id=1, source_target_pairs={{0,2},{1,3},{2,4},{3,5},{4,6},{5,7},{6,8},{7,9},{8,10},{9,11},{10,... | collective-permute-start | bytes 983048 | tf_op jit(solution)/shard_map/ppermute | solution.py:18
  15.5 10.5 %collective-permute-start = (bf16[163840]{0:T(1024)(128)(2,1)}, bf16[163840]{0:T(1024)(128)(2,1)S(1)}, u32[]{:S(2)}, u32[]{:S(2)}) collective-permute-start(bf16[163840]{0:T(1024)(128)(2,1)} %constant_dynamic-update-slice_fusion.14), channel_id=1, source_target_pairs={{0,1},{1,2},{2,3},{3,4},{4,5},{5,6},{6,7},{7,8},{8,9},{9,10},{10,1... | collective-permute-start | bytes 983048 | tf_op jit(solution)/shard_map/ppermute | solution.py:18
  38.0 3.5 %copy-start.4 = (bf16[8,384,128]{1,2,0:T(8,128)(2,1)}, bf16[8,384,128]{1,2,0:T(8,128)(2,1)S(1)}, u32[]{:S(2)}) copy-start(bf16[8,384,128]{1,2,0:T(8,128)(2,1)S(1)} %bitcast_convert_fusion) | copy-start | bytes 2359300
  38.0 1.4 copy-start.9
  38.0 1.5 copy-start.22
  39.5 2.0 %copy-start.14 = (bf16[384,512]{1,0:T(8,128)(2,1)S(1)}, bf16[384,512]{1,0:T(8,128)(2,1)}, u32[]{:S(2)}) copy-start(bf16[384,512]{1,0:T(8,128)(2,1)} %param.24) | copy-start | bytes 1179652
  41.5 1.7 %copy-start.11 = (bf16[1024,384]{1,0:T(8,128)(2,1)}, bf16[1024,384]{1,0:T(8,128)(2,1)S(1)}, u32[]{:S(2)}) copy-start(bf16[1024,384]{1,0:T(8,128)(2,1)S(1)} %get-tuple-element.9) | copy-start | bytes 2359300
  41.5 2.3 %copy-start.1 = (bf16[16,128,512]{2,1,0:T(8,128)(2,1)S(1)}, bf16[16,128,512]{2,1,0:T(8,128)(2,1)}, u32[]{:S(2)}) copy-start(bf16[16,128,512]{2,1,0:T(8,128)(2,1)} %gather_fusion.2) | copy-start | bytes 6291460
  41.5 2.3 %copy-start.23 = (s32[1024]{0:T(1024)S(1)}, s32[1024]{0:T(1024)}, u32[]{:S(2)}) copy-start(s32[1024]{0:T(1024)} %param.20) | copy-start | bytes 12292
  47.5 1.6 %copy-start.24 = (f32[1024,384]{1,0:T(8,128)S(1)}, f32[1024,384]{1,0:T(8,128)}, u32[]{:S(2)}) copy-start(f32[1024,384]{1,0:T(8,128)} %get-tuple-element.10) | copy-start | bytes 4718596
  50.3 2.5 %copy-start.2 = (bf16[1024,512]{1,0:T(8,128)(2,1)S(1)}, bf16[1024,512]{1,0:T(8,128)(2,1)}, u32[]{:S(2)}) copy-start(bf16[1024,512]{1,0:T(8,128)(2,1)} %convolution_convert_fusion) | copy-start | bytes 3145732
  69.7 1.4 copy-start.7
  71.4 1.6 %copy-start.6 = (f32[2,32,11776]{2,1,0:T(8,128)}, f32[2,32,11776]{2,1,0:T(8,128)S(1)}, u32[]{:S(2)}) copy-start(f32[2,32,11776]{2,1,0:T(8,128)S(1)} %constant_dynamic-update-slice_fusion.10) | copy-start | bytes 9043972
  73.1 4.8 %collective-permute-start.4 = (bf16[32,11776]{1,0:T(8,128)(2,1)S(1)}, bf16[32,11776]{1,0:T(8,128)(2,1)S(1)}, u32[]{:S(2)}, u32[]{:S(2)}) collective-permute-start(bf16[32,11776]{1,0:T(8,128)(2,1)S(1)} %fusion.9), channel_id=1, source_target_pairs={{0,1},{1,0},{2,3},{3,2},{4,5},{5,4},{6,7},{7,6},{8,9},{9,8},{10,11... | collective-permute-start | bytes 2261000 | tf_op jit(solution)/shard_map/ppermute | solution.py:23
  79.5 15.2 %collective-permute-start.5 = (bf16[8,11776]{1,0:T(8,128)(2,1)S(1)}, bf16[8,11776]{1,0:T(8,128)(2,1)S(1)}, u32[]{:S(2)}, u32[]{:S(2)}) collective-permute-start(bf16[8,11776]{1,0:T(8,128)(2,1)S(1)} %get-tuple-element.4), channel_id=1, source_target_pairs={{0,2},{1,3},{2,4},{3,5},{4,6},{5,7},{6,0},{7,1},{8,10},{9,11},{10,... | collective-permute-start | bytes 565256 | tf_op jit(solution)/shard_map/ppermute | solution.py:89
  89.4 13.6 %collective-permute-start.7 = (bf16[8,11776]{1,0:T(8,128)(2,1)S(1)}, bf16[8,11776]{1,0:T(8,128)(2,1)S(1)}, u32[]{:S(2)}, u32[]{:S(2)}) collective-permute-start(bf16[8,11776]{1,0:T(8,128)(2,1)S(1)} %get-tuple-element.5), channel_id=1, source_target_pairs={{0,6},{1,7},{2,0},{3,1},{4,2},{5,3},{6,4},{7,5},{8,14},{9,15},{10,... | collective-permute-start | bytes 565256 | tf_op jit(solution)/shard_map/ppermute | solution.py:89
  91.3 11.7 %collective-permute-start.6 = (bf16[8,11776]{1,0:T(8,128)(2,1)S(1)}, bf16[8,11776]{1,0:T(8,128)(2,1)S(1)}, u32[]{:S(2)}, u32[]{:S(2)}) collective-permute-start(bf16[8,11776]{1,0:T(8,128)(2,1)S(1)} %get-tuple-element.6), channel_id=1, source_target_pairs={{0,4},{1,5},{2,6},{3,7},{4,0},{5,1},{6,2},{7,3},{8,12},{9,13},{10,... | collective-permute-start | bytes 565256 | tf_op jit(solution)/shard_map/ppermute | solution.py:89
  103.3 6.5 %collective-permute-start.8 = (bf16[4,11776]{1,0:T(4,128)(2,1)S(1)}, bf16[4,11776]{1,0:T(4,128)(2,1)S(1)}, u32[]{:S(2)}, u32[]{:S(2)}) collective-permute-start(bf16[4,11776]{1,0:T(4,128)(2,1)S(1)} %fusion.15), channel_id=1, source_target_pairs={{0,8},{1,57},{2,10},{3,59},{4,12},{5,61},{6,14},{7,63},{8,0},{9,17... | collective-permute-start | bytes 282632 | tf_op jit(solution)/shard_map/ppermute | solution.py:120
  110.0 6.9 %collective-permute-start.9 = (bf16[2,11776]{1,0:T(2,128)(2,1)S(1)}, bf16[2,11776]{1,0:T(2,128)(2,1)S(1)}, u32[]{:S(2)}, u32[]{:S(2)}) collective-permute-start(bf16[2,11776]{1,0:T(2,128)(2,1)S(1)} %fusion.16), channel_id=1, source_target_pairs={{0,16},{1,49},{2,18},{3,51},{4,20},{5,53},{6,22},{7,55},{8,24},{9,... | collective-permute-start | bytes 141320 | tf_op jit(solution)/shard_map/ppermute | solution.py:120
  117.0 10.2 %collective-permute-start.10 = (f32[1,11776]{1,0:T(1,128)S(1)}, f32[1,11776]{1,0:T(1,128)S(1)}, u32[]{:S(2)}, u32[]{:S(2)}) collective-permute-start(f32[1,11776]{1,0:T(1,128)S(1)} %constant_dynamic-slice_fusion), channel_id=1, source_target_pairs={{0,32},{1,33},{2,34},{3,35},{4,36},{5,37},{6,38},{7,39},{8,40},{9,... | collective-permute-start | bytes 141320 | tf_op jit(solution)/shard_map/ppermute | solution.py:122
  127.3 6.3 %collective-permute-start.11 = (f32[11776]{0:T(1024)S(1)}, f32[11776]{0:T(1024)S(1)}, u32[]{:S(2)}, u32[]{:S(2)}) collective-permute-start(f32[11776]{0:T(1024)S(1)} %add_reduce_fusion), channel_id=1, source_target_pairs={{0,64},{64,0},{128,192},{192,128},{256,320},{320,256},{384,448},{4... | collective-permute-start | bytes 141320 | tf_op jit(solution)/shard_map/ppermute | solution.py:23
  133.7 8.1 %collective-permute-start.12 = (f32[11776]{0:T(1024)S(1)}, f32[11776]{0:T(1024)S(1)}, u32[]{:S(2)}, u32[]{:S(2)}) collective-permute-start(f32[11776]{0:T(1024)S(1)} %add.188), channel_id=1, source_target_pairs={{0,128},{64,192},{128,0},{192,64},{256,384},{320,448},{384,256},{4... | collective-permute-start | bytes 141320 | tf_op jit(solution)/shard_map/ppermute | solution.py:23
  141.9 11.6 %collective-permute-start.13 = (f32[11776]{0:T(1024)S(1)}, f32[11776]{0:T(1024)S(1)}, u32[]{:S(2)}, u32[]{:S(2)}) collective-permute-start(f32[11776]{0:T(1024)S(1)} %add.189), channel_id=1, source_target_pairs={{0,256},{64,320},{128,384},{192,448},{256,0},{320,64},{384,128},{4... | collective-permute-start | bytes 141320 | tf_op jit(solution)/shard_map/ppermute | solution.py:23
  (7 other events, 7.7 us)

commit v11 on v10

--- a/solution.py
+++ b/solution.py
@@ -29,16 +29,25 @@
 
 
 def neighbour_tables(blocks, send_list, patch_blocks):
-    outgoing = blocks[send_list]
-    n_send = outgoing.shape[0]
-    gauge_size = outgoing.size
-    packed = jnp.concatenate([outgoing.reshape(-1), patch_blocks.reshape(-1)])
+    n_send = send_list.shape[0]
+    width, wide = blocks.shape[2], patch_blocks.shape[2]
+    common = max(width, wide)
+    outgoing = jnp.concatenate(
+        [lax.dynamic_index_in_dim(blocks, send_list[i], 0) for i in range(n_send)], axis=0
+    )
+    packed = jnp.concatenate(
+        [
+            jnp.pad(outgoing, ((0, 0), (0, 0), (0, common - width))),
+            jnp.pad(patch_blocks, ((0, 0), (0, 0), (0, common - wide))),
+        ],
+        axis=0,
+    )
     block_parts = [blocks]
     patch_parts = [patch_blocks]
     for step_by in offsets_by:
         got = passed_along(packed, "dom", step_by)
-        block_parts.append(got[:gauge_size].reshape(n_send, BLOCK, blocks.shape[2]))
-        patch_parts.append(got[gauge_size:].reshape(patch_blocks.shape))
+        block_parts.append(got[:n_send, :, :width])
+        patch_parts.append(got[n_send:, :, :wide])
     return jnp.concatenate(block_parts, axis=0), jnp.concatenate(patch_parts, axis=0)
 
 

time: 157 us -> 164 us (1.045)
  between operations: 1.57 us -> 5.25 us
  other arithmetic: 2.68 us -> 4.93 us
    unnamed x63 -> x51, local copies, waits for them, and re-layouts: 11.6 us -> 13.8 us
    gather x1 -> x0, local copies, waits for them, and re-layouts: 1.73 us -> none  [neighbour_tables(): outgoing = blocks[send_list]]
  transfers between devices with their start and end apart: 14 -> 14, of which waited for: 11 -> 9; matrix products, arithmetic and copies ran while one was open for 2% -> 4% of each run, Pallas kernels for 0% -> 0%
where the time goes in v11:
time: 164 us; the launch traced here: 163 us
  starting transfers between devices  58.6 us (36%)
  local copies, waits for them, and re-layouts  38.4 us (23%)
  waiting for transfers between devices  37.2 us (23%)
  matrix products  18.4 us (11%)
  between operations  5.25 us (3%)
  other arithmetic  4.93 us (3%)
    ppermute x4, starting transfers between devices, swapped(): return lax.ppermute(shard, axis, [(i, i ^ mask) for i in range(count)])  22.4 us
    ppermute x3, starting transfers between devices, shifted_x(): return lax.ppermute(shard, 'dom', pairs)  15.4 us
    unnamed x51, local copies, waits for them, and re-layouts  13.8 us
    ppermute x4, starting transfers between devices, passed_along(): lax.ppermute(shard, axis, [(i, (i + by) % count) for i in range(count)])  12 us
    ppermute x2, waiting for transfers between devices, reduce_to_share(): got = lax.ppermute(other.astype(bf16), 'dom', pairs).astype(f32)  9.46 us
    ppermute x3, waiting for transfers between devices, shifted_x(): return lax.ppermute(shard, 'dom', pairs)  8.28 us
    ppermute x4, waiting for transfers between devices, swapped(): return lax.ppermute(shard, axis, [(i, i ^ mask) for i in range(count)])  8.2 us
    gather x4, local copies, waits for them, and re-layouts, reduce_to_share(): t[share_order(t.shape[0], n_dom, n_x)].reshape(2, n_y * n_x, -1)  6.89 us
  transfers between devices with their start and end apart: 14, of which 9 were waited for; matrix products, arithmetic and copies ran while one was open for 4% of the time, Pallas kernels for 0%

profile of v11, /device:TPU:6, one launch (start us, length us, event | category | flops | bytes accessed | tf_op | source)
XLA Modules:
  0.0 162.8 jit_solution(16642878746059165756)
XLA Ops:
  7.9 2.7 %collective-permute-start.3 = (bf16[3,128,512]{2,1,0:T(8,128)(2,1)S(1)}, bf16[3,128,512]{2,1,0:T(8,128)(2,1)S(1)}, u32[]{:S(2)}, u32[]{:S(2)}) collective-permute-start(bf16[3,128,512]{2,1,0:T(8,128)(2,1)S(1)} %pad_maximum_fusion), channel_id=1, source_target_pairs={{0,62},{1,63},{2,0},{3,1},{4,2},{5,3},{6,4},{7,5},{8,6},{9,7},{10,... | collective-permute-start | bytes 1179656 | tf_op jit(solution)/shard_map/ppermute | solution.py:18
  10.6 1.9 %collective-permute-start.2 = (bf16[3,128,512]{2,1,0:T(8,128)(2,1)S(1)}, bf16[3,128,512]{2,1,0:T(8,128)(2,1)S(1)}, u32[]{:S(2)}, u32[]{:S(2)}) collective-permute-start(bf16[3,128,512]{2,1,0:T(8,128)(2,1)S(1)} %pad_maximum_fusion), channel_id=1, source_target_pairs={{0,63},{1,0},{2,1},{3,2},{4,3},{5,4},{6,5},{7,6},{8,7},{9,8},{10,9... | collective-permute-start | bytes 1179656 | tf_op jit(solution)/shard_map/ppermute | solution.py:18
  12.5 5.2 %collective-permute-start.1 = (bf16[3,128,512]{2,1,0:T(8,128)(2,1)S(1)}, bf16[3,128,512]{2,1,0:T(8,128)(2,1)}, u32[]{:S(2)}, u32[]{:S(2)}) collective-permute-start(bf16[3,128,512]{2,1,0:T(8,128)(2,1)S(1)} %pad_maximum_fusion), channel_id=1, source_target_pairs={{0,2},{1,3},{2,4},{3,5},{4,6},{5,7},{6,8},{7,9},{8,10},{9,11},{10,... | collective-permute-start | bytes 1179656 | tf_op jit(solution)/shard_map/ppermute | solution.py:18
  17.8 2.1 %collective-permute-start = (bf16[3,128,512]{2,1,0:T(8,128)(2,1)S(1)}, bf16[3,128,512]{2,1,0:T(8,128)(2,1)}, u32[]{:S(2)}, u32[]{:S(2)}) collective-permute-start(bf16[3,128,512]{2,1,0:T(8,128)(2,1)S(1)} %pad_maximum_fusion), channel_id=1, source_target_pairs={{0,1},{1,2},{2,3},{3,4},{4,5},{5,6},{6,7},{7,8},{8,9},{9,10},{10,1... | collective-permute-start | bytes 1179656 | tf_op jit(solution)/shard_map/ppermute | solution.py:18
  24.2 6.0 %collective-permute-done = bf16[3,128,512]{2,1,0:T(8,128)(2,1)} collective-permute-done((bf16[3,128,512]{2,1,0:T(8,128)(2,1)S(1)}, bf16[3,128,512]{2,1,0:T(8,128)(2,1)}, u32[]{:S(2)}, u32[]{:S(2)}) %collective-permute-start) | collective-permute-done | bytes 393248 | tf_op jit(solution)/shard_map/ppermute | solution.py:18
  32.2 2.0 %gather_fusion.5 = bf16[16,128,512]{2,1,0:T(8,128)(2,1)} fusion(bf16[5,128,512]{2,1,0:T(8,128)(2,1)S(1)} %slice_dynamic-update-slice_fusion.4, s32[1024]{0:T(1024)S(1)} %get-tuple-element.17), kind=kCustom, calls=%fused_computation.5 | custom fusion | bytes 4194368 | tf_op jit(solution)/shard_map/gather | solution.py:187
  34.7 2.0 %gather_fusion.1 = bf16[16,128,512]{2,1,0:T(8,128)(2,1)} fusion(bf16[5,128,512]{2,1,0:T(8,128)(2,1)S(1)} %bitcast.80, s32[1024]{0:T(1024)S(1)} %get-tuple-element.17), kind=kCustom, calls=%fused_computation.1 | custom fusion | bytes 4194368 | tf_op jit(solution)/shard_map/gather | solution.py:186
  41.4 2.5 %gather_fusion = bf16[24,128,384]{2,1,0:T(8,128)(2,1)S(1)} fusion(bf16[16,128,384]{2,1,0:T(8,128)(2,1)} %slice_dynamic-update-slice_fusion, s32[1024]{0:T(1024)S(1)} %get-tuple-element.18), kind=kCustom, calls=%fused_computation | custom fusion | bytes 4718688 | tf_op jit(solution)/shard_map/gather | solution.py:170
  46.2 2.0 %add_convert_fusion = (bf16[1024,384]{1,0:T(8,128)(2,1)S(1)}, f32[1024,384]{1,0:T(8,128)}) fusion(bf16[1024,384]{1,0:T(8,128)(2,1)S(1)} %copy-done.9, f32[1024,384]{1,0:T(8,128)S(1)} %fusion.23, bf16[384,384]{1,0:T(8,128)(2,1)S(1)} %copy-done.17), kind=kOutput, calls=%fused_computation.13 | convolution fusion | flops 305135616 | bytes 5013504 | tf_op jit(solution)/shard_map/dot_general | solution.py:176
  50.5 3.3 %fusion.8 = bf16[8,128,256]{2,1,0:T(8,128)(2,1)S(1)} fusion(s32[8,128]{1,0:T(8,128)S(1)} %bitcast.92, bf16[8,128,512]{2,1,0:T(8,128)(2,1)} %bitcast.81, bf16[8,256,512]{2,1,0:T(8,128)(2,1)S(1)} %bitcast.77), kind=kOutput, calls=%fused_computation.27 | convolution fusion | flops 270535168 | bytes 3674112 | tf_op jit(solution)/shard_map/div | solution.py:193
  59.6 2.1 %multiply_convert_fusion = bf16[8,256,512]{2,1,0:T(8,128)(2,1)} fusion(bf16[8,128,256]{2,1,0:T(8,128)(2,1)S(1)} %fusion.8, bf16[8,128,512]{2,1,0:T(8,128)(2,1)S(1)} %bitcast.82), kind=kOutput, calls=%fused_computation.9 | convolution fusion | flops 270532608 | bytes 3670016 | tf_op jit(solution)/shard_map/bij,bie->bje/dot_general | solution.py:206
  62.9 1.9 %gather_fusion.3 = f32[384,384]{1,0:T(8,128)S(1)} fusion(f32[384,384]{1,0:T(8,128)S(1)} %copy.25, s32[1024]{0:T(1024)S(1)} %get-tuple-element.16), kind=kCustom, calls=%fused_computation.3 | custom fusion | bytes 1181184 | tf_op jit(solution)/shard_map/gather | solution.py:106
  65.8 1.7 %gather_fusion.2 = f32[384,384]{1,0:T(8,128)S(1)} fusion(f32[384,384]{1,0:T(8,128)S(1)} %fusion.24, s32[1024]{0:T(1024)S(1)} %get-tuple-element.16), kind=kCustom, calls=%fused_computation.2 | custom fusion | bytes 1181184 | tf_op jit(solution)/shard_map/gather | solution.py:106
  71.4 3.5 %fusion.26 = f32[512,512]{1,0:T(8,128)S(1)} fusion(bf16[2048,512]{1,0:T(8,128)(2,1)} %bitcast.85, bf16[2048,512]{1,0:T(8,128)(2,1)} %bitcast.86), kind=kOutput, calls=%fused_computation.82 | convolution fusion | flops 1073741824 | bytes 5242880 | tf_op jit(solution)/shard_map/dot_general | solution.py:212
  79.9 2.7 %collective-permute-start.4 = (bf16[32,11776]{1,0:T(8,128)(2,1)S(1)}, bf16[32,11776]{1,0:T(8,128)(2,1)S(1)}, u32[]{:S(2)}, u32[]{:S(2)}) collective-permute-start(bf16[32,11776]{1,0:T(8,128)(2,1)S(1)} %fusion.9), channel_id=1, source_target_pairs={{0,1},{1,0},{2,3},{3,2},{4,5},{5,4},{6,7},{7,6},{8,9},{9,8},{10,11... | collective-permute-start | bytes 2261000 | tf_op jit(solution)/shard_map/ppermute | solution.py:23
  82.8 1.7 %collective-permute-done.4 = bf16[32,11776]{1,0:T(8,128)(2,1)S(1)} collective-permute-done((bf16[32,11776]{1,0:T(8,128)(2,1)S(1)}, bf16[32,11776]{1,0:T(8,128)(2,1)S(1)}, u32[]{:S(2)}, u32[]{:S(2)}) %collective-permute-start.4) | collective-permute-done | bytes 753696 | tf_op jit(solution)/shard_map/ppermute | solution.py:23
  86.1 10.1 %collective-permute-start.5 = (bf16[8,11776]{1,0:T(8,128)(2,1)S(1)}, bf16[8,11776]{1,0:T(8,128)(2,1)S(1)}, u32[]{:S(2)}, u32[]{:S(2)}) collective-permute-start(bf16[8,11776]{1,0:T(8,128)(2,1)S(1)} %get-tuple-element.4), channel_id=1, source_target_pairs={{0,2},{1,3},{2,4},{3,5},{4,6},{5,7},{6,0},{7,1},{8,10},{9,11},{10,... | collective-permute-start | bytes 565256 | tf_op jit(solution)/shard_map/ppermute | solution.py:98
  96.2 1.9 %collective-permute-start.7 = (bf16[8,11776]{1,0:T(8,128)(2,1)S(1)}, bf16[8,11776]{1,0:T(8,128)(2,1)S(1)}, u32[]{:S(2)}, u32[]{:S(2)}) collective-permute-start(bf16[8,11776]{1,0:T(8,128)(2,1)S(1)} %get-tuple-element.5), channel_id=1, source_target_pairs={{0,6},{1,7},{2,0},{3,1},{4,2},{5,3},{6,4},{7,5},{8,14},{9,15},{10,... | collective-permute-start | bytes 565256 | tf_op jit(solution)/shard_map/ppermute | solution.py:98
  98.1 3.4 %collective-permute-start.6 = (bf16[8,11776]{1,0:T(8,128)(2,1)S(1)}, bf16[8,11776]{1,0:T(8,128)(2,1)S(1)}, u32[]{:S(2)}, u32[]{:S(2)}) collective-permute-start(bf16[8,11776]{1,0:T(8,128)(2,1)S(1)} %get-tuple-element.6), channel_id=1, source_target_pairs={{0,4},{1,5},{2,6},{3,7},{4,0},{5,1},{6,2},{7,3},{8,12},{9,13},{10,... | collective-permute-start | bytes 565256 | tf_op jit(solution)/shard_map/ppermute | solution.py:98
  101.5 8.3 %collective-permute-done.7 = bf16[8,11776]{1,0:T(8,128)(2,1)S(1)} collective-permute-done((bf16[8,11776]{1,0:T(8,128)(2,1)S(1)}, bf16[8,11776]{1,0:T(8,128)(2,1)S(1)}, u32[]{:S(2)}, u32[]{:S(2)}) %collective-permute-start.7) | collective-permute-done | bytes 188448 | tf_op jit(solution)/shard_map/ppermute | solution.py:98
  110.1 1.9 %collective-permute-start.8 = (bf16[4,11776]{1,0:T(4,128)(2,1)S(1)}, bf16[4,11776]{1,0:T(4,128)(2,1)S(1)}, u32[]{:S(2)}, u32[]{:S(2)}) collective-permute-start(bf16[4,11776]{1,0:T(4,128)(2,1)S(1)} %fusion.18), channel_id=1, source_target_pairs={{0,8},{1,57},{2,10},{3,59},{4,12},{5,61},{6,14},{7,63},{8,0},{9,17... | collective-permute-start | bytes 282632 | tf_op jit(solution)/shard_map/ppermute | solution.py:129
  112.0 4.5 %collective-permute-done.8 = bf16[4,11776]{1,0:T(4,128)(2,1)S(1)} collective-permute-done((bf16[4,11776]{1,0:T(4,128)(2,1)S(1)}, bf16[4,11776]{1,0:T(4,128)(2,1)S(1)}, u32[]{:S(2)}, u32[]{:S(2)}) %collective-permute-start.8) | collective-permute-done | bytes 94240 | tf_op jit(solution)/shard_map/ppermute | solution.py:129
  116.8 1.9 %collective-permute-start.9 = (bf16[2,11776]{1,0:T(2,128)(2,1)S(1)}, bf16[2,11776]{1,0:T(2,128)(2,1)S(1)}, u32[]{:S(2)}, u32[]{:S(2)}) collective-permute-start(bf16[2,11776]{1,0:T(2,128)(2,1)S(1)} %fusion.19), channel_id=1, source_target_pairs={{0,16},{1,49},{2,18},{3,51},{4,20},{5,53},{6,22},{7,55},{8,24},{9,... | collective-permute-start | bytes 141320 | tf_op jit(solution)/shard_map/ppermute | solution.py:129
  118.7 4.9 %collective-permute-done.9 = bf16[2,11776]{1,0:T(2,128)(2,1)S(1)} collective-permute-done((bf16[2,11776]{1,0:T(2,128)(2,1)S(1)}, bf16[2,11776]{1,0:T(2,128)(2,1)S(1)}, u32[]{:S(2)}, u32[]{:S(2)}) %collective-permute-start.9) | collective-permute-done | bytes 47136 | tf_op jit(solution)/shard_map/ppermute | solution.py:129
  123.8 5.0 %collective-permute-start.10 = (f32[1,11776]{1,0:T(1,128)S(1)}, f32[1,11776]{1,0:T(1,128)S(1)}, u32[]{:S(2)}, u32[]{:S(2)}) collective-permute-start(f32[1,11776]{1,0:T(1,128)S(1)} %constant_dynamic-slice_fusion), channel_id=1, source_target_pairs={{0,32},{1,33},{2,34},{3,35},{4,36},{5,37},{6,38},{7,39},{8,40},{9,... | collective-permute-start | bytes 141320 | tf_op jit(solution)/shard_map/ppermute | solution.py:131
  128.8 5.2 %collective-permute-done.10 = f32[1,11776]{1,0:T(1,128)S(1)} collective-permute-done((f32[1,11776]{1,0:T(1,128)S(1)}, f32[1,11776]{1,0:T(1,128)S(1)}, u32[]{:S(2)}, u32[]{:S(2)}) %collective-permute-start.10) | collective-permute-done | bytes 47136 | tf_op jit(solution)/shard_map/ppermute | solution.py:131
  134.2 4.3 %collective-permute-start.11 = (f32[11776]{0:T(1024)S(1)}, f32[11776]{0:T(1024)S(1)}, u32[]{:S(2)}, u32[]{:S(2)}) collective-permute-start(f32[11776]{0:T(1024)S(1)} %add_reduce_fusion), channel_id=1, source_target_pairs={{0,64},{64,0},{128,192},{192,128},{256,320},{320,256},{384,448},{4... | collective-permute-start | bytes 141320 | tf_op jit(solution)/shard_map/ppermute | solution.py:23
  138.4 2.1 %collective-permute-done.11 = f32[11776]{0:T(1024)S(1)} collective-permute-done((f32[11776]{0:T(1024)S(1)}, f32[11776]{0:T(1024)S(1)}, u32[]{:S(2)}, u32[]{:S(2)}) %collective-permute-start.11) | collective-permute-done | bytes 47136 | tf_op jit(solution)/shard_map/ppermute | solution.py:23
  140.5 6.1 %collective-permute-start.12 = (f32[11776]{0:T(1024)S(1)}, f32[11776]{0:T(1024)S(1)}, u32[]{:S(2)}, u32[]{:S(2)}) collective-permute-start(f32[11776]{0:T(1024)S(1)} %add.195), channel_id=1, source_target_pairs={{0,128},{64,192},{128,0},{192,64},{256,384},{320,448},{384,256},{4... | collective-permute-start | bytes 141320 | tf_op jit(solution)/shard_map/ppermute | solution.py:23
  146.6 2.1 %collective-permute-done.12 = f32[11776]{0:T(1024)S(1)} collective-permute-done((f32[11776]{0:T(1024)S(1)}, f32[11776]{0:T(1024)S(1)}, u32[]{:S(2)}, u32[]{:S(2)}) %collective-permute-start.12) | collective-permute-done | bytes 47136 | tf_op jit(solution)/shard_map/ppermute | solution.py:23
  148.7 9.3 %collective-permute-start.13 = (f32[11776]{0:T(1024)S(1)}, f32[11776]{0:T(1024)S(1)}, u32[]{:S(2)}, u32[]{:S(2)}) collective-permute-start(f32[11776]{0:T(1024)S(1)} %add.196), channel_id=1, source_target_pairs={{0,256},{64,320},{128,384},{192,448},{256,0},{320,64},{384,128},{4... | collective-permute-start | bytes 141320 | tf_op jit(solution)/shard_map/ppermute | solution.py:23
  157.9 2.4 %collective-permute-done.13 = f32[11776]{0:T(1024)S(1)} collective-permute-done((f32[11776]{0:T(1024)S(1)}, f32[11776]{0:T(1024)S(1)}, u32[]{:S(2)}, u32[]{:S(2)}) %collective-permute-start.13) | collective-permute-done | bytes 47136 | tf_op jit(solution)/shard_map/ppermute | solution.py:23
  (109 shorter events, 40.6 us)
Async XLA Ops:
  0.6 43.3 %copy-start = (bf16[8,3,128,128]{3,2,1,0:T(8,128)(2,1)S(1)}, bf16[8,3,128,128]{3,2,1,0:T(8,128)(2,1)}, u32[]{:S(2)}) copy-start(bf16[8,3,128,128]{3,2,1,0:T(8,128)(2,1)} %param.16) | copy-start | bytes 2359300
  0.6 22.6 %copy-start.8 = (bf16[1024,384]{1,0:T(8,128)(2,1)S(1)}, bf16[1024,384]{1,0:T(8,128)(2,1)}, u32[]{:S(2)}) copy-start(bf16[1024,384]{1,0:T(8,128)(2,1)} %param.15) | copy-start | bytes 2359300
  7.9 24.3 %collective-permute-start.3 = (bf16[3,128,512]{2,1,0:T(8,128)(2,1)S(1)}, bf16[3,128,512]{2,1,0:T(8,128)(2,1)S(1)}, u32[]{:S(2)}, u32[]{:S(2)}) collective-permute-start(bf16[3,128,512]{2,1,0:T(8,128)(2,1)S(1)} %pad_maximum_fusion), channel_id=1, source_target_pairs={{0,62},{1,63},{2,0},{3,1},{4,2},{5,3},{6,4},{7,5},{8,6},{9,7},{10,... | collective-permute-start | bytes 1179656 | tf_op jit(solution)/shard_map/ppermute | solution.py:18
  10.6 21.5 %collective-permute-start.2 = (bf16[3,128,512]{2,1,0:T(8,128)(2,1)S(1)}, bf16[3,128,512]{2,1,0:T(8,128)(2,1)S(1)}, u32[]{:S(2)}, u32[]{:S(2)}) collective-permute-start(bf16[3,128,512]{2,1,0:T(8,128)(2,1)S(1)} %pad_maximum_fusion), channel_id=1, source_target_pairs={{0,63},{1,0},{2,1},{3,2},{4,3},{5,4},{6,5},{7,6},{8,7},{9,8},{10,9... | collective-permute-start | bytes 1179656 | tf_op jit(solution)/shard_map/ppermute | solution.py:18
  12.5 18.7 %collective-permute-start.1 = (bf16[3,128,512]{2,1,0:T(8,128)(2,1)S(1)}, bf16[3,128,512]{2,1,0:T(8,128)(2,1)}, u32[]{:S(2)}, u32[]{:S(2)}) collective-permute-start(bf16[3,128,512]{2,1,0:T(8,128)(2,1)S(1)} %pad_maximum_fusion), channel_id=1, source_target_pairs={{0,2},{1,3},{2,4},{3,5},{4,6},{5,7},{6,8},{7,9},{8,10},{9,11},{10,... | collective-permute-start | bytes 1179656 | tf_op jit(solution)/shard_map/ppermute | solution.py:18
  17.8 12.5 %collective-permute-start = (bf16[3,128,512]{2,1,0:T(8,128)(2,1)S(1)}, bf16[3,128,512]{2,1,0:T(8,128)(2,1)}, u32[]{:S(2)}, u32[]{:S(2)}) collective-permute-start(bf16[3,128,512]{2,1,0:T(8,128)(2,1)S(1)} %pad_maximum_fusion), channel_id=1, source_target_pairs={{0,1},{1,2},{2,3},{3,4},{4,5},{5,6},{6,7},{7,8},{8,9},{9,10},{10,1... | collective-permute-start | bytes 1179656 | tf_op jit(solution)/shard_map/ppermute | solution.py:18
  32.2 2.1 %copy-start.16 = (bf16[512,512]{1,0:T(8,128)(2,1)S(1)}, bf16[512,512]{1,0:T(8,128)(2,1)}, u32[]{:S(2)}) copy-start(bf16[512,512]{1,0:T(8,128)(2,1)} %param.25) | copy-start | bytes 1572868
  44.7 3.5 %copy-start.4 = (bf16[8,384,128]{1,2,0:T(8,128)(2,1)}, bf16[8,384,128]{1,2,0:T(8,128)(2,1)S(1)}, u32[]{:S(2)}) copy-start(bf16[8,384,128]{1,2,0:T(8,128)(2,1)S(1)} %bitcast_convert_fusion) | copy-start | bytes 2359300
  44.7 1.4 copy-start.9
  44.7 1.5 copy-start.17
  46.2 2.0 %copy-start.13 = (bf16[384,512]{1,0:T(8,128)(2,1)S(1)}, bf16[384,512]{1,0:T(8,128)(2,1)}, u32[]{:S(2)}) copy-start(bf16[384,512]{1,0:T(8,128)(2,1)} %param.24) | copy-start | bytes 1179652
  48.2 1.7 %copy-start.11 = (bf16[1024,384]{1,0:T(8,128)(2,1)}, bf16[1024,384]{1,0:T(8,128)(2,1)S(1)}, u32[]{:S(2)}) copy-start(bf16[1024,384]{1,0:T(8,128)(2,1)S(1)} %get-tuple-element.13) | copy-start | bytes 2359300
  48.2 2.3 %copy-start.1 = (bf16[16,128,512]{2,1,0:T(8,128)(2,1)S(1)}, bf16[16,128,512]{2,1,0:T(8,128)(2,1)}, u32[]{:S(2)}) copy-start(bf16[16,128,512]{2,1,0:T(8,128)(2,1)} %gather_fusion.1) | copy-start | bytes 6291460
  48.2 2.3 %copy-start.18 = (s32[1024]{0:T(1024)S(1)}, s32[1024]{0:T(1024)}, u32[]{:S(2)}) copy-start(s32[1024]{0:T(1024)} %param.20) | copy-start | bytes 12292
  53.8 1.1 copy-start.12
  54.3 1.3 copy-start.14
  54.3 1.6 copy-start.19
  55.9 1.1 copy-start.5
  57.0 2.6 %copy-start.2 = (bf16[1024,512]{1,0:T(8,128)(2,1)S(1)}, bf16[1024,512]{1,0:T(8,128)(2,1)}, u32[]{:S(2)}) copy-start(bf16[1024,512]{1,0:T(8,128)(2,1)} %convolution_convert_fusion) | copy-start | bytes 3145732
  76.5 1.4 copy-start.7
  76.7 1.4 copy-start.3
  78.2 1.6 copy-start.6
  79.9 4.6 %collective-permute-start.4 = (bf16[32,11776]{1,0:T(8,128)(2,1)S(1)}, bf16[32,11776]{1,0:T(8,128)(2,1)S(1)}, u32[]{:S(2)}, u32[]{:S(2)}) collective-permute-start(bf16[32,11776]{1,0:T(8,128)(2,1)S(1)} %fusion.9), channel_id=1, source_target_pairs={{0,1},{1,0},{2,3},{3,2},{4,5},{5,4},{6,7},{7,6},{8,9},{9,8},{10,11... | collective-permute-start | bytes 2261000 | tf_op jit(solution)/shard_map/ppermute | solution.py:23
  86.1 15.4 %collective-permute-start.5 = (bf16[8,11776]{1,0:T(8,128)(2,1)S(1)}, bf16[8,11776]{1,0:T(8,128)(2,1)S(1)}, u32[]{:S(2)}, u32[]{:S(2)}) collective-permute-start(bf16[8,11776]{1,0:T(8,128)(2,1)S(1)} %get-tuple-element.4), channel_id=1, source_target_pairs={{0,2},{1,3},{2,4},{3,5},{4,6},{5,7},{6,0},{7,1},{8,10},{9,11},{10,... | collective-permute-start | bytes 565256 | tf_op jit(solution)/shard_map/ppermute | solution.py:98
  96.2 13.6 %collective-permute-start.7 = (bf16[8,11776]{1,0:T(8,128)(2,1)S(1)}, bf16[8,11776]{1,0:T(8,128)(2,1)S(1)}, u32[]{:S(2)}, u32[]{:S(2)}) collective-permute-start(bf16[8,11776]{1,0:T(8,128)(2,1)S(1)} %get-tuple-element.5), channel_id=1, source_target_pairs={{0,6},{1,7},{2,0},{3,1},{4,2},{5,3},{6,4},{7,5},{8,14},{9,15},{10,... | collective-permute-start | bytes 565256 | tf_op jit(solution)/shard_map/ppermute | solution.py:98
  98.1 11.7 %collective-permute-start.6 = (bf16[8,11776]{1,0:T(8,128)(2,1)S(1)}, bf16[8,11776]{1,0:T(8,128)(2,1)S(1)}, u32[]{:S(2)}, u32[]{:S(2)}) collective-permute-start(bf16[8,11776]{1,0:T(8,128)(2,1)S(1)} %get-tuple-element.6), channel_id=1, source_target_pairs={{0,4},{1,5},{2,6},{3,7},{4,0},{5,1},{6,2},{7,3},{8,12},{9,13},{10,... | collective-permute-start | bytes 565256 | tf_op jit(solution)/shard_map/ppermute | solution.py:98
  110.1 6.5 %collective-permute-start.8 = (bf16[4,11776]{1,0:T(4,128)(2,1)S(1)}, bf16[4,11776]{1,0:T(4,128)(2,1)S(1)}, u32[]{:S(2)}, u32[]{:S(2)}) collective-permute-start(bf16[4,11776]{1,0:T(4,128)(2,1)S(1)} %fusion.18), channel_id=1, source_target_pairs={{0,8},{1,57},{2,10},{3,59},{4,12},{5,61},{6,14},{7,63},{8,0},{9,17... | collective-permute-start | bytes 282632 | tf_op jit(solution)/shard_map/ppermute | solution.py:129
  116.8 6.9 %collective-permute-start.9 = (bf16[2,11776]{1,0:T(2,128)(2,1)S(1)}, bf16[2,11776]{1,0:T(2,128)(2,1)S(1)}, u32[]{:S(2)}, u32[]{:S(2)}) collective-permute-start(bf16[2,11776]{1,0:T(2,128)(2,1)S(1)} %fusion.19), channel_id=1, source_target_pairs={{0,16},{1,49},{2,18},{3,51},{4,20},{5,53},{6,22},{7,55},{8,24},{9,... | collective-permute-start | bytes 141320 | tf_op jit(solution)/shard_map/ppermute | solution.py:129
  123.8 10.2 %collective-permute-start.10 = (f32[1,11776]{1,0:T(1,128)S(1)}, f32[1,11776]{1,0:T(1,128)S(1)}, u32[]{:S(2)}, u32[]{:S(2)}) collective-permute-start(f32[1,11776]{1,0:T(1,128)S(1)} %constant_dynamic-slice_fusion), channel_id=1, source_target_pairs={{0,32},{1,33},{2,34},{3,35},{4,36},{5,37},{6,38},{7,39},{8,40},{9,... | collective-permute-start | bytes 141320 | tf_op jit(solution)/shard_map/ppermute | solution.py:131
  134.2 6.3 %collective-permute-start.11 = (f32[11776]{0:T(1024)S(1)}, f32[11776]{0:T(1024)S(1)}, u32[]{:S(2)}, u32[]{:S(2)}) collective-permute-start(f32[11776]{0:T(1024)S(1)} %add_reduce_fusion), channel_id=1, source_target_pairs={{0,64},{64,0},{128,192},{192,128},{256,320},{320,256},{384,448},{4... | collective-permute-start | bytes 141320 | tf_op jit(solution)/shard_map/ppermute | solution.py:23
  140.5 8.2 %collective-permute-start.12 = (f32[11776]{0:T(1024)S(1)}, f32[11776]{0:T(1024)S(1)}, u32[]{:S(2)}, u32[]{:S(2)}) collective-permute-start(f32[11776]{0:T(1024)S(1)} %add.195), channel_id=1, source_target_pairs={{0,128},{64,192},{128,0},{192,64},{256,384},{320,448},{384,256},{4... | collective-permute-start | bytes 141320 | tf_op jit(solution)/shard_map/ppermute | solution.py:23
  148.7 11.6 %collective-permute-start.13 = (f32[11776]{0:T(1024)S(1)}, f32[11776]{0:T(1024)S(1)}, u32[]{:S(2)}, u32[]{:S(2)}) collective-permute-start(f32[11776]{0:T(1024)S(1)} %add.196), channel_id=1, source_target_pairs={{0,256},{64,320},{128,384},{192,448},{256,0},{320,64},{384,128},{4... | collective-permute-start | bytes 141320 | tf_op jit(solution)/shard_map/ppermute | solution.py:23
  (2 other events, 2.1 us)

commit v12 on v10

--- a/solution.py
+++ b/solution.py
@@ -93,9 +93,8 @@
     bf16 = jnp.bfloat16
     f32 = jnp.float32
     n_y = n_dom // (2 * n_x)
-    flat = jnp.concatenate(
-        [t[share_order(t.shape[0], n_dom, n_x)].reshape(2, n_y * n_x, -1) for t in terms], axis=2
-    )
+    by_dest = jnp.concatenate([t.reshape(n_dom, -1) for t in terms], axis=1)
+    flat = by_dest[share_order(n_dom, n_dom, n_x)].reshape(2, n_y * n_x, -1)
     width = flat.shape[2]
     me = lax.axis_index("dom")
     core = me % 2

time: 157 us -> 165 us (1.051)
  starting transfers between devices: 58.6 us -> 47 us
  waiting for transfers between devices: 35.7 us -> 44.3 us
  other arithmetic: 2.68 us -> 6.23 us
  local copies, waits for them, and re-layouts: 37.9 us -> 41.4 us
  matrix products: 19.5 us -> 22.4 us
    unnamed x63 -> x56, local copies, waits for them, and re-layouts: 11.6 us -> 5.39 us
    ppermute x4, starting transfers between devices: 22.6 us -> 16.5 us  [swapped(): return lax.ppermute(shard, axis, [(i, i ^ mask) for i in range(count)])]
    ppermute x4, waiting for transfers between devices: 4.61 us -> 9.38 us  [passed_along(): lax.ppermute(shard, axis, [(i, (i + by) % count) for i in range(count)])]
    ppermute x3, starting transfers between devices: 15.2 us -> 10.5 us  [shifted_x(): return lax.ppermute(shard, 'dom', pairs)]
    slice x4, local copies, waits for them, and re-layouts: 0.95 us -> 4.97 us  [neighbour_tables(): patch_parts.append(got[gauge_size:].reshape(patch_blocks.shape))]
    slice x4, local copies, waits for them, and re-layouts: 0.05 us -> 3.76 us  [neighbour_tables(): block_parts.append(got[:gauge_size].reshape(n_send, BLOCK, blocks.shape[2]))]
    ppermute x4, waiting for transfers between devices: 8.16 us -> 11.1 us  [swapped(): return lax.ppermute(shard, axis, [(i, i ^ mask) for i in range(count)])]
    concatenate x0 -> x1, other arithmetic: none -> 2.87 us  [reduce_to_share(): by_dest = jnp.concatenate([t.reshape(n_dom, -1) for t in terms], axis=1)]
  transfers between devices with their start and end apart: 14 -> 14, of which waited for: 11 -> 12; matrix products, arithmetic and copies ran while one was open for 2% -> 2% of each run, Pallas kernels for 0% -> 0%
where the time goes in v12:
time: 165 us; the launch traced here: 163 us
  starting transfers between devices  47 us (28%)
  waiting for transfers between devices  44.3 us (27%)
  local copies, waits for them, and re-layouts  41.4 us (25%)
  matrix products  22.4 us (14%)
  other arithmetic  6.23 us (4%)
    ppermute x4, starting transfers between devices, swapped(): return lax.ppermute(shard, axis, [(i, i ^ mask) for i in range(count)])  16.5 us
    ppermute x4, starting transfers between devices, passed_along(): lax.ppermute(shard, axis, [(i, (i + by) % count) for i in range(count)])  11.1 us
    ppermute x4, waiting for transfers between devices, swapped(): return lax.ppermute(shard, axis, [(i, i ^ mask) for i in range(count)])  11.1 us
    ppermute x3, starting transfers between devices, shifted_x(): return lax.ppermute(shard, 'dom', pairs)  10.5 us
    ppermute x4, waiting for transfers between devices, passed_along(): lax.ppermute(shard, axis, [(i, (i + by) % count) for i in range(count)])  9.38 us
    ppermute x3, waiting for transfers between devices, shifted_x(): return lax.ppermute(shard, 'dom', pairs)  9.18 us
    ppermute x2, waiting for transfers between devices, reduce_to_share(): got = lax.ppermute(other.astype(bf16), 'dom', pairs).astype(f32)  8.64 us
    gather x1, local copies, waits for them, and re-layouts, reduce_to_share(): flat = by_dest[share_order(n_dom, n_dom, n_x)].reshape(2, n_y * n_x, -1)  6.34 us
  transfers between devices with their start and end apart: 14, of which 12 were waited for; matrix products, arithmetic and copies ran while one was open for 2% of the time, Pallas kernels for 0%

profile of v12, /device:TPU:6, one launch (start us, length us, event | category | flops | bytes accessed | tf_op | source)
XLA Modules:
  0.0 162.8 jit_solution(7497117431782001583)
XLA Ops:
  8.4 3.4 %collective-permute-start.1 = (bf16[163840]{0:T(1024)(128)(2,1)}, bf16[163840]{0:T(1024)(128)(2,1)}, u32[]{:S(2)}, u32[]{:S(2)}) collective-permute-start(bf16[163840]{0:T(1024)(128)(2,1)} %constant_dynamic-update-slice_fusion.10), channel_id=1, source_target_pairs={{0,2},{1,3},{2,4},{3,5},{4,6},{5,7},{6,8},{7,9},{8,10},{9,11},{10,... | collective-permute-start | bytes 983048 | tf_op jit(solution)/shard_map/ppermute | solution.py:18
  11.8 3.4 %collective-permute-start.2 = (bf16[163840]{0:T(1024)(128)(2,1)}, bf16[163840]{0:T(1024)(128)(2,1)}, u32[]{:S(2)}, u32[]{:S(2)}) collective-permute-start(bf16[163840]{0:T(1024)(128)(2,1)} %constant_dynamic-update-slice_fusion.10), channel_id=1, source_target_pairs={{0,63},{1,0},{2,1},{3,2},{4,3},{5,4},{6,5},{7,6},{8,7},{9,8},{10,9... | collective-permute-start | bytes 983048 | tf_op jit(solution)/shard_map/ppermute | solution.py:18
  15.2 2.4 %collective-permute-start.3 = (bf16[163840]{0:T(1024)(128)(2,1)}, bf16[163840]{0:T(1024)(128)(2,1)}, u32[]{:S(2)}, u32[]{:S(2)}) collective-permute-start(bf16[163840]{0:T(1024)(128)(2,1)} %constant_dynamic-update-slice_fusion.10), channel_id=1, source_target_pairs={{0,62},{1,63},{2,0},{3,1},{4,2},{5,3},{6,4},{7,5},{8,6},{9,7},{10,... | collective-permute-start | bytes 983048 | tf_op jit(solution)/shard_map/ppermute | solution.py:18
  23.4 7.8 %collective-permute-done.3 = bf16[163840]{0:T(1024)(128)(2,1)} collective-permute-done((bf16[163840]{0:T(1024)(128)(2,1)}, bf16[163840]{0:T(1024)(128)(2,1)}, u32[]{:S(2)}, u32[]{:S(2)}) %collective-permute-start.3) | collective-permute-done | bytes 327712 | tf_op jit(solution)/shard_map/ppermute | solution.py:18
  41.3 2.5 %gather_fusion.1 = bf16[24,128,384]{2,1,0:T(8,128)(2,1)S(1)} fusion(bf16[16,128,384]{2,1,0:T(8,128)(2,1)} %copy-done.2, s32[1024]{0:T(1024)S(1)} %get-tuple-element.13), kind=kCustom, calls=%fused_computation.1 | custom fusion | bytes 4718688 | tf_op jit(solution)/shard_map/gather | solution.py:160
  46.1 2.0 %add_convert_fusion = (bf16[1024,384]{1,0:T(8,128)(2,1)S(1)}, f32[1024,384]{1,0:T(8,128)}) fusion(bf16[1024,384]{1,0:T(8,128)(2,1)S(1)} %copy-done.8, f32[1024,384]{1,0:T(8,128)S(1)} %fusion.19, bf16[384,384]{1,0:T(8,128)(2,1)S(1)} %copy-done.20), kind=kOutput, calls=%fused_computation.12 | convolution fusion | flops 305135616 | bytes 5013504 | tf_op jit(solution)/shard_map/dot_general | solution.py:166
  53.1 4.2 %fusion.8 = bf16[8,128,256]{2,1,0:T(8,128)(2,1)} fusion(s32[8,128]{1,0:T(8,128)S(1)} %bitcast.96, bf16[8,128,512]{2,1,0:T(8,128)(2,1)} %bitcast.84, bf16[8,256,512]{2,1,0:T(8,128)(2,1)S(1)} %bitcast.80), kind=kOutput, calls=%fused_computation.26 | convolution fusion | flops 270535168 | bytes 3674112 | tf_op jit(solution)/shard_map/div | solution.py:183
  63.4 2.1 %multiply_convert_fusion = bf16[8,256,512]{2,1,0:T(8,128)(2,1)} fusion(bf16[8,128,256]{2,1,0:T(8,128)(2,1)S(1)} %copy-done.6, bf16[8,128,512]{2,1,0:T(8,128)(2,1)S(1)} %bitcast.85), kind=kOutput, calls=%fused_computation.7 | convolution fusion | flops 270532608 | bytes 3670016 | tf_op jit(solution)/shard_map/bij,bie->bje/dot_general | solution.py:196
  65.4 2.0 %gather_fusion.3 = bf16[16,128,512]{2,1,0:T(8,128)(2,1)} fusion(bf16[5,128,512]{2,1,0:T(8,128)(2,1)S(1)} %constant_dynamic-update-slice_fusion.6, s32[1024]{0:T(1024)S(1)} %get-tuple-element.12), kind=kCustom, calls=%fused_computation.3 | custom fusion | bytes 4194368 | tf_op jit(solution)/shard_map/gather | solution.py:177
  70.3 4.5 %fusion.22 = f32[512,512]{1,0:T(8,128)} fusion(bf16[2048,512]{1,0:T(8,128)(2,1)} %bitcast.89, bf16[2048,512]{1,0:T(8,128)(2,1)} %bitcast.88), kind=kOutput, calls=%fused_computation.72 | convolution fusion | flops 1073741824 | bytes 5242880 | tf_op jit(solution)/shard_map/dot_general | solution.py:202
  76.2 2.9 %pad_maximum_fusion = f32[64,11776]{1,0:T(8,128)} fusion(f32[64,4096]{1,0:T(8,128)S(1)} %reshape.152, f32[64,3072]{1,0:T(8,128)S(1)} %reshape.149, f32[64,2304]{1,0:T(8,128)} %reshape.148, f32[64,2304]{1,0:T(8,128)S(1)} %reshape.147), kind=kLoop, calls=%fused_computation.8 | loop fusion | flops 2260992 | bytes 6029312 | tf_op jit(solution)/shard_map/concatenate | solution.py:96
  79.1 6.3 %gather_fusion.4 = f32[64,11776]{1,0:T(8,128)} fusion(f32[64,11776]{1,0:T(8,128)} %pad_maximum_fusion, s32[1024]{0:T(1024)S(1)} %get-tuple-element.11), kind=kCustom, calls=%fused_computation.4 | custom fusion | bytes 6029568 | tf_op jit(solution)/shard_map/gather | solution.py:97
  86.9 1.9 %collective-permute-start.4 = (bf16[32,11776]{1,0:T(8,128)(2,1)S(1)}, bf16[32,11776]{1,0:T(8,128)(2,1)S(1)}, u32[]{:S(2)}, u32[]{:S(2)}) collective-permute-start(bf16[32,11776]{1,0:T(8,128)(2,1)S(1)} %fusion.9), channel_id=1, source_target_pairs={{0,1},{1,0},{2,3},{3,2},{4,5},{5,4},{6,7},{7,6},{8,9},{9,8},{10,11... | collective-permute-start | bytes 2261000 | tf_op jit(solution)/shard_map/ppermute | solution.py:23
  88.9 2.1 %collective-permute-done.4 = bf16[32,11776]{1,0:T(8,128)(2,1)S(1)} collective-permute-done((bf16[32,11776]{1,0:T(8,128)(2,1)S(1)}, bf16[32,11776]{1,0:T(8,128)(2,1)S(1)}, u32[]{:S(2)}, u32[]{:S(2)}) %collective-permute-start.4) | collective-permute-done | bytes 753696 | tf_op jit(solution)/shard_map/ppermute | solution.py:23
  92.6 5.8 %collective-permute-start.5 = (bf16[8,11776]{1,0:T(8,128)(2,1)S(1)}, bf16[8,11776]{1,0:T(8,128)(2,1)S(1)}, u32[]{:S(2)}, u32[]{:S(2)}) collective-permute-start(bf16[8,11776]{1,0:T(8,128)(2,1)S(1)} %get-tuple-element.4), channel_id=1, source_target_pairs={{0,2},{1,3},{2,4},{3,5},{4,6},{5,7},{6,0},{7,1},{8,10},{9,11},{10,... | collective-permute-start | bytes 565256 | tf_op jit(solution)/shard_map/ppermute | solution.py:89
  98.4 1.9 %collective-permute-start.6 = (bf16[8,11776]{1,0:T(8,128)(2,1)S(1)}, bf16[8,11776]{1,0:T(8,128)(2,1)S(1)}, u32[]{:S(2)}, u32[]{:S(2)}) collective-permute-start(bf16[8,11776]{1,0:T(8,128)(2,1)S(1)} %get-tuple-element.6), channel_id=1, source_target_pairs={{0,4},{1,5},{2,6},{3,7},{4,0},{5,1},{6,2},{7,3},{8,12},{9,13},{10,... | collective-permute-start | bytes 565256 | tf_op jit(solution)/shard_map/ppermute | solution.py:89
  100.4 2.8 %collective-permute-start.7 = (bf16[8,11776]{1,0:T(8,128)(2,1)S(1)}, bf16[8,11776]{1,0:T(8,128)(2,1)S(1)}, u32[]{:S(2)}, u32[]{:S(2)}) collective-permute-start(bf16[8,11776]{1,0:T(8,128)(2,1)S(1)} %get-tuple-element.5), channel_id=1, source_target_pairs={{0,6},{1,7},{2,0},{3,1},{4,2},{5,3},{6,4},{7,5},{8,14},{9,15},{10,... | collective-permute-start | bytes 565256 | tf_op jit(solution)/shard_map/ppermute | solution.py:89
  103.2 3.6 %collective-permute-done.5 = bf16[8,11776]{1,0:T(8,128)(2,1)S(1)} collective-permute-done((bf16[8,11776]{1,0:T(8,128)(2,1)S(1)}, bf16[8,11776]{1,0:T(8,128)(2,1)S(1)}, u32[]{:S(2)}, u32[]{:S(2)}) %collective-permute-start.5) | collective-permute-done | bytes 188448 | tf_op jit(solution)/shard_map/ppermute | solution.py:89
  106.7 2.7 %collective-permute-done.6 = bf16[8,11776]{1,0:T(8,128)(2,1)S(1)} collective-permute-done((bf16[8,11776]{1,0:T(8,128)(2,1)S(1)}, bf16[8,11776]{1,0:T(8,128)(2,1)S(1)}, u32[]{:S(2)}, u32[]{:S(2)}) %collective-permute-start.6) | collective-permute-done | bytes 188448 | tf_op jit(solution)/shard_map/ppermute | solution.py:89
  109.5 2.9 %collective-permute-done.7 = bf16[8,11776]{1,0:T(8,128)(2,1)S(1)} collective-permute-done((bf16[8,11776]{1,0:T(8,128)(2,1)S(1)}, bf16[8,11776]{1,0:T(8,128)(2,1)S(1)}, u32[]{:S(2)}, u32[]{:S(2)}) %collective-permute-start.7) | collective-permute-done | bytes 188448 | tf_op jit(solution)/shard_map/ppermute | solution.py:89
  112.6 1.9 %collective-permute-start.8 = (bf16[4,11776]{1,0:T(4,128)(2,1)S(1)}, bf16[4,11776]{1,0:T(4,128)(2,1)S(1)}, u32[]{:S(2)}, u32[]{:S(2)}) collective-permute-start(bf16[4,11776]{1,0:T(4,128)(2,1)S(1)} %fusion.15), channel_id=1, source_target_pairs={{0,8},{1,57},{2,10},{3,59},{4,12},{5,61},{6,14},{7,63},{8,0},{9,17... | collective-permute-start | bytes 282632 | tf_op jit(solution)/shard_map/ppermute | solution.py:119
  114.6 4.5 %collective-permute-done.8 = bf16[4,11776]{1,0:T(4,128)(2,1)S(1)} collective-permute-done((bf16[4,11776]{1,0:T(4,128)(2,1)S(1)}, bf16[4,11776]{1,0:T(4,128)(2,1)S(1)}, u32[]{:S(2)}, u32[]{:S(2)}) %collective-permute-start.8) | collective-permute-done | bytes 94240 | tf_op jit(solution)/shard_map/ppermute | solution.py:119
  119.4 2.9 %collective-permute-start.9 = (bf16[2,11776]{1,0:T(2,128)(2,1)S(1)}, bf16[2,11776]{1,0:T(2,128)(2,1)S(1)}, u32[]{:S(2)}, u32[]{:S(2)}) collective-permute-start(bf16[2,11776]{1,0:T(2,128)(2,1)S(1)} %fusion.16), channel_id=1, source_target_pairs={{0,16},{1,49},{2,18},{3,51},{4,20},{5,53},{6,22},{7,55},{8,24},{9,... | collective-permute-start | bytes 141320 | tf_op jit(solution)/shard_map/ppermute | solution.py:119
  122.2 4.1 %collective-permute-done.9 = bf16[2,11776]{1,0:T(2,128)(2,1)S(1)} collective-permute-done((bf16[2,11776]{1,0:T(2,128)(2,1)S(1)}, bf16[2,11776]{1,0:T(2,128)(2,1)S(1)}, u32[]{:S(2)}, u32[]{:S(2)}) %collective-permute-start.9) | collective-permute-done | bytes 47136 | tf_op jit(solution)/shard_map/ppermute | solution.py:119
  126.4 4.1 %collective-permute-start.10 = (f32[1,11776]{1,0:T(1,128)S(1)}, f32[1,11776]{1,0:T(1,128)S(1)}, u32[]{:S(2)}, u32[]{:S(2)}) collective-permute-start(f32[1,11776]{1,0:T(1,128)S(1)} %constant_dynamic-slice_fusion), channel_id=1, source_target_pairs={{0,32},{1,33},{2,34},{3,35},{4,36},{5,37},{6,38},{7,39},{8,40},{9,... | collective-permute-start | bytes 141320 | tf_op jit(solution)/shard_map/ppermute | solution.py:121
  130.6 6.0 %collective-permute-done.10 = f32[1,11776]{1,0:T(1,128)S(1)} collective-permute-done((f32[1,11776]{1,0:T(1,128)S(1)}, f32[1,11776]{1,0:T(1,128)S(1)}, u32[]{:S(2)}, u32[]{:S(2)}) %collective-permute-start.10) | collective-permute-done | bytes 47136 | tf_op jit(solution)/shard_map/ppermute | solution.py:121
  136.8 1.9 %collective-permute-start.11 = (f32[11776]{0:T(1024)S(1)}, f32[11776]{0:T(1024)S(1)}, u32[]{:S(2)}, u32[]{:S(2)}) collective-permute-start(f32[11776]{0:T(1024)S(1)} %add_reduce_fusion), channel_id=1, source_target_pairs={{0,64},{64,0},{128,192},{192,128},{256,320},{320,256},{384,448},{4... | collective-permute-start | bytes 141320 | tf_op jit(solution)/shard_map/ppermute | solution.py:23
  138.7 4.1 %collective-permute-done.11 = f32[11776]{0:T(1024)S(1)} collective-permute-done((f32[11776]{0:T(1024)S(1)}, f32[11776]{0:T(1024)S(1)}, u32[]{:S(2)}, u32[]{:S(2)}) %collective-permute-start.11) | collective-permute-done | bytes 47136 | tf_op jit(solution)/shard_map/ppermute | solution.py:23
  142.7 4.1 %collective-permute-start.12 = (f32[11776]{0:T(1024)S(1)}, f32[11776]{0:T(1024)S(1)}, u32[]{:S(2)}, u32[]{:S(2)}) collective-permute-start(f32[11776]{0:T(1024)S(1)} %add.176), channel_id=1, source_target_pairs={{0,128},{64,192},{128,0},{192,64},{256,384},{320,448},{384,256},{4... | collective-permute-start | bytes 141320 | tf_op jit(solution)/shard_map/ppermute | solution.py:23
  146.8 2.8 %collective-permute-done.12 = f32[11776]{0:T(1024)S(1)} collective-permute-done((f32[11776]{0:T(1024)S(1)}, f32[11776]{0:T(1024)S(1)}, u32[]{:S(2)}, u32[]{:S(2)}) %collective-permute-start.12) | collective-permute-done | bytes 47136 | tf_op jit(solution)/shard_map/ppermute | solution.py:23
  149.6 8.6 %collective-permute-start.13 = (f32[11776]{0:T(1024)S(1)}, f32[11776]{0:T(1024)S(1)}, u32[]{:S(2)}, u32[]{:S(2)}) collective-permute-start(f32[11776]{0:T(1024)S(1)} %add.177), channel_id=1, source_target_pairs={{0,256},{64,320},{128,384},{192,448},{256,0},{320,64},{384,128},{4... | collective-permute-start | bytes 141320 | tf_op jit(solution)/shard_map/ppermute | solution.py:23
  158.2 2.1 %collective-permute-done.13 = f32[11776]{0:T(1024)S(1)} collective-permute-done((f32[11776]{0:T(1024)S(1)}, f32[11776]{0:T(1024)S(1)}, u32[]{:S(2)}, u32[]{:S(2)}) %collective-permute-start.13) | collective-permute-done | bytes 47136 | tf_op jit(solution)/shard_map/ppermute | solution.py:23
  (127 shorter events, 47.0 us)
Async XLA Ops:
  0.6 43.2 %copy-start = (bf16[8,3,128,128]{3,2,1,0:T(8,128)(2,1)S(1)}, bf16[8,3,128,128]{3,2,1,0:T(8,128)(2,1)}, u32[]{:S(2)}) copy-start(bf16[8,3,128,128]{3,2,1,0:T(8,128)(2,1)} %param.13) | copy-start | bytes 2359300
  0.6 17.3 %copy-start.18 = (s32[64]{0:T(128)S(1)}, s32[64]{0:T(128)}, u32[]{:S(2)}) copy-start(s32[64]{0:T(128)} %constant.151) | copy-start | bytes 772
  0.7 17.0 %copy-start.7 = (bf16[1024,384]{1,0:T(8,128)(2,1)S(1)}, bf16[1024,384]{1,0:T(8,128)(2,1)}, u32[]{:S(2)}) copy-start(bf16[1024,384]{1,0:T(8,128)(2,1)} %param.12) | copy-start | bytes 2359300
  0.7 17.3 %copy-start.12 = (bf16[128,512]{1,0:T(8,128)(2,1)S(1)}, bf16[128,512]{1,0:T(8,128)(2,1)}, u32[]{:S(2)}) copy-start(bf16[128,512]{1,0:T(8,128)(2,1)} %param.18) | copy-start | bytes 393220
  0.7 17.1 %copy-start.17 = (s32[8,2]{0,1:T(2,128)S(1)}, s32[8,2]{0,1:T(2,128)}, u32[]{:S(2)}) copy-start(s32[8,2]{0,1:T(2,128)} %param.16) | copy-start | bytes 196
  6.5 12.1 %collective-permute-start = (bf16[163840]{0:T(1024)(128)(2,1)}, bf16[163840]{0:T(1024)(128)(2,1)}, u32[]{:S(2)}, u32[]{:S(2)}) collective-permute-start(bf16[163840]{0:T(1024)(128)(2,1)} %constant_dynamic-update-slice_fusion.10), channel_id=1, source_target_pairs={{0,1},{1,2},{2,3},{3,4},{4,5},{5,6},{6,7},{7,8},{8,9},{9,10},{10,1... | collective-permute-start | bytes 983048 | tf_op jit(solution)/shard_map/ppermute | solution.py:18
  8.4 12.9 %collective-permute-start.1 = (bf16[163840]{0:T(1024)(128)(2,1)}, bf16[163840]{0:T(1024)(128)(2,1)}, u32[]{:S(2)}, u32[]{:S(2)}) collective-permute-start(bf16[163840]{0:T(1024)(128)(2,1)} %constant_dynamic-update-slice_fusion.10), channel_id=1, source_target_pairs={{0,2},{1,3},{2,4},{3,5},{4,6},{5,7},{6,8},{7,9},{8,10},{9,11},{10,... | collective-permute-start | bytes 983048 | tf_op jit(solution)/shard_map/ppermute | solution.py:18
  11.8 10.5 %collective-permute-start.2 = (bf16[163840]{0:T(1024)(128)(2,1)}, bf16[163840]{0:T(1024)(128)(2,1)}, u32[]{:S(2)}, u32[]{:S(2)}) collective-permute-start(bf16[163840]{0:T(1024)(128)(2,1)} %constant_dynamic-update-slice_fusion.10), channel_id=1, source_target_pairs={{0,63},{1,0},{2,1},{3,2},{4,3},{5,4},{6,5},{7,6},{8,7},{9,8},{10,9... | collective-permute-start | bytes 983048 | tf_op jit(solution)/shard_map/ppermute | solution.py:18
  15.2 16.0 %collective-permute-start.3 = (bf16[163840]{0:T(1024)(128)(2,1)}, bf16[163840]{0:T(1024)(128)(2,1)}, u32[]{:S(2)}, u32[]{:S(2)}) collective-permute-start(bf16[163840]{0:T(1024)(128)(2,1)} %constant_dynamic-update-slice_fusion.10), channel_id=1, source_target_pairs={{0,62},{1,63},{2,0},{3,1},{4,2},{5,3},{6,4},{7,5},{8,6},{9,7},{10,... | collective-permute-start | bytes 983048 | tf_op jit(solution)/shard_map/ppermute | solution.py:18
  44.6 3.6 %copy-start.4 = (bf16[8,384,128]{1,2,0:T(8,128)(2,1)}, bf16[8,384,128]{1,2,0:T(8,128)(2,1)S(1)}, u32[]{:S(2)}) copy-start(bf16[8,384,128]{1,2,0:T(8,128)(2,1)S(1)} %bitcast_convert_fusion) | copy-start | bytes 2359300
  44.6 1.5 copy-start.20
  46.1 2.1 %copy-start.14 = (bf16[384,512]{1,0:T(8,128)(2,1)S(1)}, bf16[384,512]{1,0:T(8,128)(2,1)}, u32[]{:S(2)}) copy-start(bf16[384,512]{1,0:T(8,128)(2,1)} %param.21) | copy-start | bytes 1179652
  48.1 3.2 %copy-start.10 = (bf16[1024,384]{1,0:T(8,128)(2,1)}, bf16[1024,384]{1,0:T(8,128)(2,1)S(1)}, u32[]{:S(2)}) copy-start(bf16[1024,384]{1,0:T(8,128)(2,1)S(1)} %get-tuple-element.9) | copy-start | bytes 2359300
  48.1 1.7 %copy-start.1 = (bf16[5,128,512]{2,1,0:T(8,128)(2,1)S(1)}, bf16[5,128,512]{2,1,0:T(8,128)(2,1)}, u32[]{:S(2)}) copy-start(bf16[5,128,512]{2,1,0:T(8,128)(2,1)} %bitcast_dynamic-update-slice_fusion) | copy-start | bytes 1966084
  48.1 1.8 %copy-start.13 = (bf16[1,128,512]{2,1,0:T(8,128)(2,1)S(1)}, bf16[1,128,512]{2,1,0:T(8,128)(2,1)}, u32[]{:S(2)}) copy-start(bf16[1,128,512]{2,1,0:T(8,128)(2,1)} %reshape.142) | copy-start | bytes 393220
  48.1 1.8 %copy-start.19 = (bf16[512,512]{1,0:T(8,128)(2,1)S(1)}, bf16[512,512]{1,0:T(8,128)(2,1)}, u32[]{:S(2)}) copy-start(bf16[512,512]{1,0:T(8,128)(2,1)} %param.22) | copy-start | bytes 1572868
  51.3 1.8 %copy-start.21 = (s32[1024]{0:T(1024)S(1)}, s32[1024]{0:T(1024)}, u32[]{:S(2)}) copy-start(s32[1024]{0:T(1024)} %param.17) | copy-start | bytes 12292
  57.3 1.6 %copy-start.15 = (bf16[384,512]{1,0:T(8,128)(2,1)S(1)}, bf16[384,512]{1,0:T(8,128)(2,1)}, u32[]{:S(2)}) copy-start(bf16[384,512]{1,0:T(8,128)(2,1)} %param.21) | copy-start | bytes 1179652
  57.3 1.7 %copy-start.22 = (f32[1024,384]{1,0:T(8,128)S(1)}, f32[1024,384]{1,0:T(8,128)}, u32[]{:S(2)}) copy-start(f32[1024,384]{1,0:T(8,128)} %get-tuple-element.10) | copy-start | bytes 4718596
  60.1 1.7 %copy-start.11 = (bf16[1024,384]{1,0:T(8,128)(2,1)S(1)}, bf16[1024,384]{1,0:T(8,128)(2,1)}, u32[]{:S(2)}) copy-start(bf16[1024,384]{1,0:T(8,128)(2,1)} %copy-done.10) | copy-start | bytes 2359300
  61.9 1.5 copy-start.3
  61.9 1.5 copy-start.6
  86.9 4.1 %collective-permute-start.4 = (bf16[32,11776]{1,0:T(8,128)(2,1)S(1)}, bf16[32,11776]{1,0:T(8,128)(2,1)S(1)}, u32[]{:S(2)}, u32[]{:S(2)}) collective-permute-start(bf16[32,11776]{1,0:T(8,128)(2,1)S(1)} %fusion.9), channel_id=1, source_target_pairs={{0,1},{1,0},{2,3},{3,2},{4,5},{5,4},{6,7},{7,6},{8,9},{9,8},{10,11... | collective-permute-start | bytes 2261000 | tf_op jit(solution)/shard_map/ppermute | solution.py:23
  92.6 14.1 %collective-permute-start.5 = (bf16[8,11776]{1,0:T(8,128)(2,1)S(1)}, bf16[8,11776]{1,0:T(8,128)(2,1)S(1)}, u32[]{:S(2)}, u32[]{:S(2)}) collective-permute-start(bf16[8,11776]{1,0:T(8,128)(2,1)S(1)} %get-tuple-element.4), channel_id=1, source_target_pairs={{0,2},{1,3},{2,4},{3,5},{4,6},{5,7},{6,0},{7,1},{8,10},{9,11},{10,... | collective-permute-start | bytes 565256 | tf_op jit(solution)/shard_map/ppermute | solution.py:89
  98.4 11.0 %collective-permute-start.6 = (bf16[8,11776]{1,0:T(8,128)(2,1)S(1)}, bf16[8,11776]{1,0:T(8,128)(2,1)S(1)}, u32[]{:S(2)}, u32[]{:S(2)}) collective-permute-start(bf16[8,11776]{1,0:T(8,128)(2,1)S(1)} %get-tuple-element.6), channel_id=1, source_target_pairs={{0,4},{1,5},{2,6},{3,7},{4,0},{5,1},{6,2},{7,3},{8,12},{9,13},{10,... | collective-permute-start | bytes 565256 | tf_op jit(solution)/shard_map/ppermute | solution.py:89
  100.4 12.0 %collective-permute-start.7 = (bf16[8,11776]{1,0:T(8,128)(2,1)S(1)}, bf16[8,11776]{1,0:T(8,128)(2,1)S(1)}, u32[]{:S(2)}, u32[]{:S(2)}) collective-permute-start(bf16[8,11776]{1,0:T(8,128)(2,1)S(1)} %get-tuple-element.5), channel_id=1, source_target_pairs={{0,6},{1,7},{2,0},{3,1},{4,2},{5,3},{6,4},{7,5},{8,14},{9,15},{10,... | collective-permute-start | bytes 565256 | tf_op jit(solution)/shard_map/ppermute | solution.py:89
  112.6 6.5 %collective-permute-start.8 = (bf16[4,11776]{1,0:T(4,128)(2,1)S(1)}, bf16[4,11776]{1,0:T(4,128)(2,1)S(1)}, u32[]{:S(2)}, u32[]{:S(2)}) collective-permute-start(bf16[4,11776]{1,0:T(4,128)(2,1)S(1)} %fusion.15), channel_id=1, source_target_pairs={{0,8},{1,57},{2,10},{3,59},{4,12},{5,61},{6,14},{7,63},{8,0},{9,17... | collective-permute-start | bytes 282632 | tf_op jit(solution)/shard_map/ppermute | solution.py:119
  119.4 7.0 %collective-permute-start.9 = (bf16[2,11776]{1,0:T(2,128)(2,1)S(1)}, bf16[2,11776]{1,0:T(2,128)(2,1)S(1)}, u32[]{:S(2)}, u32[]{:S(2)}) collective-permute-start(bf16[2,11776]{1,0:T(2,128)(2,1)S(1)} %fusion.16), channel_id=1, source_target_pairs={{0,16},{1,49},{2,18},{3,51},{4,20},{5,53},{6,22},{7,55},{8,24},{9,... | collective-permute-start | bytes 141320 | tf_op jit(solution)/shard_map/ppermute | solution.py:119
  126.4 10.2 %collective-permute-start.10 = (f32[1,11776]{1,0:T(1,128)S(1)}, f32[1,11776]{1,0:T(1,128)S(1)}, u32[]{:S(2)}, u32[]{:S(2)}) collective-permute-start(f32[1,11776]{1,0:T(1,128)S(1)} %constant_dynamic-slice_fusion), channel_id=1, source_target_pairs={{0,32},{1,33},{2,34},{3,35},{4,36},{5,37},{6,38},{7,39},{8,40},{9,... | collective-permute-start | bytes 141320 | tf_op jit(solution)/shard_map/ppermute | solution.py:121
  136.8 6.0 %collective-permute-start.11 = (f32[11776]{0:T(1024)S(1)}, f32[11776]{0:T(1024)S(1)}, u32[]{:S(2)}, u32[]{:S(2)}) collective-permute-start(f32[11776]{0:T(1024)S(1)} %add_reduce_fusion), channel_id=1, source_target_pairs={{0,64},{64,0},{128,192},{192,128},{256,320},{320,256},{384,448},{4... | collective-permute-start | bytes 141320 | tf_op jit(solution)/shard_map/ppermute | solution.py:23
  142.7 6.9 %collective-permute-start.12 = (f32[11776]{0:T(1024)S(1)}, f32[11776]{0:T(1024)S(1)}, u32[]{:S(2)}, u32[]{:S(2)}) collective-permute-start(f32[11776]{0:T(1024)S(1)} %add.176), channel_id=1, source_target_pairs={{0,128},{64,192},{128,0},{192,64},{256,384},{320,448},{384,256},{4... | collective-permute-start | bytes 141320 | tf_op jit(solution)/shard_map/ppermute | solution.py:23
  149.6 10.7 %collective-permute-start.13 = (f32[11776]{0:T(1024)S(1)}, f32[11776]{0:T(1024)S(1)}, u32[]{:S(2)}, u32[]{:S(2)}) collective-permute-start(f32[11776]{0:T(1024)S(1)} %add.177), channel_id=1, source_target_pairs={{0,256},{64,320},{128,384},{192,448},{256,0},{320,64},{384,128},{4... | collective-permute-start | bytes 141320 | tf_op jit(solution)/shard_map/ppermute | solution.py:23
  (5 other events, 5.9 us)

commit v13 on v10

--- a/solution.py
+++ b/solution.py
@@ -123,10 +123,10 @@
         held = mine + got
     share = held.reshape(-1)
     n_region = lax.axis_size("region")
-    step = 1
-    while step < n_region:
+    step = n_region // 2
+    while step >= 1:
         share = share + swapped(share, "region", step)
-        step *= 2
+        step //= 2
     pieces = []
     start = 0
     for t in terms:

time: 157 us -> 157 us (level)
  no operation moved by 1% of the time
where the time goes in v13:
time: 157 us; the launch traced here: 156 us
  starting transfers between devices  58 us (37%)
  local copies, waits for them, and re-layouts  37.9 us (24%)
  waiting for transfers between devices  36.1 us (23%)
  matrix products  19.5 us (12%)
  other arithmetic  2.68 us (2%)
  between operations  1.57 us (1%)
    ppermute x4, starting transfers between devices, swapped(): return lax.ppermute(shard, axis, [(i, i ^ mask) for i in range(count)])  22 us
    ppermute x3, starting transfers between devices, shifted_x(): return lax.ppermute(shard, 'dom', pairs)  15.2 us
    ppermute x4, starting transfers between devices, passed_along(): lax.ppermute(shard, axis, [(i, (i + by) % count) for i in range(count)])  12 us
    unnamed x63, local copies, waits for them, and re-layouts  11.6 us
    ppermute x2, waiting for transfers between devices, reduce_to_share(): got = lax.ppermute(other.astype(bf16), 'dom', pairs).astype(f32)  9.46 us
    ppermute x4, waiting for transfers between devices, swapped(): return lax.ppermute(shard, axis, [(i, i ^ mask) for i in range(count)])  8.54 us
    ppermute x3, waiting for transfers between devices, shifted_x(): return lax.ppermute(shard, 'dom', pairs)  8.28 us
    gather x4, local copies, waits for them, and re-layouts, reduce_to_share(): t[share_order(t.shape[0], n_dom, n_x)].reshape(2, n_y * n_x, -1)  6.89 us
  transfers between devices with their start and end apart: 14, of which 11 were waited for; matrix products, arithmetic and copies ran while one was open for 2% of the time, Pallas kernels for 0%

profile of v13, /device:TPU:6, one launch (start us, length us, event | category | flops | bytes accessed | tf_op | source)
XLA Modules:
  0.0 155.8 jit_solution(1168215122435997341)
XLA Ops:
  5.6 2.7 %collective-permute-start.3 = (bf16[163840]{0:T(1024)(128)(2,1)}, bf16[163840]{0:T(1024)(128)(2,1)S(1)}, u32[]{:S(2)}, u32[]{:S(2)}) collective-permute-start(bf16[163840]{0:T(1024)(128)(2,1)} %constant_dynamic-update-slice_fusion.14), channel_id=1, source_target_pairs={{0,62},{1,63},{2,0},{3,1},{4,2},{5,3},{6,4},{7,5},{8,6},{9,7},{10,... | collective-permute-start | bytes 983048 | tf_op jit(solution)/shard_map/ppermute | solution.py:18
  8.4 1.9 %collective-permute-start.2 = (bf16[163840]{0:T(1024)(128)(2,1)}, bf16[163840]{0:T(1024)(128)(2,1)S(1)}, u32[]{:S(2)}, u32[]{:S(2)}) collective-permute-start(bf16[163840]{0:T(1024)(128)(2,1)} %constant_dynamic-update-slice_fusion.14), channel_id=1, source_target_pairs={{0,63},{1,0},{2,1},{3,2},{4,3},{5,4},{6,5},{7,6},{8,7},{9,8},{10,9... | collective-permute-start | bytes 983048 | tf_op jit(solution)/shard_map/ppermute | solution.py:18
  10.3 5.2 %collective-permute-start.1 = (bf16[163840]{0:T(1024)(128)(2,1)}, bf16[163840]{0:T(1024)(128)(2,1)S(1)}, u32[]{:S(2)}, u32[]{:S(2)}) collective-permute-start(bf16[163840]{0:T(1024)(128)(2,1)} %constant_dynamic-update-slice_fusion.14), channel_id=1, source_target_pairs={{0,2},{1,3},{2,4},{3,5},{4,6},{5,7},{6,8},{7,9},{8,10},{9,11},{10,... | collective-permute-start | bytes 983048 | tf_op jit(solution)/shard_map/ppermute | solution.py:18
  15.5 2.1 %collective-permute-start = (bf16[163840]{0:T(1024)(128)(2,1)}, bf16[163840]{0:T(1024)(128)(2,1)S(1)}, u32[]{:S(2)}, u32[]{:S(2)}) collective-permute-start(bf16[163840]{0:T(1024)(128)(2,1)} %constant_dynamic-update-slice_fusion.14), channel_id=1, source_target_pairs={{0,1},{1,2},{2,3},{3,4},{4,5},{5,6},{6,7},{7,8},{8,9},{9,10},{10,1... | collective-permute-start | bytes 983048 | tf_op jit(solution)/shard_map/ppermute | solution.py:18
  21.4 2.4 %collective-permute-done.1 = bf16[163840]{0:T(1024)(128)(2,1)S(1)} collective-permute-done((bf16[163840]{0:T(1024)(128)(2,1)}, bf16[163840]{0:T(1024)(128)(2,1)S(1)}, u32[]{:S(2)}, u32[]{:S(2)}) %collective-permute-start.1) | collective-permute-done | bytes 327712 | tf_op jit(solution)/shard_map/ppermute | solution.py:18
  24.1 1.9 %collective-permute-done = bf16[163840]{0:T(1024)(128)(2,1)S(1)} collective-permute-done((bf16[163840]{0:T(1024)(128)(2,1)}, bf16[163840]{0:T(1024)(128)(2,1)S(1)}, u32[]{:S(2)}, u32[]{:S(2)}) %collective-permute-start) | collective-permute-done | bytes 327712 | tf_op jit(solution)/shard_map/ppermute | solution.py:18
  26.3 2.0 %gather_fusion.6 = bf16[16,128,512]{2,1,0:T(8,128)(2,1)} fusion(bf16[5,128,512]{2,1,0:T(8,128)(2,1)S(1)} %constant_dynamic-update-slice_fusion.6, s32[1024]{0:T(1024)S(1)} %get-tuple-element.13), kind=kCustom, calls=%fused_computation.6 | custom fusion | bytes 4194368 | tf_op jit(solution)/shard_map/gather | solution.py:178
  29.9 2.0 %gather_fusion.2 = bf16[16,128,512]{2,1,0:T(8,128)(2,1)} fusion(bf16[5,128,512]{2,1,0:T(8,128)(2,1)S(1)} %bitcast.80, s32[1024]{0:T(1024)S(1)} %get-tuple-element.13), kind=kCustom, calls=%fused_computation.2 | custom fusion | bytes 4194368 | tf_op jit(solution)/shard_map/gather | solution.py:177
  34.7 2.5 %gather_fusion.1 = bf16[24,128,384]{2,1,0:T(8,128)(2,1)S(1)} fusion(bf16[16,128,384]{2,1,0:T(8,128)(2,1)} %constant_dynamic-update-slice_fusion.1, s32[1024]{0:T(1024)S(1)} %get-tuple-element.14), kind=kCustom, calls=%fused_computation.1 | custom fusion | bytes 4718688 | tf_op jit(solution)/shard_map/gather | solution.py:161
  39.5 2.0 %add_convert_fusion = (bf16[1024,384]{1,0:T(8,128)(2,1)S(1)}, f32[1024,384]{1,0:T(8,128)}) fusion(bf16[1024,384]{1,0:T(8,128)(2,1)S(1)} %copy-done.9, f32[1024,384]{1,0:T(8,128)S(1)} %fusion.19, bf16[384,384]{1,0:T(8,128)(2,1)S(1)} %copy-done.22), kind=kOutput, calls=%fused_computation.14 | convolution fusion | flops 305135616 | bytes 5013504 | tf_op jit(solution)/shard_map/dot_general | solution.py:167
  43.7 3.3 %fusion.8 = bf16[8,128,256]{2,1,0:T(8,128)(2,1)S(1)} fusion(s32[8,128]{1,0:T(8,128)S(1)} %bitcast.93, bf16[8,128,512]{2,1,0:T(8,128)(2,1)} %bitcast.81, bf16[8,256,512]{2,1,0:T(8,128)(2,1)S(1)} %bitcast.77), kind=kOutput, calls=%fused_computation.28 | convolution fusion | flops 270535168 | bytes 3674112 | tf_op jit(solution)/shard_map/div | solution.py:184
  52.8 2.1 %multiply_convert_fusion = bf16[8,256,512]{2,1,0:T(8,128)(2,1)} fusion(bf16[8,128,256]{2,1,0:T(8,128)(2,1)S(1)} %fusion.8, bf16[8,128,512]{2,1,0:T(8,128)(2,1)S(1)} %bitcast.82), kind=kOutput, calls=%fused_computation.10 | convolution fusion | flops 270532608 | bytes 3670016 | tf_op jit(solution)/shard_map/bij,bie->bje/dot_general | solution.py:197
  56.2 1.9 %gather_fusion.4 = f32[384,384]{1,0:T(8,128)S(1)} fusion(f32[384,384]{1,0:T(8,128)S(1)} %copy.25, s32[1024]{0:T(1024)S(1)} %get-tuple-element.12), kind=kCustom, calls=%fused_computation.4 | custom fusion | bytes 1181184 | tf_op jit(solution)/shard_map/gather | solution.py:97
  64.6 3.5 %fusion.22 = f32[512,512]{1,0:T(8,128)S(1)} fusion(bf16[2048,512]{1,0:T(8,128)(2,1)} %bitcast.85, bf16[2048,512]{1,0:T(8,128)(2,1)} %bitcast.86), kind=kOutput, calls=%fused_computation.79 | convolution fusion | flops 1073741824 | bytes 5242880 | tf_op jit(solution)/shard_map/dot_general | solution.py:203
  73.1 3.0 %collective-permute-start.4 = (bf16[32,11776]{1,0:T(8,128)(2,1)S(1)}, bf16[32,11776]{1,0:T(8,128)(2,1)S(1)}, u32[]{:S(2)}, u32[]{:S(2)}) collective-permute-start(bf16[32,11776]{1,0:T(8,128)(2,1)S(1)} %fusion.9), channel_id=1, source_target_pairs={{0,1},{1,0},{2,3},{3,2},{4,5},{5,4},{6,7},{7,6},{8,9},{9,8},{10,11... | collective-permute-start | bytes 2261000 | tf_op jit(solution)/shard_map/ppermute | solution.py:23
  76.2 1.7 %collective-permute-done.4 = bf16[32,11776]{1,0:T(8,128)(2,1)S(1)} collective-permute-done((bf16[32,11776]{1,0:T(8,128)(2,1)S(1)}, bf16[32,11776]{1,0:T(8,128)(2,1)S(1)}, u32[]{:S(2)}, u32[]{:S(2)}) %collective-permute-start.4) | collective-permute-done | bytes 753696 | tf_op jit(solution)/shard_map/ppermute | solution.py:23
  79.5 9.9 %collective-permute-start.5 = (bf16[8,11776]{1,0:T(8,128)(2,1)S(1)}, bf16[8,11776]{1,0:T(8,128)(2,1)S(1)}, u32[]{:S(2)}, u32[]{:S(2)}) collective-permute-start(bf16[8,11776]{1,0:T(8,128)(2,1)S(1)} %get-tuple-element.4), channel_id=1, source_target_pairs={{0,2},{1,3},{2,4},{3,5},{4,6},{5,7},{6,0},{7,1},{8,10},{9,11},{10,... | collective-permute-start | bytes 565256 | tf_op jit(solution)/shard_map/ppermute | solution.py:89
  89.4 1.9 %collective-permute-start.7 = (bf16[8,11776]{1,0:T(8,128)(2,1)S(1)}, bf16[8,11776]{1,0:T(8,128)(2,1)S(1)}, u32[]{:S(2)}, u32[]{:S(2)}) collective-permute-start(bf16[8,11776]{1,0:T(8,128)(2,1)S(1)} %get-tuple-element.5), channel_id=1, source_target_pairs={{0,6},{1,7},{2,0},{3,1},{4,2},{5,3},{6,4},{7,5},{8,14},{9,15},{10,... | collective-permute-start | bytes 565256 | tf_op jit(solution)/shard_map/ppermute | solution.py:89
  91.3 3.4 %collective-permute-start.6 = (bf16[8,11776]{1,0:T(8,128)(2,1)S(1)}, bf16[8,11776]{1,0:T(8,128)(2,1)S(1)}, u32[]{:S(2)}, u32[]{:S(2)}) collective-permute-start(bf16[8,11776]{1,0:T(8,128)(2,1)S(1)} %get-tuple-element.6), channel_id=1, source_target_pairs={{0,4},{1,5},{2,6},{3,7},{4,0},{5,1},{6,2},{7,3},{8,12},{9,13},{10,... | collective-permute-start | bytes 565256 | tf_op jit(solution)/shard_map/ppermute | solution.py:89
  94.7 8.3 %collective-permute-done.7 = bf16[8,11776]{1,0:T(8,128)(2,1)S(1)} collective-permute-done((bf16[8,11776]{1,0:T(8,128)(2,1)S(1)}, bf16[8,11776]{1,0:T(8,128)(2,1)S(1)}, u32[]{:S(2)}, u32[]{:S(2)}) %collective-permute-start.7) | collective-permute-done | bytes 188448 | tf_op jit(solution)/shard_map/ppermute | solution.py:89
  103.3 1.9 %collective-permute-start.8 = (bf16[4,11776]{1,0:T(4,128)(2,1)S(1)}, bf16[4,11776]{1,0:T(4,128)(2,1)S(1)}, u32[]{:S(2)}, u32[]{:S(2)}) collective-permute-start(bf16[4,11776]{1,0:T(4,128)(2,1)S(1)} %fusion.15), channel_id=1, source_target_pairs={{0,8},{1,57},{2,10},{3,59},{4,12},{5,61},{6,14},{7,63},{8,0},{9,17... | collective-permute-start | bytes 282632 | tf_op jit(solution)/shard_map/ppermute | solution.py:120
  105.2 4.5 %collective-permute-done.8 = bf16[4,11776]{1,0:T(4,128)(2,1)S(1)} collective-permute-done((bf16[4,11776]{1,0:T(4,128)(2,1)S(1)}, bf16[4,11776]{1,0:T(4,128)(2,1)S(1)}, u32[]{:S(2)}, u32[]{:S(2)}) %collective-permute-start.8) | collective-permute-done | bytes 94240 | tf_op jit(solution)/shard_map/ppermute | solution.py:120
  110.0 1.9 %collective-permute-start.9 = (bf16[2,11776]{1,0:T(2,128)(2,1)S(1)}, bf16[2,11776]{1,0:T(2,128)(2,1)S(1)}, u32[]{:S(2)}, u32[]{:S(2)}) collective-permute-start(bf16[2,11776]{1,0:T(2,128)(2,1)S(1)} %fusion.16), channel_id=1, source_target_pairs={{0,16},{1,49},{2,18},{3,51},{4,20},{5,53},{6,22},{7,55},{8,24},{9,... | collective-permute-start | bytes 141320 | tf_op jit(solution)/shard_map/ppermute | solution.py:120
  111.9 4.9 %collective-permute-done.9 = bf16[2,11776]{1,0:T(2,128)(2,1)S(1)} collective-permute-done((bf16[2,11776]{1,0:T(2,128)(2,1)S(1)}, bf16[2,11776]{1,0:T(2,128)(2,1)S(1)}, u32[]{:S(2)}, u32[]{:S(2)}) %collective-permute-start.9) | collective-permute-done | bytes 47136 | tf_op jit(solution)/shard_map/ppermute | solution.py:120
  117.0 5.0 %collective-permute-start.10 = (f32[1,11776]{1,0:T(1,128)S(1)}, f32[1,11776]{1,0:T(1,128)S(1)}, u32[]{:S(2)}, u32[]{:S(2)}) collective-permute-start(f32[1,11776]{1,0:T(1,128)S(1)} %constant_dynamic-slice_fusion), channel_id=1, source_target_pairs={{0,32},{1,33},{2,34},{3,35},{4,36},{5,37},{6,38},{7,39},{8,40},{9,... | collective-permute-start | bytes 141320 | tf_op jit(solution)/shard_map/ppermute | solution.py:122
  122.0 5.2 %collective-permute-done.10 = f32[1,11776]{1,0:T(1,128)S(1)} collective-permute-done((f32[1,11776]{1,0:T(1,128)S(1)}, f32[1,11776]{1,0:T(1,128)S(1)}, u32[]{:S(2)}, u32[]{:S(2)}) %collective-permute-start.10) | collective-permute-done | bytes 47136 | tf_op jit(solution)/shard_map/ppermute | solution.py:122
  127.3 10.9 %collective-permute-start.11 = (f32[11776]{0:T(1024)S(1)}, f32[11776]{0:T(1024)S(1)}, u32[]{:S(2)}, u32[]{:S(2)}) collective-permute-start(f32[11776]{0:T(1024)S(1)} %add_reduce_fusion), channel_id=1, source_target_pairs={{0,256},{64,320},{128,384},{192,448},{256,0},{320,64},{384,128},{4... | collective-permute-start | bytes 141320 | tf_op jit(solution)/shard_map/ppermute | solution.py:23
  138.3 2.1 %collective-permute-done.11 = f32[11776]{0:T(1024)S(1)} collective-permute-done((f32[11776]{0:T(1024)S(1)}, f32[11776]{0:T(1024)S(1)}, u32[]{:S(2)}, u32[]{:S(2)}) %collective-permute-start.11) | collective-permute-done | bytes 47136 | tf_op jit(solution)/shard_map/ppermute | solution.py:23
  140.4 4.8 %collective-permute-start.12 = (f32[11776]{0:T(1024)S(1)}, f32[11776]{0:T(1024)S(1)}, u32[]{:S(2)}, u32[]{:S(2)}) collective-permute-start(f32[11776]{0:T(1024)S(1)} %add.188), channel_id=1, source_target_pairs={{0,128},{64,192},{128,0},{192,64},{256,384},{320,448},{384,256},{4... | collective-permute-start | bytes 141320 | tf_op jit(solution)/shard_map/ppermute | solution.py:23
  145.2 2.1 %collective-permute-done.12 = f32[11776]{0:T(1024)S(1)} collective-permute-done((f32[11776]{0:T(1024)S(1)}, f32[11776]{0:T(1024)S(1)}, u32[]{:S(2)}, u32[]{:S(2)}) %collective-permute-start.12) | collective-permute-done | bytes 47136 | tf_op jit(solution)/shard_map/ppermute | solution.py:23
  147.3 3.3 %collective-permute-start.13 = (f32[11776]{0:T(1024)S(1)}, f32[11776]{0:T(1024)S(1)}, u32[]{:S(2)}, u32[]{:S(2)}) collective-permute-start(f32[11776]{0:T(1024)S(1)} %add.189), channel_id=1, source_target_pairs={{0,64},{64,0},{128,192},{192,128},{256,320},{320,256},{384,448},{4... | collective-permute-start | bytes 141320 | tf_op jit(solution)/shard_map/ppermute | solution.py:23
  150.6 2.6 %collective-permute-done.13 = f32[11776]{0:T(1024)S(1)} collective-permute-done((f32[11776]{0:T(1024)S(1)}, f32[11776]{0:T(1024)S(1)}, u32[]{:S(2)}, u32[]{:S(2)}) %collective-permute-start.13) | collective-permute-done | bytes 47136 | tf_op jit(solution)/shard_map/ppermute | solution.py:23
  (138 shorter events, 40.9 us)
Async XLA Ops:
  0.6 36.6 %copy-start = (bf16[8,3,128,128]{3,2,1,0:T(8,128)(2,1)S(1)}, bf16[8,3,128,128]{3,2,1,0:T(8,128)(2,1)}, u32[]{:S(2)}) copy-start(bf16[8,3,128,128]{3,2,1,0:T(8,128)(2,1)} %param.16) | copy-start | bytes 2359300
  0.6 18.4 %copy-start.19 = (s32[512]{0:T(512)S(1)}, s32[512]{0:T(512)}, u32[]{:S(2)}) copy-start(s32[512]{0:T(512)} %constant.164) | copy-start | bytes 6148
  0.7 18.4 %copy-start.20 = (s32[384]{0:T(512)S(1)}, s32[384]{0:T(512)}, u32[]{:S(2)}) copy-start(s32[384]{0:T(512)} %constant.161) | copy-start | bytes 4612
  0.7 18.4 %copy-start.13 = (bf16[128,512]{1,0:T(8,128)(2,1)S(1)}, bf16[128,512]{1,0:T(8,128)(2,1)}, u32[]{:S(2)}) copy-start(bf16[128,512]{1,0:T(8,128)(2,1)} %param.21) | copy-start | bytes 393220
  0.7 17.0 %copy-start.8 = (bf16[1024,384]{1,0:T(8,128)(2,1)S(1)}, bf16[1024,384]{1,0:T(8,128)(2,1)}, u32[]{:S(2)}) copy-start(bf16[1024,384]{1,0:T(8,128)(2,1)} %param.15) | copy-start | bytes 2359300
  0.7 18.0 %copy-start.21 = (s32[8,2]{0,1:T(2,128)S(1)}, s32[8,2]{0,1:T(2,128)}, u32[]{:S(2)}) copy-start(s32[8,2]{0,1:T(2,128)} %param.19) | copy-start | bytes 196
  0.7 18.0 %copy-start.18 = (s32[8,3]{0,1:T(4,128)S(1)}, s32[8,3]{0,1:T(4,128)}, u32[]{:S(2)}) copy-start(s32[8,3]{0,1:T(4,128)} %param.17) | copy-start | bytes 292
  5.6 13.7 %collective-permute-start.3 = (bf16[163840]{0:T(1024)(128)(2,1)}, bf16[163840]{0:T(1024)(128)(2,1)S(1)}, u32[]{:S(2)}, u32[]{:S(2)}) collective-permute-start(bf16[163840]{0:T(1024)(128)(2,1)} %constant_dynamic-update-slice_fusion.14), channel_id=1, source_target_pairs={{0,62},{1,63},{2,0},{3,1},{4,2},{5,3},{6,4},{7,5},{8,6},{9,7},{10,... | collective-permute-start | bytes 983048 | tf_op jit(solution)/shard_map/ppermute | solution.py:18
  8.4 11.2 %collective-permute-start.2 = (bf16[163840]{0:T(1024)(128)(2,1)}, bf16[163840]{0:T(1024)(128)(2,1)S(1)}, u32[]{:S(2)}, u32[]{:S(2)}) collective-permute-start(bf16[163840]{0:T(1024)(128)(2,1)} %constant_dynamic-update-slice_fusion.14), channel_id=1, source_target_pairs={{0,63},{1,0},{2,1},{3,2},{4,3},{5,4},{6,5},{7,6},{8,7},{9,8},{10,9... | collective-permute-start | bytes 983048 | tf_op jit(solution)/shard_map/ppermute | solution.py:18
  10.3 13.5 %collective-permute-start.1 = (bf16[163840]{0:T(1024)(128)(2,1)}, bf16[163840]{0:T(1024)(128)(2,1)S(1)}, u32[]{:S(2)}, u32[]{:S(2)}) collective-permute-start(bf16[163840]{0:T(1024)(128)(2,1)} %constant_dynamic-update-slice_fusion.14), channel_id=1, source_target_pairs={{0,2},{1,3},{2,4},{3,5},{4,6},{5,7},{6,8},{7,9},{8,10},{9,11},{10,... | collective-permute-start | bytes 983048 | tf_op jit(solution)/shard_map/ppermute | solution.py:18
  15.5 10.5 %collective-permute-start = (bf16[163840]{0:T(1024)(128)(2,1)}, bf16[163840]{0:T(1024)(128)(2,1)S(1)}, u32[]{:S(2)}, u32[]{:S(2)}) collective-permute-start(bf16[163840]{0:T(1024)(128)(2,1)} %constant_dynamic-update-slice_fusion.14), channel_id=1, source_target_pairs={{0,1},{1,2},{2,3},{3,4},{4,5},{5,6},{6,7},{7,8},{8,9},{9,10},{10,1... | collective-permute-start | bytes 983048 | tf_op jit(solution)/shard_map/ppermute | solution.py:18
  38.0 3.5 %copy-start.4 = (bf16[8,384,128]{1,2,0:T(8,128)(2,1)}, bf16[8,384,128]{1,2,0:T(8,128)(2,1)S(1)}, u32[]{:S(2)}) copy-start(bf16[8,384,128]{1,2,0:T(8,128)(2,1)S(1)} %bitcast_convert_fusion) | copy-start | bytes 2359300
  38.0 1.4 copy-start.9
  38.0 1.5 copy-start.22
  39.5 2.0 %copy-start.14 = (bf16[384,512]{1,0:T(8,128)(2,1)S(1)}, bf16[384,512]{1,0:T(8,128)(2,1)}, u32[]{:S(2)}) copy-start(bf16[384,512]{1,0:T(8,128)(2,1)} %param.24) | copy-start | bytes 1179652
  41.5 1.7 %copy-start.11 = (bf16[1024,384]{1,0:T(8,128)(2,1)}, bf16[1024,384]{1,0:T(8,128)(2,1)S(1)}, u32[]{:S(2)}) copy-start(bf16[1024,384]{1,0:T(8,128)(2,1)S(1)} %get-tuple-element.9) | copy-start | bytes 2359300
  41.5 2.3 %copy-start.1 = (bf16[16,128,512]{2,1,0:T(8,128)(2,1)S(1)}, bf16[16,128,512]{2,1,0:T(8,128)(2,1)}, u32[]{:S(2)}) copy-start(bf16[16,128,512]{2,1,0:T(8,128)(2,1)} %gather_fusion.2) | copy-start | bytes 6291460
  41.5 2.3 %copy-start.23 = (s32[1024]{0:T(1024)S(1)}, s32[1024]{0:T(1024)}, u32[]{:S(2)}) copy-start(s32[1024]{0:T(1024)} %param.20) | copy-start | bytes 12292
  47.5 1.6 %copy-start.24 = (f32[1024,384]{1,0:T(8,128)S(1)}, f32[1024,384]{1,0:T(8,128)}, u32[]{:S(2)}) copy-start(f32[1024,384]{1,0:T(8,128)} %get-tuple-element.10) | copy-start | bytes 4718596
  50.3 2.5 %copy-start.2 = (bf16[1024,512]{1,0:T(8,128)(2,1)S(1)}, bf16[1024,512]{1,0:T(8,128)(2,1)}, u32[]{:S(2)}) copy-start(bf16[1024,512]{1,0:T(8,128)(2,1)} %convolution_convert_fusion) | copy-start | bytes 3145732
  69.7 1.4 copy-start.7
  71.4 1.6 %copy-start.6 = (f32[2,32,11776]{2,1,0:T(8,128)}, f32[2,32,11776]{2,1,0:T(8,128)S(1)}, u32[]{:S(2)}) copy-start(f32[2,32,11776]{2,1,0:T(8,128)S(1)} %constant_dynamic-update-slice_fusion.10) | copy-start | bytes 9043972
  73.1 4.8 %collective-permute-start.4 = (bf16[32,11776]{1,0:T(8,128)(2,1)S(1)}, bf16[32,11776]{1,0:T(8,128)(2,1)S(1)}, u32[]{:S(2)}, u32[]{:S(2)}) collective-permute-start(bf16[32,11776]{1,0:T(8,128)(2,1)S(1)} %fusion.9), channel_id=1, source_target_pairs={{0,1},{1,0},{2,3},{3,2},{4,5},{5,4},{6,7},{7,6},{8,9},{9,8},{10,11... | collective-permute-start | bytes 2261000 | tf_op jit(solution)/shard_map/ppermute | solution.py:23
  79.5 15.2 %collective-permute-start.5 = (bf16[8,11776]{1,0:T(8,128)(2,1)S(1)}, bf16[8,11776]{1,0:T(8,128)(2,1)S(1)}, u32[]{:S(2)}, u32[]{:S(2)}) collective-permute-start(bf16[8,11776]{1,0:T(8,128)(2,1)S(1)} %get-tuple-element.4), channel_id=1, source_target_pairs={{0,2},{1,3},{2,4},{3,5},{4,6},{5,7},{6,0},{7,1},{8,10},{9,11},{10,... | collective-permute-start | bytes 565256 | tf_op jit(solution)/shard_map/ppermute | solution.py:89
  89.4 13.6 %collective-permute-start.7 = (bf16[8,11776]{1,0:T(8,128)(2,1)S(1)}, bf16[8,11776]{1,0:T(8,128)(2,1)S(1)}, u32[]{:S(2)}, u32[]{:S(2)}) collective-permute-start(bf16[8,11776]{1,0:T(8,128)(2,1)S(1)} %get-tuple-element.5), channel_id=1, source_target_pairs={{0,6},{1,7},{2,0},{3,1},{4,2},{5,3},{6,4},{7,5},{8,14},{9,15},{10,... | collective-permute-start | bytes 565256 | tf_op jit(solution)/shard_map/ppermute | solution.py:89
  91.3 11.7 %collective-permute-start.6 = (bf16[8,11776]{1,0:T(8,128)(2,1)S(1)}, bf16[8,11776]{1,0:T(8,128)(2,1)S(1)}, u32[]{:S(2)}, u32[]{:S(2)}) collective-permute-start(bf16[8,11776]{1,0:T(8,128)(2,1)S(1)} %get-tuple-element.6), channel_id=1, source_target_pairs={{0,4},{1,5},{2,6},{3,7},{4,0},{5,1},{6,2},{7,3},{8,12},{9,13},{10,... | collective-permute-start | bytes 565256 | tf_op jit(solution)/shard_map/ppermute | solution.py:89
  103.3 6.5 %collective-permute-start.8 = (bf16[4,11776]{1,0:T(4,128)(2,1)S(1)}, bf16[4,11776]{1,0:T(4,128)(2,1)S(1)}, u32[]{:S(2)}, u32[]{:S(2)}) collective-permute-start(bf16[4,11776]{1,0:T(4,128)(2,1)S(1)} %fusion.15), channel_id=1, source_target_pairs={{0,8},{1,57},{2,10},{3,59},{4,12},{5,61},{6,14},{7,63},{8,0},{9,17... | collective-permute-start | bytes 282632 | tf_op jit(solution)/shard_map/ppermute | solution.py:120
  110.0 6.9 %collective-permute-start.9 = (bf16[2,11776]{1,0:T(2,128)(2,1)S(1)}, bf16[2,11776]{1,0:T(2,128)(2,1)S(1)}, u32[]{:S(2)}, u32[]{:S(2)}) collective-permute-start(bf16[2,11776]{1,0:T(2,128)(2,1)S(1)} %fusion.16), channel_id=1, source_target_pairs={{0,16},{1,49},{2,18},{3,51},{4,20},{5,53},{6,22},{7,55},{8,24},{9,... | collective-permute-start | bytes 141320 | tf_op jit(solution)/shard_map/ppermute | solution.py:120
  117.0 10.2 %collective-permute-start.10 = (f32[1,11776]{1,0:T(1,128)S(1)}, f32[1,11776]{1,0:T(1,128)S(1)}, u32[]{:S(2)}, u32[]{:S(2)}) collective-permute-start(f32[1,11776]{1,0:T(1,128)S(1)} %constant_dynamic-slice_fusion), channel_id=1, source_target_pairs={{0,32},{1,33},{2,34},{3,35},{4,36},{5,37},{6,38},{7,39},{8,40},{9,... | collective-permute-start | bytes 141320 | tf_op jit(solution)/shard_map/ppermute | solution.py:122
  127.3 13.0 %collective-permute-start.11 = (f32[11776]{0:T(1024)S(1)}, f32[11776]{0:T(1024)S(1)}, u32[]{:S(2)}, u32[]{:S(2)}) collective-permute-start(f32[11776]{0:T(1024)S(1)} %add_reduce_fusion), channel_id=1, source_target_pairs={{0,256},{64,320},{128,384},{192,448},{256,0},{320,64},{384,128},{4... | collective-permute-start | bytes 141320 | tf_op jit(solution)/shard_map/ppermute | solution.py:23
  140.4 6.9 %collective-permute-start.12 = (f32[11776]{0:T(1024)S(1)}, f32[11776]{0:T(1024)S(1)}, u32[]{:S(2)}, u32[]{:S(2)}) collective-permute-start(f32[11776]{0:T(1024)S(1)} %add.188), channel_id=1, source_target_pairs={{0,128},{64,192},{128,0},{192,64},{256,384},{320,448},{384,256},{4... | collective-permute-start | bytes 141320 | tf_op jit(solution)/shard_map/ppermute | solution.py:23
  147.3 6.0 %collective-permute-start.13 = (f32[11776]{0:T(1024)S(1)}, f32[11776]{0:T(1024)S(1)}, u32[]{:S(2)}, u32[]{:S(2)}) collective-permute-start(f32[11776]{0:T(1024)S(1)} %add.189), channel_id=1, source_target_pairs={{0,64},{64,0},{128,192},{192,128},{256,320},{320,256},{384,448},{4... | collective-permute-start | bytes 141320 | tf_op jit(solution)/shard_map/ppermute | solution.py:23
  (7 other events, 7.7 us)

commit v14 on v13

--- a/solution.py
+++ b/solution.py
@@ -157,6 +157,7 @@
     count = couplings.shape[0]
     blocks = gauges.reshape(count, BLOCK, width)
     patch_blocks = patches.reshape(-1, BLOCK, wide)
+    self_part = lax.optimization_barrier(jnp.dot(gauges, self_weight, preferred_element_type=f32))
     block_table, patch_table = neighbour_tables(blocks, send_list, patch_blocks)
     picked = block_table[adjacency]
     message = (
@@ -164,9 +165,7 @@
         .astype(bf16)
         .reshape(-1, width)
     )
-    pre_act = jnp.dot(message, message_weight, preferred_element_type=f32) + jnp.dot(
-        gauges, self_weight, preferred_element_type=f32
-    )
+    pre_act = jnp.dot(message, message_weight, preferred_element_type=f32) + self_part
     hidden = (gauges.astype(f32) + jax.nn.silu(pre_act)).astype(bf16)
     queries = jnp.dot(hidden, output_weight, preferred_element_type=f32).astype(bf16)
     table_keys = (

time: 157 us -> 156 us (level)
  matrix products: 19.5 us -> 21.7 us
    unnamed x63 -> x61, local copies, waits for them, and re-layouts: 11.6 us -> 11 us
  transfers between devices with their start and end apart: 14 -> 14, of which waited for: 11 -> 10; matrix products, arithmetic and copies ran while one was open for 2% -> 3% of each run, Pallas kernels for 0% -> 0%
where the time goes in v14:
time: 156 us; the launch traced here: 155 us
  starting transfers between devices  58 us (37%)
  local copies, waits for them, and re-layouts  36.5 us (23%)
  waiting for transfers between devices  34.9 us (22%)
  matrix products  21.7 us (14%)
  other arithmetic  2.68 us (2%)
  between operations  1.57 us (1%)
    ppermute x4, starting transfers between devices, swapped(): return lax.ppermute(shard, axis, [(i, i ^ mask) for i in range(count)])  22 us
    ppermute x3, starting transfers between devices, shifted_x(): return lax.ppermute(shard, 'dom', pairs)  15.2 us
    ppermute x4, starting transfers between devices, passed_along(): lax.ppermute(shard, axis, [(i, (i + by) % count) for i in range(count)])  12 us
    unnamed x61, local copies, waits for them, and re-layouts  11 us
    ppermute x2, waiting for transfers between devices, reduce_to_share(): got = lax.ppermute(other.astype(bf16), 'dom', pairs).astype(f32)  9.46 us
    ppermute x4, waiting for transfers between devices, swapped(): return lax.ppermute(shard, axis, [(i, i ^ mask) for i in range(count)])  8.51 us
    ppermute x3, waiting for transfers between devices, shifted_x(): return lax.ppermute(shard, 'dom', pairs)  8.28 us
    gather x4, local copies, waits for them, and re-layouts, reduce_to_share(): t[share_order(t.shape[0], n_dom, n_x)].reshape(2, n_y * n_x, -1)  6.89 us
  transfers between devices with their start and end apart: 14, of which 10 were waited for; matrix products, arithmetic and copies ran while one was open for 3% of the time, Pallas kernels for 0%

profile of v14, /device:TPU:6, one launch (start us, length us, event | category | flops | bytes accessed | tf_op | source)
XLA Modules:
  0.0 155.3 jit_solution(8760223903534569010)
XLA Ops:
  5.6 2.7 %collective-permute-start.3 = (bf16[163840]{0:T(1024)(128)(2,1)}, bf16[163840]{0:T(1024)(128)(2,1)S(1)}, u32[]{:S(2)}, u32[]{:S(2)}) collective-permute-start(bf16[163840]{0:T(1024)(128)(2,1)} %constant_dynamic-update-slice_fusion.14), channel_id=1, source_target_pairs={{0,62},{1,63},{2,0},{3,1},{4,2},{5,3},{6,4},{7,5},{8,6},{9,7},{10,... | collective-permute-start | bytes 983048 | tf_op jit(solution)/shard_map/ppermute | solution.py:18
  8.3 1.9 %collective-permute-start.2 = (bf16[163840]{0:T(1024)(128)(2,1)}, bf16[163840]{0:T(1024)(128)(2,1)S(1)}, u32[]{:S(2)}, u32[]{:S(2)}) collective-permute-start(bf16[163840]{0:T(1024)(128)(2,1)} %constant_dynamic-update-slice_fusion.14), channel_id=1, source_target_pairs={{0,63},{1,0},{2,1},{3,2},{4,3},{5,4},{6,5},{7,6},{8,7},{9,8},{10,9... | collective-permute-start | bytes 983048 | tf_op jit(solution)/shard_map/ppermute | solution.py:18
  10.3 5.2 %collective-permute-start.1 = (bf16[163840]{0:T(1024)(128)(2,1)}, bf16[163840]{0:T(1024)(128)(2,1)S(1)}, u32[]{:S(2)}, u32[]{:S(2)}) collective-permute-start(bf16[163840]{0:T(1024)(128)(2,1)} %constant_dynamic-update-slice_fusion.14), channel_id=1, source_target_pairs={{0,2},{1,3},{2,4},{3,5},{4,6},{5,7},{6,8},{7,9},{8,10},{9,11},{10,... | collective-permute-start | bytes 983048 | tf_op jit(solution)/shard_map/ppermute | solution.py:18
  15.5 2.1 %collective-permute-start = (bf16[163840]{0:T(1024)(128)(2,1)}, bf16[163840]{0:T(1024)(128)(2,1)S(1)}, u32[]{:S(2)}, u32[]{:S(2)}) collective-permute-start(bf16[163840]{0:T(1024)(128)(2,1)} %constant_dynamic-update-slice_fusion.14), channel_id=1, source_target_pairs={{0,1},{1,2},{2,3},{3,4},{4,5},{5,6},{6,7},{7,8},{8,9},{9,10},{10,1... | collective-permute-start | bytes 983048 | tf_op jit(solution)/shard_map/ppermute | solution.py:18
  19.0 2.8 %fusion.19 = f32[1024,384]{1,0:T(8,128)} fusion(bf16[1024,384]{1,0:T(8,128)(2,1)S(1)} %copy-done.3, bf16[384,384]{1,0:T(8,128)(2,1)} %param.23), kind=kOutput, calls=%fused_computation.76 | convolution fusion | flops 301989888 | bytes 2654208 | tf_op jit(solution)/shard_map/dot_general | solution.py:160
  24.0 1.9 %collective-permute-done = bf16[163840]{0:T(1024)(128)(2,1)S(1)} collective-permute-done((bf16[163840]{0:T(1024)(128)(2,1)}, bf16[163840]{0:T(1024)(128)(2,1)S(1)}, u32[]{:S(2)}, u32[]{:S(2)}) %collective-permute-start) | collective-permute-done | bytes 327712 | tf_op jit(solution)/shard_map/ppermute | solution.py:18
  26.3 2.0 %gather_fusion.6 = bf16[16,128,512]{2,1,0:T(8,128)(2,1)} fusion(bf16[5,128,512]{2,1,0:T(8,128)(2,1)S(1)} %constant_dynamic-update-slice_fusion.6, s32[1024]{0:T(1024)S(1)} %get-tuple-element.13), kind=kCustom, calls=%fused_computation.6 | custom fusion | bytes 4194368 | tf_op jit(solution)/shard_map/gather | solution.py:177
  29.9 2.0 %gather_fusion.2 = bf16[16,128,512]{2,1,0:T(8,128)(2,1)} fusion(bf16[5,128,512]{2,1,0:T(8,128)(2,1)S(1)} %bitcast.80, s32[1024]{0:T(1024)S(1)} %get-tuple-element.13), kind=kCustom, calls=%fused_computation.2 | custom fusion | bytes 4194368 | tf_op jit(solution)/shard_map/gather | solution.py:176
  34.7 2.5 %gather_fusion.1 = bf16[24,128,384]{2,1,0:T(8,128)(2,1)S(1)} fusion(bf16[16,128,384]{2,1,0:T(8,128)(2,1)} %constant_dynamic-update-slice_fusion.1, s32[1024]{0:T(1024)S(1)} %get-tuple-element.14), kind=kCustom, calls=%fused_computation.1 | custom fusion | bytes 4718688 | tf_op jit(solution)/shard_map/gather | solution.py:162
  39.0 2.0 %add_convert_fusion = (bf16[1024,384]{1,0:T(8,128)(2,1)S(1)}, f32[1024,384]{1,0:T(8,128)}) fusion(bf16[1024,384]{1,0:T(8,128)(2,1)S(1)} %copy-done.4, f32[1024,384]{1,0:T(8,128)S(1)} %copy-done.9, bf16[1024,384]{1,0:T(8,128)(2,1)S(1)} %bitcast.89, bf16[384,384]{1,0:T(8,128)(2,1)S(1)} %copy-done.21), kind=kOutput, calls=%fused_computation.14 | convolution fusion | flops 305135616 | bytes 5799936 | tf_op jit(solution)/shard_map/dot_general | solution.py:168
  43.3 3.3 %fusion.8 = bf16[8,128,256]{2,1,0:T(8,128)(2,1)S(1)} fusion(s32[8,128]{1,0:T(8,128)S(1)} %bitcast.93, bf16[8,128,512]{2,1,0:T(8,128)(2,1)} %bitcast.81, bf16[8,256,512]{2,1,0:T(8,128)(2,1)S(1)} %bitcast.77), kind=kOutput, calls=%fused_computation.28 | convolution fusion | flops 270535168 | bytes 3674112 | tf_op jit(solution)/shard_map/div | solution.py:183
  52.4 2.1 %multiply_convert_fusion = bf16[8,256,512]{2,1,0:T(8,128)(2,1)} fusion(bf16[8,128,256]{2,1,0:T(8,128)(2,1)S(1)} %fusion.8, bf16[8,128,512]{2,1,0:T(8,128)(2,1)S(1)} %bitcast.82), kind=kOutput, calls=%fused_computation.10 | convolution fusion | flops 270532608 | bytes 3670016 | tf_op jit(solution)/shard_map/bij,bie->bje/dot_general | solution.py:196
  55.8 1.9 %gather_fusion.4 = f32[384,384]{1,0:T(8,128)S(1)} fusion(f32[384,384]{1,0:T(8,128)S(1)} %copy.25, s32[1024]{0:T(1024)S(1)} %get-tuple-element.12), kind=kCustom, calls=%fused_computation.4 | custom fusion | bytes 1181184 | tf_op jit(solution)/shard_map/gather | solution.py:97
  64.2 3.5 %fusion.22 = f32[512,512]{1,0:T(8,128)S(1)} fusion(bf16[2048,512]{1,0:T(8,128)(2,1)} %bitcast.85, bf16[2048,512]{1,0:T(8,128)(2,1)} %bitcast.86), kind=kOutput, calls=%fused_computation.79 | convolution fusion | flops 1073741824 | bytes 5242880 | tf_op jit(solution)/shard_map/dot_general | solution.py:202
  72.7 2.9 %collective-permute-start.4 = (bf16[32,11776]{1,0:T(8,128)(2,1)S(1)}, bf16[32,11776]{1,0:T(8,128)(2,1)S(1)}, u32[]{:S(2)}, u32[]{:S(2)}) collective-permute-start(bf16[32,11776]{1,0:T(8,128)(2,1)S(1)} %fusion.9), channel_id=1, source_target_pairs={{0,1},{1,0},{2,3},{3,2},{4,5},{5,4},{6,7},{7,6},{8,9},{9,8},{10,11... | collective-permute-start | bytes 2261000 | tf_op jit(solution)/shard_map/ppermute | solution.py:23
  75.8 1.7 %collective-permute-done.4 = bf16[32,11776]{1,0:T(8,128)(2,1)S(1)} collective-permute-done((bf16[32,11776]{1,0:T(8,128)(2,1)S(1)}, bf16[32,11776]{1,0:T(8,128)(2,1)S(1)}, u32[]{:S(2)}, u32[]{:S(2)}) %collective-permute-start.4) | collective-permute-done | bytes 753696 | tf_op jit(solution)/shard_map/ppermute | solution.py:23
  79.1 9.9 %collective-permute-start.5 = (bf16[8,11776]{1,0:T(8,128)(2,1)S(1)}, bf16[8,11776]{1,0:T(8,128)(2,1)S(1)}, u32[]{:S(2)}, u32[]{:S(2)}) collective-permute-start(bf16[8,11776]{1,0:T(8,128)(2,1)S(1)} %get-tuple-element.4), channel_id=1, source_target_pairs={{0,2},{1,3},{2,4},{3,5},{4,6},{5,7},{6,0},{7,1},{8,10},{9,11},{10,... | collective-permute-start | bytes 565256 | tf_op jit(solution)/shard_map/ppermute | solution.py:89
  89.0 1.9 %collective-permute-start.7 = (bf16[8,11776]{1,0:T(8,128)(2,1)S(1)}, bf16[8,11776]{1,0:T(8,128)(2,1)S(1)}, u32[]{:S(2)}, u32[]{:S(2)}) collective-permute-start(bf16[8,11776]{1,0:T(8,128)(2,1)S(1)} %get-tuple-element.5), channel_id=1, source_target_pairs={{0,6},{1,7},{2,0},{3,1},{4,2},{5,3},{6,4},{7,5},{8,14},{9,15},{10,... | collective-permute-start | bytes 565256 | tf_op jit(solution)/shard_map/ppermute | solution.py:89
  90.9 3.4 %collective-permute-start.6 = (bf16[8,11776]{1,0:T(8,128)(2,1)S(1)}, bf16[8,11776]{1,0:T(8,128)(2,1)S(1)}, u32[]{:S(2)}, u32[]{:S(2)}) collective-permute-start(bf16[8,11776]{1,0:T(8,128)(2,1)S(1)} %get-tuple-element.6), channel_id=1, source_target_pairs={{0,4},{1,5},{2,6},{3,7},{4,0},{5,1},{6,2},{7,3},{8,12},{9,13},{10,... | collective-permute-start | bytes 565256 | tf_op jit(solution)/shard_map/ppermute | solution.py:89
  94.3 8.3 %collective-permute-done.7 = bf16[8,11776]{1,0:T(8,128)(2,1)S(1)} collective-permute-done((bf16[8,11776]{1,0:T(8,128)(2,1)S(1)}, bf16[8,11776]{1,0:T(8,128)(2,1)S(1)}, u32[]{:S(2)}, u32[]{:S(2)}) %collective-permute-start.7) | collective-permute-done | bytes 188448 | tf_op jit(solution)/shard_map/ppermute | solution.py:89
  102.8 1.9 %collective-permute-start.8 = (bf16[4,11776]{1,0:T(4,128)(2,1)S(1)}, bf16[4,11776]{1,0:T(4,128)(2,1)S(1)}, u32[]{:S(2)}, u32[]{:S(2)}) collective-permute-start(bf16[4,11776]{1,0:T(4,128)(2,1)S(1)} %fusion.15), channel_id=1, source_target_pairs={{0,8},{1,57},{2,10},{3,59},{4,12},{5,61},{6,14},{7,63},{8,0},{9,17... | collective-permute-start | bytes 282632 | tf_op jit(solution)/shard_map/ppermute | solution.py:120
  104.8 4.5 %collective-permute-done.8 = bf16[4,11776]{1,0:T(4,128)(2,1)S(1)} collective-permute-done((bf16[4,11776]{1,0:T(4,128)(2,1)S(1)}, bf16[4,11776]{1,0:T(4,128)(2,1)S(1)}, u32[]{:S(2)}, u32[]{:S(2)}) %collective-permute-start.8) | collective-permute-done | bytes 94240 | tf_op jit(solution)/shard_map/ppermute | solution.py:120
  109.6 1.9 %collective-permute-start.9 = (bf16[2,11776]{1,0:T(2,128)(2,1)S(1)}, bf16[2,11776]{1,0:T(2,128)(2,1)S(1)}, u32[]{:S(2)}, u32[]{:S(2)}) collective-permute-start(bf16[2,11776]{1,0:T(2,128)(2,1)S(1)} %fusion.16), channel_id=1, source_target_pairs={{0,16},{1,49},{2,18},{3,51},{4,20},{5,53},{6,22},{7,55},{8,24},{9,... | collective-permute-start | bytes 141320 | tf_op jit(solution)/shard_map/ppermute | solution.py:120
  111.5 4.9 %collective-permute-done.9 = bf16[2,11776]{1,0:T(2,128)(2,1)S(1)} collective-permute-done((bf16[2,11776]{1,0:T(2,128)(2,1)S(1)}, bf16[2,11776]{1,0:T(2,128)(2,1)S(1)}, u32[]{:S(2)}, u32[]{:S(2)}) %collective-permute-start.9) | collective-permute-done | bytes 47136 | tf_op jit(solution)/shard_map/ppermute | solution.py:120
  116.6 5.0 %collective-permute-start.10 = (f32[1,11776]{1,0:T(1,128)S(1)}, f32[1,11776]{1,0:T(1,128)S(1)}, u32[]{:S(2)}, u32[]{:S(2)}) collective-permute-start(f32[1,11776]{1,0:T(1,128)S(1)} %constant_dynamic-slice_fusion), channel_id=1, source_target_pairs={{0,32},{1,33},{2,34},{3,35},{4,36},{5,37},{6,38},{7,39},{8,40},{9,... | collective-permute-start | bytes 141320 | tf_op jit(solution)/shard_map/ppermute | solution.py:122
  121.6 5.2 %collective-permute-done.10 = f32[1,11776]{1,0:T(1,128)S(1)} collective-permute-done((f32[1,11776]{1,0:T(1,128)S(1)}, f32[1,11776]{1,0:T(1,128)S(1)}, u32[]{:S(2)}, u32[]{:S(2)}) %collective-permute-start.10) | collective-permute-done | bytes 47136 | tf_op jit(solution)/shard_map/ppermute | solution.py:122
  126.9 10.9 %collective-permute-start.11 = (f32[11776]{0:T(1024)S(1)}, f32[11776]{0:T(1024)S(1)}, u32[]{:S(2)}, u32[]{:S(2)}) collective-permute-start(f32[11776]{0:T(1024)S(1)} %add_reduce_fusion), channel_id=1, source_target_pairs={{0,256},{64,320},{128,384},{192,448},{256,0},{320,64},{384,128},{4... | collective-permute-start | bytes 141320 | tf_op jit(solution)/shard_map/ppermute | solution.py:23
  137.8 2.1 %collective-permute-done.11 = f32[11776]{0:T(1024)S(1)} collective-permute-done((f32[11776]{0:T(1024)S(1)}, f32[11776]{0:T(1024)S(1)}, u32[]{:S(2)}, u32[]{:S(2)}) %collective-permute-start.11) | collective-permute-done | bytes 47136 | tf_op jit(solution)/shard_map/ppermute | solution.py:23
  139.9 4.8 %collective-permute-start.12 = (f32[11776]{0:T(1024)S(1)}, f32[11776]{0:T(1024)S(1)}, u32[]{:S(2)}, u32[]{:S(2)}) collective-permute-start(f32[11776]{0:T(1024)S(1)} %add.188), channel_id=1, source_target_pairs={{0,128},{64,192},{128,0},{192,64},{256,384},{320,448},{384,256},{4... | collective-permute-start | bytes 141320 | tf_op jit(solution)/shard_map/ppermute | solution.py:23
  144.8 2.1 %collective-permute-done.12 = f32[11776]{0:T(1024)S(1)} collective-permute-done((f32[11776]{0:T(1024)S(1)}, f32[11776]{0:T(1024)S(1)}, u32[]{:S(2)}, u32[]{:S(2)}) %collective-permute-start.12) | collective-permute-done | bytes 47136 | tf_op jit(solution)/shard_map/ppermute | solution.py:23
  146.9 3.4 %collective-permute-start.13 = (f32[11776]{0:T(1024)S(1)}, f32[11776]{0:T(1024)S(1)}, u32[]{:S(2)}, u32[]{:S(2)}) collective-permute-start(f32[11776]{0:T(1024)S(1)} %add.189), channel_id=1, source_target_pairs={{0,64},{64,0},{128,192},{192,128},{256,320},{320,256},{384,448},{4... | collective-permute-start | bytes 141320 | tf_op jit(solution)/shard_map/ppermute | solution.py:23
  150.2 2.6 %collective-permute-done.13 = f32[11776]{0:T(1024)S(1)} collective-permute-done((f32[11776]{0:T(1024)S(1)}, f32[11776]{0:T(1024)S(1)}, u32[]{:S(2)}, u32[]{:S(2)}) %collective-permute-start.13) | collective-permute-done | bytes 47136 | tf_op jit(solution)/shard_map/ppermute | solution.py:23
  (136 shorter events, 40.2 us)
Async XLA Ops:
  0.6 36.6 %copy-start = (bf16[8,3,128,128]{3,2,1,0:T(8,128)(2,1)S(1)}, bf16[8,3,128,128]{3,2,1,0:T(8,128)(2,1)}, u32[]{:S(2)}) copy-start(bf16[8,3,128,128]{3,2,1,0:T(8,128)(2,1)} %param.16) | copy-start | bytes 2359300
  0.6 17.0 %copy-start.3 = (bf16[1024,384]{1,0:T(8,128)(2,1)S(1)}, bf16[1024,384]{1,0:T(8,128)(2,1)}, u32[]{:S(2)}) copy-start(bf16[1024,384]{1,0:T(8,128)(2,1)} %param.15) | copy-start | bytes 2359300
  0.7 18.0 %copy-start.20 = (s32[8,2]{0,1:T(2,128)S(1)}, s32[8,2]{0,1:T(2,128)}, u32[]{:S(2)}) copy-start(s32[8,2]{0,1:T(2,128)} %param.19) | copy-start | bytes 196
  0.7 18.0 %copy-start.17 = (s32[8,3]{0,1:T(4,128)S(1)}, s32[8,3]{0,1:T(4,128)}, u32[]{:S(2)}) copy-start(s32[8,3]{0,1:T(4,128)} %param.17) | copy-start | bytes 292
  5.6 16.2 %collective-permute-start.3 = (bf16[163840]{0:T(1024)(128)(2,1)}, bf16[163840]{0:T(1024)(128)(2,1)S(1)}, u32[]{:S(2)}, u32[]{:S(2)}) collective-permute-start(bf16[163840]{0:T(1024)(128)(2,1)} %constant_dynamic-update-slice_fusion.14), channel_id=1, source_target_pairs={{0,62},{1,63},{2,0},{3,1},{4,2},{5,3},{6,4},{7,5},{8,6},{9,7},{10,... | collective-permute-start | bytes 983048 | tf_op jit(solution)/shard_map/ppermute | solution.py:18
  8.3 13.7 %collective-permute-start.2 = (bf16[163840]{0:T(1024)(128)(2,1)}, bf16[163840]{0:T(1024)(128)(2,1)S(1)}, u32[]{:S(2)}, u32[]{:S(2)}) collective-permute-start(bf16[163840]{0:T(1024)(128)(2,1)} %constant_dynamic-update-slice_fusion.14), channel_id=1, source_target_pairs={{0,63},{1,0},{2,1},{3,2},{4,3},{5,4},{6,5},{7,6},{8,7},{9,8},{10,9... | collective-permute-start | bytes 983048 | tf_op jit(solution)/shard_map/ppermute | solution.py:18
  10.3 13.5 %collective-permute-start.1 = (bf16[163840]{0:T(1024)(128)(2,1)}, bf16[163840]{0:T(1024)(128)(2,1)S(1)}, u32[]{:S(2)}, u32[]{:S(2)}) collective-permute-start(bf16[163840]{0:T(1024)(128)(2,1)} %constant_dynamic-update-slice_fusion.14), channel_id=1, source_target_pairs={{0,2},{1,3},{2,4},{3,5},{4,6},{5,7},{6,8},{7,9},{8,10},{9,11},{10,... | collective-permute-start | bytes 983048 | tf_op jit(solution)/shard_map/ppermute | solution.py:18
  15.5 10.5 %collective-permute-start = (bf16[163840]{0:T(1024)(128)(2,1)}, bf16[163840]{0:T(1024)(128)(2,1)S(1)}, u32[]{:S(2)}, u32[]{:S(2)}) collective-permute-start(bf16[163840]{0:T(1024)(128)(2,1)} %constant_dynamic-update-slice_fusion.14), channel_id=1, source_target_pairs={{0,1},{1,2},{2,3},{3,4},{4,5},{5,6},{6,7},{7,8},{8,9},{9,10},{10,1... | collective-permute-start | bytes 983048 | tf_op jit(solution)/shard_map/ppermute | solution.py:18
  17.6 4.1 %copy-start.18 = (s32[512]{0:T(512)S(1)}, s32[512]{0:T(512)}, u32[]{:S(2)}) copy-start(s32[512]{0:T(512)} %constant.164) | copy-start | bytes 6148
  17.7 4.1 %copy-start.19 = (s32[384]{0:T(512)S(1)}, s32[384]{0:T(512)}, u32[]{:S(2)}) copy-start(s32[384]{0:T(512)} %constant.161) | copy-start | bytes 4612
  17.7 4.1 %copy-start.14 = (bf16[128,512]{1,0:T(8,128)(2,1)S(1)}, bf16[128,512]{1,0:T(8,128)(2,1)}, u32[]{:S(2)}) copy-start(bf16[128,512]{1,0:T(8,128)(2,1)} %param.21) | copy-start | bytes 393220
  37.2 1.6 %copy-start.9 = (f32[1024,384]{1,0:T(8,128)S(1)}, f32[1024,384]{1,0:T(8,128)}, u32[]{:S(2)}) copy-start(f32[1024,384]{1,0:T(8,128)} %fusion.19) | copy-start | bytes 4718596
  37.3 1.8 %copy-start.21 = (bf16[384,384]{1,0:T(8,128)(2,1)S(1)}, bf16[384,384]{1,0:T(8,128)(2,1)}, u32[]{:S(2)}) copy-start(bf16[384,384]{1,0:T(8,128)(2,1)} %param.22) | copy-start | bytes 884740
  38.0 3.1 %copy-start.12 = (bf16[8,384,128]{1,2,0:T(8,128)(2,1)}, bf16[8,384,128]{1,2,0:T(8,128)(2,1)S(1)}, u32[]{:S(2)}) copy-start(bf16[8,384,128]{1,2,0:T(8,128)(2,1)S(1)} %bitcast_convert_fusion) | copy-start | bytes 2359300
  39.0 2.0 %copy-start.15 = (bf16[384,512]{1,0:T(8,128)(2,1)S(1)}, bf16[384,512]{1,0:T(8,128)(2,1)}, u32[]{:S(2)}) copy-start(bf16[384,512]{1,0:T(8,128)(2,1)} %param.24) | copy-start | bytes 1179652
  41.1 1.7 %copy-start.10 = (bf16[1024,384]{1,0:T(8,128)(2,1)}, bf16[1024,384]{1,0:T(8,128)(2,1)S(1)}, u32[]{:S(2)}) copy-start(bf16[1024,384]{1,0:T(8,128)(2,1)S(1)} %get-tuple-element.9) | copy-start | bytes 2359300
  41.1 2.3 %copy-start.1 = (bf16[16,128,512]{2,1,0:T(8,128)(2,1)S(1)}, bf16[16,128,512]{2,1,0:T(8,128)(2,1)}, u32[]{:S(2)}) copy-start(bf16[16,128,512]{2,1,0:T(8,128)(2,1)} %gather_fusion.2) | copy-start | bytes 6291460
  41.1 2.3 %copy-start.22 = (s32[1024]{0:T(1024)S(1)}, s32[1024]{0:T(1024)}, u32[]{:S(2)}) copy-start(s32[1024]{0:T(1024)} %param.20) | copy-start | bytes 12292
  47.1 1.6 %copy-start.23 = (f32[1024,384]{1,0:T(8,128)S(1)}, f32[1024,384]{1,0:T(8,128)}, u32[]{:S(2)}) copy-start(f32[1024,384]{1,0:T(8,128)} %get-tuple-element.10) | copy-start | bytes 4718596
  49.8 2.6 %copy-start.2 = (bf16[1024,512]{1,0:T(8,128)(2,1)S(1)}, bf16[1024,512]{1,0:T(8,128)(2,1)}, u32[]{:S(2)}) copy-start(bf16[1024,512]{1,0:T(8,128)(2,1)} %convolution_convert_fusion) | copy-start | bytes 3145732
  69.3 1.4 copy-start.8
  71.0 1.6 %copy-start.7 = (f32[2,32,11776]{2,1,0:T(8,128)}, f32[2,32,11776]{2,1,0:T(8,128)S(1)}, u32[]{:S(2)}) copy-start(f32[2,32,11776]{2,1,0:T(8,128)S(1)} %constant_dynamic-update-slice_fusion.10) | copy-start | bytes 9043972
  72.7 4.8 %collective-permute-start.4 = (bf16[32,11776]{1,0:T(8,128)(2,1)S(1)}, bf16[32,11776]{1,0:T(8,128)(2,1)S(1)}, u32[]{:S(2)}, u32[]{:S(2)}) collective-permute-start(bf16[32,11776]{1,0:T(8,128)(2,1)S(1)} %fusion.9), channel_id=1, source_target_pairs={{0,1},{1,0},{2,3},{3,2},{4,5},{5,4},{6,7},{7,6},{8,9},{9,8},{10,11... | collective-permute-start | bytes 2261000 | tf_op jit(solution)/shard_map/ppermute | solution.py:23
  79.1 15.2 %collective-permute-start.5 = (bf16[8,11776]{1,0:T(8,128)(2,1)S(1)}, bf16[8,11776]{1,0:T(8,128)(2,1)S(1)}, u32[]{:S(2)}, u32[]{:S(2)}) collective-permute-start(bf16[8,11776]{1,0:T(8,128)(2,1)S(1)} %get-tuple-element.4), channel_id=1, source_target_pairs={{0,2},{1,3},{2,4},{3,5},{4,6},{5,7},{6,0},{7,1},{8,10},{9,11},{10,... | collective-permute-start | bytes 565256 | tf_op jit(solution)/shard_map/ppermute | solution.py:89
  89.0 13.6 %collective-permute-start.7 = (bf16[8,11776]{1,0:T(8,128)(2,1)S(1)}, bf16[8,11776]{1,0:T(8,128)(2,1)S(1)}, u32[]{:S(2)}, u32[]{:S(2)}) collective-permute-start(bf16[8,11776]{1,0:T(8,128)(2,1)S(1)} %get-tuple-element.5), channel_id=1, source_target_pairs={{0,6},{1,7},{2,0},{3,1},{4,2},{5,3},{6,4},{7,5},{8,14},{9,15},{10,... | collective-permute-start | bytes 565256 | tf_op jit(solution)/shard_map/ppermute | solution.py:89
  90.9 11.7 %collective-permute-start.6 = (bf16[8,11776]{1,0:T(8,128)(2,1)S(1)}, bf16[8,11776]{1,0:T(8,128)(2,1)S(1)}, u32[]{:S(2)}, u32[]{:S(2)}) collective-permute-start(bf16[8,11776]{1,0:T(8,128)(2,1)S(1)} %get-tuple-element.6), channel_id=1, source_target_pairs={{0,4},{1,5},{2,6},{3,7},{4,0},{5,1},{6,2},{7,3},{8,12},{9,13},{10,... | collective-permute-start | bytes 565256 | tf_op jit(solution)/shard_map/ppermute | solution.py:89
  102.8 6.5 %collective-permute-start.8 = (bf16[4,11776]{1,0:T(4,128)(2,1)S(1)}, bf16[4,11776]{1,0:T(4,128)(2,1)S(1)}, u32[]{:S(2)}, u32[]{:S(2)}) collective-permute-start(bf16[4,11776]{1,0:T(4,128)(2,1)S(1)} %fusion.15), channel_id=1, source_target_pairs={{0,8},{1,57},{2,10},{3,59},{4,12},{5,61},{6,14},{7,63},{8,0},{9,17... | collective-permute-start | bytes 282632 | tf_op jit(solution)/shard_map/ppermute | solution.py:120
  109.6 6.9 %collective-permute-start.9 = (bf16[2,11776]{1,0:T(2,128)(2,1)S(1)}, bf16[2,11776]{1,0:T(2,128)(2,1)S(1)}, u32[]{:S(2)}, u32[]{:S(2)}) collective-permute-start(bf16[2,11776]{1,0:T(2,128)(2,1)S(1)} %fusion.16), channel_id=1, source_target_pairs={{0,16},{1,49},{2,18},{3,51},{4,20},{5,53},{6,22},{7,55},{8,24},{9,... | collective-permute-start | bytes 141320 | tf_op jit(solution)/shard_map/ppermute | solution.py:120
  116.6 10.2 %collective-permute-start.10 = (f32[1,11776]{1,0:T(1,128)S(1)}, f32[1,11776]{1,0:T(1,128)S(1)}, u32[]{:S(2)}, u32[]{:S(2)}) collective-permute-start(f32[1,11776]{1,0:T(1,128)S(1)} %constant_dynamic-slice_fusion), channel_id=1, source_target_pairs={{0,32},{1,33},{2,34},{3,35},{4,36},{5,37},{6,38},{7,39},{8,40},{9,... | collective-permute-start | bytes 141320 | tf_op jit(solution)/shard_map/ppermute | solution.py:122
  126.9 13.0 %collective-permute-start.11 = (f32[11776]{0:T(1024)S(1)}, f32[11776]{0:T(1024)S(1)}, u32[]{:S(2)}, u32[]{:S(2)}) collective-permute-start(f32[11776]{0:T(1024)S(1)} %add_reduce_fusion), channel_id=1, source_target_pairs={{0,256},{64,320},{128,384},{192,448},{256,0},{320,64},{384,128},{4... | collective-permute-start | bytes 141320 | tf_op jit(solution)/shard_map/ppermute | solution.py:23
  139.9 6.9 %collective-permute-start.12 = (f32[11776]{0:T(1024)S(1)}, f32[11776]{0:T(1024)S(1)}, u32[]{:S(2)}, u32[]{:S(2)}) collective-permute-start(f32[11776]{0:T(1024)S(1)} %add.188), channel_id=1, source_target_pairs={{0,128},{64,192},{128,0},{192,64},{256,384},{320,448},{384,256},{4... | collective-permute-start | bytes 141320 | tf_op jit(solution)/shard_map/ppermute | solution.py:23
  146.9 6.0 %collective-permute-start.13 = (f32[11776]{0:T(1024)S(1)}, f32[11776]{0:T(1024)S(1)}, u32[]{:S(2)}, u32[]{:S(2)}) collective-permute-start(f32[11776]{0:T(1024)S(1)} %add.189), channel_id=1, source_target_pairs={{0,64},{64,0},{128,192},{192,128},{256,320},{320,256},{384,448},{4... | collective-permute-start | bytes 141320 | tf_op jit(solution)/shard_map/ppermute | solution.py:23
  (6 other events, 7.2 us)

commit v15 on v14

--- a/solution.py
+++ b/solution.py
@@ -124,14 +124,16 @@
     share = held.reshape(-1)
     n_region = lax.axis_size("region")
     step = n_region // 2
-    while step >= 1:
+    while step > 1:
         share = share + swapped(share, "region", step)
         step //= 2
+    partner = swapped(share, "region", 1)
     pieces = []
     start = 0
     for t in terms:
         size = t.size // n_dom
-        pieces.append(share[start : start + size].reshape(t.shape[0] // n_dom, t.shape[1]))
+        piece = share[start : start + size] + partner[start : start + size]
+        pieces.append(piece.astype(bf16).reshape(t.shape[0] // n_dom, t.shape[1]))
         start += size
     return pieces
 
@@ -208,7 +210,7 @@
     shares = reduce_to_share(
         [grad_message, grad_self, grad_output, grad_patch], lax.axis_size("dom"), n_x
     )
-    return tuple(s.astype(bf16) for s in shares)
+    return tuple(shares)
 
 
 def solution(mesh):

time: 156 us -> 156 us (level)
  no operation moved by 1% of the time
where the time goes in v15:
time: 156 us; the launch traced here: 155 us
  starting transfers between devices  58 us (37%)
  local copies, waits for them, and re-layouts  36.5 us (23%)
  waiting for transfers between devices  34.9 us (22%)
  matrix products  21.7 us (14%)
  other arithmetic  2.69 us (2%)
    ppermute x4, starting transfers between devices, swapped(): return lax.ppermute(shard, axis, [(i, i ^ mask) for i in range(count)])  22 us
    ppermute x3, starting transfers between devices, shifted_x(): return lax.ppermute(shard, 'dom', pairs)  15.2 us
    ppermute x4, starting transfers between devices, passed_along(): lax.ppermute(shard, axis, [(i, (i + by) % count) for i in range(count)])  12 us
    unnamed x61, local copies, waits for them, and re-layouts  11 us
    ppermute x2, waiting for transfers between devices, reduce_to_share(): got = lax.ppermute(other.astype(bf16), 'dom', pairs).astype(f32)  9.46 us
    ppermute x4, waiting for transfers between devices, swapped(): return lax.ppermute(shard, axis, [(i, i ^ mask) for i in range(count)])  8.51 us
    ppermute x3, waiting for transfers between devices, shifted_x(): return lax.ppermute(shard, 'dom', pairs)  8.28 us
    gather x4, local copies, waits for them, and re-layouts, reduce_to_share(): t[share_order(t.shape[0], n_dom, n_x)].reshape(2, n_y * n_x, -1)  6.89 us
  transfers between devices with their start and end apart: 14, of which 10 were waited for; matrix products, arithmetic and copies ran while one was open for 3% of the time, Pallas kernels for 0%

profile of v15, /device:TPU:6, one launch (start us, length us, event | category | flops | bytes accessed | tf_op | source)
XLA Modules:
  0.0 155.3 jit_solution(17216152512100846983)
XLA Ops:
  5.6 2.7 %collective-permute-start.3 = (bf16[163840]{0:T(1024)(128)(2,1)}, bf16[163840]{0:T(1024)(128)(2,1)S(1)}, u32[]{:S(2)}, u32[]{:S(2)}) collective-permute-start(bf16[163840]{0:T(1024)(128)(2,1)} %constant_dynamic-update-slice_fusion.14), channel_id=1, source_target_pairs={{0,62},{1,63},{2,0},{3,1},{4,2},{5,3},{6,4},{7,5},{8,6},{9,7},{10,... | collective-permute-start | bytes 983048 | tf_op jit(solution)/shard_map/ppermute | solution.py:18
  8.3 1.9 %collective-permute-start.2 = (bf16[163840]{0:T(1024)(128)(2,1)}, bf16[163840]{0:T(1024)(128)(2,1)S(1)}, u32[]{:S(2)}, u32[]{:S(2)}) collective-permute-start(bf16[163840]{0:T(1024)(128)(2,1)} %constant_dynamic-update-slice_fusion.14), channel_id=1, source_target_pairs={{0,63},{1,0},{2,1},{3,2},{4,3},{5,4},{6,5},{7,6},{8,7},{9,8},{10,9... | collective-permute-start | bytes 983048 | tf_op jit(solution)/shard_map/ppermute | solution.py:18
  10.3 5.2 %collective-permute-start.1 = (bf16[163840]{0:T(1024)(128)(2,1)}, bf16[163840]{0:T(1024)(128)(2,1)S(1)}, u32[]{:S(2)}, u32[]{:S(2)}) collective-permute-start(bf16[163840]{0:T(1024)(128)(2,1)} %constant_dynamic-update-slice_fusion.14), channel_id=1, source_target_pairs={{0,2},{1,3},{2,4},{3,5},{4,6},{5,7},{6,8},{7,9},{8,10},{9,11},{10,... | collective-permute-start | bytes 983048 | tf_op jit(solution)/shard_map/ppermute | solution.py:18
  15.5 2.1 %collective-permute-start = (bf16[163840]{0:T(1024)(128)(2,1)}, bf16[163840]{0:T(1024)(128)(2,1)S(1)}, u32[]{:S(2)}, u32[]{:S(2)}) collective-permute-start(bf16[163840]{0:T(1024)(128)(2,1)} %constant_dynamic-update-slice_fusion.14), channel_id=1, source_target_pairs={{0,1},{1,2},{2,3},{3,4},{4,5},{5,6},{6,7},{7,8},{8,9},{9,10},{10,1... | collective-permute-start | bytes 983048 | tf_op jit(solution)/shard_map/ppermute | solution.py:18
  19.0 2.8 %fusion.22 = f32[1024,384]{1,0:T(8,128)} fusion(bf16[1024,384]{1,0:T(8,128)(2,1)S(1)} %copy-done.3, bf16[384,384]{1,0:T(8,128)(2,1)} %param.23), kind=kOutput, calls=%fused_computation.82 | convolution fusion | flops 301989888 | bytes 2654208 | tf_op jit(solution)/shard_map/dot_general | solution.py:162
  24.0 1.9 %collective-permute-done = bf16[163840]{0:T(1024)(128)(2,1)S(1)} collective-permute-done((bf16[163840]{0:T(1024)(128)(2,1)}, bf16[163840]{0:T(1024)(128)(2,1)S(1)}, u32[]{:S(2)}, u32[]{:S(2)}) %collective-permute-start) | collective-permute-done | bytes 327712 | tf_op jit(solution)/shard_map/ppermute | solution.py:18
  26.3 2.0 %gather_fusion.6 = bf16[16,128,512]{2,1,0:T(8,128)(2,1)} fusion(bf16[5,128,512]{2,1,0:T(8,128)(2,1)S(1)} %constant_dynamic-update-slice_fusion.6, s32[1024]{0:T(1024)S(1)} %get-tuple-element.13), kind=kCustom, calls=%fused_computation.6 | custom fusion | bytes 4194368 | tf_op jit(solution)/shard_map/gather | solution.py:179
  29.9 2.0 %gather_fusion.2 = bf16[16,128,512]{2,1,0:T(8,128)(2,1)} fusion(bf16[5,128,512]{2,1,0:T(8,128)(2,1)S(1)} %bitcast.80, s32[1024]{0:T(1024)S(1)} %get-tuple-element.13), kind=kCustom, calls=%fused_computation.2 | custom fusion | bytes 4194368 | tf_op jit(solution)/shard_map/gather | solution.py:178
  34.7 2.5 %gather_fusion.1 = bf16[24,128,384]{2,1,0:T(8,128)(2,1)S(1)} fusion(bf16[16,128,384]{2,1,0:T(8,128)(2,1)} %constant_dynamic-update-slice_fusion.1, s32[1024]{0:T(1024)S(1)} %get-tuple-element.14), kind=kCustom, calls=%fused_computation.1 | custom fusion | bytes 4718688 | tf_op jit(solution)/shard_map/gather | solution.py:164
  39.0 2.0 %add_convert_fusion = (bf16[1024,384]{1,0:T(8,128)(2,1)S(1)}, f32[1024,384]{1,0:T(8,128)}) fusion(bf16[1024,384]{1,0:T(8,128)(2,1)S(1)} %copy-done.4, f32[1024,384]{1,0:T(8,128)S(1)} %copy-done.9, bf16[1024,384]{1,0:T(8,128)(2,1)S(1)} %bitcast.89, bf16[384,384]{1,0:T(8,128)(2,1)S(1)} %copy-done.21), kind=kOutput, calls=%fused_computation.14 | convolution fusion | flops 305135616 | bytes 5799936 | tf_op jit(solution)/shard_map/dot_general | solution.py:170
  43.3 3.3 %fusion.8 = bf16[8,128,256]{2,1,0:T(8,128)(2,1)S(1)} fusion(s32[8,128]{1,0:T(8,128)S(1)} %bitcast.93, bf16[8,128,512]{2,1,0:T(8,128)(2,1)} %bitcast.81, bf16[8,256,512]{2,1,0:T(8,128)(2,1)S(1)} %bitcast.77), kind=kOutput, calls=%fused_computation.28 | convolution fusion | flops 270535168 | bytes 3674112 | tf_op jit(solution)/shard_map/div | solution.py:185
  52.4 2.1 %multiply_convert_fusion = bf16[8,256,512]{2,1,0:T(8,128)(2,1)} fusion(bf16[8,128,256]{2,1,0:T(8,128)(2,1)S(1)} %fusion.8, bf16[8,128,512]{2,1,0:T(8,128)(2,1)S(1)} %bitcast.82), kind=kOutput, calls=%fused_computation.10 | convolution fusion | flops 270532608 | bytes 3670016 | tf_op jit(solution)/shard_map/bij,bie->bje/dot_general | solution.py:198
  55.8 1.9 %gather_fusion.4 = f32[384,384]{1,0:T(8,128)S(1)} fusion(f32[384,384]{1,0:T(8,128)S(1)} %copy.25, s32[1024]{0:T(1024)S(1)} %get-tuple-element.12), kind=kCustom, calls=%fused_computation.4 | custom fusion | bytes 1181184 | tf_op jit(solution)/shard_map/gather | solution.py:97
  64.2 3.5 %fusion.25 = f32[512,512]{1,0:T(8,128)S(1)} fusion(bf16[2048,512]{1,0:T(8,128)(2,1)} %bitcast.85, bf16[2048,512]{1,0:T(8,128)(2,1)} %bitcast.86), kind=kOutput, calls=%fused_computation.85 | convolution fusion | flops 1073741824 | bytes 5242880 | tf_op jit(solution)/shard_map/dot_general | solution.py:204
  72.7 2.9 %collective-permute-start.4 = (bf16[32,11776]{1,0:T(8,128)(2,1)S(1)}, bf16[32,11776]{1,0:T(8,128)(2,1)S(1)}, u32[]{:S(2)}, u32[]{:S(2)}) collective-permute-start(bf16[32,11776]{1,0:T(8,128)(2,1)S(1)} %fusion.9), channel_id=1, source_target_pairs={{0,1},{1,0},{2,3},{3,2},{4,5},{5,4},{6,7},{7,6},{8,9},{9,8},{10,11... | collective-permute-start | bytes 2261000 | tf_op jit(solution)/shard_map/ppermute | solution.py:23
  75.8 1.7 %collective-permute-done.4 = bf16[32,11776]{1,0:T(8,128)(2,1)S(1)} collective-permute-done((bf16[32,11776]{1,0:T(8,128)(2,1)S(1)}, bf16[32,11776]{1,0:T(8,128)(2,1)S(1)}, u32[]{:S(2)}, u32[]{:S(2)}) %collective-permute-start.4) | collective-permute-done | bytes 753696 | tf_op jit(solution)/shard_map/ppermute | solution.py:23
  79.1 9.9 %collective-permute-start.5 = (bf16[8,11776]{1,0:T(8,128)(2,1)S(1)}, bf16[8,11776]{1,0:T(8,128)(2,1)S(1)}, u32[]{:S(2)}, u32[]{:S(2)}) collective-permute-start(bf16[8,11776]{1,0:T(8,128)(2,1)S(1)} %get-tuple-element.4), channel_id=1, source_target_pairs={{0,2},{1,3},{2,4},{3,5},{4,6},{5,7},{6,0},{7,1},{8,10},{9,11},{10,... | collective-permute-start | bytes 565256 | tf_op jit(solution)/shard_map/ppermute | solution.py:89
  89.0 1.9 %collective-permute-start.7 = (bf16[8,11776]{1,0:T(8,128)(2,1)S(1)}, bf16[8,11776]{1,0:T(8,128)(2,1)S(1)}, u32[]{:S(2)}, u32[]{:S(2)}) collective-permute-start(bf16[8,11776]{1,0:T(8,128)(2,1)S(1)} %get-tuple-element.5), channel_id=1, source_target_pairs={{0,6},{1,7},{2,0},{3,1},{4,2},{5,3},{6,4},{7,5},{8,14},{9,15},{10,... | collective-permute-start | bytes 565256 | tf_op jit(solution)/shard_map/ppermute | solution.py:89
  90.9 3.4 %collective-permute-start.6 = (bf16[8,11776]{1,0:T(8,128)(2,1)S(1)}, bf16[8,11776]{1,0:T(8,128)(2,1)S(1)}, u32[]{:S(2)}, u32[]{:S(2)}) collective-permute-start(bf16[8,11776]{1,0:T(8,128)(2,1)S(1)} %get-tuple-element.6), channel_id=1, source_target_pairs={{0,4},{1,5},{2,6},{3,7},{4,0},{5,1},{6,2},{7,3},{8,12},{9,13},{10,... | collective-permute-start | bytes 565256 | tf_op jit(solution)/shard_map/ppermute | solution.py:89
  94.3 8.3 %collective-permute-done.7 = bf16[8,11776]{1,0:T(8,128)(2,1)S(1)} collective-permute-done((bf16[8,11776]{1,0:T(8,128)(2,1)S(1)}, bf16[8,11776]{1,0:T(8,128)(2,1)S(1)}, u32[]{:S(2)}, u32[]{:S(2)}) %collective-permute-start.7) | collective-permute-done | bytes 188448 | tf_op jit(solution)/shard_map/ppermute | solution.py:89
  102.8 1.9 %collective-permute-start.8 = (bf16[4,11776]{1,0:T(4,128)(2,1)S(1)}, bf16[4,11776]{1,0:T(4,128)(2,1)S(1)}, u32[]{:S(2)}, u32[]{:S(2)}) collective-permute-start(bf16[4,11776]{1,0:T(4,128)(2,1)S(1)} %fusion.15), channel_id=1, source_target_pairs={{0,8},{1,57},{2,10},{3,59},{4,12},{5,61},{6,14},{7,63},{8,0},{9,17... | collective-permute-start | bytes 282632 | tf_op jit(solution)/shard_map/ppermute | solution.py:120
  104.8 4.5 %collective-permute-done.8 = bf16[4,11776]{1,0:T(4,128)(2,1)S(1)} collective-permute-done((bf16[4,11776]{1,0:T(4,128)(2,1)S(1)}, bf16[4,11776]{1,0:T(4,128)(2,1)S(1)}, u32[]{:S(2)}, u32[]{:S(2)}) %collective-permute-start.8) | collective-permute-done | bytes 94240 | tf_op jit(solution)/shard_map/ppermute | solution.py:120
  109.6 1.9 %collective-permute-start.9 = (bf16[2,11776]{1,0:T(2,128)(2,1)S(1)}, bf16[2,11776]{1,0:T(2,128)(2,1)S(1)}, u32[]{:S(2)}, u32[]{:S(2)}) collective-permute-start(bf16[2,11776]{1,0:T(2,128)(2,1)S(1)} %fusion.16), channel_id=1, source_target_pairs={{0,16},{1,49},{2,18},{3,51},{4,20},{5,53},{6,22},{7,55},{8,24},{9,... | collective-permute-start | bytes 141320 | tf_op jit(solution)/shard_map/ppermute | solution.py:120
  111.5 4.9 %collective-permute-done.9 = bf16[2,11776]{1,0:T(2,128)(2,1)S(1)} collective-permute-done((bf16[2,11776]{1,0:T(2,128)(2,1)S(1)}, bf16[2,11776]{1,0:T(2,128)(2,1)S(1)}, u32[]{:S(2)}, u32[]{:S(2)}) %collective-permute-start.9) | collective-permute-done | bytes 47136 | tf_op jit(solution)/shard_map/ppermute | solution.py:120
  116.6 5.0 %collective-permute-start.10 = (f32[1,11776]{1,0:T(1,128)S(1)}, f32[1,11776]{1,0:T(1,128)S(1)}, u32[]{:S(2)}, u32[]{:S(2)}) collective-permute-start(f32[1,11776]{1,0:T(1,128)S(1)} %constant_dynamic-slice_fusion), channel_id=1, source_target_pairs={{0,32},{1,33},{2,34},{3,35},{4,36},{5,37},{6,38},{7,39},{8,40},{9,... | collective-permute-start | bytes 141320 | tf_op jit(solution)/shard_map/ppermute | solution.py:122
  121.6 5.2 %collective-permute-done.10 = f32[1,11776]{1,0:T(1,128)S(1)} collective-permute-done((f32[1,11776]{1,0:T(1,128)S(1)}, f32[1,11776]{1,0:T(1,128)S(1)}, u32[]{:S(2)}, u32[]{:S(2)}) %collective-permute-start.10) | collective-permute-done | bytes 47136 | tf_op jit(solution)/shard_map/ppermute | solution.py:122
  126.9 10.9 %collective-permute-start.11 = (f32[11776]{0:T(1024)S(1)}, f32[11776]{0:T(1024)S(1)}, u32[]{:S(2)}, u32[]{:S(2)}) collective-permute-start(f32[11776]{0:T(1024)S(1)} %add_reduce_fusion), channel_id=1, source_target_pairs={{0,256},{64,320},{128,384},{192,448},{256,0},{320,64},{384,128},{4... | collective-permute-start | bytes 141320 | tf_op jit(solution)/shard_map/ppermute | solution.py:23
  137.8 2.1 %collective-permute-done.11 = f32[11776]{0:T(1024)S(1)} collective-permute-done((f32[11776]{0:T(1024)S(1)}, f32[11776]{0:T(1024)S(1)}, u32[]{:S(2)}, u32[]{:S(2)}) %collective-permute-start.11) | collective-permute-done | bytes 47136 | tf_op jit(solution)/shard_map/ppermute | solution.py:23
  139.9 4.8 %collective-permute-start.12 = (f32[11776]{0:T(1024)S(1)}, f32[11776]{0:T(1024)S(1)}, u32[]{:S(2)}, u32[]{:S(2)}) collective-permute-start(f32[11776]{0:T(1024)S(1)} %add.205), channel_id=1, source_target_pairs={{0,128},{64,192},{128,0},{192,64},{256,384},{320,448},{384,256},{4... | collective-permute-start | bytes 141320 | tf_op jit(solution)/shard_map/ppermute | solution.py:23
  144.8 2.1 %collective-permute-done.12 = f32[11776]{0:T(1024)S(1)} collective-permute-done((f32[11776]{0:T(1024)S(1)}, f32[11776]{0:T(1024)S(1)}, u32[]{:S(2)}, u32[]{:S(2)}) %collective-permute-start.12) | collective-permute-done | bytes 47136 | tf_op jit(solution)/shard_map/ppermute | solution.py:23
  146.9 3.4 %collective-permute-start.13 = (f32[11776]{0:T(1024)S(1)}, f32[11776]{0:T(1024)S(1)}, u32[]{:S(2)}, u32[]{:S(2)}) collective-permute-start(f32[11776]{0:T(1024)S(1)} %add.206), channel_id=1, source_target_pairs={{0,64},{64,0},{128,192},{192,128},{256,320},{320,256},{384,448},{4... | collective-permute-start | bytes 141320 | tf_op jit(solution)/shard_map/ppermute | solution.py:23
  150.2 2.6 %collective-permute-done.13 = f32[11776]{0:T(1024)S(1)} collective-permute-done((f32[11776]{0:T(1024)S(1)}, f32[11776]{0:T(1024)S(1)}, u32[]{:S(2)}, u32[]{:S(2)}) %collective-permute-start.13) | collective-permute-done | bytes 47136 | tf_op jit(solution)/shard_map/ppermute | solution.py:23
  (135 shorter events, 40.2 us)
Async XLA Ops:
  0.6 36.6 %copy-start = (bf16[8,3,128,128]{3,2,1,0:T(8,128)(2,1)S(1)}, bf16[8,3,128,128]{3,2,1,0:T(8,128)(2,1)}, u32[]{:S(2)}) copy-start(bf16[8,3,128,128]{3,2,1,0:T(8,128)(2,1)} %param.16) | copy-start | bytes 2359300
  0.6 17.0 %copy-start.3 = (bf16[1024,384]{1,0:T(8,128)(2,1)S(1)}, bf16[1024,384]{1,0:T(8,128)(2,1)}, u32[]{:S(2)}) copy-start(bf16[1024,384]{1,0:T(8,128)(2,1)} %param.15) | copy-start | bytes 2359300
  0.7 18.0 %copy-start.20 = (s32[8,2]{0,1:T(2,128)S(1)}, s32[8,2]{0,1:T(2,128)}, u32[]{:S(2)}) copy-start(s32[8,2]{0,1:T(2,128)} %param.19) | copy-start | bytes 196
  0.7 18.0 %copy-start.17 = (s32[8,3]{0,1:T(4,128)S(1)}, s32[8,3]{0,1:T(4,128)}, u32[]{:S(2)}) copy-start(s32[8,3]{0,1:T(4,128)} %param.17) | copy-start | bytes 292
  5.6 16.2 %collective-permute-start.3 = (bf16[163840]{0:T(1024)(128)(2,1)}, bf16[163840]{0:T(1024)(128)(2,1)S(1)}, u32[]{:S(2)}, u32[]{:S(2)}) collective-permute-start(bf16[163840]{0:T(1024)(128)(2,1)} %constant_dynamic-update-slice_fusion.14), channel_id=1, source_target_pairs={{0,62},{1,63},{2,0},{3,1},{4,2},{5,3},{6,4},{7,5},{8,6},{9,7},{10,... | collective-permute-start | bytes 983048 | tf_op jit(solution)/shard_map/ppermute | solution.py:18
  8.3 13.7 %collective-permute-start.2 = (bf16[163840]{0:T(1024)(128)(2,1)}, bf16[163840]{0:T(1024)(128)(2,1)S(1)}, u32[]{:S(2)}, u32[]{:S(2)}) collective-permute-start(bf16[163840]{0:T(1024)(128)(2,1)} %constant_dynamic-update-slice_fusion.14), channel_id=1, source_target_pairs={{0,63},{1,0},{2,1},{3,2},{4,3},{5,4},{6,5},{7,6},{8,7},{9,8},{10,9... | collective-permute-start | bytes 983048 | tf_op jit(solution)/shard_map/ppermute | solution.py:18
  10.3 13.5 %collective-permute-start.1 = (bf16[163840]{0:T(1024)(128)(2,1)}, bf16[163840]{0:T(1024)(128)(2,1)S(1)}, u32[]{:S(2)}, u32[]{:S(2)}) collective-permute-start(bf16[163840]{0:T(1024)(128)(2,1)} %constant_dynamic-update-slice_fusion.14), channel_id=1, source_target_pairs={{0,2},{1,3},{2,4},{3,5},{4,6},{5,7},{6,8},{7,9},{8,10},{9,11},{10,... | collective-permute-start | bytes 983048 | tf_op jit(solution)/shard_map/ppermute | solution.py:18
  15.5 10.5 %collective-permute-start = (bf16[163840]{0:T(1024)(128)(2,1)}, bf16[163840]{0:T(1024)(128)(2,1)S(1)}, u32[]{:S(2)}, u32[]{:S(2)}) collective-permute-start(bf16[163840]{0:T(1024)(128)(2,1)} %constant_dynamic-update-slice_fusion.14), channel_id=1, source_target_pairs={{0,1},{1,2},{2,3},{3,4},{4,5},{5,6},{6,7},{7,8},{8,9},{9,10},{10,1... | collective-permute-start | bytes 983048 | tf_op jit(solution)/shard_map/ppermute | solution.py:18
  17.6 4.1 %copy-start.18 = (s32[512]{0:T(512)S(1)}, s32[512]{0:T(512)}, u32[]{:S(2)}) copy-start(s32[512]{0:T(512)} %constant.164) | copy-start | bytes 6148
  17.7 4.1 %copy-start.19 = (s32[384]{0:T(512)S(1)}, s32[384]{0:T(512)}, u32[]{:S(2)}) copy-start(s32[384]{0:T(512)} %constant.161) | copy-start | bytes 4612
  17.7 4.1 %copy-start.14 = (bf16[128,512]{1,0:T(8,128)(2,1)S(1)}, bf16[128,512]{1,0:T(8,128)(2,1)}, u32[]{:S(2)}) copy-start(bf16[128,512]{1,0:T(8,128)(2,1)} %param.21) | copy-start | bytes 393220
  37.2 1.6 %copy-start.9 = (f32[1024,384]{1,0:T(8,128)S(1)}, f32[1024,384]{1,0:T(8,128)}, u32[]{:S(2)}) copy-start(f32[1024,384]{1,0:T(8,128)} %fusion.22) | copy-start | bytes 4718596
  37.3 1.8 %copy-start.21 = (bf16[384,384]{1,0:T(8,128)(2,1)S(1)}, bf16[384,384]{1,0:T(8,128)(2,1)}, u32[]{:S(2)}) copy-start(bf16[384,384]{1,0:T(8,128)(2,1)} %param.22) | copy-start | bytes 884740
  38.0 3.1 %copy-start.12 = (bf16[8,384,128]{1,2,0:T(8,128)(2,1)}, bf16[8,384,128]{1,2,0:T(8,128)(2,1)S(1)}, u32[]{:S(2)}) copy-start(bf16[8,384,128]{1,2,0:T(8,128)(2,1)S(1)} %bitcast_convert_fusion) | copy-start | bytes 2359300
  39.0 2.0 %copy-start.15 = (bf16[384,512]{1,0:T(8,128)(2,1)S(1)}, bf16[384,512]{1,0:T(8,128)(2,1)}, u32[]{:S(2)}) copy-start(bf16[384,512]{1,0:T(8,128)(2,1)} %param.24) | copy-start | bytes 1179652
  41.1 1.7 %copy-start.10 = (bf16[1024,384]{1,0:T(8,128)(2,1)}, bf16[1024,384]{1,0:T(8,128)(2,1)S(1)}, u32[]{:S(2)}) copy-start(bf16[1024,384]{1,0:T(8,128)(2,1)S(1)} %get-tuple-element.9) | copy-start | bytes 2359300
  41.1 2.3 %copy-start.1 = (bf16[16,128,512]{2,1,0:T(8,128)(2,1)S(1)}, bf16[16,128,512]{2,1,0:T(8,128)(2,1)}, u32[]{:S(2)}) copy-start(bf16[16,128,512]{2,1,0:T(8,128)(2,1)} %gather_fusion.2) | copy-start | bytes 6291460
  41.1 2.3 %copy-start.22 = (s32[1024]{0:T(1024)S(1)}, s32[1024]{0:T(1024)}, u32[]{:S(2)}) copy-start(s32[1024]{0:T(1024)} %param.20) | copy-start | bytes 12292
  47.1 1.6 %copy-start.23 = (f32[1024,384]{1,0:T(8,128)S(1)}, f32[1024,384]{1,0:T(8,128)}, u32[]{:S(2)}) copy-start(f32[1024,384]{1,0:T(8,128)} %get-tuple-element.10) | copy-start | bytes 4718596
  49.8 2.6 %copy-start.2 = (bf16[1024,512]{1,0:T(8,128)(2,1)S(1)}, bf16[1024,512]{1,0:T(8,128)(2,1)}, u32[]{:S(2)}) copy-start(bf16[1024,512]{1,0:T(8,128)(2,1)} %convolution_convert_fusion) | copy-start | bytes 3145732
  69.3 1.4 copy-start.8
  71.0 1.6 %copy-start.7 = (f32[2,32,11776]{2,1,0:T(8,128)}, f32[2,32,11776]{2,1,0:T(8,128)S(1)}, u32[]{:S(2)}) copy-start(f32[2,32,11776]{2,1,0:T(8,128)S(1)} %constant_dynamic-update-slice_fusion.10) | copy-start | bytes 9043972
  72.7 4.8 %collective-permute-start.4 = (bf16[32,11776]{1,0:T(8,128)(2,1)S(1)}, bf16[32,11776]{1,0:T(8,128)(2,1)S(1)}, u32[]{:S(2)}, u32[]{:S(2)}) collective-permute-start(bf16[32,11776]{1,0:T(8,128)(2,1)S(1)} %fusion.9), channel_id=1, source_target_pairs={{0,1},{1,0},{2,3},{3,2},{4,5},{5,4},{6,7},{7,6},{8,9},{9,8},{10,11... | collective-permute-start | bytes 2261000 | tf_op jit(solution)/shard_map/ppermute | solution.py:23
  79.1 15.2 %collective-permute-start.5 = (bf16[8,11776]{1,0:T(8,128)(2,1)S(1)}, bf16[8,11776]{1,0:T(8,128)(2,1)S(1)}, u32[]{:S(2)}, u32[]{:S(2)}) collective-permute-start(bf16[8,11776]{1,0:T(8,128)(2,1)S(1)} %get-tuple-element.4), channel_id=1, source_target_pairs={{0,2},{1,3},{2,4},{3,5},{4,6},{5,7},{6,0},{7,1},{8,10},{9,11},{10,... | collective-permute-start | bytes 565256 | tf_op jit(solution)/shard_map/ppermute | solution.py:89
  89.0 13.6 %collective-permute-start.7 = (bf16[8,11776]{1,0:T(8,128)(2,1)S(1)}, bf16[8,11776]{1,0:T(8,128)(2,1)S(1)}, u32[]{:S(2)}, u32[]{:S(2)}) collective-permute-start(bf16[8,11776]{1,0:T(8,128)(2,1)S(1)} %get-tuple-element.5), channel_id=1, source_target_pairs={{0,6},{1,7},{2,0},{3,1},{4,2},{5,3},{6,4},{7,5},{8,14},{9,15},{10,... | collective-permute-start | bytes 565256 | tf_op jit(solution)/shard_map/ppermute | solution.py:89
  90.9 11.7 %collective-permute-start.6 = (bf16[8,11776]{1,0:T(8,128)(2,1)S(1)}, bf16[8,11776]{1,0:T(8,128)(2,1)S(1)}, u32[]{:S(2)}, u32[]{:S(2)}) collective-permute-start(bf16[8,11776]{1,0:T(8,128)(2,1)S(1)} %get-tuple-element.6), channel_id=1, source_target_pairs={{0,4},{1,5},{2,6},{3,7},{4,0},{5,1},{6,2},{7,3},{8,12},{9,13},{10,... | collective-permute-start | bytes 565256 | tf_op jit(solution)/shard_map/ppermute | solution.py:89
  102.8 6.5 %collective-permute-start.8 = (bf16[4,11776]{1,0:T(4,128)(2,1)S(1)}, bf16[4,11776]{1,0:T(4,128)(2,1)S(1)}, u32[]{:S(2)}, u32[]{:S(2)}) collective-permute-start(bf16[4,11776]{1,0:T(4,128)(2,1)S(1)} %fusion.15), channel_id=1, source_target_pairs={{0,8},{1,57},{2,10},{3,59},{4,12},{5,61},{6,14},{7,63},{8,0},{9,17... | collective-permute-start | bytes 282632 | tf_op jit(solution)/shard_map/ppermute | solution.py:120
  109.6 6.9 %collective-permute-start.9 = (bf16[2,11776]{1,0:T(2,128)(2,1)S(1)}, bf16[2,11776]{1,0:T(2,128)(2,1)S(1)}, u32[]{:S(2)}, u32[]{:S(2)}) collective-permute-start(bf16[2,11776]{1,0:T(2,128)(2,1)S(1)} %fusion.16), channel_id=1, source_target_pairs={{0,16},{1,49},{2,18},{3,51},{4,20},{5,53},{6,22},{7,55},{8,24},{9,... | collective-permute-start | bytes 141320 | tf_op jit(solution)/shard_map/ppermute | solution.py:120
  116.6 10.2 %collective-permute-start.10 = (f32[1,11776]{1,0:T(1,128)S(1)}, f32[1,11776]{1,0:T(1,128)S(1)}, u32[]{:S(2)}, u32[]{:S(2)}) collective-permute-start(f32[1,11776]{1,0:T(1,128)S(1)} %constant_dynamic-slice_fusion), channel_id=1, source_target_pairs={{0,32},{1,33},{2,34},{3,35},{4,36},{5,37},{6,38},{7,39},{8,40},{9,... | collective-permute-start | bytes 141320 | tf_op jit(solution)/shard_map/ppermute | solution.py:122
  126.9 13.0 %collective-permute-start.11 = (f32[11776]{0:T(1024)S(1)}, f32[11776]{0:T(1024)S(1)}, u32[]{:S(2)}, u32[]{:S(2)}) collective-permute-start(f32[11776]{0:T(1024)S(1)} %add_reduce_fusion), channel_id=1, source_target_pairs={{0,256},{64,320},{128,384},{192,448},{256,0},{320,64},{384,128},{4... | collective-permute-start | bytes 141320 | tf_op jit(solution)/shard_map/ppermute | solution.py:23
  139.9 6.9 %collective-permute-start.12 = (f32[11776]{0:T(1024)S(1)}, f32[11776]{0:T(1024)S(1)}, u32[]{:S(2)}, u32[]{:S(2)}) collective-permute-start(f32[11776]{0:T(1024)S(1)} %add.205), channel_id=1, source_target_pairs={{0,128},{64,192},{128,0},{192,64},{256,384},{320,448},{384,256},{4... | collective-permute-start | bytes 141320 | tf_op jit(solution)/shard_map/ppermute | solution.py:23
  146.9 6.0 %collective-permute-start.13 = (f32[11776]{0:T(1024)S(1)}, f32[11776]{0:T(1024)S(1)}, u32[]{:S(2)}, u32[]{:S(2)}) collective-permute-start(f32[11776]{0:T(1024)S(1)} %add.206), channel_id=1, source_target_pairs={{0,64},{64,0},{128,192},{192,128},{256,320},{320,256},{384,448},{4... | collective-permute-start | bytes 141320 | tf_op jit(solution)/shard_map/ppermute | solution.py:23
  (6 other events, 7.2 us)
